TPU v7x, 32 devices: a whole 2x2x4 slice. The times are simulated.
32 devices in a mesh: gx: 8 (over z, y), gy: 4 (over x, core).
Axes of the slice: x: 2, y: 2, z: 4, core: 2. Of those that a mesh axis runs over, the one named last changes fastest.
Arguments:
- queries: bfloat16 [8, 768, 2560], P('gx', 'gy'), may hold values from -7 to 7
- new_kv: bfloat16 [8, 768, 512], P('gx', 'gy'), may hold values from -7 to 7
- cache_pool: bfloat16 [8, 2048, 512], P('gx', 'gy'), may hold values from -6 to 6
- lengths: int32 [8], P('gx'), may hold values from 0 to 32768, as said below
- owner: int32 [8, 4], P('gx'), may hold values from 0 to 3, each once within a row
- w_out: bfloat16 [2560, 2560], P(None, ('gx', 'gy')), may hold values from -0.125 to 0.125
- last_residual: bfloat16 [8, 2560], P(None, ('gx', 'gy')), may hold values from -6 to 6
- norm_gain: bfloat16 [2560], replicated, may hold values from 0.5 to 1.5
- head: bfloat16 [256000, 2560], P(('gx', 'gy')), may hold values from -11 to 11
- targets: int32 [8], replicated, may hold values from 0 to 255999
Outputs:
- mixed_out: bfloat16 [8, 768, 2560], P('gx', 'gy')
- new_cache: bfloat16 [8, 2048, 512], P('gx', 'gy')
- log_norm: float32 [8], replicated
- top_logit: float32 [8], replicated
- target_logprob: float32 [8], replicated
Inputs may be any that keep to these rules, and one draw needn't show every extreme that they name: `lengths`: in every draw one request has seen 32768 tokens and one has seen none. `owner`: each row names every block index once.
All inputs are finite; a program needn't handle non-finite values.
Results may differ from a plain program's by a relative error of at most 0.0042.
Values may be sent and summed in bfloat16 or wider, within the bound.
No kernel may reach another device: no remote copies, remote signals or barrier semaphores. Data moves between devices by JAX's collectives and lax.ppermute only.
A program may use at most 128 MiB of HBM per device.

v0:
```python
import math

import jax
import jax.numpy as jnp
from jax import lax
from jax.sharding import PartitionSpec as P


def on_device(
    queries, new_kv, cache_pool, lengths, owner, w_out, last_residual, norm_gain, head, targets
):
    req_local, new_local, model_cols = queries.shape
    slot_count = cache_pool.shape[1]
    entry_width = new_kv.shape[2]
    head_dim = entry_width // 2
    head_count = model_cols // head_dim
    group_pos = lax.axis_size("gy")
    my_index = lax.axis_index("gy")
    new_total = new_local * group_pos
    window_len = slot_count * group_pos
    keep_len = window_len - new_total
    score_scale = 1.0 / math.sqrt(head_dim)
    query_heads = queries.reshape(req_local, new_local, head_count, head_dim)
    query_pos = my_index * new_local + jnp.arange(new_local, dtype=jnp.int32)
    first_slot = window_len - lengths
    block_ids = jnp.arange(group_pos, dtype=jnp.int32)
    matches = owner[:, :, None] == block_ids[None, None, :]
    logical = jnp.sum(jnp.where(matches, block_ids[None, :, None], 0), axis=1)
    own_block = lax.dynamic_index_in_dim(logical, my_index, axis=1, keepdims=False)
    slot_ids = jnp.arange(slot_count, dtype=jnp.int32)
    new_ids = jnp.arange(new_local, dtype=jnp.int32)
    target_slot = own_block[:, None] * slot_count + slot_ids[None, :]
    from_old = target_slot < keep_len
    old_slot = jnp.minimum(target_slot + new_total, window_len - 1)
    old_block = jnp.take_along_axis(owner, old_slot // slot_count, axis=1)
    pool_row = old_block * slot_count + old_slot % slot_count
    new_row = jnp.maximum(target_slot - keep_len, 0)
    source_cache = jnp.where(from_old, pool_row, -1)
    source_new = jnp.where(from_old, -1, new_row)

    def cache_keys(shard_ids):
        chosen = jnp.take(logical, shard_ids, axis=1)
        slot_pos = (chosen[:, :, None] * slot_count + slot_ids[None, None, :]).reshape(
            req_local, -1
        )
        return (slot_pos[:, None, :] >= query_pos[None, :, None]) & (
            slot_pos[:, None, :] >= first_slot[:, None, None]
        )

    def new_keys(shard_ids):
        positions = (shard_ids[:, None] * new_local + new_ids[None, :]).reshape(-1)
        seen_new = positions[None, :] <= query_pos[:, None]
        return seen_new[None]

    def attend(carried, key_rows, visible):
        running_max, weight_sum, accumulated = carried
        scores = (
            jnp.einsum(
                "rthd,rnd->rthn",
                query_heads,
                key_rows[:, :, :head_dim],
                preferred_element_type=jnp.float32,
            )
            * score_scale
        )
        allowed = visible[:, :, None, :]
        block_max = jnp.max(jnp.where(allowed, scores, -1e30), axis=3)
        new_max = jnp.maximum(running_max, block_max)
        weights = jnp.where(allowed, jnp.exp(scores - new_max[..., None]), 0.0)
        rescale = jnp.exp(running_max - new_max)
        weight_sum = rescale * weight_sum + jnp.sum(weights, axis=3)
        accumulated = rescale[..., None] * accumulated + jnp.einsum(
            "rthn,rnd->rthd",
            weights.astype(jnp.bfloat16),
            key_rows[:, :, head_dim:],
            preferred_element_type=jnp.float32,
        )
        return (new_max, weight_sum, accumulated)

    def copy_rows(fresh_block, part_rows, source, base_row):
        local_row = source - base_row
        inside = (local_row >= 0) & (local_row < part_rows.shape[1])
        clipped = jnp.clip(local_row, 0, part_rows.shape[1] - 1)
        picked = jnp.take_along_axis(part_rows, clipped[:, :, None], axis=1)
        return jnp.where(inside[:, :, None], picked, fresh_block)

    def make_step(shard_width, source, layout_kind, carried, shard_rows):
        shard_count = shard_rows.shape[1] // shard_width
        group_size = math.gcd(shard_count, 4)

        def turn_body(turn_index, inner_state):
            offset = turn_index * group_size * shard_width
            part_rows = lax.dynamic_slice_in_dim(shard_rows, offset, group_size * shard_width, 1)
            shard_ids = turn_index * group_size + jnp.arange(group_size, dtype=jnp.int32)
            if layout_kind == "cache":
                key_rows = part_rows
                visible = cache_keys(shard_ids)
            else:
                key_rows = part_rows
                visible = new_keys(shard_ids)
            softmax_state = lax.cond(
                jnp.any(visible),
                lambda state: attend(state, key_rows, visible),
                lambda state: state,
                inner_state[:3],
            )
            fresh_block = copy_rows(inner_state[3], part_rows, source, offset)
            return softmax_state + (fresh_block,)

        return lax.fori_loop(0, shard_count // group_size, turn_body, carried)

    initial = (
        jnp.full((req_local, new_local, head_count), -1e30, jnp.float32),
        jnp.zeros((req_local, new_local, head_count), jnp.float32),
        jnp.zeros((req_local, new_local, head_count, head_dim), jnp.float32),
        jnp.zeros((req_local, slot_count, entry_width), jnp.bfloat16),
    )
    carried = make_step(
        slot_count,
        source_cache,
        "cache",
        initial,
        lax.all_gather(cache_pool, "gy", axis=1, tiled=True),
    )
    carried = make_step(
        new_local, source_new, "new", carried, lax.all_gather(new_kv, "gy", axis=1, tiled=True)
    )
    running_max, weight_sum, accumulated, fresh_block = carried
    mixed_out = (
        (accumulated / weight_sum[..., None])
        .astype(jnp.bfloat16)
        .reshape(req_local, new_local, model_cols)
    )
    last_local = mixed_out[:, new_local - 1, :]
    group_req = lax.axis_size("gx")
    holder = (my_index == group_pos - 1).astype(jnp.float32)
    padded = jnp.zeros((req_local * group_req, model_cols), jnp.float32)
    padded = lax.dynamic_update_slice_in_dim(
        padded, last_local.astype(jnp.float32) * holder, lax.axis_index("gx") * req_local, 0
    )
    last_mixed = lax.psum(padded, ("gx", "gy")).astype(jnp.bfloat16)
    last_hidden = (
        last_residual.astype(jnp.float32)
        + jnp.dot(last_mixed, w_out, preferred_element_type=jnp.float32)
    ).astype(jnp.bfloat16)
    full_hidden = lax.all_gather(last_hidden, ("gx", "gy"), axis=1, tiled=True).astype(jnp.float32)
    normed = (
        full_hidden
        * lax.rsqrt(jnp.mean(full_hidden * full_hidden, axis=1, keepdims=True) + 1e-06)
        * norm_gain.astype(jnp.float32)
    ).astype(jnp.bfloat16)
    logits = lax.dot_general(
        normed, head, (((1,), (1,)), ((), ())), preferred_element_type=jnp.float32
    )
    vocab_local = head.shape[0]
    local_target = targets - lax.axis_index(("gx", "gy")) * vocab_local
    target_hit = jnp.arange(vocab_local, dtype=jnp.int32)[None, :] == local_target[:, None]
    picked = jnp.sum(jnp.where(target_hit, logits, 0.0), axis=1)
    local_top = jnp.max(logits, axis=1)
    top_logit = lax.pmax(local_top, ("gx", "gy"))
    exp_total, picked = lax.psum(
        (jnp.sum(jnp.exp(logits - top_logit[:, None]), axis=1), picked), ("gx", "gy")
    )
    log_norm = top_logit + jnp.log(exp_total)
    return (mixed_out, fresh_block, log_norm, top_logit, picked - log_norm)


def solution(mesh):
    placed = (
        P("gx", "gy", None),
        P("gx", "gy", None),
        P("gx", "gy", None),
        P("gx"),
        P("gx", None),
        P(None, ("gx", "gy")),
        P(None, ("gx", "gy")),
        P(),
        P(("gx", "gy"), None),
        P(),
    )
    return jax.shard_map(
        on_device,
        mesh=mesh,
        in_specs=placed,
        out_specs=(P("gx", "gy", None), P("gx", "gy", None), P(), P(), P()),
        check_vma=False,
    )
```

profile of v0, /device:TPU:0, one launch (start us, length us, event | category | flops | bytes accessed | tf_op | source)
XLA Modules:
  0.0 262.6 jit_solution(15581894182387955175)
XLA Ops:
  8.6 1.5 copy.34
  17.0 1.5 fusion.55
  18.4 2.6 compare_select_fusion
  21.1 14.6 %all_gather.10 = bf16[1,768,512]{2,1,0:T(8,128)(2,1)S(1)} all-gather(bf16[1,192,512]{2,1,0:T(8,128)(2,1)} %param.15), channel_id=1, replica_groups=mesh['gx'=8,'gy'=4] {'gy'}, dimensions={1}, use_global_device_ids=true | all-gather | bytes 983040 | tf_op jit(solution)/shard_map/all_gather | solution.py:126
  35.7 2.6 gather_fusion.1
  38.3 1.4 broadcast_in_dim.173
  40.3 2.6 compare_select_fusion.3
  44.7 15.8 %conditional.2 = ((f32[1,192,10]{1,2,0:T(8,128)S(1)}, f32[1,192,10]{1,2,0:T(8,128)S(1)}, f32[1,192,10,256]{3,1,2,0:T(8,128)})) conditional(s32[]{:T(128)} %convert_element_type.54, (f32[1,192,10]{1,2,0:T(8,128)S(1)}, f32[1,192,10]{1,2,0:T(8,128)S(1)}, f32[1,192,10,256]{3,1,2,0:T(8,128)}) %tuple.31, (pred[1,192,2048]{2,1,0:T(8,128)(4,1)S(1)}, ...), branch_computations={%region_3.4_spmd, %region_4.7_spmd} | conditional | flops 4070774272 | bytes 63906876 | solution.py:101
  44.7 5.7 %select_reduce_fusion = (f32[192,10]{0,1:T(8,128)S(1)}, f32[192,10,2048]{2,0,1:T(8,128)S(1)}) fusion(pred[192,2048]{1,0:T(8,128)(4,1)S(1)} %bitcast.103, bf16[1,2048,512]{2,1,0:T(8,128)(2,1)} %get-tuple-element.118, bf16[1,192,10,256]{1,3,2,0:T(8,128)(2,1)S(1)} %get-tuple-element.209), kind=kOutput, calls=%fused_computation.4 | convolution fusion | flops 2025060480 | bytes 18161152 | tf_op jit(solution)/shard_map/while/body/eval_jaxpr/cond/branch_1_fun/rthd,rnd->rthn/dot_general | solution.py:58
  50.4 5.4 %bitcast_add_fusion = f32[1,192,10,256]{3,1,2,0:T(8,128)} fusion(f32[1,192,10,256]{3,1,2,0:T(8,128)} %get-tuple-element.120, f32[192,10,2048]{2,0,1:T(8,128)S(1)} %get-tuple-element.243, f32[192,10]{0,1:T(8,128)S(1)} %bitcast.109, pred[192,2048]{1,0:T(8,128)(4,1)S(1)} %bitcast.104, bf16[1,2048,512]{2,1,0:T(8,128)(2,1)S(1)} %copy-done.2, ...), kind=kOutput, calls=%fused_computation.9 | convolution fusion | flops 2029977600 | bytes 21135360 | tf_op jit(solution)/shard_map/while/body/eval_jaxpr/cond/branch_1_fun/rthn,rnd->rthd/dot_general | solution.py:72
  55.8 4.7 %fusion.1 = f32[192,10]{0,1:T(8,128)S(1)} fusion(f32[192,10,2048]{2,0,1:T(8,128)S(1)} %get-tuple-element.243, f32[192,10]{0,1:T(8,128)S(1)} %bitcast.110, pred[192,2048]{1,0:T(8,128)(4,1)S(1)} %bitcast.105), kind=kLoop, calls=%fused_computation.6 | loop fusion | flops 15726720 | bytes 16137216 | tf_op jit(solution)/shard_map/while/body/eval_jaxpr/cond/branch_1_fun/reduce_sum | solution.py:71
  60.5 7.6 %conditional.3 = ((f32[1,192,10]{1,2,0:T(8,128)S(1)}, f32[1,192,10,256]{3,1,2,0:T(8,128)})) conditional(s32[]{:T(128)} %convert_element_type.53, (f32[1,192,10]{1,2,0:T(8,128)S(1)}, f32[1,192,10,256]{3,1,2,0:T(8,128)}) %tuple.33, (s32[768]{0:T(1024)S(1)}, s32[192]{0:T(256)S(1)}, bf16[1,192,10,256]{1,3,2,0:T(8,128)(2,1)S(1)}, ...), branch_computations={%region_7.8_spmd, %region_8.11_spmd} | conditional | flops 1527307776 | bytes 24442648 | solution.py:101
  60.6 1.7 select_reduce_fusion.1
  62.4 3.7 %bitcast_add_fusion.2 = f32[1,192,10,256]{3,1,2,0:T(8,128)} fusion(f32[1,192,10,256]{3,1,2,0:T(8,128)} %get-tuple-element.138, f32[192,10,768]{2,0,1:T(8,128)S(1)} %get-tuple-element.241, f32[192,10]{0,1:T(8,128)S(1)} %get-tuple-element.239, pred[192,768]{1,0:T(8,128)(4,1)S(1)} %broadcast_compare_fusion, f32[192,10]{0,1:T(8,128)S(1)} %get-tuple-element.238, ...), kind=kOutput, calls=%fused_computation.31 | convolution fusion | flops 761856000 | bytes 10403840 | tf_op jit(solution)/shard_map/while/body/eval_jaxpr/cond/branch_1_fun/rthn,rnd->rthd/dot_general | solution.py:72
  66.1 1.7 fusion.17
  68.1 1.9 divide_convert_fusion
  70.6 1.4 copy.39
  72.8 41.4 %psum.21 = bf16[8,2560]{1,0:T(8,128)(2,1)S(1)} all-reduce(f32[8,2560]{1,0:T(8,128)S(1)} %dynamic_update_slice.3), channel_id=1, replica_groups=mesh['gx'=8,'gy'=4] {'gx','gy'}, use_global_device_ids=true, to_apply=%region_11.12 | all-reduce | flops 20480 | bytes 122880 | tf_op jit(solution)/shard_map/psum | solution.py:141
  114.5 40.6 %all-gather = bf16[32,80,8]{1,2,0:T(8,128)(2,1)S(1)} all-gather(bf16[1,80,8]{1,2,0:T(8,128)(2,1)S(1)} %fusion.37), channel_id=1, replica_groups=mesh['gx'=8,'gy'=4] {'gx','gy'}, dimensions={0}, use_global_device_ids=true | all-gather | bytes 42240 | tf_op jit(solution)/shard_map/all_gather | solution.py:146
  155.4 17.4 %fusion.56 = (f32[8]{0:T(128)S(1)}, f32[8,8000]{1,0:T(8,128)S(1)}) fusion(bf16[8000,2560]{1,0:T(8,128)(2,1)} %param.22, f32[2560,8]{0,1:T(8,128)S(1)} %reshape.940, f32[2560]{0:T(1024)S(1)} %convert_element_type.62, f32[8]{0:T(128)S(1)} %add_rsqrt_fusion), kind=kOutput, calls=%fused_computation.123 | convolution fusion | flops 327805440 | bytes 41308224 | tf_op jit(solution)/shard_map/dot_general | solution.py:152
  172.7 36.9 %pmax.7 = f32[8]{0:T(128)S(1)} all-reduce(f32[8]{0:T(128)S(1)} %get-tuple-element.250), channel_id=1, replica_groups=mesh['gx'=8,'gy'=4] {'gx','gy'}, use_global_device_ids=true, to_apply=%region_14.15 | all-reduce | flops 8 | bytes 64 | tf_op jit(solution)/shard_map/pmax | solution.py:160
  209.9 41.2 %all-reduce = (f32[8]{0:T(128)S(1)}, f32[8]{0:T(128)S(1)}) all-reduce(f32[8]{0:T(128)S(1)} %get-tuple-element.227, f32[8]{0:T(128)S(1)} %get-tuple-element.226), channel_id=1, replica_groups=mesh['gx'=8,'gy'=4] {'gx','gy'}, use_global_device_ids=true, to_apply=%region_16.17 | all-reduce | flops 16 | bytes 128 | tf_op jit(solution)/shard_map/psum | solution.py:161
  251.7 2.1 gather_fusion.2
  253.8 1.9 fusion.39
  (60 shorter events, 10.9 us)
Async XLA Ops:
  7.2 107.1 %copy-start = (bf16[2560,80]{0,1:T(8,128)(2,1)S(1)}, bf16[2560,80]{0,1:T(8,128)(2,1)}, u32[]{:S(2)}) copy-start(bf16[2560,80]{0,1:T(8,128)(2,1)} %param.19) | copy-start | bytes 1228804
  7.2 36.3 %copy-start.6 = (s32[8]{0:T(128)S(1)}, s32[8]{0:T(128)}, u32[]{:S(2)}) copy-start(s32[8]{0:T(128)} %param.23) | copy-start | bytes 100
  7.2 37.5 %all-gather.3.cloned.1.call-start = ((), (), s32[]{:S(2)}) async-start(), calls=%async_computation | async-start | bytes 2621440 | tf_op jit(solution)/shard_map/all_gather | solution.py:123
  44.7 5.7 %copy-start.2 = (bf16[1,2048,512]{2,1,0:T(8,128)(2,1)S(1)}, bf16[1,2048,512]{2,1,0:T(8,128)(2,1)}, u32[]{:S(2)}) copy-start(bf16[1,2048,512]{2,1,0:T(8,128)(2,1)} %get-tuple-element.118) | copy-start | bytes 6291460 | tf_op jit(solution)/shard_map/while/body/eval_jaxpr/cond
  68.1 46.2 %copy-start.4 = (bf16[8,80]{1,0:T(8,128)(2,1)S(1)}, bf16[8,80]{1,0:T(8,128)(2,1)}, u32[]{:S(2)}) copy-start(bf16[8,80]{1,0:T(8,128)(2,1)} %param.20) | copy-start | bytes 3844
  155.3 96.3 %copy-start.1 = (bf16[1,2048,512]{2,1,0:T(8,128)(2,1)S(1)}, bf16[1,2048,512]{2,1,0:T(8,128)(2,1)}, u32[]{:S(2)}) copy-start(bf16[1,2048,512]{2,1,0:T(8,128)(2,1)} %all-gather.3.cloned.1.call-done) | copy-start | bytes 6291460
  155.3 98.4 %copy-start.3 = (bf16[512,512]{1,0:T(8,128)(2,1)S(1)}, bf16[512,512]{1,0:T(8,128)(2,1)}, u32[]{:S(2)}) copy-start(bf16[512,512]{1,0:T(8,128)(2,1)} %gather_fusion.1) | copy-start | bytes 1572868
  209.7 42.0 %copy-start.5 = (f32[8]{0:T(128)}, f32[8]{0:T(128)S(1)}, u32[]{:S(2)}) copy-start(f32[8]{0:T(128)S(1)} %pmax.7) | copy-start | bytes 100
Sparse Core Ops, SparseCore 0:
  9.6 29.4 all-gather.2
where the time goes:
time: 263 us
  blocking collectives  175 us (67%)
  matrix products  34.1 us (13%)
  other arithmetic  23 us (9%)
  between operations  16.9 us (6%)
  local copies, waits for them, and re-layouts  12.9 us (5%)
    psum x1, blocking collectives, on_device(): last_mixed = lax.psum(padded, ('gx', 'gy')).astype(jnp.bfloat16)  41.4 us
    psum x1, blocking collectives, on_device(): lax.psum((jnp.sum(jnp.exp(logits - top_logit[:, None]), axis=1), picked),...  41.2 us
    all_gather x1, blocking collectives, on_device(): lax.all_gather(last_hidden, ('gx', 'gy'), axis=1, tiled=True)  40.6 us
    pmax x1, blocking collectives, on_device(): top_logit = lax.pmax(local_top, ('gx', 'gy'))  36.9 us
    dot_general x1, matrix products, on_device(): lax.dot_general(normed, head, (((1,), (1,)), ((), ())), preferred_element...  17.4 us
    all_gather x1, blocking collectives, on_device(): lax.all_gather(new_kv, 'gy', axis=1, tiled=True)  14.6 us
    dot_general x2, matrix products, attend(): jnp.einsum('rthn,rnd->rthd', weights.astype(jnp.bfloat16), key_rows[:, :,...  9.09 us
    dot_general x2, matrix products, attend(): jnp.einsum('rthd,rnd->rthn', query_heads, key_rows[:, :, :head_dim], pref...  7.42 us
  transfers between devices with their start and end apart: 1, of which 0 were waited for; matrix products, arithmetic and copies ran while one was open for 7% of the time, Pallas kernels for 0%

commit v1 on v0

--- a/solution.py
+++ b/solution.py
@@ -4,6 +4,65 @@
 import jax.numpy as jnp
 from jax import lax
 from jax.sharding import PartitionSpec as P
+
+
+def xor_pairs(count, bit):
+    return [(i, i ^ bit) for i in range(count)]
+
+
+def is_pow2(count):
+    return count & (count - 1) == 0
+
+
+def butterfly_sum(x, axis):
+    count = lax.axis_size(axis)
+    if not is_pow2(count):
+        return lax.psum(x, axis)
+    bit = 1
+    while bit < count:
+        x = x + lax.ppermute(x, axis, xor_pairs(count, bit))
+        bit *= 2
+    return x
+
+
+def butterfly_gather(x, axis, dim):
+    count = lax.axis_size(axis)
+    if not is_pow2(count):
+        return lax.all_gather(x, axis, axis=dim, tiled=True)
+    index = lax.axis_index(axis)
+    bit = 1
+    while bit < count:
+        other = lax.ppermute(x, axis, xor_pairs(count, bit))
+        low = (index & bit) == 0
+        x = jnp.where(
+            low, jnp.concatenate([x, other], dim), jnp.concatenate([other, x], dim)
+        )
+        bit *= 2
+    return x
+
+
+def combine_stats(top, total, picked, top_o, total_o, picked_o):
+    best = jnp.maximum(top, top_o)
+    total = total * jnp.exp(top - best) + total_o * jnp.exp(top_o - best)
+    return best, total, picked + picked_o
+
+
+def butterfly_stats(top, total, picked):
+    for axis in ("gy", "gx"):
+        count = lax.axis_size(axis)
+        if not is_pow2(count):
+            tops = lax.all_gather(top, axis)
+            best = jnp.max(tops, axis=0)
+            total = jnp.sum(lax.all_gather(total, axis) * jnp.exp(tops - best), axis=0)
+            top, picked = best, lax.psum(picked, axis)
+            continue
+        bit = 1
+        while bit < count:
+            packed = jnp.stack([top, total, picked])
+            other = lax.ppermute(packed, axis, xor_pairs(count, bit))
+            top, total, picked = combine_stats(top, total, picked, other[0], other[1], other[2])
+            bit *= 2
+    return top, total, picked
 
 
 def on_device(
@@ -133,17 +192,16 @@
     )
     last_local = mixed_out[:, new_local - 1, :]
     group_req = lax.axis_size("gx")
-    holder = (my_index == group_pos - 1).astype(jnp.float32)
-    padded = jnp.zeros((req_local * group_req, model_cols), jnp.float32)
-    padded = lax.dynamic_update_slice_in_dim(
-        padded, last_local.astype(jnp.float32) * holder, lax.axis_index("gx") * req_local, 0
-    )
-    last_mixed = lax.psum(padded, ("gx", "gy")).astype(jnp.bfloat16)
+    holder = my_index == group_pos - 1
+    last_local = jnp.where(holder, last_local, jnp.zeros_like(last_local))
+    last_mixed = butterfly_gather(butterfly_sum(last_local, "gy"), "gx", 0)
     last_hidden = (
         last_residual.astype(jnp.float32)
         + jnp.dot(last_mixed, w_out, preferred_element_type=jnp.float32)
     ).astype(jnp.bfloat16)
-    full_hidden = lax.all_gather(last_hidden, ("gx", "gy"), axis=1, tiled=True).astype(jnp.float32)
+    full_hidden = butterfly_gather(butterfly_gather(last_hidden, "gy", 1), "gx", 1).astype(
+        jnp.float32
+    )
     normed = (
         full_hidden
         * lax.rsqrt(jnp.mean(full_hidden * full_hidden, axis=1, keepdims=True) + 1e-06)
@@ -157,10 +215,8 @@
     target_hit = jnp.arange(vocab_local, dtype=jnp.int32)[None, :] == local_target[:, None]
     picked = jnp.sum(jnp.where(target_hit, logits, 0.0), axis=1)
     local_top = jnp.max(logits, axis=1)
-    top_logit = lax.pmax(local_top, ("gx", "gy"))
-    exp_total, picked = lax.psum(
-        (jnp.sum(jnp.exp(logits - top_logit[:, None]), axis=1), picked), ("gx", "gy")
-    )
+    local_total = jnp.sum(jnp.exp(logits - local_top[:, None]), axis=1)
+    top_logit, exp_total, picked = butterfly_stats(local_top, local_total, picked)
     log_norm = top_logit + jnp.log(exp_total)
     return (mixed_out, fresh_block, log_norm, top_logit, picked - log_norm)
 

time: 263 us -> 143 us (0.54)
  blocking collectives: 175 us -> 14 us
  waiting for transfers between devices: 0.68 us -> 23.1 us
  starting transfers between devices: 0.04 us -> 17.9 us
    psum x2 -> x0, blocking collectives: 82.6 us -> none  [the longest x1 41.4 us: on_device(): last_mixed = lax.psum(padded, ('gx', 'gy')).astype(jnp.bfloat16)]
    all_gather x1 -> x0, blocking collectives: 40.6 us -> none  [on_device(): lax.all_gather(last_hidden, ('gx', 'gy'), axis=1, tiled=True)]
    pmax x1 -> x0, blocking collectives: 36.9 us -> none  [on_device(): top_logit = lax.pmax(local_top, ('gx', 'gy'))]
    ppermute x0 -> x15, starting transfers between devices: none -> 17.9 us  [the longest x8 11.5 us: butterfly_gather(): other = lax.ppermute(x, axis, xor_pairs(count, bit))]
    ppermute x0 -> x15, waiting for transfers between devices: none -> 14.4 us  [the longest x8 8.69 us: butterfly_gather(): other = lax.ppermute(x, axis, xor_pairs(count, bit))]
    all_gather x1, waiting for transfers between devices: 0.01 us -> 7.93 us  [on_device(): lax.all_gather(cache_pool, 'gy', axis=1, tiled=True)]
    dot_general x2, matrix products: 9.09 us -> 5.61 us  [attend(): jnp.einsum('rthn,rnd->rthd', weights.astype(jnp.bfloat16), key_rows[:, :,...]
  transfers between devices with their start and end apart: 1 -> 16, of which waited for: 0 -> 13; matrix products, arithmetic and copies ran while one was open for 7% -> 18% of each run, Pallas kernels for 0% -> 0%
where the time goes in v1:
time: 143 us; the launch traced here: 142 us
  matrix products  32.3 us (23%)
  other arithmetic  24.4 us (17%)
  waiting for transfers between devices  23.1 us (16%)
  starting transfers between devices  17.9 us (13%)
  between operations  17 us (12%)
  blocking collectives  14 us (10%)
  local copies, waits for them, and re-layouts  13.5 us (9%)
    dot_general x1, matrix products, on_device(): lax.dot_general(normed, head, (((1,), (1,)), ((), ())), preferred_element...  17.2 us
    all_gather x1, blocking collectives, on_device(): lax.all_gather(new_kv, 'gy', axis=1, tiled=True)  14 us
    ppermute x8, starting transfers between devices, butterfly_gather(): other = lax.ppermute(x, axis, xor_pairs(count, bit))  11.5 us
    dot_general x2, matrix products, attend(): jnp.einsum('rthd,rnd->rthn', query_heads, key_rows[:, :, :head_dim], pref...  9.22 us
    ppermute x8, waiting for transfers between devices, butterfly_gather(): other = lax.ppermute(x, axis, xor_pairs(count, bit))  8.69 us
    all_gather x1, waiting for transfers between devices, on_device(): lax.all_gather(cache_pool, 'gy', axis=1, tiled=True)  7.93 us
    reduce_sum x2, other arithmetic, attend(): weight_sum = rescale * weight_sum + jnp.sum(weights, axis=3)  6.45 us
    dot_general x2, matrix products, attend(): jnp.einsum('rthn,rnd->rthd', weights.astype(jnp.bfloat16), key_rows[:, :,...  5.61 us
  transfers between devices with their start and end apart: 16, of which 13 were waited for; matrix products, arithmetic and copies ran while one was open for 18% of the time, Pallas kernels for 0%

profile of v1, /device:TPU:0, one launch (start us, length us, event | category | flops | bytes accessed | tf_op | source)
XLA Modules:
  0.0 142.4 jit_solution(11402589868878103821)
XLA Ops:
  8.6 2.4 %copy.26 = bf16[1,192,2560]{1,2,0:T(8,128)(2,1)} copy(bf16[1,192,2560]{2,1,0:T(8,128)(2,1)} %param.14) | data formatting | bytes 1966080 | tf_op args[0]
  16.7 14.0 %all_gather.7 = bf16[1,768,512]{2,1,0:T(8,128)(2,1)S(1)} all-gather(bf16[1,192,512]{2,1,0:T(8,128)(2,1)S(1)} %copy-done.5), channel_id=1, replica_groups=mesh['gx'=8,'gy'=4] {'gy'}, dimensions={1}, use_global_device_ids=true | all-gather | bytes 983040 | tf_op jit(solution)/shard_map/all_gather | solution.py:185
  30.7 7.9 %all-gather.2.cloned.1.call-done = bf16[1,2048,512]{2,1,0:T(8,128)(2,1)} async-done(((bf16[1,512,512]{2,1,0:T(8,128)(2,1)}), bf16[1,2048,512]{2,1,0:T(8,128)(2,1)}) %all-gather.2.cloned.1.call-update) | async-done | bytes 2097168 | tf_op jit(solution)/shard_map/all_gather | solution.py:182
  38.6 14.4 %conditional.2 = ((f32[1,192,10]{1,2,0:T(8,128)S(1)}, f32[1,192,10]{1,2,0:T(8,128)S(1)}, f32[1,192,10,256]{3,1,2,0:T(8,128)S(1)})) conditional(s32[]{:T(128)} %convert_element_type.36, (f32[1,192,10]{1,2,0:T(8,128)S(1)}, f32[1,192,10]{1,2,0:T(8,128)S(1)}, f32[1,192,10,256]{3,1,2,0:T(8,128)S(1)}) %tuple.31, (pred[1,192,2048]{2,1,0:T(8,128)(4,1)}, ...), branch_computations={%region_3.4_spmd, %region_4.7_spmd} | conditional | flops 4070774272 | bytes 65807448 | solution.py:160
  38.6 6.2 %select_reduce_fusion = (f32[192,10]{0,1:T(8,128)S(1)}, f32[192,10,2048]{2,0,1:T(8,128)S(1)}) fusion(pred[192,2048]{1,0:T(8,128)(4,1)} %bitcast.230, bf16[1,2048,512]{2,1,0:T(8,128)(2,1)} %get-tuple-element.118, bf16[1,192,10,256]{1,3,2,0:T(8,128)(2,1)} %get-tuple-element.191), kind=kOutput, calls=%fused_computation.4 | convolution fusion | flops 2025060480 | bytes 18488832 | tf_op jit(solution)/shard_map/while/body/eval_jaxpr/cond/branch_1_fun/rthd,rnd->rthn/dot_general | solution.py:117
  44.9 3.4 %bitcast_add_fusion = f32[1,192,10,256]{3,1,2,0:T(8,128)S(1)} fusion(f32[1,192,10,256]{3,1,2,0:T(8,128)S(1)} %get-tuple-element.120, f32[192,10,2048]{2,0,1:T(8,128)S(1)} %get-tuple-element.230, f32[192,10]{0,1:T(8,128)S(1)} %bitcast.236, pred[192,2048]{1,0:T(8,128)(4,1)S(1)} %bitcast.231, bf16[1,2048,512]{2,1,0:T(8,128)(2,1)S(1)} %copy-done.2, ...), kind=kOutput, calls=%fused_computation.9 | convolution fusion | flops 2029977600 | bytes 21135360 | tf_op jit(solution)/shard_map/while/body/eval_jaxpr/cond/branch_1_fun/rthn,rnd->rthd/dot_general | solution.py:131
  48.3 4.7 %fusion.1 = f32[192,10]{0,1:T(8,128)S(1)} fusion(f32[192,10,2048]{2,0,1:T(8,128)S(1)} %get-tuple-element.230, f32[192,10]{0,1:T(8,128)S(1)} %bitcast.237, pred[192,2048]{1,0:T(8,128)(4,1)S(1)} %bitcast.232), kind=kLoop, calls=%fused_computation.6 | loop fusion | flops 15726720 | bytes 16137216 | tf_op jit(solution)/shard_map/while/body/eval_jaxpr/cond/branch_1_fun/reduce_sum | solution.py:130
  53.0 7.4 %conditional.3 = ((f32[1,192,10]{1,2,0:T(8,128)S(1)}, f32[1,192,10,256]{3,1,2,0:T(8,128)S(1)})) conditional(s32[]{:T(128)} %convert_element_type.35, (f32[1,192,10]{1,2,0:T(8,128)S(1)}, f32[1,192,10,256]{3,1,2,0:T(8,128)S(1)}) %tuple.33, (s32[768]{0:T(1024)S(1)}, s32[192]{0:T(256)S(1)}, bf16[1,192,10,256]{1,3,2,0:T(8,128)(2,1)}, ...), branch_computations={%region_7.8_spmd, %region_8.11_spmd} | conditional | flops 1527307776 | bytes 24114968 | solution.py:160
  53.4 3.0 %select_reduce_fusion.1 = (f32[192,10]{0,1:T(8,128)S(1)}, f32[192,10,768]{2,0,1:T(8,128)S(1)}) fusion(pred[192,768]{1,0:T(8,128)(4,1)S(1)} %broadcast_compare_fusion, bf16[1,768,512]{2,1,0:T(8,128)(2,1)S(1)} %get-tuple-element.136, bf16[1,192,10,256]{1,3,2,0:T(8,128)(2,1)} %get-tuple-element.198), kind=kOutput, calls=%fused_computation.23 | convolution fusion | flops 759396480 | bytes 7429632 | tf_op jit(solution)/shard_map/while/body/eval_jaxpr/cond/branch_1_fun/rthd,rnd->rthn/dot_general | solution.py:117
  56.4 2.2 %bitcast_add_fusion.2 = f32[1,192,10,256]{3,1,2,0:T(8,128)S(1)} fusion(f32[1,192,10,256]{3,1,2,0:T(8,128)S(1)} %get-tuple-element.138, f32[192,10,768]{2,0,1:T(8,128)S(1)} %get-tuple-element.228, f32[192,10]{0,1:T(8,128)S(1)} %get-tuple-element.226, pred[192,768]{1,0:T(8,128)(4,1)S(1)} %broadcast_compare_fusion, f32[192,10]{0,1:T(8,128)S(1)} %get-tuple-element.225, ...), kind=kOutput, calls=%fused_computation.31 | convolution fusion | flops 761856000 | bytes 10403840 | tf_op jit(solution)/shard_map/while/body/eval_jaxpr/cond/branch_1_fun/rthn,rnd->rthd/dot_general | solution.py:131
  65.9 2.9 %collective-permute-done.1 = bf16[1,2560]{1,0:T(2,128)(2,1)S(1)} collective-permute-done((bf16[1,2560]{1,0:T(2,128)(2,1)S(1)}, bf16[1,2560]{1,0:T(2,128)(2,1)S(1)}, u32[]{:S(2)}, u32[]{:S(2)}) %collective-permute-start.1) | collective-permute-done | bytes 5152 | tf_op jit(solution)/shard_map/ppermute | solution.py:23
  74.2 2.6 %compare_select_fusion.3 = s32[512,1]{0,1:T(1,128)S(1)} fusion(s32[]{:T(128)} %bitcast.31, s32[]{:T(128)} %bitcast.32, s32[]{:T(128)} %bitcast.34, s32[]{:T(128)} %bitcast.33, s32[]{:T(128)} %bitcast.27), kind=kLoop, calls=%fused_computation.84 | loop fusion | flops 13824 | bytes 2068 | tf_op jit(solution)/shard_map/jit(take_along_axis)/gather | solution.py:94
  76.9 2.7 %collective-permute-start.4 = (bf16[4,2560]{1,0:T(4,128)(2,1)S(1)}, bf16[4,2560]{1,0:T(4,128)(2,1)S(1)}, u32[]{:S(2)}, u32[]{:S(2)}) collective-permute-start(bf16[4,2560]{1,0:T(4,128)(2,1)S(1)} %maximum_select_fusion.3), channel_id=1, source_target_pairs={{0,16},{4,20},{8,24},{12,28},{16,0},{20,4},{24,8},{28,12},{1,17},{... | collective-permute-start | bytes 61448 | tf_op jit(solution)/shard_map/ppermute | solution.py:35
  84.6 2.1 %collective-permute-done.6 = bf16[8,160]{1,0:T(8,128)(2,1)S(1)} collective-permute-done((bf16[8,160]{1,0:T(8,128)(2,1)S(1)}, bf16[8,160]{1,0:T(8,128)(2,1)S(1)}, u32[]{:S(2)}, u32[]{:S(2)}) %collective-permute-start.6) | collective-permute-done | bytes 2592 | tf_op jit(solution)/shard_map/ppermute | solution.py:35
  88.3 2.6 %compare_select_fusion = (s32[512,1]{0,1:T(1,128)S(1)}, s32[512,1]{0,1:T(1,128)S(1)}) fusion(s32[]{:T(128)} %bitcast.27, s32[]{:T(128)} %bitcast.34, s32[]{:T(128)} %bitcast.33, s32[]{:T(128)} %bitcast.32, s32[]{:T(128)} %bitcast.31), kind=kLoop, calls=%fused_computation.79 | loop fusion | flops 25600 | bytes 4116 | tf_op jit(solution)/shard_map/while/body/eval_jaxpr/jit(take_along_axis)/select_n | solution.py:143
  92.7 2.0 %collective-permute-done.8 = bf16[8,640]{1,0:T(8,128)(2,1)S(1)} collective-permute-done((bf16[8,640]{1,0:T(8,128)(2,1)S(1)}, bf16[8,640]{1,0:T(8,128)(2,1)S(1)}, u32[]{:S(2)}, u32[]{:S(2)}) %collective-permute-start.8) | collective-permute-done | bytes 10272 | tf_op jit(solution)/shard_map/ppermute | solution.py:35
  94.7 2.0 %collective-permute-start.9 = (bf16[8,1280]{1,0:T(8,128)(2,1)S(1)}, bf16[8,1280]{1,0:T(8,128)(2,1)S(1)}, u32[]{:S(2)}, u32[]{:S(2)}) collective-permute-start(bf16[8,1280]{1,0:T(8,128)(2,1)S(1)} %maximum_select_fusion.4), channel_id=1, source_target_pairs={{0,16},{4,20},{8,24},{12,28},{16,0},{20,4},{24,8},{28,12},{1,17},{... | collective-permute-start | bytes 61448 | tf_op jit(solution)/shard_map/ppermute | solution.py:35
  97.4 2.0 %collective-permute-done.9 = bf16[8,1280]{1,0:T(8,128)(2,1)S(1)} collective-permute-done((bf16[8,1280]{1,0:T(8,128)(2,1)S(1)}, bf16[8,1280]{1,0:T(8,128)(2,1)S(1)}, u32[]{:S(2)}, u32[]{:S(2)}) %collective-permute-start.9) | collective-permute-done | bytes 20512 | tf_op jit(solution)/shard_map/ppermute | solution.py:35
  99.6 17.2 %fusion.84 = (f32[8]{0:T(128)S(1)}, f32[8,8000]{1,0:T(8,128)S(1)}) fusion(bf16[8000,2560]{1,0:T(8,128)(2,1)} %param.22, f32[2560]{0:T(1024)S(1)} %convert_element_type.41, f32[8]{0:T(128)S(1)} %add_rsqrt_fusion, bf16[8,1280]{1,0:T(8,128)(2,1)S(1)} %maximum_select_fusion.4, bf16[8,1280]{1,0:T(8,128)(2,1)S(1)} %collective-permute-done.9, pred[]{:T(512)S(6)} %eq.60), kind=kOutput, calls=%fused_computation.194 | convolution fusion | flops 328010240 | bytes 41267264 | tf_op jit(solution)/shard_map/dot_general | solution.py:210
  120.1 2.9 %gather_fusion.1 = bf16[512,512]{1,0:T(8,128)(2,1)} fusion(bf16[768,512]{1,0:T(8,128)(2,1)S(1)} %bitcast.226, s32[1024]{0:T(1024)} %pad_clamp_fusion.1), kind=kCustom, calls=%fused_computation.1 | custom fusion | bytes 1050624 | tf_op jit(solution)/shard_map/while/body/eval_jaxpr/jit(take_along_axis)/gather | solution.py:143
  124.1 2.1 %gather_fusion.2 = bf16[512,512]{1,0:T(8,128)(2,1)S(1)} fusion(bf16[2048,512]{1,0:T(8,128)(2,1)S(1)} %bitcast.227, s32[1024]{0:T(1024)} %pad_clamp_fusion), kind=kCustom, calls=%fused_computation.2 | custom fusion | bytes 1050624 | tf_op jit(solution)/shard_map/while/body/eval_jaxpr/jit(take_along_axis)/gather | solution.py:143
  127.8 2.3 %fusion.39 = bf16[1,512,512]{2,1,0:T(8,128)(2,1)} fusion(bf16[512,512]{1,0:T(8,128)(2,1)S(1)} %gather_fusion.2, bf16[512,512]{1,0:T(8,128)(2,1)} %gather_fusion.1, pred[512]{0:T(512)(128)(4,1)} %compare_and_fusion.1, pred[512]{0:T(512)(128)(4,1)} %get-tuple-element.221, pred[512]{0:T(512)(128)(4,1)S(1)} %get-tuple-element.247, ...), kind=kLoop, calls=%fused_computation.55 | loop fusion | flops 1048576 | bytes 1574912 | tf_op jit(solution)/shard_map/while/body/eval_jaxpr/jit(_where)/select_n | solution.py:144
  130.4 2.1 %collective-permute-start.14 = (f32[3,8]{1,0:T(4,128)S(1)}, f32[3,8]{1,0:T(4,128)S(1)}, u32[]{:S(2)}, u32[]{:S(2)}) collective-permute-start(f32[3,8]{1,0:T(4,128)S(1)} %pad_maximum_fusion.4), channel_id=1, source_target_pairs={{0,16},{4,20},{8,24},{12,28},{16,0},{20,4},{24,8},{28,12},{1,17},{... | collective-permute-start | bytes 296 | tf_op jit(solution)/shard_map/ppermute | solution.py:62
  132.5 2.3 %copy.30 = bf16[1,192,2560]{2,1,0:T(8,128)(2,1)} copy(bf16[1,192,2560]{1,2,0:T(8,128)(2,1)} %bitcast.229) | data formatting | bytes 1966080
  (113 shorter events, 33.2 us)
Async XLA Ops:
  7.2 74.5 %copy-start = (bf16[2560,80]{0,1:T(8,128)(2,1)S(1)}, bf16[2560,80]{0,1:T(8,128)(2,1)}, u32[]{:S(2)}) copy-start(bf16[2560,80]{0,1:T(8,128)(2,1)} %param.19) | copy-start | bytes 1228804
  7.2 31.4 %all-gather.2.cloned.1.call-start = ((), (), s32[]{:S(2)}) async-start(), calls=%async_computation | async-start | bytes 2621440 | tf_op jit(solution)/shard_map/all_gather | solution.py:182
  60.4 9.9 %copy-start.10 = (s32[1,4]{1,0:T(1,128)S(1)}, s32[1,4]{1,0:T(1,128)}, u32[]{:S(2)}) copy-start(s32[1,4]{1,0:T(1,128)} %param.18) | copy-start | bytes 52
  60.4 21.2 %copy-start.12 = (bf16[8,80]{1,0:T(8,128)(2,1)S(1)}, bf16[8,80]{1,0:T(8,128)(2,1)}, u32[]{:S(2)}) copy-start(bf16[8,80]{1,0:T(8,128)(2,1)} %param.20) | copy-start | bytes 3844
  60.5 23.6 %copy-start.13 = (s32[8]{0:T(128)S(1)}, s32[8]{0:T(128)}, u32[]{:S(2)}) copy-start(s32[8]{0:T(128)} %param.23) | copy-start | bytes 100
  60.5 36.9 %copy-start.11 = (bf16[2560]{0:T(1024)(128)(2,1)S(1)}, bf16[2560]{0:T(1024)(128)(2,1)}, u32[]{:S(2)}) copy-start(bf16[2560]{0:T(1024)(128)(2,1)} %param.21) | copy-start | bytes 15364
  63.3 36.3 %copy-start.3 = (bf16[1,192,10,256]{1,3,2,0:T(8,128)(2,1)}, bf16[1,192,10,256]{1,3,2,0:T(8,128)(2,1)S(1)}, u32[]{:S(2)}) copy-start(bf16[1,192,10,256]{1,3,2,0:T(8,128)(2,1)S(1)} %copy.29) | copy-start | bytes 2949124
  63.8 1.2 collective-permute-start
  65.0 3.7 %collective-permute-start.1 = (bf16[1,2560]{1,0:T(2,128)(2,1)S(1)}, bf16[1,2560]{1,0:T(2,128)(2,1)S(1)}, u32[]{:S(2)}, u32[]{:S(2)}) collective-permute-start(bf16[1,2560]{1,0:T(2,128)(2,1)S(1)} %reshape_add_fusion), channel_id=1, source_target_pairs={{0,2},{1,3},{2,0},{3,1},{4,6},{5,7},{6,4},{7,5},{8,10},{9,11},{10,... | collective-permute-start | bytes 15368 | tf_op jit(solution)/shard_map/ppermute | solution.py:23
  68.8 3.7 %collective-permute-start.2 = (bf16[1,2560]{1,0:T(2,128)(2,1)S(1)}, bf16[1,2560]{1,0:T(2,128)(2,1)S(1)}, u32[]{:S(2)}, u32[]{:S(2)}) collective-permute-start(bf16[1,2560]{1,0:T(2,128)(2,1)S(1)} %add.886), channel_id=1, source_target_pairs={{0,4},{4,0},{8,12},{12,8},{16,20},{20,16},{24,28},{28,24},{1,5},{5... | collective-permute-start | bytes 15368 | tf_op jit(solution)/shard_map/ppermute | solution.py:35
  72.6 4.3 %collective-permute-start.3 = (bf16[2,2560]{1,0:T(2,128)(2,1)S(1)}, bf16[2,2560]{1,0:T(2,128)(2,1)S(1)}, u32[]{:S(2)}, u32[]{:S(2)}) collective-permute-start(bf16[2,2560]{1,0:T(2,128)(2,1)S(1)} %broadcast_select_fusion), channel_id=1, source_target_pairs={{0,8},{4,12},{8,0},{12,4},{16,24},{20,28},{24,16},{28,20},{1,9},{5... | collective-permute-start | bytes 30728 | tf_op jit(solution)/shard_map/ppermute | solution.py:35
  76.9 4.7 %collective-permute-start.4 = (bf16[4,2560]{1,0:T(4,128)(2,1)S(1)}, bf16[4,2560]{1,0:T(4,128)(2,1)S(1)}, u32[]{:S(2)}, u32[]{:S(2)}) collective-permute-start(bf16[4,2560]{1,0:T(4,128)(2,1)S(1)} %maximum_select_fusion.3), channel_id=1, source_target_pairs={{0,16},{4,20},{8,24},{12,28},{16,0},{20,4},{24,8},{28,12},{1,17},{... | collective-permute-start | bytes 61448 | tf_op jit(solution)/shard_map/ppermute | solution.py:35
  81.9 1.2 collective-permute-start.5
  83.1 3.6 %collective-permute-start.6 = (bf16[8,160]{1,0:T(8,128)(2,1)S(1)}, bf16[8,160]{1,0:T(8,128)(2,1)S(1)}, u32[]{:S(2)}, u32[]{:S(2)}) collective-permute-start(bf16[8,160]{1,0:T(8,128)(2,1)S(1)} %maximum_select_fusion.8), channel_id=1, source_target_pairs={{0,2},{1,3},{2,0},{3,1},{4,6},{5,7},{6,4},{7,5},{8,10},{9,11},{10,... | collective-permute-start | bytes 7688 | tf_op jit(solution)/shard_map/ppermute | solution.py:35
  86.8 4.2 %collective-permute-start.7 = (bf16[8,320]{1,0:T(8,128)(2,1)S(1)}, bf16[8,320]{1,0:T(8,128)(2,1)S(1)}, u32[]{:S(2)}, u32[]{:S(2)}) collective-permute-start(bf16[8,320]{1,0:T(8,128)(2,1)S(1)} %maximum_select_fusion.7), channel_id=1, source_target_pairs={{0,4},{4,0},{8,12},{12,8},{16,20},{20,16},{24,28},{28,24},{1,5},{5... | collective-permute-start | bytes 15368 | tf_op jit(solution)/shard_map/ppermute | solution.py:35
  91.1 3.7 %collective-permute-start.8 = (bf16[8,640]{1,0:T(8,128)(2,1)S(1)}, bf16[8,640]{1,0:T(8,128)(2,1)S(1)}, u32[]{:S(2)}, u32[]{:S(2)}) collective-permute-start(bf16[8,640]{1,0:T(8,128)(2,1)S(1)} %maximum_select_fusion.5), channel_id=1, source_target_pairs={{0,8},{4,12},{8,0},{12,4},{16,24},{20,28},{24,16},{28,20},{1,9},{5... | collective-permute-start | bytes 30728 | tf_op jit(solution)/shard_map/ppermute | solution.py:35
  94.7 4.7 %collective-permute-start.9 = (bf16[8,1280]{1,0:T(8,128)(2,1)S(1)}, bf16[8,1280]{1,0:T(8,128)(2,1)S(1)}, u32[]{:S(2)}, u32[]{:S(2)}) collective-permute-start(bf16[8,1280]{1,0:T(8,128)(2,1)S(1)} %maximum_select_fusion.4), channel_id=1, source_target_pairs={{0,16},{4,20},{8,24},{12,28},{16,0},{20,4},{24,8},{28,12},{1,17},{... | collective-permute-start | bytes 61448 | tf_op jit(solution)/shard_map/ppermute | solution.py:35
  117.9 1.2 collective-permute-start.10
  119.2 3.9 %collective-permute-start.11 = (f32[3,8]{1,0:T(4,128)S(1)}, f32[3,8]{1,0:T(4,128)S(1)}, u32[]{:S(2)}, u32[]{:S(2)}) collective-permute-start(f32[3,8]{1,0:T(4,128)S(1)} %pad_maximum_fusion.1), channel_id=1, source_target_pairs={{0,2},{1,3},{2,0},{3,1},{4,6},{5,7},{6,4},{7,5},{8,10},{9,11},{10,... | collective-permute-start | bytes 296 | tf_op jit(solution)/shard_map/ppermute | solution.py:62
  120.1 14.8 %copy-start.7 = (f32[8]{0:T(128)S(1)}, f32[8]{0:T(128)}, u32[]{:S(2)}) copy-start(f32[8]{0:T(128)} %copy-done.6) | copy-start | bytes 100
  120.1 14.8 %copy-start.9 = (f32[8]{0:T(128)S(1)}, f32[8]{0:T(128)}, u32[]{:S(2)}) copy-start(f32[8]{0:T(128)} %copy-done.8) | copy-start | bytes 100
  123.0 3.7 %collective-permute-start.12 = (f32[3,8]{1,0:T(4,128)S(1)}, f32[3,8]{1,0:T(4,128)S(1)}, u32[]{:S(2)}, u32[]{:S(2)}) collective-permute-start(f32[3,8]{1,0:T(4,128)S(1)} %pad_maximum_fusion.2), channel_id=1, source_target_pairs={{0,4},{4,0},{8,12},{12,8},{16,20},{20,16},{24,28},{28,24},{1,5},{5... | collective-permute-start | bytes 296 | tf_op jit(solution)/shard_map/ppermute | solution.py:62
  126.7 3.7 %collective-permute-start.13 = (f32[3,8]{1,0:T(4,128)S(1)}, f32[3,8]{1,0:T(4,128)S(1)}, u32[]{:S(2)}, u32[]{:S(2)}) collective-permute-start(f32[3,8]{1,0:T(4,128)S(1)} %pad_maximum_fusion.3), channel_id=1, source_target_pairs={{0,8},{4,12},{8,0},{12,4},{16,24},{20,28},{24,16},{28,20},{1,9},{5... | collective-permute-start | bytes 296 | tf_op jit(solution)/shard_map/ppermute | solution.py:62
  130.4 4.5 %collective-permute-start.14 = (f32[3,8]{1,0:T(4,128)S(1)}, f32[3,8]{1,0:T(4,128)S(1)}, u32[]{:S(2)}, u32[]{:S(2)}) collective-permute-start(f32[3,8]{1,0:T(4,128)S(1)} %pad_maximum_fusion.4), channel_id=1, source_target_pairs={{0,16},{4,20},{8,24},{12,28},{16,0},{20,4},{24,8},{28,12},{1,17},{... | collective-permute-start | bytes 296 | tf_op jit(solution)/shard_map/ppermute | solution.py:62
  (6 other events, 32.7 us)
Sparse Core Ops, SparseCore 0:
  9.6 29.0 all-gather.1

commit v2 on v1

v2 whole, which is shorter than its diff:
```python
import functools
import math

import jax
import jax.numpy as jnp
from jax import lax
from jax.experimental import pallas as pl
from jax.sharding import PartitionSpec as P


def xor_pairs(count, bit):
    return [(i, i ^ bit) for i in range(count)]


def is_pow2(count):
    return count & (count - 1) == 0


def butterfly_sum(x, axis):
    count = lax.axis_size(axis)
    if not is_pow2(count):
        return lax.psum(x, axis)
    bit = 1
    while bit < count:
        x = x + lax.ppermute(x, axis, xor_pairs(count, bit))
        bit *= 2
    return x


def butterfly_gather(x, axis, dim):
    count = lax.axis_size(axis)
    if not is_pow2(count):
        return lax.all_gather(x, axis, axis=dim, tiled=True)
    index = lax.axis_index(axis)
    bit = 1
    while bit < count:
        other = lax.ppermute(x, axis, xor_pairs(count, bit))
        low = (index & bit) == 0
        x = jnp.where(
            low, jnp.concatenate([x, other], dim), jnp.concatenate([other, x], dim)
        )
        bit *= 2
    return x


def combine_stats(top, total, picked, top_o, total_o, picked_o):
    best = jnp.maximum(top, top_o)
    total = total * jnp.exp(top - best) + total_o * jnp.exp(top_o - best)
    return best, total, picked + picked_o


def butterfly_stats(top, total, picked):
    for axis in ("gy", "gx"):
        count = lax.axis_size(axis)
        if not is_pow2(count):
            tops = lax.all_gather(top, axis)
            best = jnp.max(tops, axis=0)
            total = jnp.sum(lax.all_gather(total, axis) * jnp.exp(tops - best), axis=0)
            top, picked = best, lax.psum(picked, axis)
            continue
        bit = 1
        while bit < count:
            packed = jnp.stack([top, total, picked])
            other = lax.ppermute(packed, axis, xor_pairs(count, bit))
            top, total, picked = combine_stats(top, total, picked, other[0], other[1], other[2])
            bit *= 2
    return top, total, picked


def gather_order(count, bits):
    order = [[device] for device in range(count)]
    for bit in bits:
        order = [
            order[d] + order[d ^ bit] if d & bit == 0 else order[d ^ bit] + order[d]
            for d in range(count)
        ]
    return order[0]


def gather_blocks(x, axis, dim):
    count = lax.axis_size(axis)
    if not is_pow2(count):
        return lax.all_gather(x, axis, axis=dim, tiled=True), list(range(count))
    bits = []
    bit = count // 2
    while bit >= 1:
        bits.append(bit)
        bit //= 2
    index = lax.axis_index(axis)
    for bit in bits:
        other = lax.ppermute(x, axis, xor_pairs(count, bit))
        low = (index & bit) == 0
        x = jnp.where(
            low, jnp.concatenate([x, other], dim), jnp.concatenate([other, x], dim)
        )
    return x, gather_order(count, bits)


def attention_kernel(
    qpos_ref, cache_hi_ref, new_lo_ref, q_ref, kc_ref, vc_ref, kn_ref, vn_ref, out_ref, *, scale
):
    query = q_ref[0]
    dims = (((1,), (1,)), ((), ()))
    score_c = lax.dot_general(query, kc_ref[0], dims, preferred_element_type=jnp.float32) * scale
    score_n = lax.dot_general(query, kn_ref[0], dims, preferred_element_type=jnp.float32) * scale
    position = qpos_ref[...]
    seen_c = position <= cache_hi_ref[0]
    seen_n = new_lo_ref[0] <= position
    peak = jnp.maximum(
        jnp.max(jnp.where(seen_c, score_c, -jnp.inf), axis=1, keepdims=True),
        jnp.max(jnp.where(seen_n, score_n, -jnp.inf), axis=1, keepdims=True),
    )
    weight_c = jnp.where(seen_c, jnp.exp(score_c - peak), 0.0)
    weight_n = jnp.where(seen_n, jnp.exp(score_n - peak), 0.0)
    total = jnp.sum(weight_c, axis=1, keepdims=True) + jnp.sum(weight_n, axis=1, keepdims=True)
    mixed = jnp.dot(
        weight_c.astype(jnp.bfloat16), vc_ref[0], preferred_element_type=jnp.float32
    ) + jnp.dot(weight_n.astype(jnp.bfloat16), vn_ref[0], preferred_element_type=jnp.float32)
    out_ref[0] = (mixed / total).astype(out_ref.dtype)


def attend(queries, cache_keys, new_keys, query_pos, cache_hi, new_lo, head_dim):
    req_local, new_local, model_cols = queries.shape
    head_count = model_cols // head_dim
    cache_rows = cache_keys.shape[1]
    new_rows = new_keys.shape[1]
    kernel = functools.partial(attention_kernel, scale=1.0 / math.sqrt(head_dim))
    return pl.pallas_call(
        kernel,
        grid=(req_local, head_count),
        in_specs=[
            pl.BlockSpec((new_local, 1), lambda r, h: (0, 0)),
            pl.BlockSpec((1, 1, cache_rows), lambda r, h: (r, 0, 0)),
            pl.BlockSpec((1, 1, new_rows), lambda r, h: (r, 0, 0)),
            pl.BlockSpec((1, new_local, head_dim), lambda r, h: (r, 0, h)),
            pl.BlockSpec((1, cache_rows, head_dim), lambda r, h: (r, 0, 0)),
            pl.BlockSpec((1, cache_rows, head_dim), lambda r, h: (r, 0, 1)),
            pl.BlockSpec((1, new_rows, head_dim), lambda r, h: (r, 0, 0)),
            pl.BlockSpec((1, new_rows, head_dim), lambda r, h: (r, 0, 1)),
        ],
        out_specs=pl.BlockSpec((1, new_local, head_dim), lambda r, h: (r, 0, h)),
        out_shape=jax.ShapeDtypeStruct(queries.shape, queries.dtype),
    )(query_pos, cache_hi, new_lo, queries, cache_keys, cache_keys, new_keys, new_keys)


def on_device(
    queries, new_kv, cache_pool, lengths, owner, w_out, last_residual, norm_gain, head, targets
):
    req_local, new_local, model_cols = queries.shape
    slot_count = cache_pool.shape[1]
    entry_width = new_kv.shape[2]
    head_dim = entry_width // 2
    group_pos = lax.axis_size("gy")
    my_index = lax.axis_index("gy")
    new_total = new_local * group_pos
    window_len = slot_count * group_pos
    keep_len = window_len - new_total
    query_pos = (my_index * new_local + jnp.arange(new_local, dtype=jnp.int32))[:, None]
    first_slot = window_len - lengths
    block_ids = jnp.arange(group_pos, dtype=jnp.int32)
    matches = owner[:, :, None] == block_ids[None, None, :]
    logical = jnp.sum(jnp.where(matches, block_ids[None, :, None], 0), axis=1)
    own_block = lax.dynamic_index_in_dim(logical, my_index, axis=1, keepdims=False)

    cache_keys, cache_order = gather_blocks(cache_pool, "gy", 1)
    new_keys, new_order = gather_blocks(new_kv, "gy", 1)
    slot_ids = jnp.arange(slot_count, dtype=jnp.int32)
    new_ids = jnp.arange(new_local, dtype=jnp.int32)
    cache_stored = jnp.asarray(cache_order, jnp.int32)
    chosen = jnp.take(logical, cache_stored, axis=1)
    slot_pos = (chosen[:, :, None] * slot_count + slot_ids[None, None, :]).reshape(req_local, -1)
    cache_hi = jnp.where(slot_pos >= first_slot[:, None], slot_pos, -1)[:, None, :]
    new_pos = (jnp.asarray(new_order, jnp.int32)[:, None] * new_local + new_ids[None, :]).reshape(-1)
    new_lo = jnp.broadcast_to(new_pos[None, None, :], (req_local, 1, new_pos.shape[0]))
    mixed_out = attend(queries, cache_keys, new_keys, query_pos, cache_hi, new_lo, head_dim)

    cache_at = jnp.asarray([cache_order.index(s) for s in range(group_pos)], jnp.int32)
    new_at = jnp.asarray([new_order.index(c) for c in range(group_pos)], jnp.int32)
    target_slot = own_block[:, None] * slot_count + slot_ids[None, :]
    from_old = target_slot < keep_len
    old_slot = jnp.minimum(target_slot + new_total, window_len - 1)
    old_block = jnp.take_along_axis(owner, old_slot // slot_count, axis=1)
    cache_row = jnp.take(cache_at, old_block) * slot_count + old_slot % slot_count
    new_slot = jnp.maximum(target_slot - keep_len, 0)
    new_row = jnp.take(new_at, new_slot // new_local) * new_local + new_slot % new_local
    from_cache = jnp.take_along_axis(cache_keys, cache_row[:, :, None], axis=1)
    from_new = jnp.take_along_axis(new_keys, new_row[:, :, None], axis=1)
    fresh_block = jnp.where(from_old[:, :, None], from_cache, from_new)

    last_local = mixed_out[:, new_local - 1, :]
    group_req = lax.axis_size("gx")
    holder = my_index == group_pos - 1
    last_local = jnp.where(holder, last_local, jnp.zeros_like(last_local))
    last_mixed = butterfly_gather(butterfly_sum(last_local, "gy"), "gx", 0)
    last_hidden = (
        last_residual.astype(jnp.float32)
        + jnp.dot(last_mixed, w_out, preferred_element_type=jnp.float32)
    ).astype(jnp.bfloat16)
    full_hidden = butterfly_gather(butterfly_gather(last_hidden, "gy", 1), "gx", 1).astype(
        jnp.float32
    )
    normed = (
        full_hidden
        * lax.rsqrt(jnp.mean(full_hidden * full_hidden, axis=1, keepdims=True) + 1e-06)
        * norm_gain.astype(jnp.float32)
    ).astype(jnp.bfloat16)
    logits = lax.dot_general(
        normed, head, (((1,), (1,)), ((), ())), preferred_element_type=jnp.float32
    )
    vocab_local = head.shape[0]
    local_target = targets - lax.axis_index(("gx", "gy")) * vocab_local
    target_hit = jnp.arange(vocab_local, dtype=jnp.int32)[None, :] == local_target[:, None]
    picked = jnp.sum(jnp.where(target_hit, logits, 0.0), axis=1)
    local_top = jnp.max(logits, axis=1)
    local_total = jnp.sum(jnp.exp(logits - local_top[:, None]), axis=1)
    top_logit, exp_total, picked = butterfly_stats(local_top, local_total, picked)
    log_norm = top_logit + jnp.log(exp_total)
    return (mixed_out, fresh_block, log_norm, top_logit, picked - log_norm)


def solution(mesh):
    placed = (
        P("gx", "gy", None),
        P("gx", "gy", None),
        P("gx", "gy", None),
        P("gx"),
        P("gx", None),
        P(None, ("gx", "gy")),
        P(None, ("gx", "gy")),
        P(),
        P(("gx", "gy"), None),
        P(),
    )
    return jax.shard_map(
        on_device,
        mesh=mesh,
        in_specs=placed,
        out_specs=(P("gx", "gy", None), P("gx", "gy", None), P(), P(), P()),
        check_vma=False,
    )
```

time: 143 us -> 123 us (0.86)
  Pallas kernels: 0 us -> 22.6 us
  between operations: 17 us -> 2.15 us
  matrix products: 32.3 us -> 17.5 us
  blocking collectives: 14 us -> 0 us
  starting transfers between devices: 17.9 us -> 28.1 us
  other arithmetic: 24.4 us -> 17.9 us
  local copies, waits for them, and re-layouts: 13.5 us -> 7.9 us
  waiting for transfers between devices: 23.1 us -> 26.4 us
    pallas_call x0 -> x1, Pallas kernels: none -> 22.6 us  [attend(): pl.pallas_call(kernel, grid=(req_local, head_count), in_specs=[pl.BlockSp...]
    dot_general x4 -> x0, matrix products: 14.8 us -> none  [the longest x2 9.22 us: attend(): jnp.einsum('rthd,rnd->rthn', query_heads, key_rows[:, :, :head_dim], pref...]
    all_gather x1 -> x0, blocking collectives: 14 us -> none  [on_device(): lax.all_gather(new_kv, 'gy', axis=1, tiled=True)]
    ppermute x0 -> x4, waiting for transfers between devices: none -> 10.2 us  [gather_blocks(): other = lax.ppermute(x, axis, xor_pairs(count, bit))]
    all_gather x1 -> x0, waiting for transfers between devices: 7.93 us -> none  [on_device(): lax.all_gather(cache_pool, 'gy', axis=1, tiled=True)]
    select_n x2 -> x7, other arithmetic: 4.96 us -> 12.1 us  [the longest x4 6.71 us: gather_blocks(): jnp.where(low, jnp.concatenate([x, other], dim), jnp.concatenate([other,...]
    reduce_sum x2 -> x0, other arithmetic: 6.45 us -> none  [attend(): weight_sum = rescale * weight_sum + jnp.sum(weights, axis=3)]
    unnamed x28 -> x22, local copies, waits for them, and re-layouts: 4.78 us -> 0.05 us
  transfers between devices with their start and end apart: 16 -> 19, of which waited for: 13 -> 13; matrix products, arithmetic and copies ran while one was open for 18% -> 17% of each run, Pallas kernels for 0% -> 0%
where the time goes in v2:
time: 123 us
  starting transfers between devices  28.1 us (23%)
  waiting for transfers between devices  26.4 us (21%)
  Pallas kernels  22.6 us (18%)
  other arithmetic  17.9 us (15%)
  matrix products  17.5 us (14%)
  local copies, waits for them, and re-layouts  7.9 us (6%)
  between operations  2.15 us (2%)
    pallas_call x1, Pallas kernels, attend(): pl.pallas_call(kernel, grid=(req_local, head_count), in_specs=[pl.BlockSp...  22.6 us
    dot_general x1, matrix products, on_device(): lax.dot_general(normed, head, (((1,), (1,)), ((), ())), preferred_element...  17.3 us
    ppermute x8, starting transfers between devices, butterfly_gather(): other = lax.ppermute(x, axis, xor_pairs(count, bit))  15.2 us
    ppermute x8, waiting for transfers between devices, butterfly_gather(): other = lax.ppermute(x, axis, xor_pairs(count, bit))  10.3 us
    ppermute x4, waiting for transfers between devices, gather_blocks(): other = lax.ppermute(x, axis, xor_pairs(count, bit))  10.2 us
    ppermute x5, starting transfers between devices, butterfly_stats(): other = lax.ppermute(packed, axis, xor_pairs(count, bit))  7.06 us
    select_n x4, other arithmetic, gather_blocks(): jnp.where(low, jnp.concatenate([x, other], dim), jnp.concatenate([other,...  6.71 us
    ppermute x4, starting transfers between devices, gather_blocks(): other = lax.ppermute(x, axis, xor_pairs(count, bit))  3.47 us
  transfers between devices with their start and end apart: 19, of which 13 were waited for; matrix products, arithmetic and copies ran while one was open for 17% of the time, Pallas kernels for 0%

profile of v2, /device:TPU:0, one launch (start us, length us, event | category | flops | bytes accessed | tf_op | source)
XLA Modules:
  0.0 122.5 jit_solution(1116221700087504219)
XLA Ops:
  0.7 3.0 %collective-permute-start = (bf16[1,512,512]{2,1,0:T(8,128)(2,1)}, bf16[1,512,512]{2,1,0:T(8,128)(2,1)S(1)}, u32[]{:S(2)}, u32[]{:S(2)}) collective-permute-start(bf16[1,512,512]{2,1,0:T(8,128)(2,1)} %param.18), channel_id=1, source_target_pairs={{0,2},{1,3},{2,0},{3,1},{4,6},{5,7},{6,4},{7,5},{8,10},{9,11},{10,... | collective-permute-start | bytes 1572872 | tf_op jit(solution)/shard_map/ppermute | solution.py:91
  6.6 10.0 %collective-permute-done = bf16[1,512,512]{2,1,0:T(8,128)(2,1)S(1)} collective-permute-done((bf16[1,512,512]{2,1,0:T(8,128)(2,1)}, bf16[1,512,512]{2,1,0:T(8,128)(2,1)S(1)}, u32[]{:S(2)}, u32[]{:S(2)}) %collective-permute-start) | collective-permute-done | bytes 524320 | tf_op jit(solution)/shard_map/ppermute | solution.py:91
  16.6 2.6 %maximum_select_fusion.2 = bf16[1,1024,512]{2,1,0:T(8,128)(2,1)} fusion(bf16[1,512,512]{2,1,0:T(8,128)(2,1)S(1)} %collective-permute-done, bf16[1,512,512]{2,1,0:T(8,128)(2,1)} %param.18, pred[]{:T(512)S(6)} %eq.66), kind=kLoop, calls=%fused_computation.8 | loop fusion | flops 4718592 | bytes 2097153 | tf_op jit(solution)/shard_map/jit(_where)/select_n | solution.py:93
  24.5 2.0 %maximum_select_fusion.kc_ref.vc_ref = bf16[1,2048,512]{2,1,0:T(8,128)(2,1)} fusion(bf16[1,1024,512]{2,1,0:T(8,128)(2,1)S(1)} %collective-permute-done.1, bf16[1,1024,512]{2,1,0:T(8,128)(2,1)S(1)} %fusion.1, pred[]{:T(512)S(6)} %eq.65), kind=kLoop, calls=%fused_computation.3 | loop fusion | flops 9437184 | bytes 4194305 | tf_op jit(solution)/shard_map/jit(_where)/select_n | solution.py:93
  26.5 22.6 %shard_map.176 = bf16[1,192,2560]{2,1,0:T(8,128)(2,1)} custom-call(s32[192,1]{1,0:T(8,128)} %iota_add_fusion.qpos_ref, s32[1,1,2048]{2,1,0:T(1,128)} %compare_select_fusion.cache_hi_ref, s32[1,1,768]{2,1,0:T(1,128)} %add.441.new_lo_ref, bf16[1,192,2560]{2,1,0:T(8,128)(2,1)} %q_ref.1, bf16[1,2048,512]{2,1,0:T(8,128)(2,1)} %maximum_select_fusion.kc_ref.vc_ref, ...), custom_call_target="tpu_custom_call" | custom-call | tf_op jit(solution)/shard_map/pallas_call | solution.py:128
  51.9 2.1 %collective-permute-start.5 = (bf16[1,2560]{1,0:T(2,128)(2,1)S(1)}, bf16[1,2560]{1,0:T(2,128)(2,1)S(1)}, u32[]{:S(2)}, u32[]{:S(2)}) collective-permute-start(bf16[1,2560]{1,0:T(2,128)(2,1)S(1)} %fusion.48), channel_id=1, source_target_pairs={{0,2},{1,3},{2,0},{3,1},{4,6},{5,7},{6,4},{7,5},{8,10},{9,11},{10,... | collective-permute-start | bytes 15368 | tf_op jit(solution)/shard_map/ppermute | solution.py:25
  54.1 1.7 %collective-permute-done.5 = bf16[1,2560]{1,0:T(2,128)(2,1)S(1)} collective-permute-done((bf16[1,2560]{1,0:T(2,128)(2,1)S(1)}, bf16[1,2560]{1,0:T(2,128)(2,1)S(1)}, u32[]{:S(2)}, u32[]{:S(2)}) %collective-permute-start.5) | collective-permute-done | bytes 5152 | tf_op jit(solution)/shard_map/ppermute | solution.py:25
  55.7 2.1 %collective-permute-start.6 = (bf16[1,2560]{1,0:T(2,128)(2,1)S(1)}, bf16[1,2560]{1,0:T(2,128)(2,1)S(1)}, u32[]{:S(2)}, u32[]{:S(2)}) collective-permute-start(bf16[1,2560]{1,0:T(2,128)(2,1)S(1)} %add.470), channel_id=1, source_target_pairs={{0,4},{4,0},{8,12},{12,8},{16,20},{20,16},{24,28},{28,24},{1,5},{5... | collective-permute-start | bytes 15368 | tf_op jit(solution)/shard_map/ppermute | solution.py:37
  57.9 1.7 %collective-permute-done.6 = bf16[1,2560]{1,0:T(2,128)(2,1)S(1)} collective-permute-done((bf16[1,2560]{1,0:T(2,128)(2,1)S(1)}, bf16[1,2560]{1,0:T(2,128)(2,1)S(1)}, u32[]{:S(2)}, u32[]{:S(2)}) %collective-permute-start.6) | collective-permute-done | bytes 5152 | tf_op jit(solution)/shard_map/ppermute | solution.py:37
  59.6 2.1 %collective-permute-start.7 = (bf16[2,2560]{1,0:T(2,128)(2,1)S(1)}, bf16[2,2560]{1,0:T(2,128)(2,1)S(1)}, u32[]{:S(2)}, u32[]{:S(2)}) collective-permute-start(bf16[2,2560]{1,0:T(2,128)(2,1)S(1)} %broadcast_select_fusion.1), channel_id=1, source_target_pairs={{0,8},{4,12},{8,0},{12,4},{16,24},{20,28},{24,16},{28,20},{1,9},{5... | collective-permute-start | bytes 30728 | tf_op jit(solution)/shard_map/ppermute | solution.py:37
  63.4 3.1 %collective-permute-start.8 = (bf16[4,2560]{1,0:T(4,128)(2,1)S(1)}, bf16[4,2560]{1,0:T(4,128)(2,1)S(1)}, u32[]{:S(2)}, u32[]{:S(2)}) collective-permute-start(bf16[4,2560]{1,0:T(4,128)(2,1)S(1)} %maximum_select_fusion.9), channel_id=1, source_target_pairs={{0,16},{4,20},{8,24},{12,28},{16,0},{20,4},{24,8},{28,12},{1,17},{... | collective-permute-start | bytes 61448 | tf_op jit(solution)/shard_map/ppermute | solution.py:37
  66.5 1.7 %collective-permute-done.8 = bf16[4,2560]{1,0:T(4,128)(2,1)S(1)} collective-permute-done((bf16[4,2560]{1,0:T(4,128)(2,1)S(1)}, bf16[4,2560]{1,0:T(4,128)(2,1)S(1)}, u32[]{:S(2)}, u32[]{:S(2)}) %collective-permute-start.8) | collective-permute-done | bytes 20512 | tf_op jit(solution)/shard_map/ppermute | solution.py:37
  69.7 1.8 %collective-permute-start.10 = (bf16[8,160]{1,0:T(8,128)(2,1)S(1)}, bf16[8,160]{1,0:T(8,128)(2,1)S(1)}, u32[]{:S(2)}, u32[]{:S(2)}) collective-permute-start(bf16[8,160]{1,0:T(8,128)(2,1)S(1)} %maximum_select_fusion.14), channel_id=1, source_target_pairs={{0,2},{1,3},{2,0},{3,1},{4,6},{5,7},{6,4},{7,5},{8,10},{9,11},{10,... | collective-permute-start | bytes 7688 | tf_op jit(solution)/shard_map/ppermute | solution.py:37
  73.4 1.8 %collective-permute-start.11 = (bf16[8,320]{1,0:T(8,128)(2,1)S(1)}, bf16[8,320]{1,0:T(8,128)(2,1)S(1)}, u32[]{:S(2)}, u32[]{:S(2)}) collective-permute-start(bf16[8,320]{1,0:T(8,128)(2,1)S(1)} %maximum_select_fusion.13), channel_id=1, source_target_pairs={{0,4},{4,0},{8,12},{12,8},{16,20},{20,16},{24,28},{28,24},{1,5},{5... | collective-permute-start | bytes 15368 | tf_op jit(solution)/shard_map/ppermute | solution.py:37
  75.3 2.7 %compare_select_fusion.4 = (s32[512,1]{0,1:T(1,128)S(1)}, s32[1,512]{1,0:T(1,128)S(1)}, s32[512,1]{0,1:T(1,128)S(1)}) fusion(s32[]{:T(128)} %bitcast.12, s32[]{:T(128)} %bitcast.11, s32[]{:T(128)} %bitcast.10, s32[]{:T(128)} %bitcast.9, s32[]{:T(128)} %bitcast.8), kind=kLoop, calls=%fused_computation.44 | loop fusion | flops 54272 | bytes 6164 | tf_op jit(solution)/shard_map/jit(take_along_axis)/select_n | solution.py:186
  79.6 2.1 %collective-permute-done.12 = bf16[8,640]{1,0:T(8,128)(2,1)S(1)} collective-permute-done((bf16[8,640]{1,0:T(8,128)(2,1)S(1)}, bf16[8,640]{1,0:T(8,128)(2,1)S(1)}, u32[]{:S(2)}, u32[]{:S(2)}) %collective-permute-start.12) | collective-permute-done | bytes 10272 | tf_op jit(solution)/shard_map/ppermute | solution.py:37
  81.7 2.6 %collective-permute-start.13 = (bf16[8,1280]{1,0:T(8,128)(2,1)S(1)}, bf16[8,1280]{1,0:T(8,128)(2,1)S(1)}, u32[]{:S(2)}, u32[]{:S(2)}) collective-permute-start(bf16[8,1280]{1,0:T(8,128)(2,1)S(1)} %maximum_select_fusion.10), channel_id=1, source_target_pairs={{0,16},{4,20},{8,24},{12,28},{16,0},{20,4},{24,8},{28,12},{1,17},{... | collective-permute-start | bytes 61448 | tf_op jit(solution)/shard_map/ppermute | solution.py:37
  84.3 2.1 %collective-permute-done.13 = bf16[8,1280]{1,0:T(8,128)(2,1)S(1)} collective-permute-done((bf16[8,1280]{1,0:T(8,128)(2,1)S(1)}, bf16[8,1280]{1,0:T(8,128)(2,1)S(1)}, u32[]{:S(2)}, u32[]{:S(2)}) %collective-permute-start.13) | collective-permute-done | bytes 20512 | tf_op jit(solution)/shard_map/ppermute | solution.py:37
  86.5 17.3 %fusion.45 = (f32[8]{0:T(128)S(1)}, f32[8,8000]{1,0:T(8,128)S(1)}) fusion(bf16[8000,2560]{1,0:T(8,128)(2,1)} %param.24, f32[2560]{0:T(1024)S(1)} %convert_element_type.18, f32[8]{0:T(128)S(1)} %add_rsqrt_fusion, bf16[8,1280]{1,0:T(8,128)(2,1)S(1)} %maximum_select_fusion.10, bf16[8,1280]{1,0:T(8,128)(2,1)S(1)} %collective-permute-done.13, pred[]{:T(512)S(6)} %eq.67), kind=kOutput, calls=%fused_computation.151 | convolution fusion | flops 328010240 | bytes 41267264 | tf_op jit(solution)/shard_map/dot_general | solution.py:207
  107.0 2.1 %collective-permute-done.15 = f32[3,8]{1,0:T(4,128)S(1)} collective-permute-done((f32[3,8]{1,0:T(4,128)S(1)}, f32[3,8]{1,0:T(4,128)S(1)}, u32[]{:S(2)}, u32[]{:S(2)}) %collective-permute-start.15) | collective-permute-done | bytes 128 | tf_op jit(solution)/shard_map/ppermute | solution.py:64
  110.1 2.6 %gather_fusion.2 = bf16[512,512]{1,0:T(8,128)(2,1)} fusion(bf16[768,512]{1,0:T(8,128)(2,1)S(1)} %bitcast.182, s32[1024]{0:T(1024)S(1)} %pad_clamp_fusion), kind=kCustom, calls=%fused_computation.2 | custom fusion | bytes 1050624 | tf_op jit(solution)/shard_map/jit(take_along_axis)/gather | solution.py:187
  114.4 2.6 %gather_fusion.1 = bf16[512,512]{1,0:T(8,128)(2,1)} fusion(bf16[2048,512]{1,0:T(8,128)(2,1)S(1)} %bitcast.183, s32[1024]{0:T(1024)S(1)} %pad_clamp_fusion.1), kind=kCustom, calls=%fused_computation.1 | custom fusion | bytes 1050624 | tf_op jit(solution)/shard_map/jit(take_along_axis)/gather | solution.py:186
  117.1 2.8 %collective-permute-start.18 = (f32[3,8]{1,0:T(4,128)S(1)}, f32[3,8]{1,0:T(4,128)S(1)}, u32[]{:S(2)}, u32[]{:S(2)}) collective-permute-start(f32[3,8]{1,0:T(4,128)S(1)} %pad_maximum_fusion.4), channel_id=1, source_target_pairs={{0,16},{4,20},{8,24},{12,28},{16,0},{20,4},{24,8},{28,12},{1,17},{... | collective-permute-start | bytes 296 | tf_op jit(solution)/shard_map/ppermute | solution.py:64
  119.9 2.1 %fusion.2 = bf16[1,512,512]{2,1,0:T(8,128)(2,1)} fusion(bf16[512,512]{1,0:T(8,128)(2,1)S(1)} %copy-done.4, bf16[512,512]{1,0:T(8,128)(2,1)} %gather_fusion.1, pred[512]{0:T(512)(128)(4,1)S(1)} %get-tuple-element.33, pred[512]{0:T(512)(128)(4,1)S(1)} %compare_and_fusion.1, pred[512]{0:T(512)(128)(4,1)S(1)} %get-tuple-element.32), kind=kLoop, calls=%fused_computation.11 | loop fusion | flops 786432 | bytes 1574400 | tf_op jit(solution)/shard_map/jit(_where)/select_n | solution.py:188
  (92 shorter events, 23.0 us)
Async XLA Ops:
  0.6 67.6 %copy-start = (bf16[2560,80]{0,1:T(8,128)(2,1)S(1)}, bf16[2560,80]{0,1:T(8,128)(2,1)}, u32[]{:S(2)}) copy-start(bf16[2560,80]{0,1:T(8,128)(2,1)} %param.21) | copy-start | bytes 1228804
  0.7 16.0 %collective-permute-start = (bf16[1,512,512]{2,1,0:T(8,128)(2,1)}, bf16[1,512,512]{2,1,0:T(8,128)(2,1)S(1)}, u32[]{:S(2)}, u32[]{:S(2)}) collective-permute-start(bf16[1,512,512]{2,1,0:T(8,128)(2,1)} %param.18), channel_id=1, source_target_pairs={{0,2},{1,3},{2,0},{3,1},{4,6},{5,7},{6,4},{7,5},{8,10},{9,11},{10,... | collective-permute-start | bytes 1572872 | tf_op jit(solution)/shard_map/ppermute | solution.py:91
  3.7 16.3 %collective-permute-start.2 = (bf16[1,192,512]{2,1,0:T(8,128)(2,1)}, bf16[1,192,512]{2,1,0:T(8,128)(2,1)S(1)}, u32[]{:S(2)}, u32[]{:S(2)}) collective-permute-start(bf16[1,192,512]{2,1,0:T(8,128)(2,1)} %param.17), channel_id=1, source_target_pairs={{0,2},{1,3},{2,0},{3,1},{4,6},{5,7},{6,4},{7,5},{8,10},{9,11},{10,... | collective-permute-start | bytes 589832 | tf_op jit(solution)/shard_map/ppermute | solution.py:91
  19.3 5.2 %collective-permute-start.1 = (bf16[1,1024,512]{2,1,0:T(8,128)(2,1)}, bf16[1,1024,512]{2,1,0:T(8,128)(2,1)S(1)}, u32[]{:S(2)}, u32[]{:S(2)}) collective-permute-start(bf16[1,1024,512]{2,1,0:T(8,128)(2,1)} %maximum_select_fusion.2), channel_id=1, source_target_pairs={{0,1},{1,0},{2,3},{3,2},{4,5},{5,4},{6,7},{7,6},{8,9},{9,8},{10,11... | collective-permute-start | bytes 3145736 | tf_op jit(solution)/shard_map/ppermute | solution.py:91
  20.9 2.4 %collective-permute-start.3 = (bf16[1,384,512]{2,1,0:T(8,128)(2,1)}, bf16[1,384,512]{2,1,0:T(8,128)(2,1)S(1)}, u32[]{:S(2)}, u32[]{:S(2)}) collective-permute-start(bf16[1,384,512]{2,1,0:T(8,128)(2,1)} %maximum_select_fusion.5), channel_id=1, source_target_pairs={{0,1},{1,0},{2,3},{3,2},{4,5},{5,4},{6,7},{7,6},{8,9},{9,8},{10,11... | collective-permute-start | bytes 1179656 | tf_op jit(solution)/shard_map/ppermute | solution.py:91
  26.5 41.8 %copy-start.8 = (bf16[8,80]{1,0:T(8,128)(2,1)S(1)}, bf16[8,80]{1,0:T(8,128)(2,1)}, u32[]{:S(2)}) copy-start(bf16[8,80]{1,0:T(8,128)(2,1)} %param.22) | copy-start | bytes 3844
  26.5 45.1 %copy-start.6 = (s32[1,4]{1,0:T(1,128)S(1)}, s32[1,4]{1,0:T(1,128)}, u32[]{:S(2)}) copy-start(s32[1,4]{1,0:T(1,128)} %param.20) | copy-start | bytes 52
  26.5 57.8 %copy-start.10 = (s32[8]{0:T(128)S(1)}, s32[8]{0:T(128)}, u32[]{:S(2)}) copy-start(s32[8]{0:T(128)} %param.25) | copy-start | bytes 100
  26.5 57.8 %copy-start.7 = (bf16[2560]{0:T(1024)(128)(2,1)S(1)}, bf16[2560]{0:T(1024)(128)(2,1)}, u32[]{:S(2)}) copy-start(bf16[2560]{0:T(1024)(128)(2,1)} %param.23) | copy-start | bytes 15364
  49.9 1.2 %collective-permute-start.4 = (bf16[1,2560]{1,0:T(2,128)(2,1)S(1)}, bf16[1,2560]{1,0:T(2,128)(2,1)S(1)}, u32[]{:S(2)}, u32[]{:S(2)}) collective-permute-start(bf16[1,2560]{1,0:T(2,128)(2,1)S(1)} %fusion.17), channel_id=1, source_target_pairs={{0,1},{1,0},{2,3},{3,2},{4,5},{5,4},{6,7},{7,6},{8,9},{9,8},{10,11... | collective-permute-start | bytes 15368 | tf_op jit(solution)/shard_map/ppermute | solution.py:25
  51.9 3.8 %collective-permute-start.5 = (bf16[1,2560]{1,0:T(2,128)(2,1)S(1)}, bf16[1,2560]{1,0:T(2,128)(2,1)S(1)}, u32[]{:S(2)}, u32[]{:S(2)}) collective-permute-start(bf16[1,2560]{1,0:T(2,128)(2,1)S(1)} %fusion.48), channel_id=1, source_target_pairs={{0,2},{1,3},{2,0},{3,1},{4,6},{5,7},{6,4},{7,5},{8,10},{9,11},{10,... | collective-permute-start | bytes 15368 | tf_op jit(solution)/shard_map/ppermute | solution.py:25
  55.7 3.8 %collective-permute-start.6 = (bf16[1,2560]{1,0:T(2,128)(2,1)S(1)}, bf16[1,2560]{1,0:T(2,128)(2,1)S(1)}, u32[]{:S(2)}, u32[]{:S(2)}) collective-permute-start(bf16[1,2560]{1,0:T(2,128)(2,1)S(1)} %add.470), channel_id=1, source_target_pairs={{0,4},{4,0},{8,12},{12,8},{16,20},{20,16},{24,28},{28,24},{1,5},{5... | collective-permute-start | bytes 15368 | tf_op jit(solution)/shard_map/ppermute | solution.py:37
  59.6 3.8 %collective-permute-start.7 = (bf16[2,2560]{1,0:T(2,128)(2,1)S(1)}, bf16[2,2560]{1,0:T(2,128)(2,1)S(1)}, u32[]{:S(2)}, u32[]{:S(2)}) collective-permute-start(bf16[2,2560]{1,0:T(2,128)(2,1)S(1)} %broadcast_select_fusion.1), channel_id=1, source_target_pairs={{0,8},{4,12},{8,0},{12,4},{16,24},{20,28},{24,16},{28,20},{1,9},{5... | collective-permute-start | bytes 30728 | tf_op jit(solution)/shard_map/ppermute | solution.py:37
  63.4 4.9 %collective-permute-start.8 = (bf16[4,2560]{1,0:T(4,128)(2,1)S(1)}, bf16[4,2560]{1,0:T(4,128)(2,1)S(1)}, u32[]{:S(2)}, u32[]{:S(2)}) collective-permute-start(bf16[4,2560]{1,0:T(4,128)(2,1)S(1)} %maximum_select_fusion.9), channel_id=1, source_target_pairs={{0,16},{4,20},{8,24},{12,28},{16,0},{20,4},{24,8},{28,12},{1,17},{... | collective-permute-start | bytes 61448 | tf_op jit(solution)/shard_map/ppermute | solution.py:37
  68.5 1.2 collective-permute-start.9
  69.7 3.6 %collective-permute-start.10 = (bf16[8,160]{1,0:T(8,128)(2,1)S(1)}, bf16[8,160]{1,0:T(8,128)(2,1)S(1)}, u32[]{:S(2)}, u32[]{:S(2)}) collective-permute-start(bf16[8,160]{1,0:T(8,128)(2,1)S(1)} %maximum_select_fusion.14), channel_id=1, source_target_pairs={{0,2},{1,3},{2,0},{3,1},{4,6},{5,7},{6,4},{7,5},{8,10},{9,11},{10,... | collective-permute-start | bytes 7688 | tf_op jit(solution)/shard_map/ppermute | solution.py:37
  73.4 4.5 %collective-permute-start.11 = (bf16[8,320]{1,0:T(8,128)(2,1)S(1)}, bf16[8,320]{1,0:T(8,128)(2,1)S(1)}, u32[]{:S(2)}, u32[]{:S(2)}) collective-permute-start(bf16[8,320]{1,0:T(8,128)(2,1)S(1)} %maximum_select_fusion.13), channel_id=1, source_target_pairs={{0,4},{4,0},{8,12},{12,8},{16,20},{20,16},{24,28},{28,24},{1,5},{5... | collective-permute-start | bytes 15368 | tf_op jit(solution)/shard_map/ppermute | solution.py:37
  78.0 3.7 %collective-permute-start.12 = (bf16[8,640]{1,0:T(8,128)(2,1)S(1)}, bf16[8,640]{1,0:T(8,128)(2,1)S(1)}, u32[]{:S(2)}, u32[]{:S(2)}) collective-permute-start(bf16[8,640]{1,0:T(8,128)(2,1)S(1)} %maximum_select_fusion.11), channel_id=1, source_target_pairs={{0,8},{4,12},{8,0},{12,4},{16,24},{20,28},{24,16},{28,20},{1,9},{5... | collective-permute-start | bytes 30728 | tf_op jit(solution)/shard_map/ppermute | solution.py:37
  81.7 4.7 %collective-permute-start.13 = (bf16[8,1280]{1,0:T(8,128)(2,1)S(1)}, bf16[8,1280]{1,0:T(8,128)(2,1)S(1)}, u32[]{:S(2)}, u32[]{:S(2)}) collective-permute-start(bf16[8,1280]{1,0:T(8,128)(2,1)S(1)} %maximum_select_fusion.10), channel_id=1, source_target_pairs={{0,16},{4,20},{8,24},{12,28},{16,0},{20,4},{24,8},{28,12},{1,17},{... | collective-permute-start | bytes 61448 | tf_op jit(solution)/shard_map/ppermute | solution.py:37
  104.2 1.2 collective-permute-start.14
  105.4 3.7 %collective-permute-start.15 = (f32[3,8]{1,0:T(4,128)S(1)}, f32[3,8]{1,0:T(4,128)S(1)}, u32[]{:S(2)}, u32[]{:S(2)}) collective-permute-start(f32[3,8]{1,0:T(4,128)S(1)} %pad_maximum_fusion.1), channel_id=1, source_target_pairs={{0,2},{1,3},{2,0},{3,1},{4,6},{5,7},{6,4},{7,5},{8,10},{9,11},{10,... | collective-permute-start | bytes 296 | tf_op jit(solution)/shard_map/ppermute | solution.py:64
  109.1 3.7 %collective-permute-start.16 = (f32[3,8]{1,0:T(4,128)S(1)}, f32[3,8]{1,0:T(4,128)S(1)}, u32[]{:S(2)}, u32[]{:S(2)}) collective-permute-start(f32[3,8]{1,0:T(4,128)S(1)} %pad_maximum_fusion.2), channel_id=1, source_target_pairs={{0,4},{4,0},{8,12},{12,8},{16,20},{20,16},{24,28},{28,24},{1,5},{5... | collective-permute-start | bytes 296 | tf_op jit(solution)/shard_map/ppermute | solution.py:64
  112.8 4.3 %collective-permute-start.17 = (f32[3,8]{1,0:T(4,128)S(1)}, f32[3,8]{1,0:T(4,128)S(1)}, u32[]{:S(2)}, u32[]{:S(2)}) collective-permute-start(f32[3,8]{1,0:T(4,128)S(1)} %pad_maximum_fusion.3), channel_id=1, source_target_pairs={{0,8},{4,12},{8,0},{12,4},{16,24},{20,28},{24,16},{28,20},{1,9},{5... | collective-permute-start | bytes 296 | tf_op jit(solution)/shard_map/ppermute | solution.py:64
  117.1 4.9 %collective-permute-start.18 = (f32[3,8]{1,0:T(4,128)S(1)}, f32[3,8]{1,0:T(4,128)S(1)}, u32[]{:S(2)}, u32[]{:S(2)}) collective-permute-start(f32[3,8]{1,0:T(4,128)S(1)} %pad_maximum_fusion.4), channel_id=1, source_target_pairs={{0,16},{4,20},{8,24},{12,28},{16,0},{20,4},{24,8},{28,12},{1,17},{... | collective-permute-start | bytes 296 | tf_op jit(solution)/shard_map/ppermute | solution.py:64
  (6 other events, 91.0 us)

commit v3 on v2

--- a/solution.py
+++ b/solution.py
@@ -67,80 +67,92 @@
     return top, total, picked
 
 
-def gather_order(count, bits):
-    order = [[device] for device in range(count)]
-    for bit in bits:
-        order = [
-            order[d] + order[d ^ bit] if d & bit == 0 else order[d ^ bit] + order[d]
-            for d in range(count)
-        ]
-    return order[0]
-
-
-def gather_blocks(x, axis, dim):
+def exchange_pieces(x, axis, dim):
     count = lax.axis_size(axis)
     if not is_pow2(count):
-        return lax.all_gather(x, axis, axis=dim, tiled=True), list(range(count))
-    bits = []
+        return [(lax.all_gather(x, axis, axis=dim, tiled=True), list(range(count)))], False
+    pieces = [(x, [0])]
+    if count == 1:
+        return pieces, True
+    near = lax.ppermute(x, axis, xor_pairs(count, 1))
+    held, held_masks, far = x, [0], []
     bit = count // 2
-    while bit >= 1:
-        bits.append(bit)
+    while bit > 1:
+        other = lax.ppermute(held, axis, xor_pairs(count, bit))
+        other_masks = [m ^ bit for m in held_masks]
+        far.append((other, other_masks))
+        held = jnp.concatenate([held, other], dim)
+        held_masks = held_masks + other_masks
         bit //= 2
-    index = lax.axis_index(axis)
-    for bit in bits:
-        other = lax.ppermute(x, axis, xor_pairs(count, bit))
-        low = (index & bit) == 0
-        x = jnp.where(
-            low, jnp.concatenate([x, other], dim), jnp.concatenate([other, x], dim)
+    pieces.append((near, [1]))
+    if far:
+        far_rows = jnp.concatenate([p for p, _ in far], dim) if len(far) > 1 else far[0][0]
+        far_masks = [m for _, masks in far for m in masks]
+        pieces.append((lax.ppermute(far_rows, axis, xor_pairs(count, 1)), [m ^ 1 for m in far_masks]))
+        pieces.extend(far)
+    return pieces, True
+
+
+def piece_sources(masks, by_xor, my_index):
+    masks = jnp.asarray(masks, jnp.int32)
+    return jnp.bitwise_xor(masks, my_index) if by_xor else masks
+
+
+def attention_kernel(qpos_ref, *refs, kinds, scale):
+    count = len(kinds)
+    bound_refs = refs[:count]
+    q_ref = refs[count]
+    kv_refs = refs[count + 1 : count + 1 + 2 * count]
+    out_ref = refs[-1]
+    query = q_ref[0]
+    position = qpos_ref[...]
+    dims = (((1,), (1,)), ((), ()))
+    masked = []
+    for i, kind in enumerate(kinds):
+        score = (
+            lax.dot_general(query, kv_refs[2 * i][0], dims, preferred_element_type=jnp.float32)
+            * scale
         )
-    return x, gather_order(count, bits)
-
-
-def attention_kernel(
-    qpos_ref, cache_hi_ref, new_lo_ref, q_ref, kc_ref, vc_ref, kn_ref, vn_ref, out_ref, *, scale
-):
-    query = q_ref[0]
-    dims = (((1,), (1,)), ((), ()))
-    score_c = lax.dot_general(query, kc_ref[0], dims, preferred_element_type=jnp.float32) * scale
-    score_n = lax.dot_general(query, kn_ref[0], dims, preferred_element_type=jnp.float32) * scale
-    position = qpos_ref[...]
-    seen_c = position <= cache_hi_ref[0]
-    seen_n = new_lo_ref[0] <= position
-    peak = jnp.maximum(
-        jnp.max(jnp.where(seen_c, score_c, -jnp.inf), axis=1, keepdims=True),
-        jnp.max(jnp.where(seen_n, score_n, -jnp.inf), axis=1, keepdims=True),
-    )
-    weight_c = jnp.where(seen_c, jnp.exp(score_c - peak), 0.0)
-    weight_n = jnp.where(seen_n, jnp.exp(score_n - peak), 0.0)
-    total = jnp.sum(weight_c, axis=1, keepdims=True) + jnp.sum(weight_n, axis=1, keepdims=True)
-    mixed = jnp.dot(
-        weight_c.astype(jnp.bfloat16), vc_ref[0], preferred_element_type=jnp.float32
-    ) + jnp.dot(weight_n.astype(jnp.bfloat16), vn_ref[0], preferred_element_type=jnp.float32)
+        bound = bound_refs[i][0]
+        seen = position <= bound if kind == "hi" else bound <= position
+        masked.append(jnp.where(seen, score, -jnp.inf))
+    peak = functools.reduce(jnp.maximum, [jnp.max(m, axis=1, keepdims=True) for m in masked])
+    weights = [jnp.exp(m - peak) for m in masked]
+    total = functools.reduce(jnp.add, [jnp.sum(w, axis=1, keepdims=True) for w in weights])
+    mixed = functools.reduce(
+        jnp.add,
+        [
+            jnp.dot(w.astype(jnp.bfloat16), kv_refs[2 * i + 1][0], preferred_element_type=jnp.float32)
+            for i, w in enumerate(weights)
+        ],
+    )
     out_ref[0] = (mixed / total).astype(out_ref.dtype)
 
 
-def attend(queries, cache_keys, new_keys, query_pos, cache_hi, new_lo, head_dim):
+def attend(queries, query_pos, pieces, head_dim):
     req_local, new_local, model_cols = queries.shape
     head_count = model_cols // head_dim
-    cache_rows = cache_keys.shape[1]
-    new_rows = new_keys.shape[1]
-    kernel = functools.partial(attention_kernel, scale=1.0 / math.sqrt(head_dim))
+    kinds = [kind for kind, _, _ in pieces]
+    kernel = functools.partial(attention_kernel, kinds=kinds, scale=1.0 / math.sqrt(head_dim))
+    bound_specs = [
+        pl.BlockSpec((1, 1, rows.shape[1]), lambda r, h: (r, 0, 0)) for _, rows, _ in pieces
+    ]
+    kv_specs = []
+    kv_args = []
+    for _, rows, _ in pieces:
+        kv_specs.append(pl.BlockSpec((1, rows.shape[1], head_dim), lambda r, h: (r, 0, 0)))
+        kv_specs.append(pl.BlockSpec((1, rows.shape[1], head_dim), lambda r, h: (r, 0, 1)))
+        kv_args.extend([rows, rows])
     return pl.pallas_call(
         kernel,
         grid=(req_local, head_count),
-        in_specs=[
-            pl.BlockSpec((new_local, 1), lambda r, h: (0, 0)),
-            pl.BlockSpec((1, 1, cache_rows), lambda r, h: (r, 0, 0)),
-            pl.BlockSpec((1, 1, new_rows), lambda r, h: (r, 0, 0)),
-            pl.BlockSpec((1, new_local, head_dim), lambda r, h: (r, 0, h)),
-            pl.BlockSpec((1, cache_rows, head_dim), lambda r, h: (r, 0, 0)),
-            pl.BlockSpec((1, cache_rows, head_dim), lambda r, h: (r, 0, 1)),
-            pl.BlockSpec((1, new_rows, head_dim), lambda r, h: (r, 0, 0)),
-            pl.BlockSpec((1, new_rows, head_dim), lambda r, h: (r, 0, 1)),
-        ],
+        in_specs=[pl.BlockSpec((new_local, 1), lambda r, h: (0, 0))]
+        + bound_specs
+        + [pl.BlockSpec((1, new_local, head_dim), lambda r, h: (r, 0, h))]
+        + kv_specs,
         out_specs=pl.BlockSpec((1, new_local, head_dim), lambda r, h: (r, 0, h)),
         out_shape=jax.ShapeDtypeStruct(queries.shape, queries.dtype),
-    )(query_pos, cache_hi, new_lo, queries, cache_keys, cache_keys, new_keys, new_keys)
+    )(query_pos, *[bound for _, _, bound in pieces], queries, *kv_args)
 
 
 def on_device(
@@ -161,28 +173,43 @@
     matches = owner[:, :, None] == block_ids[None, None, :]
     logical = jnp.sum(jnp.where(matches, block_ids[None, :, None], 0), axis=1)
     own_block = lax.dynamic_index_in_dim(logical, my_index, axis=1, keepdims=False)
-
-    cache_keys, cache_order = gather_blocks(cache_pool, "gy", 1)
-    new_keys, new_order = gather_blocks(new_kv, "gy", 1)
     slot_ids = jnp.arange(slot_count, dtype=jnp.int32)
     new_ids = jnp.arange(new_local, dtype=jnp.int32)
-    cache_stored = jnp.asarray(cache_order, jnp.int32)
-    chosen = jnp.take(logical, cache_stored, axis=1)
-    slot_pos = (chosen[:, :, None] * slot_count + slot_ids[None, None, :]).reshape(req_local, -1)
-    cache_hi = jnp.where(slot_pos >= first_slot[:, None], slot_pos, -1)[:, None, :]
-    new_pos = (jnp.asarray(new_order, jnp.int32)[:, None] * new_local + new_ids[None, :]).reshape(-1)
-    new_lo = jnp.broadcast_to(new_pos[None, None, :], (req_local, 1, new_pos.shape[0]))
-    mixed_out = attend(queries, cache_keys, new_keys, query_pos, cache_hi, new_lo, head_dim)
-
-    cache_at = jnp.asarray([cache_order.index(s) for s in range(group_pos)], jnp.int32)
-    new_at = jnp.asarray([new_order.index(c) for c in range(group_pos)], jnp.int32)
+
+    cache_pieces, cache_xor = exchange_pieces(cache_pool, "gy", 1)
+    new_pieces, new_xor = exchange_pieces(new_kv, "gy", 1)
+    pieces = []
+    for rows, masks in cache_pieces:
+        stored = piece_sources(masks, cache_xor, my_index)
+        chosen = jnp.take(logical, stored, axis=1)
+        slot_pos = (chosen[:, :, None] * slot_count + slot_ids[None, None, :]).reshape(req_local, -1)
+        cache_hi = jnp.where(slot_pos >= first_slot[:, None], slot_pos, -1)[:, None, :]
+        pieces.append(("hi", rows, cache_hi))
+    for rows, masks in new_pieces:
+        chunk = piece_sources(masks, new_xor, my_index)
+        new_pos = (chunk[:, None] * new_local + new_ids[None, :]).reshape(-1)
+        new_lo = jnp.broadcast_to(new_pos[None, None, :], (req_local, 1, new_pos.shape[0]))
+        pieces.append(("lo", rows, new_lo))
+    mixed_out = attend(queries, query_pos, pieces, head_dim)
+
+    cache_masks = [m for _, masks in cache_pieces for m in masks]
+    new_masks = [m for _, masks in new_pieces for m in masks]
+    cache_at = jnp.asarray([cache_masks.index(s) for s in range(group_pos)], jnp.int32)
+    new_at = jnp.asarray([new_masks.index(c) for c in range(group_pos)], jnp.int32)
+    cache_keys = jnp.concatenate([rows for rows, _ in cache_pieces], axis=1)
+    new_keys = jnp.concatenate([rows for rows, _ in new_pieces], axis=1)
     target_slot = own_block[:, None] * slot_count + slot_ids[None, :]
     from_old = target_slot < keep_len
     old_slot = jnp.minimum(target_slot + new_total, window_len - 1)
     old_block = jnp.take_along_axis(owner, old_slot // slot_count, axis=1)
+    if cache_xor:
+        old_block = jnp.bitwise_xor(old_block, my_index)
     cache_row = jnp.take(cache_at, old_block) * slot_count + old_slot % slot_count
     new_slot = jnp.maximum(target_slot - keep_len, 0)
-    new_row = jnp.take(new_at, new_slot // new_local) * new_local + new_slot % new_local
+    new_chunk = new_slot // new_local
+    if new_xor:
+        new_chunk = jnp.bitwise_xor(new_chunk, my_index)
+    new_row = jnp.take(new_at, new_chunk) * new_local + new_slot % new_local
     from_cache = jnp.take_along_axis(cache_keys, cache_row[:, :, None], axis=1)
     from_new = jnp.take_along_axis(new_keys, new_row[:, :, None], axis=1)
     fresh_block = jnp.where(from_old[:, :, None], from_cache, from_new)

time: 123 us -> 121 us (0.984)
  between operations: 2.15 us -> 4.84 us
  Pallas kernels: 22.6 us -> 20.2 us
  waiting for transfers between devices: 26.4 us -> 24.4 us
  other arithmetic: 17.9 us -> 16.6 us
    select_n x4 -> x0, other arithmetic: 6.71 us -> none  [gather_blocks(): jnp.where(low, jnp.concatenate([x, other], dim), jnp.concatenate([other,...]
    pallas_call x1, Pallas kernels: 22.6 us -> 20.2 us  [attend(): pl.pallas_call(kernel, grid=(req_local, head_count), in_specs=[pl.BlockSp...]
    unnamed x22 -> x54, local copies, waits for them, and re-layouts: 0.05 us -> 2.23 us
    ppermute x4 -> x6, waiting for transfers between devices: 10.2 us -> 9.5 us  [the longest x2 9.35 us: exchange_pieces(): other = lax.ppermute(held, axis, xor_pairs(count, bit))]
    ppermute x4 -> x6, starting transfers between devices: 3.47 us -> 3.6 us  [the longest x2 3.08 us: exchange_pieces(): other = lax.ppermute(held, axis, xor_pairs(count, bit))]
  transfers between devices with their start and end apart: 19 -> 21, of which waited for: 13 -> 16; matrix products, arithmetic and copies ran while one was open for 17% -> 15% of each run, Pallas kernels for 0% -> 0%
where the time goes in v3:
time: 121 us; the launch traced here: 120 us
  starting transfers between devices  28.3 us (23%)
  waiting for transfers between devices  24.4 us (20%)
  Pallas kernels  20.2 us (17%)
  matrix products  17.5 us (14%)
  other arithmetic  16.6 us (14%)
  local copies, waits for them, and re-layouts  8.29 us (7%)
  between operations  4.84 us (4%)
    pallas_call x1, Pallas kernels, attend(): pl.pallas_call(kernel, grid=(req_local, head_count), in_specs=[pl.BlockSp...  20.2 us
    dot_general x1, matrix products, on_device(): lax.dot_general(normed, head, (((1,), (1,)), ((), ())), preferred_element...  17.3 us
    ppermute x8, starting transfers between devices, butterfly_gather(): other = lax.ppermute(x, axis, xor_pairs(count, bit))  14.8 us
    ppermute x8, waiting for transfers between devices, butterfly_gather(): other = lax.ppermute(x, axis, xor_pairs(count, bit))  10.6 us
    ppermute x2, waiting for transfers between devices, exchange_pieces(): other = lax.ppermute(held, axis, xor_pairs(count, bit))  9.35 us
    ppermute x5, starting transfers between devices, butterfly_stats(): other = lax.ppermute(packed, axis, xor_pairs(count, bit))  7.69 us
    ppermute x2, starting transfers between devices, exchange_pieces(): other = lax.ppermute(held, axis, xor_pairs(count, bit))  3.08 us
    select_n x1, other arithmetic, on_device(): from_cache = jnp.take_along_axis(cache_keys, cache_row[:, :, None], axis=1)  2.68 us
  transfers between devices with their start and end apart: 21, of which 16 were waited for; matrix products, arithmetic and copies ran while one was open for 15% of the time, Pallas kernels for 0%

profile of v3, /device:TPU:0, one launch (start us, length us, event | category | flops | bytes accessed | tf_op | source)
XLA Modules:
  0.0 120.1 jit_solution(4024999774613502682)
XLA Ops:
  0.6 3.0 %collective-permute-start.1 = (bf16[1,512,512]{2,1,0:T(8,128)(2,1)}, bf16[1,512,512]{2,1,0:T(8,128)(2,1)S(1)}, u32[]{:S(2)}, u32[]{:S(2)}) collective-permute-start(bf16[1,512,512]{2,1,0:T(8,128)(2,1)} %refs_10_.1), channel_id=1, source_target_pairs={{0,2},{1,3},{2,0},{3,1},{4,6},{5,7},{6,4},{7,5},{8,10},{9,11},{10,... | collective-permute-start | bytes 1572872 | tf_op jit(solution)/shard_map/ppermute | solution.py:81
  8.8 7.8 %collective-permute-done.1.refs_15_.refs_16_ = bf16[1,512,512]{2,1,0:T(8,128)(2,1)S(1)} collective-permute-done((bf16[1,512,512]{2,1,0:T(8,128)(2,1)}, bf16[1,512,512]{2,1,0:T(8,128)(2,1)S(1)}, u32[]{:S(2)}, u32[]{:S(2)}) %collective-permute-start.1) | collective-permute-done | bytes 524320 | tf_op jit(solution)/shard_map/ppermute | solution.py:81
  18.4 1.6 %collective-permute-done.4.refs_23_.refs_24_ = bf16[1,192,512]{2,1,0:T(8,128)(2,1)S(1)} collective-permute-done((bf16[1,192,512]{2,1,0:T(8,128)(2,1)}, bf16[1,192,512]{2,1,0:T(8,128)(2,1)S(1)}, u32[]{:S(2)}, u32[]{:S(2)}) %collective-permute-start.4) | collective-permute-done | bytes 196640 | tf_op jit(solution)/shard_map/ppermute | solution.py:81
  22.5 20.2 %shard_map.230 = bf16[1,192,2560]{2,1,0:T(8,128)(2,1)} custom-call(s32[192,1]{1,0:T(8,128)} %iota_add_fusion.qpos_ref, s32[1,1,512]{2,1,0:T(1,128)} %get-tuple-element.84.refs_0_, s32[1,1,512]{2,1,0:T(1,128)} %get-tuple-element.83.refs_1_, s32[1,1,512]{2,1,0:T(1,128)} %get-tuple-element.82.refs_2_, s32[1,1,512]{2,1,0:T(1,128)} %get-tuple-element.81.refs_3_, ...), custom_call_target="tpu_custom_call" | custom-call | tf_op jit(solution)/shard_map/pallas_call | solution.py:146
  45.6 1.8 %collective-permute-start.7 = (bf16[1,2560]{1,0:T(2,128)(2,1)S(1)}, bf16[1,2560]{1,0:T(2,128)(2,1)S(1)}, u32[]{:S(2)}, u32[]{:S(2)}) collective-permute-start(bf16[1,2560]{1,0:T(2,128)(2,1)S(1)} %fusion.47), channel_id=1, source_target_pairs={{0,2},{1,3},{2,0},{3,1},{4,6},{5,7},{6,4},{7,5},{8,10},{9,11},{10,... | collective-permute-start | bytes 15368 | tf_op jit(solution)/shard_map/ppermute | solution.py:25
  49.3 1.8 %collective-permute-start.8 = (bf16[1,2560]{1,0:T(2,128)(2,1)S(1)}, bf16[1,2560]{1,0:T(2,128)(2,1)S(1)}, u32[]{:S(2)}, u32[]{:S(2)}) collective-permute-start(bf16[1,2560]{1,0:T(2,128)(2,1)S(1)} %add.615), channel_id=1, source_target_pairs={{0,4},{4,0},{8,12},{12,8},{16,20},{20,16},{24,28},{28,24},{1,5},{5... | collective-permute-start | bytes 15368 | tf_op jit(solution)/shard_map/ppermute | solution.py:37
  51.2 1.9 %collective-permute-done.8 = bf16[1,2560]{1,0:T(2,128)(2,1)S(1)} collective-permute-done((bf16[1,2560]{1,0:T(2,128)(2,1)S(1)}, bf16[1,2560]{1,0:T(2,128)(2,1)S(1)}, u32[]{:S(2)}, u32[]{:S(2)}) %collective-permute-start.8) | collective-permute-done | bytes 5152 | tf_op jit(solution)/shard_map/ppermute | solution.py:37
  53.1 1.9 %collective-permute-start.9 = (bf16[2,2560]{1,0:T(2,128)(2,1)S(1)}, bf16[2,2560]{1,0:T(2,128)(2,1)S(1)}, u32[]{:S(2)}, u32[]{:S(2)}) collective-permute-start(bf16[2,2560]{1,0:T(2,128)(2,1)S(1)} %broadcast_select_fusion.1), channel_id=1, source_target_pairs={{0,8},{4,12},{8,0},{12,4},{16,24},{20,28},{24,16},{28,20},{1,9},{5... | collective-permute-start | bytes 30728 | tf_op jit(solution)/shard_map/ppermute | solution.py:37
  56.9 2.9 %collective-permute-start.10 = (bf16[4,2560]{1,0:T(4,128)(2,1)S(1)}, bf16[4,2560]{1,0:T(4,128)(2,1)S(1)}, u32[]{:S(2)}, u32[]{:S(2)}) collective-permute-start(bf16[4,2560]{1,0:T(4,128)(2,1)S(1)} %maximum_select_fusion.3), channel_id=1, source_target_pairs={{0,16},{4,20},{8,24},{12,28},{16,0},{20,4},{24,8},{28,12},{1,17},{... | collective-permute-start | bytes 61448 | tf_op jit(solution)/shard_map/ppermute | solution.py:37
  61.9 2.7 %compare_select_fusion.3 = (s32[512,1]{0,1:T(1,128)S(1)}, s32[1,512]{1,0:T(1,128)S(1)}, s32[512,1]{0,1:T(1,128)S(1)}) fusion(s32[]{:T(128)} %axis_index.14, s32[]{:T(128)} %bitcast.19, s32[]{:T(128)} %bitcast.18, s32[]{:T(128)} %bitcast.17, s32[]{:T(128)} %bitcast.16, s32[]{:T(128)} %bitcast.15), kind=kLoop, calls=%fused_computation.36 | loop fusion | flops 55296 | bytes 6168 | tf_op jit(solution)/shard_map/jit(take_along_axis)/select_n | solution.py:213
  64.7 1.7 %collective-permute-start.12 = (bf16[8,160]{1,0:T(8,128)(2,1)S(1)}, bf16[8,160]{1,0:T(8,128)(2,1)S(1)}, u32[]{:S(2)}, u32[]{:S(2)}) collective-permute-start(bf16[8,160]{1,0:T(8,128)(2,1)S(1)} %maximum_select_fusion.8), channel_id=1, source_target_pairs={{0,2},{1,3},{2,0},{3,1},{4,6},{5,7},{6,4},{7,5},{8,10},{9,11},{10,... | collective-permute-start | bytes 7688 | tf_op jit(solution)/shard_map/ppermute | solution.py:37
  68.4 1.8 %collective-permute-start.13 = (bf16[8,320]{1,0:T(8,128)(2,1)S(1)}, bf16[8,320]{1,0:T(8,128)(2,1)S(1)}, u32[]{:S(2)}, u32[]{:S(2)}) collective-permute-start(bf16[8,320]{1,0:T(8,128)(2,1)S(1)} %maximum_select_fusion.7), channel_id=1, source_target_pairs={{0,4},{4,0},{8,12},{12,8},{16,20},{20,16},{24,28},{28,24},{1,5},{5... | collective-permute-start | bytes 15368 | tf_op jit(solution)/shard_map/ppermute | solution.py:37
  70.2 1.9 %collective-permute-done.13 = bf16[8,320]{1,0:T(8,128)(2,1)S(1)} collective-permute-done((bf16[8,320]{1,0:T(8,128)(2,1)S(1)}, bf16[8,320]{1,0:T(8,128)(2,1)S(1)}, u32[]{:S(2)}, u32[]{:S(2)}) %collective-permute-start.13) | collective-permute-done | bytes 5152 | tf_op jit(solution)/shard_map/ppermute | solution.py:37
  72.1 1.8 %collective-permute-start.14 = (bf16[8,640]{1,0:T(8,128)(2,1)S(1)}, bf16[8,640]{1,0:T(8,128)(2,1)S(1)}, u32[]{:S(2)}, u32[]{:S(2)}) collective-permute-start(bf16[8,640]{1,0:T(8,128)(2,1)S(1)} %maximum_select_fusion.5), channel_id=1, source_target_pairs={{0,8},{4,12},{8,0},{12,4},{16,24},{20,28},{24,16},{28,20},{1,9},{5... | collective-permute-start | bytes 30728 | tf_op jit(solution)/shard_map/ppermute | solution.py:37
  73.9 1.8 %collective-permute-done.14 = bf16[8,640]{1,0:T(8,128)(2,1)S(1)} collective-permute-done((bf16[8,640]{1,0:T(8,128)(2,1)S(1)}, bf16[8,640]{1,0:T(8,128)(2,1)S(1)}, u32[]{:S(2)}, u32[]{:S(2)}) %collective-permute-start.14) | collective-permute-done | bytes 10272 | tf_op jit(solution)/shard_map/ppermute | solution.py:37
  75.8 2.8 %collective-permute-start.15 = (bf16[8,1280]{1,0:T(8,128)(2,1)S(1)}, bf16[8,1280]{1,0:T(8,128)(2,1)S(1)}, u32[]{:S(2)}, u32[]{:S(2)}) collective-permute-start(bf16[8,1280]{1,0:T(8,128)(2,1)S(1)} %maximum_select_fusion.4), channel_id=1, source_target_pairs={{0,16},{4,20},{8,24},{12,28},{16,0},{20,4},{24,8},{28,12},{1,17},{... | collective-permute-start | bytes 61448 | tf_op jit(solution)/shard_map/ppermute | solution.py:37
  80.6 17.3 %fusion.44 = (f32[8]{0:T(128)S(1)}, f32[8,8000]{1,0:T(8,128)S(1)}) fusion(bf16[8000,2560]{1,0:T(8,128)(2,1)} %param.30, f32[2560]{0:T(1024)S(1)} %convert_element_type.18, f32[8]{0:T(128)S(1)} %add_rsqrt_fusion, bf16[8,1280]{1,0:T(8,128)(2,1)S(1)} %maximum_select_fusion.4, bf16[8,1280]{1,0:T(8,128)(2,1)S(1)} %collective-permute-done.15, pred[]{:T(512)S(6)} %eq.61), kind=kOutput, calls=%fused_computation.149 | convolution fusion | flops 328010240 | bytes 41267264 | tf_op jit(solution)/shard_map/dot_general | solution.py:234
  100.1 1.8 %collective-permute-start.17 = (f32[3,8]{1,0:T(4,128)S(1)}, f32[3,8]{1,0:T(4,128)S(1)}, u32[]{:S(2)}, u32[]{:S(2)}) collective-permute-start(f32[3,8]{1,0:T(4,128)S(1)} %pad_maximum_fusion.1), channel_id=1, source_target_pairs={{0,2},{1,3},{2,0},{3,1},{4,6},{5,7},{6,4},{7,5},{8,10},{9,11},{10,... | collective-permute-start | bytes 296 | tf_op jit(solution)/shard_map/ppermute | solution.py:64
  101.9 2.7 %gather_fusion.1 = bf16[512,512]{1,0:T(8,128)(2,1)} fusion(bf16[768,512]{1,0:T(8,128)(2,1)S(1)} %maximum_bitcast_fusion.1, s32[1024]{0:T(1024)S(1)} %pad_clamp_fusion), kind=kCustom, calls=%fused_computation.1 | custom fusion | bytes 1050624 | tf_op jit(solution)/shard_map/jit(take_along_axis)/gather | solution.py:214
  105.2 1.5 %collective-permute-start.18 = (f32[3,8]{1,0:T(4,128)S(1)}, f32[3,8]{1,0:T(4,128)S(1)}, u32[]{:S(2)}, u32[]{:S(2)}) collective-permute-start(f32[3,8]{1,0:T(4,128)S(1)} %pad_maximum_fusion.2), channel_id=1, source_target_pairs={{0,4},{4,0},{8,12},{12,8},{16,20},{20,16},{24,28},{28,24},{1,5},{5... | collective-permute-start | bytes 296 | tf_op jit(solution)/shard_map/ppermute | solution.py:64
  109.4 1.6 %collective-permute-start.19 = (f32[3,8]{1,0:T(4,128)}, f32[3,8]{1,0:T(4,128)}, u32[]{:S(2)}, u32[]{:S(2)}) collective-permute-start(f32[3,8]{1,0:T(4,128)} %pad_maximum_fusion.3), channel_id=1, source_target_pairs={{0,8},{4,12},{8,0},{12,4},{16,24},{20,28},{24,16},{28,20},{1,9},{5... | collective-permute-start | bytes 296 | tf_op jit(solution)/shard_map/ppermute | solution.py:64
  111.1 2.1 %gather_fusion = bf16[512,512]{1,0:T(8,128)(2,1)S(1)} fusion(bf16[2048,512]{1,0:T(8,128)(2,1)S(1)} %maximum_bitcast_fusion, s32[1024]{0:T(1024)} %pad_clamp_fusion.1), kind=kCustom, calls=%fused_computation | custom fusion | bytes 1050624 | tf_op jit(solution)/shard_map/jit(take_along_axis)/gather | solution.py:213
  114.2 2.7 %collective-permute-start.20 = (f32[3,8]{1,0:T(4,128)S(1)}, f32[3,8]{1,0:T(4,128)S(1)}, u32[]{:S(2)}, u32[]{:S(2)}) collective-permute-start(f32[3,8]{1,0:T(4,128)S(1)} %pad_maximum_fusion.4), channel_id=1, source_target_pairs={{0,16},{4,20},{8,24},{12,28},{16,0},{20,4},{24,8},{28,12},{1,17},{... | collective-permute-start | bytes 296 | tf_op jit(solution)/shard_map/ppermute | solution.py:64
  116.9 1.8 %fusion.1 = bf16[1,512,512]{2,1,0:T(8,128)(2,1)} fusion(bf16[512,512]{1,0:T(8,128)(2,1)S(1)} %copy-done.6, bf16[512,512]{1,0:T(8,128)(2,1)S(1)} %gather_fusion, pred[512]{0:T(512)(128)(4,1)} %get-tuple-element.90, pred[512]{0:T(512)(128)(4,1)} %compare_and_fusion.1, pred[512]{0:T(512)(128)(4,1)} %get-tuple-element.89), kind=kLoop, calls=%fused_computation.7 | loop fusion | flops 786432 | bytes 1574400 | tf_op jit(solution)/shard_map/jit(_where)/select_n | solution.py:215
  (118 shorter events, 26.5 us)
Async XLA Ops:
  0.6 61.0 %copy-start = (bf16[2560,80]{0,1:T(8,128)(2,1)S(1)}, bf16[2560,80]{0,1:T(8,128)(2,1)}, u32[]{:S(2)}) copy-start(bf16[2560,80]{0,1:T(8,128)(2,1)} %param.27) | copy-start | bytes 1228804
  0.6 16.0 %collective-permute-start.1 = (bf16[1,512,512]{2,1,0:T(8,128)(2,1)}, bf16[1,512,512]{2,1,0:T(8,128)(2,1)S(1)}, u32[]{:S(2)}, u32[]{:S(2)}) collective-permute-start(bf16[1,512,512]{2,1,0:T(8,128)(2,1)} %refs_10_.1), channel_id=1, source_target_pairs={{0,2},{1,3},{2,0},{3,1},{4,6},{5,7},{6,4},{7,5},{8,10},{9,11},{10,... | collective-permute-start | bytes 1572872 | tf_op jit(solution)/shard_map/ppermute | solution.py:81
  3.7 17.8 %collective-permute-start = (bf16[1,512,512]{2,1,0:T(8,128)(2,1)}, bf16[1,512,512]{2,1,0:T(8,128)(2,1)S(1)}, u32[]{:S(2)}, u32[]{:S(2)}) collective-permute-start(bf16[1,512,512]{2,1,0:T(8,128)(2,1)} %refs_10_.1), channel_id=1, source_target_pairs={{0,1},{1,0},{2,3},{3,2},{4,5},{5,4},{6,7},{7,6},{8,9},{9,8},{10,11... | collective-permute-start | bytes 1572872 | tf_op jit(solution)/shard_map/ppermute | solution.py:77
  3.7 17.6 %collective-permute-start.3 = (bf16[1,192,512]{2,1,0:T(8,128)(2,1)}, bf16[1,192,512]{2,1,0:T(8,128)(2,1)S(1)}, u32[]{:S(2)}, u32[]{:S(2)}) collective-permute-start(bf16[1,192,512]{2,1,0:T(8,128)(2,1)} %refs_18_.1), channel_id=1, source_target_pairs={{0,1},{1,0},{2,3},{3,2},{4,5},{5,4},{6,7},{7,6},{8,9},{9,8},{10,11... | collective-permute-start | bytes 589832 | tf_op jit(solution)/shard_map/ppermute | solution.py:77
  4.2 15.8 %collective-permute-start.4 = (bf16[1,192,512]{2,1,0:T(8,128)(2,1)}, bf16[1,192,512]{2,1,0:T(8,128)(2,1)S(1)}, u32[]{:S(2)}, u32[]{:S(2)}) collective-permute-start(bf16[1,192,512]{2,1,0:T(8,128)(2,1)} %refs_18_.1), channel_id=1, source_target_pairs={{0,2},{1,3},{2,0},{3,1},{4,6},{5,7},{6,4},{7,5},{8,10},{9,11},{10,... | collective-permute-start | bytes 589832 | tf_op jit(solution)/shard_map/ppermute | solution.py:81
  16.6 4.8 %collective-permute-start.2 = (bf16[1,512,512]{2,1,0:T(8,128)(2,1)S(1)}, bf16[1,512,512]{2,1,0:T(8,128)(2,1)S(1)}, u32[]{:S(2)}, u32[]{:S(2)}) collective-permute-start(bf16[1,512,512]{2,1,0:T(8,128)(2,1)S(1)} %collective-permute-done.1.refs_15_.refs_16_), channel_id=1, source_target_pairs={{0,1},{1,0},{2,3},{3,2},{4,5},{5,4},{6,7},{7,6},{8,9},{9,8},{10,11... | collective-permute-start | bytes 1572872 | tf_op jit(solution)/shard_map/ppermute | solution.py:91
  20.0 1.4 %collective-permute-start.5 = (bf16[1,192,512]{2,1,0:T(8,128)(2,1)S(1)}, bf16[1,192,512]{2,1,0:T(8,128)(2,1)S(1)}, u32[]{:S(2)}, u32[]{:S(2)}) collective-permute-start(bf16[1,192,512]{2,1,0:T(8,128)(2,1)S(1)} %collective-permute-done.4.refs_23_.refs_24_), channel_id=1, source_target_pairs={{0,1},{1,0},{2,3},{3,2},{4,5},{5,4},{6,7},{7,6},{8,9},{9,8},{10,11... | collective-permute-start | bytes 589832 | tf_op jit(solution)/shard_map/ppermute | solution.py:91
  22.5 47.6 %copy-start.26 = (s32[8]{0:T(128)S(1)}, s32[8]{0:T(128)}, u32[]{:S(2)}) copy-start(s32[8]{0:T(128)} %param.31) | copy-start | bytes 100
  22.5 56.7 %copy-start.18 = (bf16[2560]{0:T(1024)(128)(2,1)S(1)}, bf16[2560]{0:T(1024)(128)(2,1)}, u32[]{:S(2)}) copy-start(bf16[2560]{0:T(1024)(128)(2,1)} %param.29) | copy-start | bytes 15364
  43.5 1.3 %collective-permute-start.6 = (bf16[1,2560]{1,0:T(2,128)(2,1)S(1)}, bf16[1,2560]{1,0:T(2,128)(2,1)S(1)}, u32[]{:S(2)}, u32[]{:S(2)}) collective-permute-start(bf16[1,2560]{1,0:T(2,128)(2,1)S(1)} %fusion.15), channel_id=1, source_target_pairs={{0,1},{1,0},{2,3},{3,2},{4,5},{5,4},{6,7},{7,6},{8,9},{9,8},{10,11... | collective-permute-start | bytes 15368 | tf_op jit(solution)/shard_map/ppermute | solution.py:25
  45.6 3.7 %collective-permute-start.7 = (bf16[1,2560]{1,0:T(2,128)(2,1)S(1)}, bf16[1,2560]{1,0:T(2,128)(2,1)S(1)}, u32[]{:S(2)}, u32[]{:S(2)}) collective-permute-start(bf16[1,2560]{1,0:T(2,128)(2,1)S(1)} %fusion.47), channel_id=1, source_target_pairs={{0,2},{1,3},{2,0},{3,1},{4,6},{5,7},{6,4},{7,5},{8,10},{9,11},{10,... | collective-permute-start | bytes 15368 | tf_op jit(solution)/shard_map/ppermute | solution.py:25
  49.3 3.7 %collective-permute-start.8 = (bf16[1,2560]{1,0:T(2,128)(2,1)S(1)}, bf16[1,2560]{1,0:T(2,128)(2,1)S(1)}, u32[]{:S(2)}, u32[]{:S(2)}) collective-permute-start(bf16[1,2560]{1,0:T(2,128)(2,1)S(1)} %add.615), channel_id=1, source_target_pairs={{0,4},{4,0},{8,12},{12,8},{16,20},{20,16},{24,28},{28,24},{1,5},{5... | collective-permute-start | bytes 15368 | tf_op jit(solution)/shard_map/ppermute | solution.py:37
  53.1 3.7 %collective-permute-start.9 = (bf16[2,2560]{1,0:T(2,128)(2,1)S(1)}, bf16[2,2560]{1,0:T(2,128)(2,1)S(1)}, u32[]{:S(2)}, u32[]{:S(2)}) collective-permute-start(bf16[2,2560]{1,0:T(2,128)(2,1)S(1)} %broadcast_select_fusion.1), channel_id=1, source_target_pairs={{0,8},{4,12},{8,0},{12,4},{16,24},{20,28},{24,16},{28,20},{1,9},{5... | collective-permute-start | bytes 30728 | tf_op jit(solution)/shard_map/ppermute | solution.py:37
  56.9 4.7 %collective-permute-start.10 = (bf16[4,2560]{1,0:T(4,128)(2,1)S(1)}, bf16[4,2560]{1,0:T(4,128)(2,1)S(1)}, u32[]{:S(2)}, u32[]{:S(2)}) collective-permute-start(bf16[4,2560]{1,0:T(4,128)(2,1)S(1)} %maximum_select_fusion.3), channel_id=1, source_target_pairs={{0,16},{4,20},{8,24},{12,28},{16,0},{20,4},{24,8},{28,12},{1,17},{... | collective-permute-start | bytes 61448 | tf_op jit(solution)/shard_map/ppermute | solution.py:37
  61.9 2.7 %collective-permute-start.11 = (bf16[8,80]{1,0:T(8,128)(2,1)S(1)}, bf16[8,80]{1,0:T(8,128)(2,1)S(1)}, u32[]{:S(2)}, u32[]{:S(2)}) collective-permute-start(bf16[8,80]{1,0:T(8,128)(2,1)S(1)} %fusion), channel_id=1, source_target_pairs={{0,1},{1,0},{2,3},{3,2},{4,5},{5,4},{6,7},{7,6},{8,9},{9,8},{10,11... | collective-permute-start | bytes 3848 | tf_op jit(solution)/shard_map/ppermute | solution.py:37
  64.7 3.6 %collective-permute-start.12 = (bf16[8,160]{1,0:T(8,128)(2,1)S(1)}, bf16[8,160]{1,0:T(8,128)(2,1)S(1)}, u32[]{:S(2)}, u32[]{:S(2)}) collective-permute-start(bf16[8,160]{1,0:T(8,128)(2,1)S(1)} %maximum_select_fusion.8), channel_id=1, source_target_pairs={{0,2},{1,3},{2,0},{3,1},{4,6},{5,7},{6,4},{7,5},{8,10},{9,11},{10,... | collective-permute-start | bytes 7688 | tf_op jit(solution)/shard_map/ppermute | solution.py:37
  68.4 3.6 %collective-permute-start.13 = (bf16[8,320]{1,0:T(8,128)(2,1)S(1)}, bf16[8,320]{1,0:T(8,128)(2,1)S(1)}, u32[]{:S(2)}, u32[]{:S(2)}) collective-permute-start(bf16[8,320]{1,0:T(8,128)(2,1)S(1)} %maximum_select_fusion.7), channel_id=1, source_target_pairs={{0,4},{4,0},{8,12},{12,8},{16,20},{20,16},{24,28},{28,24},{1,5},{5... | collective-permute-start | bytes 15368 | tf_op jit(solution)/shard_map/ppermute | solution.py:37
  72.1 3.7 %collective-permute-start.14 = (bf16[8,640]{1,0:T(8,128)(2,1)S(1)}, bf16[8,640]{1,0:T(8,128)(2,1)S(1)}, u32[]{:S(2)}, u32[]{:S(2)}) collective-permute-start(bf16[8,640]{1,0:T(8,128)(2,1)S(1)} %maximum_select_fusion.5), channel_id=1, source_target_pairs={{0,8},{4,12},{8,0},{12,4},{16,24},{20,28},{24,16},{28,20},{1,9},{5... | collective-permute-start | bytes 30728 | tf_op jit(solution)/shard_map/ppermute | solution.py:37
  75.8 4.7 %collective-permute-start.15 = (bf16[8,1280]{1,0:T(8,128)(2,1)S(1)}, bf16[8,1280]{1,0:T(8,128)(2,1)S(1)}, u32[]{:S(2)}, u32[]{:S(2)}) collective-permute-start(bf16[8,1280]{1,0:T(8,128)(2,1)S(1)} %maximum_select_fusion.4), channel_id=1, source_target_pairs={{0,16},{4,20},{8,24},{12,28},{16,0},{20,4},{24,8},{28,12},{1,17},{... | collective-permute-start | bytes 61448 | tf_op jit(solution)/shard_map/ppermute | solution.py:37
  98.3 1.2 %collective-permute-start.16 = (f32[3,8]{1,0:T(4,128)S(1)}, f32[3,8]{1,0:T(4,128)S(1)}, u32[]{:S(2)}, u32[]{:S(2)}) collective-permute-start(f32[3,8]{1,0:T(4,128)S(1)} %pad_maximum_fusion), channel_id=1, source_target_pairs={{0,1},{1,0},{2,3},{3,2},{4,5},{5,4},{6,7},{7,6},{8,9},{9,8},{10,11... | collective-permute-start | bytes 296 | tf_op jit(solution)/shard_map/ppermute | solution.py:64
  100.1 4.5 %collective-permute-start.17 = (f32[3,8]{1,0:T(4,128)S(1)}, f32[3,8]{1,0:T(4,128)S(1)}, u32[]{:S(2)}, u32[]{:S(2)}) collective-permute-start(f32[3,8]{1,0:T(4,128)S(1)} %pad_maximum_fusion.1), channel_id=1, source_target_pairs={{0,2},{1,3},{2,0},{3,1},{4,6},{5,7},{6,4},{7,5},{8,10},{9,11},{10,... | collective-permute-start | bytes 296 | tf_op jit(solution)/shard_map/ppermute | solution.py:64
  105.2 3.6 %collective-permute-start.18 = (f32[3,8]{1,0:T(4,128)S(1)}, f32[3,8]{1,0:T(4,128)S(1)}, u32[]{:S(2)}, u32[]{:S(2)}) collective-permute-start(f32[3,8]{1,0:T(4,128)S(1)} %pad_maximum_fusion.2), channel_id=1, source_target_pairs={{0,4},{4,0},{8,12},{12,8},{16,20},{20,16},{24,28},{28,24},{1,5},{5... | collective-permute-start | bytes 296 | tf_op jit(solution)/shard_map/ppermute | solution.py:64
  109.4 4.0 %collective-permute-start.19 = (f32[3,8]{1,0:T(4,128)}, f32[3,8]{1,0:T(4,128)}, u32[]{:S(2)}, u32[]{:S(2)}) collective-permute-start(f32[3,8]{1,0:T(4,128)} %pad_maximum_fusion.3), channel_id=1, source_target_pairs={{0,8},{4,12},{8,0},{12,4},{16,24},{20,28},{24,16},{28,20},{1,9},{5... | collective-permute-start | bytes 296 | tf_op jit(solution)/shard_map/ppermute | solution.py:64
  114.2 4.5 %collective-permute-start.20 = (f32[3,8]{1,0:T(4,128)S(1)}, f32[3,8]{1,0:T(4,128)S(1)}, u32[]{:S(2)}, u32[]{:S(2)}) collective-permute-start(f32[3,8]{1,0:T(4,128)S(1)} %pad_maximum_fusion.4), channel_id=1, source_target_pairs={{0,16},{4,20},{8,24},{12,28},{16,0},{20,4},{24,8},{28,12},{1,17},{... | collective-permute-start | bytes 296 | tf_op jit(solution)/shard_map/ppermute | solution.py:64
  (24 other events, 191.2 us)

commit v4 on v3

--- a/solution.py
+++ b/solution.py
@@ -70,11 +70,11 @@
 def exchange_pieces(x, axis, dim):
     count = lax.axis_size(axis)
     if not is_pow2(count):
-        return [(lax.all_gather(x, axis, axis=dim, tiled=True), list(range(count)))], False
-    pieces = [(x, [0])]
+        return [(lax.all_gather(x, axis, axis=dim, tiled=True), list(range(count)))], [], False
+    local = [(x, [0])]
     if count == 1:
-        return pieces, True
-    near = lax.ppermute(x, axis, xor_pairs(count, 1))
+        return local, [], True
+    local.append((lax.ppermute(x, axis, xor_pairs(count, 1)), [1]))
     held, held_masks, far = x, [0], []
     bit = count // 2
     while bit > 1:
@@ -84,13 +84,17 @@
         held = jnp.concatenate([held, other], dim)
         held_masks = held_masks + other_masks
         bit //= 2
-    pieces.append((near, [1]))
-    if far:
-        far_rows = jnp.concatenate([p for p, _ in far], dim) if len(far) > 1 else far[0][0]
-        far_masks = [m for _, masks in far for m in masks]
-        pieces.append((lax.ppermute(far_rows, axis, xor_pairs(count, 1)), [m ^ 1 for m in far_masks]))
-        pieces.extend(far)
-    return pieces, True
+    return local, far, True
+
+
+def forward_pieces(far_rows, far, axis):
+    count = lax.axis_size(axis)
+    masks = [m ^ 1 for _, piece_masks in far for m in piece_masks]
+    return [(lax.ppermute(far_rows, axis, xor_pairs(count, 1)), masks)]
+
+
+def joined(far, dim):
+    return jnp.concatenate([p for p, _ in far], dim) if len(far) > 1 else far[0][0]
 
 
 def piece_sources(masks, by_xor, my_index):
@@ -98,12 +102,15 @@
     return jnp.bitwise_xor(masks, my_index) if by_xor else masks
 
 
-def attention_kernel(qpos_ref, *refs, kinds, scale):
+def attention_kernel(qpos_ref, *refs, kinds, scale, prior, final):
     count = len(kinds)
     bound_refs = refs[:count]
     q_ref = refs[count]
     kv_refs = refs[count + 1 : count + 1 + 2 * count]
-    out_ref = refs[-1]
+    rest = refs[count + 1 + 2 * count :]
+    if prior:
+        acc_in, peak_in, total_in = rest[:3]
+        rest = rest[3:]
     query = q_ref[0]
     position = qpos_ref[...]
     dims = (((1,), (1,)), ((), ()))
@@ -117,6 +124,9 @@
         seen = position <= bound if kind == "hi" else bound <= position
         masked.append(jnp.where(seen, score, -jnp.inf))
     peak = functools.reduce(jnp.maximum, [jnp.max(m, axis=1, keepdims=True) for m in masked])
+    if prior:
+        old_peak = peak_in[0, 0]
+        peak = jnp.maximum(peak, old_peak)
     weights = [jnp.exp(m - peak) for m in masked]
     total = functools.reduce(jnp.add, [jnp.sum(w, axis=1, keepdims=True) for w in weights])
     mixed = functools.reduce(
@@ -126,14 +136,29 @@
             for i, w in enumerate(weights)
         ],
     )
-    out_ref[0] = (mixed / total).astype(out_ref.dtype)
-
-
-def attend(queries, query_pos, pieces, head_dim):
+    if prior:
+        rescale = jnp.exp(old_peak - peak)
+        total = total + total_in[0, 0] * rescale
+        mixed = mixed + acc_in[0] * rescale
+    if final:
+        rest[0][0] = (mixed / total).astype(rest[0].dtype)
+    else:
+        rest[0][0] = mixed
+        rest[1][0, 0] = peak
+        rest[2][0, 0] = total
+
+
+def attend(queries, query_pos, pieces, head_dim, carried, final):
     req_local, new_local, model_cols = queries.shape
     head_count = model_cols // head_dim
     kinds = [kind for kind, _, _ in pieces]
-    kernel = functools.partial(attention_kernel, kinds=kinds, scale=1.0 / math.sqrt(head_dim))
+    kernel = functools.partial(
+        attention_kernel,
+        kinds=kinds,
+        scale=1.0 / math.sqrt(head_dim),
+        prior=carried is not None,
+        final=final,
+    )
     bound_specs = [
         pl.BlockSpec((1, 1, rows.shape[1]), lambda r, h: (r, 0, 0)) for _, rows, _ in pieces
     ]
@@ -143,16 +168,34 @@
         kv_specs.append(pl.BlockSpec((1, rows.shape[1], head_dim), lambda r, h: (r, 0, 0)))
         kv_specs.append(pl.BlockSpec((1, rows.shape[1], head_dim), lambda r, h: (r, 0, 1)))
         kv_args.extend([rows, rows])
+    row_spec = pl.BlockSpec((1, new_local, head_dim), lambda r, h: (r, 0, h))
+    stat_spec = pl.BlockSpec((1, 1, new_local, 1), lambda r, h: (r, h, 0, 0))
+    stat_shape = jax.ShapeDtypeStruct((req_local, head_count, new_local, 1), jnp.float32)
+    extra_specs, extra_args = [], []
+    if carried is not None:
+        extra_specs = [row_spec, stat_spec, stat_spec]
+        extra_args = list(carried)
+    if final:
+        out_specs = row_spec
+        out_shape = jax.ShapeDtypeStruct(queries.shape, queries.dtype)
+    else:
+        out_specs = [row_spec, stat_spec, stat_spec]
+        out_shape = [
+            jax.ShapeDtypeStruct(queries.shape, jnp.float32),
+            stat_shape,
+            stat_shape,
+        ]
     return pl.pallas_call(
         kernel,
         grid=(req_local, head_count),
         in_specs=[pl.BlockSpec((new_local, 1), lambda r, h: (0, 0))]
         + bound_specs
-        + [pl.BlockSpec((1, new_local, head_dim), lambda r, h: (r, 0, h))]
-        + kv_specs,
-        out_specs=pl.BlockSpec((1, new_local, head_dim), lambda r, h: (r, 0, h)),
-        out_shape=jax.ShapeDtypeStruct(queries.shape, queries.dtype),
-    )(query_pos, *[bound for _, _, bound in pieces], queries, *kv_args)
+        + [row_spec]
+        + kv_specs
+        + extra_specs,
+        out_specs=out_specs,
+        out_shape=out_shape,
+    )(query_pos, *[bound for _, _, bound in pieces], queries, *kv_args, *extra_args)
 
 
 def on_device(
@@ -176,21 +219,48 @@
     slot_ids = jnp.arange(slot_count, dtype=jnp.int32)
     new_ids = jnp.arange(new_local, dtype=jnp.int32)
 
-    cache_pieces, cache_xor = exchange_pieces(cache_pool, "gy", 1)
-    new_pieces, new_xor = exchange_pieces(new_kv, "gy", 1)
-    pieces = []
-    for rows, masks in cache_pieces:
-        stored = piece_sources(masks, cache_xor, my_index)
-        chosen = jnp.take(logical, stored, axis=1)
-        slot_pos = (chosen[:, :, None] * slot_count + slot_ids[None, None, :]).reshape(req_local, -1)
-        cache_hi = jnp.where(slot_pos >= first_slot[:, None], slot_pos, -1)[:, None, :]
-        pieces.append(("hi", rows, cache_hi))
-    for rows, masks in new_pieces:
-        chunk = piece_sources(masks, new_xor, my_index)
-        new_pos = (chunk[:, None] * new_local + new_ids[None, :]).reshape(-1)
-        new_lo = jnp.broadcast_to(new_pos[None, None, :], (req_local, 1, new_pos.shape[0]))
-        pieces.append(("lo", rows, new_lo))
-    mixed_out = attend(queries, query_pos, pieces, head_dim)
+    cache_local, cache_far, cache_xor = exchange_pieces(cache_pool, "gy", 1)
+    new_local_pieces, new_far, new_xor = exchange_pieces(new_kv, "gy", 1)
+
+    def cache_part(group):
+        parts = []
+        for rows, masks in group:
+            stored = piece_sources(masks, cache_xor, my_index)
+            chosen = jnp.take(logical, stored, axis=1)
+            slot_pos = (chosen[:, :, None] * slot_count + slot_ids[None, None, :]).reshape(
+                req_local, -1
+            )
+            cache_hi = jnp.where(slot_pos >= first_slot[:, None], slot_pos, -1)[:, None, :]
+            parts.append(("hi", rows, cache_hi))
+        return parts
+
+    def new_part(group):
+        parts = []
+        for rows, masks in group:
+            chunk = piece_sources(masks, new_xor, my_index)
+            new_pos = (chunk[:, None] * new_local + new_ids[None, :]).reshape(-1)
+            new_lo = jnp.broadcast_to(new_pos[None, None, :], (req_local, 1, new_pos.shape[0]))
+            parts.append(("lo", rows, new_lo))
+        return parts
+
+    local_parts = cache_part(cache_local) + new_part(new_local_pieces)
+    cache_pieces = list(cache_local)
+    new_pieces = list(new_local_pieces)
+    if cache_far or new_far:
+        carried = attend(queries, query_pos, local_parts, head_dim, None, False)
+        far_parts = cache_part(cache_far) + new_part(new_far)
+        cache_rows, new_rows, carried = lax.optimization_barrier(
+            (joined(cache_far, 1), joined(new_far, 1), carried)
+        )
+        cache_fwd = forward_pieces(cache_rows, cache_far, "gy")
+        new_fwd = forward_pieces(new_rows, new_far, "gy")
+        carried = attend(queries, query_pos, far_parts, head_dim, carried, False)
+        fwd_parts = cache_part(cache_fwd) + new_part(new_fwd)
+        mixed_out = attend(queries, query_pos, fwd_parts, head_dim, carried, True)
+        cache_pieces += list(cache_far) + cache_fwd
+        new_pieces += list(new_far) + new_fwd
+    else:
+        mixed_out = attend(queries, query_pos, local_parts, head_dim, None, True)
 
     cache_masks = [m for _, masks in cache_pieces for m in masks]
     new_masks = [m for _, masks in new_pieces for m in masks]

time: 121 us -> 130 us (1.074)
  Pallas kernels: 20.2 us -> 35.3 us
  waiting for transfers between devices: 24.4 us -> 17.1 us
  starting transfers between devices: 28.3 us -> 24.7 us
  other arithmetic: 16.6 us -> 20.2 us
    pallas_call x1 -> x3, Pallas kernels: 20.2 us -> 35.3 us  [attend(): pl.pallas_call(kernel, grid=(req_local, head_count), in_specs=[pl.BlockSp...]
    ppermute x2, waiting for transfers between devices: 9.35 us -> 0.01 us  [exchange_pieces(): other = lax.ppermute(held, axis, xor_pairs(count, bit))]
    select_n x3 -> x4, other arithmetic: 3.91 us -> 6.67 us  [the longest x1 4.96 us: on_device(): from_new = jnp.take_along_axis(new_keys, new_row[:, :, None], axis=1)]
    ppermute x8, starting transfers between devices: 14.8 us -> 12.4 us  [butterfly_gather(): other = lax.ppermute(x, axis, xor_pairs(count, bit))]
    ppermute x5, starting transfers between devices: 7.69 us -> 6.21 us  [butterfly_stats(): other = lax.ppermute(packed, axis, xor_pairs(count, bit))]
    ppermute x5, waiting for transfers between devices: 2.11 us -> 3.46 us  [butterfly_stats(): other = lax.ppermute(packed, axis, xor_pairs(count, bit))]
  transfers between devices with their start and end apart: 21 -> 21, of which waited for: 16 -> 13; matrix products, arithmetic and copies ran while one was open for 15% -> 17% of each run, Pallas kernels for 0% -> 19%
where the time goes in v4:
time: 130 us; the launch traced here: 129 us
  Pallas kernels  35.3 us (27%)
  starting transfers between devices  24.7 us (19%)
  other arithmetic  20.2 us (16%)
  matrix products  17.5 us (13%)
  waiting for transfers between devices  17.1 us (13%)
  local copies, waits for them, and re-layouts  9.52 us (7%)
  between operations  4.82 us (4%)
    pallas_call x3, Pallas kernels, attend(): pl.pallas_call(kernel, grid=(req_local, head_count), in_specs=[pl.BlockSp...  35.3 us
    dot_general x1, matrix products, on_device(): lax.dot_general(normed, head, (((1,), (1,)), ((), ())), preferred_element...  17.3 us
    ppermute x8, starting transfers between devices, butterfly_gather(): other = lax.ppermute(x, axis, xor_pairs(count, bit))  12.4 us
    ppermute x8, waiting for transfers between devices, butterfly_gather(): other = lax.ppermute(x, axis, xor_pairs(count, bit))  11.3 us
    ppermute x5, starting transfers between devices, butterfly_stats(): other = lax.ppermute(packed, axis, xor_pairs(count, bit))  6.21 us
    select_n x1, other arithmetic, on_device(): from_new = jnp.take_along_axis(new_keys, new_row[:, :, None], axis=1)  4.96 us
    ppermute x5, waiting for transfers between devices, butterfly_stats(): other = lax.ppermute(packed, axis, xor_pairs(count, bit))  3.46 us
    unnamed x54, local copies, waits for them, and re-layouts  2.86 us
  transfers between devices with their start and end apart: 21, of which 13 were waited for; matrix products, arithmetic and copies ran while one was open for 17% of the time, Pallas kernels for 19%

profile of v4, /device:TPU:0, one launch (start us, length us, event | category | flops | bytes accessed | tf_op | source)
XLA Modules:
  0.0 129.1 jit_solution(320805108918470513)
XLA Ops:
  1.2 2.6 %collective-permute-start = (bf16[1,512,512]{2,1,0:T(8,128)(2,1)}, bf16[1,512,512]{2,1,0:T(8,128)(2,1)S(1)}, u32[]{:S(2)}, u32[]{:S(2)}) collective-permute-start(bf16[1,512,512]{2,1,0:T(8,128)(2,1)} %refs_6_.1), channel_id=1, source_target_pairs={{0,2},{1,3},{2,0},{3,1},{4,6},{5,7},{6,4},{7,5},{8,10},{9,11},{10,... | collective-permute-start | bytes 1572872 | tf_op jit(solution)/shard_map/ppermute | solution.py:81
  10.2 13.0 %shard_map.230 = (f32[1,192,2560]{2,1,0:T(8,128)}, f32[1,10,192,1]{3,2,1,0:T(8,128)}, f32[1,10,192,1]{3,2,1,0:T(8,128)}) custom-call(s32[192,1]{1,0:T(8,128)} %iota_add_fusion.qpos_ref, s32[1,1,512]{2,1,0:T(1,128)} %get-tuple-element.111.refs_0_, s32[1,1,512]{2,1,0:T(1,128)} %get-tuple-element.110.refs_1_, s32[1,1,192]{2,1,0:T(1,128)} %get-tuple-element.113.refs_2_, ...), custom_call_target="tpu_custom_call" | custom-call | tf_op jit(solution)/shard_map/pallas_call | solution.py:188
  27.2 11.2 %shard_map.231 = (f32[1,192,2560]{2,1,0:T(8,128)}, f32[1,10,192,1]{3,2,1,0:T(8,128)}, f32[1,10,192,1]{3,2,1,0:T(8,128)}) custom-call(s32[192,1]{1,0:T(8,128)} %iota_add_fusion.qpos_ref, s32[1,1,512]{2,1,0:T(1,128)} %compare_select_fusion.6.refs_0_, s32[1,1,192]{2,1,0:T(1,128)} %iota_add_fusion.2.refs_1_, bf16[1,192,2560]{2,1,0:T(8,128)(2,1)} %refs_2_.3, ...), custom_call_target="tpu_custom_call" | custom-call | tf_op jit(solution)/shard_map/pallas_call | solution.py:188
  39.3 11.1 %shard_map.232 = bf16[1,192,2560]{2,1,0:T(8,128)(2,1)} custom-call(s32[192,1]{1,0:T(8,128)} %iota_add_fusion.qpos_ref, s32[1,1,512]{2,1,0:T(1,128)} %compare_select_fusion.9.refs_0_, s32[1,1,192]{2,1,0:T(1,128)} %iota_add_fusion.5.refs_1_, bf16[1,192,2560]{2,1,0:T(8,128)(2,1)} %refs_2_.3, bf16[1,512,512]{2,1,0:T(8,128)(2,1)} %copy-done.5, ...), custom_call_target="tpu_custom_call" | custom-call | tf_op jit(solution)/shard_map/pallas_call | solution.py:188
  53.2 1.8 %collective-permute-start.7 = (bf16[1,2560]{1,0:T(2,128)(2,1)S(1)}, bf16[1,2560]{1,0:T(2,128)(2,1)S(1)}, u32[]{:S(2)}, u32[]{:S(2)}) collective-permute-start(bf16[1,2560]{1,0:T(2,128)(2,1)S(1)} %fusion.49), channel_id=1, source_target_pairs={{0,2},{1,3},{2,0},{3,1},{4,6},{5,7},{6,4},{7,5},{8,10},{9,11},{10,... | collective-permute-start | bytes 15368 | tf_op jit(solution)/shard_map/ppermute | solution.py:25
  57.0 1.9 %collective-permute-start.8 = (bf16[1,2560]{1,0:T(2,128)(2,1)S(1)}, bf16[1,2560]{1,0:T(2,128)(2,1)S(1)}, u32[]{:S(2)}, u32[]{:S(2)}) collective-permute-start(bf16[1,2560]{1,0:T(2,128)(2,1)S(1)} %add.615), channel_id=1, source_target_pairs={{0,4},{4,0},{8,12},{12,8},{16,20},{20,16},{24,28},{28,24},{1,5},{5... | collective-permute-start | bytes 15368 | tf_op jit(solution)/shard_map/ppermute | solution.py:37
  60.8 1.9 %collective-permute-start.9 = (bf16[2,2560]{1,0:T(2,128)(2,1)S(1)}, bf16[2,2560]{1,0:T(2,128)(2,1)S(1)}, u32[]{:S(2)}, u32[]{:S(2)}) collective-permute-start(bf16[2,2560]{1,0:T(2,128)(2,1)S(1)} %broadcast_select_fusion.1), channel_id=1, source_target_pairs={{0,8},{4,12},{8,0},{12,4},{16,24},{20,28},{24,16},{28,20},{1,9},{5... | collective-permute-start | bytes 30728 | tf_op jit(solution)/shard_map/ppermute | solution.py:37
  62.7 5.0 %compare_select_fusion.2 = (s32[512,1]{0,1:T(1,128)S(1)}, s32[1,512]{1,0:T(1,128)S(1)}, s32[512,1]{0,1:T(1,128)S(1)}, s32[1,512]{1,0:T(1,128)S(1)}) fusion(s32[]{:T(128)} %bitcast.24, s32[]{:T(128)} %bitcast.23, s32[]{:T(128)} %bitcast.22, s32[]{:T(128)} %bitcast.21, s32[]{:T(128)} %axis_index.14, s32[]{:T(128)} %bitcast.15, s32[]{:T(128)} %bitcast.19, ...), kind=kLoop, calls=%fused_computation.35 | loop fusion | flops 55296 | bytes 8232 | tf_op jit(solution)/shard_map/jit(take_along_axis)/select_n | solution.py:284
  67.7 2.7 %collective-permute-start.10 = (bf16[4,2560]{1,0:T(4,128)(2,1)S(1)}, bf16[4,2560]{1,0:T(4,128)(2,1)S(1)}, u32[]{:S(2)}, u32[]{:S(2)}) collective-permute-start(bf16[4,2560]{1,0:T(4,128)(2,1)S(1)} %maximum_select_fusion.3), channel_id=1, source_target_pairs={{0,16},{4,20},{8,24},{12,28},{16,0},{20,4},{24,8},{28,12},{1,17},{... | collective-permute-start | bytes 61448 | tf_op jit(solution)/shard_map/ppermute | solution.py:37
  70.9 1.6 %collective-permute-done.10 = bf16[4,2560]{1,0:T(4,128)(2,1)S(1)} collective-permute-done((bf16[4,2560]{1,0:T(4,128)(2,1)S(1)}, bf16[4,2560]{1,0:T(4,128)(2,1)S(1)}, u32[]{:S(2)}, u32[]{:S(2)}) %collective-permute-start.10) | collective-permute-done | bytes 20512 | tf_op jit(solution)/shard_map/ppermute | solution.py:37
  73.9 1.6 %collective-permute-start.12 = (bf16[8,160]{1,0:T(8,128)(2,1)S(1)}, bf16[8,160]{1,0:T(8,128)(2,1)S(1)}, u32[]{:S(2)}, u32[]{:S(2)}) collective-permute-start(bf16[8,160]{1,0:T(8,128)(2,1)S(1)} %maximum_select_fusion.8), channel_id=1, source_target_pairs={{0,2},{1,3},{2,0},{3,1},{4,6},{5,7},{6,4},{7,5},{8,10},{9,11},{10,... | collective-permute-start | bytes 7688 | tf_op jit(solution)/shard_map/ppermute | solution.py:37
  75.5 2.0 %collective-permute-done.12 = bf16[8,160]{1,0:T(8,128)(2,1)S(1)} collective-permute-done((bf16[8,160]{1,0:T(8,128)(2,1)S(1)}, bf16[8,160]{1,0:T(8,128)(2,1)S(1)}, u32[]{:S(2)}, u32[]{:S(2)}) %collective-permute-start.12) | collective-permute-done | bytes 2592 | tf_op jit(solution)/shard_map/ppermute | solution.py:37
  77.6 1.6 %collective-permute-start.13 = (bf16[8,320]{1,0:T(8,128)(2,1)S(1)}, bf16[8,320]{1,0:T(8,128)(2,1)S(1)}, u32[]{:S(2)}, u32[]{:S(2)}) collective-permute-start(bf16[8,320]{1,0:T(8,128)(2,1)S(1)} %maximum_select_fusion.7), channel_id=1, source_target_pairs={{0,4},{4,0},{8,12},{12,8},{16,20},{20,16},{24,28},{28,24},{1,5},{5... | collective-permute-start | bytes 15368 | tf_op jit(solution)/shard_map/ppermute | solution.py:37
  81.5 3.5 %collective-permute-done.14 = bf16[8,640]{1,0:T(8,128)(2,1)S(1)} collective-permute-done((bf16[8,640]{1,0:T(8,128)(2,1)S(1)}, bf16[8,640]{1,0:T(8,128)(2,1)S(1)}, u32[]{:S(2)}, u32[]{:S(2)}) %collective-permute-start.14) | collective-permute-done | bytes 10272 | tf_op jit(solution)/shard_map/ppermute | solution.py:37
  85.0 2.6 %collective-permute-start.15 = (bf16[8,1280]{1,0:T(8,128)(2,1)S(1)}, bf16[8,1280]{1,0:T(8,128)(2,1)S(1)}, u32[]{:S(2)}, u32[]{:S(2)}) collective-permute-start(bf16[8,1280]{1,0:T(8,128)(2,1)S(1)} %maximum_select_fusion.4), channel_id=1, source_target_pairs={{0,16},{4,20},{8,24},{12,28},{16,0},{20,4},{24,8},{28,12},{1,17},{... | collective-permute-start | bytes 61448 | tf_op jit(solution)/shard_map/ppermute | solution.py:37
  88.1 1.6 %collective-permute-done.15 = bf16[8,1280]{1,0:T(8,128)(2,1)S(1)} collective-permute-done((bf16[8,1280]{1,0:T(8,128)(2,1)S(1)}, bf16[8,1280]{1,0:T(8,128)(2,1)S(1)}, u32[]{:S(2)}, u32[]{:S(2)}) %collective-permute-start.15) | collective-permute-done | bytes 20512 | tf_op jit(solution)/shard_map/ppermute | solution.py:37
  89.9 17.3 %fusion.46 = (f32[8]{0:T(128)S(1)}, f32[8,8000]{1,0:T(8,128)S(1)}) fusion(bf16[8000,2560]{1,0:T(8,128)(2,1)} %param.30, f32[2560]{0:T(1024)S(1)} %convert_element_type.18, f32[8]{0:T(128)S(1)} %add_rsqrt_fusion, bf16[8,1280]{1,0:T(8,128)(2,1)S(1)} %maximum_select_fusion.4, bf16[8,1280]{1,0:T(8,128)(2,1)S(1)} %collective-permute-done.15, pred[]{:T(512)S(6)} %eq.61), kind=kOutput, calls=%fused_computation.150 | convolution fusion | flops 328010240 | bytes 41267264 | tf_op jit(solution)/shard_map/dot_general | solution.py:304
  109.3 1.7 %collective-permute-start.17 = (f32[3,8]{1,0:T(4,128)S(1)}, f32[3,8]{1,0:T(4,128)S(1)}, u32[]{:S(2)}, u32[]{:S(2)}) collective-permute-start(f32[3,8]{1,0:T(4,128)S(1)} %pad_maximum_fusion.1), channel_id=1, source_target_pairs={{0,2},{1,3},{2,0},{3,1},{4,6},{5,7},{6,4},{7,5},{8,10},{9,11},{10,... | collective-permute-start | bytes 296 | tf_op jit(solution)/shard_map/ppermute | solution.py:64
  111.0 2.6 %gather_fusion.1 = bf16[512,512]{1,0:T(8,128)(2,1)} fusion(bf16[768,512]{1,0:T(8,128)(2,1)S(1)} %maximum_bitcast_fusion.1, s32[1024]{0:T(1024)S(1)} %pad_clamp_fusion), kind=kCustom, calls=%fused_computation.1 | custom fusion | bytes 1050624 | tf_op jit(solution)/shard_map/jit(take_along_axis)/gather | solution.py:284
  114.2 1.5 %collective-permute-start.18 = (f32[3,8]{1,0:T(4,128)S(1)}, f32[3,8]{1,0:T(4,128)S(1)}, u32[]{:S(2)}, u32[]{:S(2)}) collective-permute-start(f32[3,8]{1,0:T(4,128)S(1)} %pad_maximum_fusion.2), channel_id=1, source_target_pairs={{0,4},{4,0},{8,12},{12,8},{16,20},{20,16},{24,28},{28,24},{1,5},{5... | collective-permute-start | bytes 296 | tf_op jit(solution)/shard_map/ppermute | solution.py:64
  118.8 2.1 %gather_fusion = bf16[512,512]{1,0:T(8,128)(2,1)S(1)} fusion(bf16[2048,512]{1,0:T(8,128)(2,1)S(1)} %maximum_bitcast_fusion, s32[1024]{0:T(1024)} %pad_clamp_fusion.1), kind=kCustom, calls=%fused_computation | custom fusion | bytes 1050624 | tf_op jit(solution)/shard_map/jit(take_along_axis)/gather | solution.py:283
  121.0 1.4 %collective-permute-done.19 = f32[3,8]{1,0:T(4,128)} collective-permute-done((f32[3,8]{1,0:T(4,128)}, f32[3,8]{1,0:T(4,128)}, u32[]{:S(2)}, u32[]{:S(2)}) %collective-permute-start.19) | collective-permute-done | bytes 128 | tf_op jit(solution)/shard_map/ppermute | solution.py:64
  123.2 2.5 %collective-permute-start.20 = (f32[3,8]{1,0:T(4,128)S(1)}, f32[3,8]{1,0:T(4,128)S(1)}, u32[]{:S(2)}, u32[]{:S(2)}) collective-permute-start(f32[3,8]{1,0:T(4,128)S(1)} %pad_maximum_fusion.4), channel_id=1, source_target_pairs={{0,16},{4,20},{8,24},{12,28},{16,0},{20,4},{24,8},{28,12},{1,17},{... | collective-permute-start | bytes 296 | tf_op jit(solution)/shard_map/ppermute | solution.py:64
  125.8 1.8 %fusion.1 = bf16[1,512,512]{2,1,0:T(8,128)(2,1)} fusion(bf16[512,512]{1,0:T(8,128)(2,1)S(1)} %copy-done.6, bf16[512,512]{1,0:T(8,128)(2,1)S(1)} %gather_fusion, pred[512]{0:T(512)(128)(4,1)} %compare_and_fusion, pred[512]{0:T(512)(128)(4,1)} %compare_and_fusion.1, pred[512]{0:T(512)(128)(4,1)} %add_compare_fusion), kind=kLoop, calls=%fused_computation.7 | loop fusion | flops 786432 | bytes 1574400 | tf_op jit(solution)/shard_map/jit(_where)/select_n | solution.py:285
  (124 shorter events, 27.8 us)
Async XLA Ops:
  0.6 71.8 %copy-start = (bf16[2560,80]{0,1:T(8,128)(2,1)S(1)}, bf16[2560,80]{0,1:T(8,128)(2,1)}, u32[]{:S(2)}) copy-start(bf16[2560,80]{0,1:T(8,128)(2,1)} %param.27) | copy-start | bytes 1228804
  0.6 8.6 %collective-permute-start.2 = (bf16[1,512,512]{2,1,0:T(8,128)(2,1)}, bf16[1,512,512]{2,1,0:T(8,128)(2,1)S(1)}, u32[]{:S(2)}, u32[]{:S(2)}) collective-permute-start(bf16[1,512,512]{2,1,0:T(8,128)(2,1)} %refs_6_.1), channel_id=1, source_target_pairs={{0,1},{1,0},{2,3},{3,2},{4,5},{5,4},{6,7},{7,6},{8,9},{9,8},{10,11... | collective-permute-start | bytes 1572872 | tf_op jit(solution)/shard_map/ppermute | solution.py:77
  1.2 22.1 %collective-permute-start = (bf16[1,512,512]{2,1,0:T(8,128)(2,1)}, bf16[1,512,512]{2,1,0:T(8,128)(2,1)S(1)}, u32[]{:S(2)}, u32[]{:S(2)}) collective-permute-start(bf16[1,512,512]{2,1,0:T(8,128)(2,1)} %refs_6_.1), channel_id=1, source_target_pairs={{0,2},{1,3},{2,0},{3,1},{4,6},{5,7},{6,4},{7,5},{8,10},{9,11},{10,... | collective-permute-start | bytes 1572872 | tf_op jit(solution)/shard_map/ppermute | solution.py:81
  3.7 5.5 %collective-permute-start.3 = (bf16[1,192,512]{2,1,0:T(8,128)(2,1)}, bf16[1,192,512]{2,1,0:T(8,128)(2,1)S(1)}, u32[]{:S(2)}, u32[]{:S(2)}) collective-permute-start(bf16[1,192,512]{2,1,0:T(8,128)(2,1)} %refs_10_.1), channel_id=1, source_target_pairs={{0,1},{1,0},{2,3},{3,2},{4,5},{5,4},{6,7},{7,6},{8,9},{9,8},{10,11... | collective-permute-start | bytes 589832 | tf_op jit(solution)/shard_map/ppermute | solution.py:77
  3.9 19.3 %collective-permute-start.1 = (bf16[1,192,512]{2,1,0:T(8,128)(2,1)}, bf16[1,192,512]{2,1,0:T(8,128)(2,1)S(1)}, u32[]{:S(2)}, u32[]{:S(2)}) collective-permute-start(bf16[1,192,512]{2,1,0:T(8,128)(2,1)} %refs_10_.1), channel_id=1, source_target_pairs={{0,2},{1,3},{2,0},{3,1},{4,6},{5,7},{6,4},{7,5},{8,10},{9,11},{10,... | collective-permute-start | bytes 589832 | tf_op jit(solution)/shard_map/ppermute | solution.py:81
  23.2 15.2 %collective-permute-start.4 = (bf16[1,512,512]{2,1,0:T(8,128)(2,1)S(1)}, bf16[1,512,512]{2,1,0:T(8,128)(2,1)S(1)}, u32[]{:S(2)}, u32[]{:S(2)}) collective-permute-start(bf16[1,512,512]{2,1,0:T(8,128)(2,1)S(1)} %collective-permute-done.refs_3_.refs_4_), channel_id=1, source_target_pairs={{0,1},{1,0},{2,3},{3,2},{4,5},{5,4},{6,7},{7,6},{8,9},{9,8},{10,11... | collective-permute-start | bytes 1572872 | tf_op jit(solution)/shard_map/ppermute | solution.py:93
  25.7 12.7 %collective-permute-start.5 = (bf16[1,192,512]{2,1,0:T(8,128)(2,1)S(1)}, bf16[1,192,512]{2,1,0:T(8,128)(2,1)S(1)}, u32[]{:S(2)}, u32[]{:S(2)}) collective-permute-start(bf16[1,192,512]{2,1,0:T(8,128)(2,1)S(1)} %collective-permute-done.1.refs_5_.refs_6_), channel_id=1, source_target_pairs={{0,1},{1,0},{2,3},{3,2},{4,5},{5,4},{6,7},{7,6},{8,9},{9,8},{10,11... | collective-permute-start | bytes 589832 | tf_op jit(solution)/shard_map/ppermute | solution.py:93
  39.3 36.2 %copy-start.26 = (s32[8]{0:T(128)S(1)}, s32[8]{0:T(128)}, u32[]{:S(2)}) copy-start(s32[8]{0:T(128)} %param.31) | copy-start | bytes 100
  39.3 48.8 %copy-start.18 = (bf16[2560]{0:T(1024)(128)(2,1)S(1)}, bf16[2560]{0:T(1024)(128)(2,1)}, u32[]{:S(2)}) copy-start(bf16[2560]{0:T(1024)(128)(2,1)} %param.29) | copy-start | bytes 15364
  51.2 1.2 collective-permute-start.6
  53.2 3.7 %collective-permute-start.7 = (bf16[1,2560]{1,0:T(2,128)(2,1)S(1)}, bf16[1,2560]{1,0:T(2,128)(2,1)S(1)}, u32[]{:S(2)}, u32[]{:S(2)}) collective-permute-start(bf16[1,2560]{1,0:T(2,128)(2,1)S(1)} %fusion.49), channel_id=1, source_target_pairs={{0,2},{1,3},{2,0},{3,1},{4,6},{5,7},{6,4},{7,5},{8,10},{9,11},{10,... | collective-permute-start | bytes 15368 | tf_op jit(solution)/shard_map/ppermute | solution.py:25
  57.0 3.7 %collective-permute-start.8 = (bf16[1,2560]{1,0:T(2,128)(2,1)S(1)}, bf16[1,2560]{1,0:T(2,128)(2,1)S(1)}, u32[]{:S(2)}, u32[]{:S(2)}) collective-permute-start(bf16[1,2560]{1,0:T(2,128)(2,1)S(1)} %add.615), channel_id=1, source_target_pairs={{0,4},{4,0},{8,12},{12,8},{16,20},{20,16},{24,28},{28,24},{1,5},{5... | collective-permute-start | bytes 15368 | tf_op jit(solution)/shard_map/ppermute | solution.py:37
  60.8 6.9 %collective-permute-start.9 = (bf16[2,2560]{1,0:T(2,128)(2,1)S(1)}, bf16[2,2560]{1,0:T(2,128)(2,1)S(1)}, u32[]{:S(2)}, u32[]{:S(2)}) collective-permute-start(bf16[2,2560]{1,0:T(2,128)(2,1)S(1)} %broadcast_select_fusion.1), channel_id=1, source_target_pairs={{0,8},{4,12},{8,0},{12,4},{16,24},{20,28},{24,16},{28,20},{1,9},{5... | collective-permute-start | bytes 30728 | tf_op jit(solution)/shard_map/ppermute | solution.py:37
  67.7 4.7 %collective-permute-start.10 = (bf16[4,2560]{1,0:T(4,128)(2,1)S(1)}, bf16[4,2560]{1,0:T(4,128)(2,1)S(1)}, u32[]{:S(2)}, u32[]{:S(2)}) collective-permute-start(bf16[4,2560]{1,0:T(4,128)(2,1)S(1)} %maximum_select_fusion.3), channel_id=1, source_target_pairs={{0,16},{4,20},{8,24},{12,28},{16,0},{20,4},{24,8},{28,12},{1,17},{... | collective-permute-start | bytes 61448 | tf_op jit(solution)/shard_map/ppermute | solution.py:37
  72.7 1.2 collective-permute-start.11
  73.9 3.6 %collective-permute-start.12 = (bf16[8,160]{1,0:T(8,128)(2,1)S(1)}, bf16[8,160]{1,0:T(8,128)(2,1)S(1)}, u32[]{:S(2)}, u32[]{:S(2)}) collective-permute-start(bf16[8,160]{1,0:T(8,128)(2,1)S(1)} %maximum_select_fusion.8), channel_id=1, source_target_pairs={{0,2},{1,3},{2,0},{3,1},{4,6},{5,7},{6,4},{7,5},{8,10},{9,11},{10,... | collective-permute-start | bytes 7688 | tf_op jit(solution)/shard_map/ppermute | solution.py:37
  77.6 3.6 %collective-permute-start.13 = (bf16[8,320]{1,0:T(8,128)(2,1)S(1)}, bf16[8,320]{1,0:T(8,128)(2,1)S(1)}, u32[]{:S(2)}, u32[]{:S(2)}) collective-permute-start(bf16[8,320]{1,0:T(8,128)(2,1)S(1)} %maximum_select_fusion.7), channel_id=1, source_target_pairs={{0,4},{4,0},{8,12},{12,8},{16,20},{20,16},{24,28},{28,24},{1,5},{5... | collective-permute-start | bytes 15368 | tf_op jit(solution)/shard_map/ppermute | solution.py:37
  81.3 3.7 %collective-permute-start.14 = (bf16[8,640]{1,0:T(8,128)(2,1)S(1)}, bf16[8,640]{1,0:T(8,128)(2,1)S(1)}, u32[]{:S(2)}, u32[]{:S(2)}) collective-permute-start(bf16[8,640]{1,0:T(8,128)(2,1)S(1)} %maximum_select_fusion.5), channel_id=1, source_target_pairs={{0,8},{4,12},{8,0},{12,4},{16,24},{20,28},{24,16},{28,20},{1,9},{5... | collective-permute-start | bytes 30728 | tf_op jit(solution)/shard_map/ppermute | solution.py:37
  85.0 4.7 %collective-permute-start.15 = (bf16[8,1280]{1,0:T(8,128)(2,1)S(1)}, bf16[8,1280]{1,0:T(8,128)(2,1)S(1)}, u32[]{:S(2)}, u32[]{:S(2)}) collective-permute-start(bf16[8,1280]{1,0:T(8,128)(2,1)S(1)} %maximum_select_fusion.4), channel_id=1, source_target_pairs={{0,16},{4,20},{8,24},{12,28},{16,0},{20,4},{24,8},{28,12},{1,17},{... | collective-permute-start | bytes 61448 | tf_op jit(solution)/shard_map/ppermute | solution.py:37
  107.5 1.2 collective-permute-start.16
  109.3 4.3 %collective-permute-start.17 = (f32[3,8]{1,0:T(4,128)S(1)}, f32[3,8]{1,0:T(4,128)S(1)}, u32[]{:S(2)}, u32[]{:S(2)}) collective-permute-start(f32[3,8]{1,0:T(4,128)S(1)} %pad_maximum_fusion.1), channel_id=1, source_target_pairs={{0,2},{1,3},{2,0},{3,1},{4,6},{5,7},{6,4},{7,5},{8,10},{9,11},{10,... | collective-permute-start | bytes 296 | tf_op jit(solution)/shard_map/ppermute | solution.py:64
  114.2 3.6 %collective-permute-start.18 = (f32[3,8]{1,0:T(4,128)S(1)}, f32[3,8]{1,0:T(4,128)S(1)}, u32[]{:S(2)}, u32[]{:S(2)}) collective-permute-start(f32[3,8]{1,0:T(4,128)S(1)} %pad_maximum_fusion.2), channel_id=1, source_target_pairs={{0,4},{4,0},{8,12},{12,8},{16,20},{20,16},{24,28},{28,24},{1,5},{5... | collective-permute-start | bytes 296 | tf_op jit(solution)/shard_map/ppermute | solution.py:64
  118.4 4.0 %collective-permute-start.19 = (f32[3,8]{1,0:T(4,128)}, f32[3,8]{1,0:T(4,128)}, u32[]{:S(2)}, u32[]{:S(2)}) collective-permute-start(f32[3,8]{1,0:T(4,128)} %pad_maximum_fusion.3), channel_id=1, source_target_pairs={{0,8},{4,12},{8,0},{12,4},{16,24},{20,28},{24,16},{28,20},{1,9},{5... | collective-permute-start | bytes 296 | tf_op jit(solution)/shard_map/ppermute | solution.py:64
  123.2 4.5 %collective-permute-start.20 = (f32[3,8]{1,0:T(4,128)S(1)}, f32[3,8]{1,0:T(4,128)S(1)}, u32[]{:S(2)}, u32[]{:S(2)}) collective-permute-start(f32[3,8]{1,0:T(4,128)S(1)} %pad_maximum_fusion.4), channel_id=1, source_target_pairs={{0,16},{4,20},{8,24},{12,28},{16,0},{20,4},{24,8},{28,12},{1,17},{... | collective-permute-start | bytes 296 | tf_op jit(solution)/shard_map/ppermute | solution.py:64
  (24 other events, 164.3 us)

commit v5 on v4

--- a/solution.py
+++ b/solution.py
@@ -125,7 +125,7 @@
         masked.append(jnp.where(seen, score, -jnp.inf))
     peak = functools.reduce(jnp.maximum, [jnp.max(m, axis=1, keepdims=True) for m in masked])
     if prior:
-        old_peak = peak_in[0, 0]
+        old_peak = peak_in[0, 0][:, :1]
         peak = jnp.maximum(peak, old_peak)
     weights = [jnp.exp(m - peak) for m in masked]
     total = functools.reduce(jnp.add, [jnp.sum(w, axis=1, keepdims=True) for w in weights])
@@ -138,14 +138,14 @@
     )
     if prior:
         rescale = jnp.exp(old_peak - peak)
-        total = total + total_in[0, 0] * rescale
+        total = total + total_in[0, 0][:, :1] * rescale
         mixed = mixed + acc_in[0] * rescale
     if final:
         rest[0][0] = (mixed / total).astype(rest[0].dtype)
     else:
         rest[0][0] = mixed
-        rest[1][0, 0] = peak
-        rest[2][0, 0] = total
+        rest[1][0, 0] = jnp.broadcast_to(peak, rest[1].shape[2:])
+        rest[2][0, 0] = jnp.broadcast_to(total, rest[2].shape[2:])
 
 
 def attend(queries, query_pos, pieces, head_dim, carried, final):
@@ -169,8 +169,8 @@
         kv_specs.append(pl.BlockSpec((1, rows.shape[1], head_dim), lambda r, h: (r, 0, 1)))
         kv_args.extend([rows, rows])
     row_spec = pl.BlockSpec((1, new_local, head_dim), lambda r, h: (r, 0, h))
-    stat_spec = pl.BlockSpec((1, 1, new_local, 1), lambda r, h: (r, h, 0, 0))
-    stat_shape = jax.ShapeDtypeStruct((req_local, head_count, new_local, 1), jnp.float32)
+    stat_spec = pl.BlockSpec((1, 1, new_local, 128), lambda r, h: (r, h, 0, 0))
+    stat_shape = jax.ShapeDtypeStruct((req_local, head_count, new_local, 128), jnp.float32)
     extra_specs, extra_args = [], []
     if carried is not None:
         extra_specs = [row_spec, stat_spec, stat_spec]

time: 130 us -> 130 us (level)
  no operation moved by 1% of the time
where the time goes in v5:
time: 130 us; the launch traced here: 129 us
  Pallas kernels  35.6 us (27%)
  starting transfers between devices  24.7 us (19%)
  other arithmetic  20.2 us (16%)
  matrix products  17.5 us (13%)
  waiting for transfers between devices  17.1 us (13%)
  local copies, waits for them, and re-layouts  9.52 us (7%)
  between operations  4.82 us (4%)
    pallas_call x3, Pallas kernels, attend(): pl.pallas_call(kernel, grid=(req_local, head_count), in_specs=[pl.BlockSp...  35.6 us
    dot_general x1, matrix products, on_device(): lax.dot_general(normed, head, (((1,), (1,)), ((), ())), preferred_element...  17.3 us
    ppermute x8, starting transfers between devices, butterfly_gather(): other = lax.ppermute(x, axis, xor_pairs(count, bit))  12.4 us
    ppermute x8, waiting for transfers between devices, butterfly_gather(): other = lax.ppermute(x, axis, xor_pairs(count, bit))  11.3 us
    ppermute x5, starting transfers between devices, butterfly_stats(): other = lax.ppermute(packed, axis, xor_pairs(count, bit))  6.21 us
    select_n x1, other arithmetic, on_device(): from_new = jnp.take_along_axis(new_keys, new_row[:, :, None], axis=1)  4.96 us
    ppermute x5, waiting for transfers between devices, butterfly_stats(): other = lax.ppermute(packed, axis, xor_pairs(count, bit))  3.47 us
    unnamed x54, local copies, waits for them, and re-layouts  2.86 us
  transfers between devices with their start and end apart: 21, of which 13 were waited for; matrix products, arithmetic and copies ran while one was open for 17% of the time, Pallas kernels for 19%

profile of v5, /device:TPU:0, one launch (start us, length us, event | category | flops | bytes accessed | tf_op | source)
XLA Modules:
  0.0 129.4 jit_solution(1327109889377392729)
XLA Ops:
  1.2 2.6 %collective-permute-start = (bf16[1,512,512]{2,1,0:T(8,128)(2,1)}, bf16[1,512,512]{2,1,0:T(8,128)(2,1)S(1)}, u32[]{:S(2)}, u32[]{:S(2)}) collective-permute-start(bf16[1,512,512]{2,1,0:T(8,128)(2,1)} %refs_6_.1), channel_id=1, source_target_pairs={{0,2},{1,3},{2,0},{3,1},{4,6},{5,7},{6,4},{7,5},{8,10},{9,11},{10,... | collective-permute-start | bytes 1572872 | tf_op jit(solution)/shard_map/ppermute | solution.py:81
  10.2 13.0 %shard_map.230 = (f32[1,192,2560]{2,1,0:T(8,128)}, f32[1,10,192,128]{3,2,1,0:T(8,128)}, f32[1,10,192,128]{3,2,1,0:T(8,128)}) custom-call(s32[192,1]{1,0:T(8,128)} %iota_add_fusion.qpos_ref, s32[1,1,512]{2,1,0:T(1,128)} %get-tuple-element.111.refs_0_, s32[1,1,512]{2,1,0:T(1,128)} %get-tuple-element.110.refs_1_, s32[1,1,192]{2,1,0:T(1,128)} %get-tuple-element.113.refs_2_, ...), custom_call_target="tpu_custom_call" | custom-call | tf_op jit(solution)/shard_map/pallas_call | solution.py:188
  27.2 11.5 %shard_map.231 = (f32[1,192,2560]{2,1,0:T(8,128)}, f32[1,10,192,128]{3,2,1,0:T(8,128)}, f32[1,10,192,128]{3,2,1,0:T(8,128)}) custom-call(s32[192,1]{1,0:T(8,128)} %iota_add_fusion.qpos_ref, s32[1,1,512]{2,1,0:T(1,128)} %compare_select_fusion.6.refs_0_, s32[1,1,192]{2,1,0:T(1,128)} %iota_add_fusion.2.refs_1_, bf16[1,192,2560]{2,1,0:T(8,128)(2,1)} %refs_2_.3, ...), custom_call_target="tpu_custom_call" | custom-call | tf_op jit(solution)/shard_map/pallas_call | solution.py:188
  39.6 11.1 %shard_map.232 = bf16[1,192,2560]{2,1,0:T(8,128)(2,1)} custom-call(s32[192,1]{1,0:T(8,128)} %iota_add_fusion.qpos_ref, s32[1,1,512]{2,1,0:T(1,128)} %compare_select_fusion.9.refs_0_, s32[1,1,192]{2,1,0:T(1,128)} %iota_add_fusion.5.refs_1_, bf16[1,192,2560]{2,1,0:T(8,128)(2,1)} %refs_2_.3, bf16[1,512,512]{2,1,0:T(8,128)(2,1)} %copy-done.5, ...), custom_call_target="tpu_custom_call" | custom-call | tf_op jit(solution)/shard_map/pallas_call | solution.py:188
  53.5 1.8 %collective-permute-start.7 = (bf16[1,2560]{1,0:T(2,128)(2,1)S(1)}, bf16[1,2560]{1,0:T(2,128)(2,1)S(1)}, u32[]{:S(2)}, u32[]{:S(2)}) collective-permute-start(bf16[1,2560]{1,0:T(2,128)(2,1)S(1)} %fusion.49), channel_id=1, source_target_pairs={{0,2},{1,3},{2,0},{3,1},{4,6},{5,7},{6,4},{7,5},{8,10},{9,11},{10,... | collective-permute-start | bytes 15368 | tf_op jit(solution)/shard_map/ppermute | solution.py:25
  57.2 1.9 %collective-permute-start.8 = (bf16[1,2560]{1,0:T(2,128)(2,1)S(1)}, bf16[1,2560]{1,0:T(2,128)(2,1)S(1)}, u32[]{:S(2)}, u32[]{:S(2)}) collective-permute-start(bf16[1,2560]{1,0:T(2,128)(2,1)S(1)} %add.615), channel_id=1, source_target_pairs={{0,4},{4,0},{8,12},{12,8},{16,20},{20,16},{24,28},{28,24},{1,5},{5... | collective-permute-start | bytes 15368 | tf_op jit(solution)/shard_map/ppermute | solution.py:37
  61.0 1.9 %collective-permute-start.9 = (bf16[2,2560]{1,0:T(2,128)(2,1)S(1)}, bf16[2,2560]{1,0:T(2,128)(2,1)S(1)}, u32[]{:S(2)}, u32[]{:S(2)}) collective-permute-start(bf16[2,2560]{1,0:T(2,128)(2,1)S(1)} %broadcast_select_fusion.1), channel_id=1, source_target_pairs={{0,8},{4,12},{8,0},{12,4},{16,24},{20,28},{24,16},{28,20},{1,9},{5... | collective-permute-start | bytes 30728 | tf_op jit(solution)/shard_map/ppermute | solution.py:37
  62.9 5.0 %compare_select_fusion.2 = (s32[512,1]{0,1:T(1,128)S(1)}, s32[1,512]{1,0:T(1,128)S(1)}, s32[512,1]{0,1:T(1,128)S(1)}, s32[1,512]{1,0:T(1,128)S(1)}) fusion(s32[]{:T(128)} %bitcast.24, s32[]{:T(128)} %bitcast.23, s32[]{:T(128)} %bitcast.22, s32[]{:T(128)} %bitcast.21, s32[]{:T(128)} %axis_index.14, s32[]{:T(128)} %bitcast.15, s32[]{:T(128)} %bitcast.19, ...), kind=kLoop, calls=%fused_computation.35 | loop fusion | flops 55296 | bytes 8232 | tf_op jit(solution)/shard_map/jit(take_along_axis)/select_n | solution.py:284
  68.0 2.7 %collective-permute-start.10 = (bf16[4,2560]{1,0:T(4,128)(2,1)S(1)}, bf16[4,2560]{1,0:T(4,128)(2,1)S(1)}, u32[]{:S(2)}, u32[]{:S(2)}) collective-permute-start(bf16[4,2560]{1,0:T(4,128)(2,1)S(1)} %maximum_select_fusion.3), channel_id=1, source_target_pairs={{0,16},{4,20},{8,24},{12,28},{16,0},{20,4},{24,8},{28,12},{1,17},{... | collective-permute-start | bytes 61448 | tf_op jit(solution)/shard_map/ppermute | solution.py:37
  71.1 1.6 %collective-permute-done.10 = bf16[4,2560]{1,0:T(4,128)(2,1)S(1)} collective-permute-done((bf16[4,2560]{1,0:T(4,128)(2,1)S(1)}, bf16[4,2560]{1,0:T(4,128)(2,1)S(1)}, u32[]{:S(2)}, u32[]{:S(2)}) %collective-permute-start.10) | collective-permute-done | bytes 20512 | tf_op jit(solution)/shard_map/ppermute | solution.py:37
  74.2 1.6 %collective-permute-start.12 = (bf16[8,160]{1,0:T(8,128)(2,1)S(1)}, bf16[8,160]{1,0:T(8,128)(2,1)S(1)}, u32[]{:S(2)}, u32[]{:S(2)}) collective-permute-start(bf16[8,160]{1,0:T(8,128)(2,1)S(1)} %maximum_select_fusion.8), channel_id=1, source_target_pairs={{0,2},{1,3},{2,0},{3,1},{4,6},{5,7},{6,4},{7,5},{8,10},{9,11},{10,... | collective-permute-start | bytes 7688 | tf_op jit(solution)/shard_map/ppermute | solution.py:37
  75.8 2.0 %collective-permute-done.12 = bf16[8,160]{1,0:T(8,128)(2,1)S(1)} collective-permute-done((bf16[8,160]{1,0:T(8,128)(2,1)S(1)}, bf16[8,160]{1,0:T(8,128)(2,1)S(1)}, u32[]{:S(2)}, u32[]{:S(2)}) %collective-permute-start.12) | collective-permute-done | bytes 2592 | tf_op jit(solution)/shard_map/ppermute | solution.py:37
  77.9 1.6 %collective-permute-start.13 = (bf16[8,320]{1,0:T(8,128)(2,1)S(1)}, bf16[8,320]{1,0:T(8,128)(2,1)S(1)}, u32[]{:S(2)}, u32[]{:S(2)}) collective-permute-start(bf16[8,320]{1,0:T(8,128)(2,1)S(1)} %maximum_select_fusion.7), channel_id=1, source_target_pairs={{0,4},{4,0},{8,12},{12,8},{16,20},{20,16},{24,28},{28,24},{1,5},{5... | collective-permute-start | bytes 15368 | tf_op jit(solution)/shard_map/ppermute | solution.py:37
  81.8 3.5 %collective-permute-done.14 = bf16[8,640]{1,0:T(8,128)(2,1)S(1)} collective-permute-done((bf16[8,640]{1,0:T(8,128)(2,1)S(1)}, bf16[8,640]{1,0:T(8,128)(2,1)S(1)}, u32[]{:S(2)}, u32[]{:S(2)}) %collective-permute-start.14) | collective-permute-done | bytes 10272 | tf_op jit(solution)/shard_map/ppermute | solution.py:37
  85.3 2.6 %collective-permute-start.15 = (bf16[8,1280]{1,0:T(8,128)(2,1)S(1)}, bf16[8,1280]{1,0:T(8,128)(2,1)S(1)}, u32[]{:S(2)}, u32[]{:S(2)}) collective-permute-start(bf16[8,1280]{1,0:T(8,128)(2,1)S(1)} %maximum_select_fusion.4), channel_id=1, source_target_pairs={{0,16},{4,20},{8,24},{12,28},{16,0},{20,4},{24,8},{28,12},{1,17},{... | collective-permute-start | bytes 61448 | tf_op jit(solution)/shard_map/ppermute | solution.py:37
  88.4 1.6 %collective-permute-done.15 = bf16[8,1280]{1,0:T(8,128)(2,1)S(1)} collective-permute-done((bf16[8,1280]{1,0:T(8,128)(2,1)S(1)}, bf16[8,1280]{1,0:T(8,128)(2,1)S(1)}, u32[]{:S(2)}, u32[]{:S(2)}) %collective-permute-start.15) | collective-permute-done | bytes 20512 | tf_op jit(solution)/shard_map/ppermute | solution.py:37
  90.1 17.3 %fusion.46 = (f32[8]{0:T(128)S(1)}, f32[8,8000]{1,0:T(8,128)S(1)}) fusion(bf16[8000,2560]{1,0:T(8,128)(2,1)} %param.30, f32[2560]{0:T(1024)S(1)} %convert_element_type.18, f32[8]{0:T(128)S(1)} %add_rsqrt_fusion, bf16[8,1280]{1,0:T(8,128)(2,1)S(1)} %maximum_select_fusion.4, bf16[8,1280]{1,0:T(8,128)(2,1)S(1)} %collective-permute-done.15, pred[]{:T(512)S(6)} %eq.61), kind=kOutput, calls=%fused_computation.150 | convolution fusion | flops 328010240 | bytes 41267264 | tf_op jit(solution)/shard_map/dot_general | solution.py:304
  109.6 1.7 %collective-permute-start.17 = (f32[3,8]{1,0:T(4,128)S(1)}, f32[3,8]{1,0:T(4,128)S(1)}, u32[]{:S(2)}, u32[]{:S(2)}) collective-permute-start(f32[3,8]{1,0:T(4,128)S(1)} %pad_maximum_fusion.1), channel_id=1, source_target_pairs={{0,2},{1,3},{2,0},{3,1},{4,6},{5,7},{6,4},{7,5},{8,10},{9,11},{10,... | collective-permute-start | bytes 296 | tf_op jit(solution)/shard_map/ppermute | solution.py:64
  111.2 2.6 %gather_fusion.1 = bf16[512,512]{1,0:T(8,128)(2,1)} fusion(bf16[768,512]{1,0:T(8,128)(2,1)S(1)} %maximum_bitcast_fusion.1, s32[1024]{0:T(1024)S(1)} %pad_clamp_fusion), kind=kCustom, calls=%fused_computation.1 | custom fusion | bytes 1050624 | tf_op jit(solution)/shard_map/jit(take_along_axis)/gather | solution.py:284
  114.5 1.5 %collective-permute-start.18 = (f32[3,8]{1,0:T(4,128)S(1)}, f32[3,8]{1,0:T(4,128)S(1)}, u32[]{:S(2)}, u32[]{:S(2)}) collective-permute-start(f32[3,8]{1,0:T(4,128)S(1)} %pad_maximum_fusion.2), channel_id=1, source_target_pairs={{0,4},{4,0},{8,12},{12,8},{16,20},{20,16},{24,28},{28,24},{1,5},{5... | collective-permute-start | bytes 296 | tf_op jit(solution)/shard_map/ppermute | solution.py:64
  119.1 2.1 %gather_fusion = bf16[512,512]{1,0:T(8,128)(2,1)S(1)} fusion(bf16[2048,512]{1,0:T(8,128)(2,1)S(1)} %maximum_bitcast_fusion, s32[1024]{0:T(1024)} %pad_clamp_fusion.1), kind=kCustom, calls=%fused_computation | custom fusion | bytes 1050624 | tf_op jit(solution)/shard_map/jit(take_along_axis)/gather | solution.py:283
  121.2 1.4 %collective-permute-done.19 = f32[3,8]{1,0:T(4,128)} collective-permute-done((f32[3,8]{1,0:T(4,128)}, f32[3,8]{1,0:T(4,128)}, u32[]{:S(2)}, u32[]{:S(2)}) %collective-permute-start.19) | collective-permute-done | bytes 128 | tf_op jit(solution)/shard_map/ppermute | solution.py:64
  123.5 2.5 %collective-permute-start.20 = (f32[3,8]{1,0:T(4,128)S(1)}, f32[3,8]{1,0:T(4,128)S(1)}, u32[]{:S(2)}, u32[]{:S(2)}) collective-permute-start(f32[3,8]{1,0:T(4,128)S(1)} %pad_maximum_fusion.4), channel_id=1, source_target_pairs={{0,16},{4,20},{8,24},{12,28},{16,0},{20,4},{24,8},{28,12},{1,17},{... | collective-permute-start | bytes 296 | tf_op jit(solution)/shard_map/ppermute | solution.py:64
  126.0 1.8 %fusion.1 = bf16[1,512,512]{2,1,0:T(8,128)(2,1)} fusion(bf16[512,512]{1,0:T(8,128)(2,1)S(1)} %copy-done.6, bf16[512,512]{1,0:T(8,128)(2,1)S(1)} %gather_fusion, pred[512]{0:T(512)(128)(4,1)} %compare_and_fusion, pred[512]{0:T(512)(128)(4,1)} %compare_and_fusion.1, pred[512]{0:T(512)(128)(4,1)} %add_compare_fusion), kind=kLoop, calls=%fused_computation.7 | loop fusion | flops 786432 | bytes 1574400 | tf_op jit(solution)/shard_map/jit(_where)/select_n | solution.py:285
  (124 shorter events, 27.8 us)
Async XLA Ops:
  0.6 72.1 %copy-start = (bf16[2560,80]{0,1:T(8,128)(2,1)S(1)}, bf16[2560,80]{0,1:T(8,128)(2,1)}, u32[]{:S(2)}) copy-start(bf16[2560,80]{0,1:T(8,128)(2,1)} %param.27) | copy-start | bytes 1228804
  0.6 8.6 %collective-permute-start.2 = (bf16[1,512,512]{2,1,0:T(8,128)(2,1)}, bf16[1,512,512]{2,1,0:T(8,128)(2,1)S(1)}, u32[]{:S(2)}, u32[]{:S(2)}) collective-permute-start(bf16[1,512,512]{2,1,0:T(8,128)(2,1)} %refs_6_.1), channel_id=1, source_target_pairs={{0,1},{1,0},{2,3},{3,2},{4,5},{5,4},{6,7},{7,6},{8,9},{9,8},{10,11... | collective-permute-start | bytes 1572872 | tf_op jit(solution)/shard_map/ppermute | solution.py:77
  1.2 22.1 %collective-permute-start = (bf16[1,512,512]{2,1,0:T(8,128)(2,1)}, bf16[1,512,512]{2,1,0:T(8,128)(2,1)S(1)}, u32[]{:S(2)}, u32[]{:S(2)}) collective-permute-start(bf16[1,512,512]{2,1,0:T(8,128)(2,1)} %refs_6_.1), channel_id=1, source_target_pairs={{0,2},{1,3},{2,0},{3,1},{4,6},{5,7},{6,4},{7,5},{8,10},{9,11},{10,... | collective-permute-start | bytes 1572872 | tf_op jit(solution)/shard_map/ppermute | solution.py:81
  3.7 5.5 %collective-permute-start.3 = (bf16[1,192,512]{2,1,0:T(8,128)(2,1)}, bf16[1,192,512]{2,1,0:T(8,128)(2,1)S(1)}, u32[]{:S(2)}, u32[]{:S(2)}) collective-permute-start(bf16[1,192,512]{2,1,0:T(8,128)(2,1)} %refs_10_.1), channel_id=1, source_target_pairs={{0,1},{1,0},{2,3},{3,2},{4,5},{5,4},{6,7},{7,6},{8,9},{9,8},{10,11... | collective-permute-start | bytes 589832 | tf_op jit(solution)/shard_map/ppermute | solution.py:77
  3.9 19.3 %collective-permute-start.1 = (bf16[1,192,512]{2,1,0:T(8,128)(2,1)}, bf16[1,192,512]{2,1,0:T(8,128)(2,1)S(1)}, u32[]{:S(2)}, u32[]{:S(2)}) collective-permute-start(bf16[1,192,512]{2,1,0:T(8,128)(2,1)} %refs_10_.1), channel_id=1, source_target_pairs={{0,2},{1,3},{2,0},{3,1},{4,6},{5,7},{6,4},{7,5},{8,10},{9,11},{10,... | collective-permute-start | bytes 589832 | tf_op jit(solution)/shard_map/ppermute | solution.py:81
  23.2 15.5 %collective-permute-start.4 = (bf16[1,512,512]{2,1,0:T(8,128)(2,1)S(1)}, bf16[1,512,512]{2,1,0:T(8,128)(2,1)S(1)}, u32[]{:S(2)}, u32[]{:S(2)}) collective-permute-start(bf16[1,512,512]{2,1,0:T(8,128)(2,1)S(1)} %collective-permute-done.refs_3_.refs_4_), channel_id=1, source_target_pairs={{0,1},{1,0},{2,3},{3,2},{4,5},{5,4},{6,7},{7,6},{8,9},{9,8},{10,11... | collective-permute-start | bytes 1572872 | tf_op jit(solution)/shard_map/ppermute | solution.py:93
  25.7 12.9 %collective-permute-start.5 = (bf16[1,192,512]{2,1,0:T(8,128)(2,1)S(1)}, bf16[1,192,512]{2,1,0:T(8,128)(2,1)S(1)}, u32[]{:S(2)}, u32[]{:S(2)}) collective-permute-start(bf16[1,192,512]{2,1,0:T(8,128)(2,1)S(1)} %collective-permute-done.1.refs_5_.refs_6_), channel_id=1, source_target_pairs={{0,1},{1,0},{2,3},{3,2},{4,5},{5,4},{6,7},{7,6},{8,9},{9,8},{10,11... | collective-permute-start | bytes 589832 | tf_op jit(solution)/shard_map/ppermute | solution.py:93
  39.5 36.2 %copy-start.26 = (s32[8]{0:T(128)S(1)}, s32[8]{0:T(128)}, u32[]{:S(2)}) copy-start(s32[8]{0:T(128)} %param.31) | copy-start | bytes 100
  39.5 48.8 %copy-start.18 = (bf16[2560]{0:T(1024)(128)(2,1)S(1)}, bf16[2560]{0:T(1024)(128)(2,1)}, u32[]{:S(2)}) copy-start(bf16[2560]{0:T(1024)(128)(2,1)} %param.29) | copy-start | bytes 15364
  51.4 1.2 collective-permute-start.6
  53.5 3.7 %collective-permute-start.7 = (bf16[1,2560]{1,0:T(2,128)(2,1)S(1)}, bf16[1,2560]{1,0:T(2,128)(2,1)S(1)}, u32[]{:S(2)}, u32[]{:S(2)}) collective-permute-start(bf16[1,2560]{1,0:T(2,128)(2,1)S(1)} %fusion.49), channel_id=1, source_target_pairs={{0,2},{1,3},{2,0},{3,1},{4,6},{5,7},{6,4},{7,5},{8,10},{9,11},{10,... | collective-permute-start | bytes 15368 | tf_op jit(solution)/shard_map/ppermute | solution.py:25
  57.2 3.7 %collective-permute-start.8 = (bf16[1,2560]{1,0:T(2,128)(2,1)S(1)}, bf16[1,2560]{1,0:T(2,128)(2,1)S(1)}, u32[]{:S(2)}, u32[]{:S(2)}) collective-permute-start(bf16[1,2560]{1,0:T(2,128)(2,1)S(1)} %add.615), channel_id=1, source_target_pairs={{0,4},{4,0},{8,12},{12,8},{16,20},{20,16},{24,28},{28,24},{1,5},{5... | collective-permute-start | bytes 15368 | tf_op jit(solution)/shard_map/ppermute | solution.py:37
  61.0 6.9 %collective-permute-start.9 = (bf16[2,2560]{1,0:T(2,128)(2,1)S(1)}, bf16[2,2560]{1,0:T(2,128)(2,1)S(1)}, u32[]{:S(2)}, u32[]{:S(2)}) collective-permute-start(bf16[2,2560]{1,0:T(2,128)(2,1)S(1)} %broadcast_select_fusion.1), channel_id=1, source_target_pairs={{0,8},{4,12},{8,0},{12,4},{16,24},{20,28},{24,16},{28,20},{1,9},{5... | collective-permute-start | bytes 30728 | tf_op jit(solution)/shard_map/ppermute | solution.py:37
  68.0 4.7 %collective-permute-start.10 = (bf16[4,2560]{1,0:T(4,128)(2,1)S(1)}, bf16[4,2560]{1,0:T(4,128)(2,1)S(1)}, u32[]{:S(2)}, u32[]{:S(2)}) collective-permute-start(bf16[4,2560]{1,0:T(4,128)(2,1)S(1)} %maximum_select_fusion.3), channel_id=1, source_target_pairs={{0,16},{4,20},{8,24},{12,28},{16,0},{20,4},{24,8},{28,12},{1,17},{... | collective-permute-start | bytes 61448 | tf_op jit(solution)/shard_map/ppermute | solution.py:37
  72.9 1.2 collective-permute-start.11
  74.2 3.6 %collective-permute-start.12 = (bf16[8,160]{1,0:T(8,128)(2,1)S(1)}, bf16[8,160]{1,0:T(8,128)(2,1)S(1)}, u32[]{:S(2)}, u32[]{:S(2)}) collective-permute-start(bf16[8,160]{1,0:T(8,128)(2,1)S(1)} %maximum_select_fusion.8), channel_id=1, source_target_pairs={{0,2},{1,3},{2,0},{3,1},{4,6},{5,7},{6,4},{7,5},{8,10},{9,11},{10,... | collective-permute-start | bytes 7688 | tf_op jit(solution)/shard_map/ppermute | solution.py:37
  77.9 3.6 %collective-permute-start.13 = (bf16[8,320]{1,0:T(8,128)(2,1)S(1)}, bf16[8,320]{1,0:T(8,128)(2,1)S(1)}, u32[]{:S(2)}, u32[]{:S(2)}) collective-permute-start(bf16[8,320]{1,0:T(8,128)(2,1)S(1)} %maximum_select_fusion.7), channel_id=1, source_target_pairs={{0,4},{4,0},{8,12},{12,8},{16,20},{20,16},{24,28},{28,24},{1,5},{5... | collective-permute-start | bytes 15368 | tf_op jit(solution)/shard_map/ppermute | solution.py:37
  81.6 3.7 %collective-permute-start.14 = (bf16[8,640]{1,0:T(8,128)(2,1)S(1)}, bf16[8,640]{1,0:T(8,128)(2,1)S(1)}, u32[]{:S(2)}, u32[]{:S(2)}) collective-permute-start(bf16[8,640]{1,0:T(8,128)(2,1)S(1)} %maximum_select_fusion.5), channel_id=1, source_target_pairs={{0,8},{4,12},{8,0},{12,4},{16,24},{20,28},{24,16},{28,20},{1,9},{5... | collective-permute-start | bytes 30728 | tf_op jit(solution)/shard_map/ppermute | solution.py:37
  85.3 4.7 %collective-permute-start.15 = (bf16[8,1280]{1,0:T(8,128)(2,1)S(1)}, bf16[8,1280]{1,0:T(8,128)(2,1)S(1)}, u32[]{:S(2)}, u32[]{:S(2)}) collective-permute-start(bf16[8,1280]{1,0:T(8,128)(2,1)S(1)} %maximum_select_fusion.4), channel_id=1, source_target_pairs={{0,16},{4,20},{8,24},{12,28},{16,0},{20,4},{24,8},{28,12},{1,17},{... | collective-permute-start | bytes 61448 | tf_op jit(solution)/shard_map/ppermute | solution.py:37
  107.8 1.2 collective-permute-start.16
  109.6 4.3 %collective-permute-start.17 = (f32[3,8]{1,0:T(4,128)S(1)}, f32[3,8]{1,0:T(4,128)S(1)}, u32[]{:S(2)}, u32[]{:S(2)}) collective-permute-start(f32[3,8]{1,0:T(4,128)S(1)} %pad_maximum_fusion.1), channel_id=1, source_target_pairs={{0,2},{1,3},{2,0},{3,1},{4,6},{5,7},{6,4},{7,5},{8,10},{9,11},{10,... | collective-permute-start | bytes 296 | tf_op jit(solution)/shard_map/ppermute | solution.py:64
  114.5 3.6 %collective-permute-start.18 = (f32[3,8]{1,0:T(4,128)S(1)}, f32[3,8]{1,0:T(4,128)S(1)}, u32[]{:S(2)}, u32[]{:S(2)}) collective-permute-start(f32[3,8]{1,0:T(4,128)S(1)} %pad_maximum_fusion.2), channel_id=1, source_target_pairs={{0,4},{4,0},{8,12},{12,8},{16,20},{20,16},{24,28},{28,24},{1,5},{5... | collective-permute-start | bytes 296 | tf_op jit(solution)/shard_map/ppermute | solution.py:64
  118.7 4.0 %collective-permute-start.19 = (f32[3,8]{1,0:T(4,128)}, f32[3,8]{1,0:T(4,128)}, u32[]{:S(2)}, u32[]{:S(2)}) collective-permute-start(f32[3,8]{1,0:T(4,128)} %pad_maximum_fusion.3), channel_id=1, source_target_pairs={{0,8},{4,12},{8,0},{12,4},{16,24},{20,28},{24,16},{28,20},{1,9},{5... | collective-permute-start | bytes 296 | tf_op jit(solution)/shard_map/ppermute | solution.py:64
  123.5 4.5 %collective-permute-start.20 = (f32[3,8]{1,0:T(4,128)S(1)}, f32[3,8]{1,0:T(4,128)S(1)}, u32[]{:S(2)}, u32[]{:S(2)}) collective-permute-start(f32[3,8]{1,0:T(4,128)S(1)} %pad_maximum_fusion.4), channel_id=1, source_target_pairs={{0,16},{4,20},{8,24},{12,28},{16,0},{20,4},{24,8},{28,12},{1,17},{... | collective-permute-start | bytes 296 | tf_op jit(solution)/shard_map/ppermute | solution.py:64
  (24 other events, 164.3 us)

commit v6 on v3

--- a/solution.py
+++ b/solution.py
@@ -129,9 +129,13 @@
     out_ref[0] = (mixed / total).astype(out_ref.dtype)
 
 
-def attend(queries, query_pos, pieces, head_dim):
+def attend(queries, query_pos, pieces, head_dim, first_head=0, head_count=None, rows=None):
     req_local, new_local, model_cols = queries.shape
-    head_count = model_cols // head_dim
+    if head_count is None:
+        head_count = model_cols // head_dim
+    if rows is not None:
+        new_local = rows
+    row_block = (new_local - 1) // new_local if rows is None else (queries.shape[1] // rows - 1)
     kinds = [kind for kind, _, _ in pieces]
     kernel = functools.partial(attention_kernel, kinds=kinds, scale=1.0 / math.sqrt(head_dim))
     bound_specs = [
@@ -146,12 +150,14 @@
     return pl.pallas_call(
         kernel,
         grid=(req_local, head_count),
-        in_specs=[pl.BlockSpec((new_local, 1), lambda r, h: (0, 0))]
+        in_specs=[pl.BlockSpec((new_local, 1), lambda r, h: (row_block, 0))]
         + bound_specs
-        + [pl.BlockSpec((1, new_local, head_dim), lambda r, h: (r, 0, h))]
+        + [pl.BlockSpec((1, new_local, head_dim), lambda r, h: (r, row_block, h + first_head))]
         + kv_specs,
         out_specs=pl.BlockSpec((1, new_local, head_dim), lambda r, h: (r, 0, h)),
-        out_shape=jax.ShapeDtypeStruct(queries.shape, queries.dtype),
+        out_shape=jax.ShapeDtypeStruct(
+            (req_local, new_local, head_count * head_dim), queries.dtype
+        ),
     )(query_pos, *[bound for _, _, bound in pieces], queries, *kv_args)
 
 
@@ -190,7 +196,17 @@
         new_pos = (chunk[:, None] * new_local + new_ids[None, :]).reshape(-1)
         new_lo = jnp.broadcast_to(new_pos[None, None, :], (req_local, 1, new_pos.shape[0]))
         pieces.append(("lo", rows, new_lo))
-    mixed_out = attend(queries, query_pos, pieces, head_dim)
+    head_count = model_cols // head_dim
+    tail_rows = 8 if new_local % 8 == 0 else new_local
+    last_rows = attend(queries, query_pos, pieces, head_dim, rows=tail_rows)
+    group = 2 if head_count % 2 == 0 else 1
+    mixed_out = jnp.concatenate(
+        [
+            attend(queries, query_pos, pieces, head_dim, first, group)
+            for first in range(0, head_count, group)
+        ],
+        axis=2,
+    )
 
     cache_masks = [m for _, masks in cache_pieces for m in masks]
     new_masks = [m for _, masks in new_pieces for m in masks]
@@ -214,7 +230,7 @@
     from_new = jnp.take_along_axis(new_keys, new_row[:, :, None], axis=1)
     fresh_block = jnp.where(from_old[:, :, None], from_cache, from_new)
 
-    last_local = mixed_out[:, new_local - 1, :]
+    last_local = last_rows[:, tail_rows - 1, :]
     group_req = lax.axis_size("gx")
     holder = my_index == group_pos - 1
     last_local = jnp.where(holder, last_local, jnp.zeros_like(last_local))

time: 121 us -> 140 us (1.16)
  Pallas kernels: 20.2 us -> 45 us
  starting transfers between devices: 28.3 us -> 22.5 us
  local copies, waits for them, and re-layouts: 8.29 us -> 13.4 us
  other arithmetic: 16.6 us -> 13.3 us
    pallas_call x1 -> x6, Pallas kernels: 20.2 us -> 45 us  [attend(): pl.pallas_call(kernel, grid=(req_local, head_count), in_specs=[pl.BlockSp...]
    ppermute x5, starting transfers between devices: 7.69 us -> 2.05 us  [butterfly_stats(): other = lax.ppermute(packed, axis, xor_pairs(count, bit))]
    ppermute x8, waiting for transfers between devices: 10.6 us -> 5.58 us  [butterfly_gather(): other = lax.ppermute(x, axis, xor_pairs(count, bit))]
    ppermute x5, waiting for transfers between devices: 2.11 us -> 6.46 us  [butterfly_stats(): other = lax.ppermute(packed, axis, xor_pairs(count, bit))]
    gather x1, local copies, waits for them, and re-layouts: 2.1 us -> 3.9 us  [on_device(): from_cache = jnp.take_along_axis(cache_keys, cache_row[:, :, None], axis=1)]
    unnamed x54 -> x40, local copies, waits for them, and re-layouts: 2.23 us -> 3.88 us
  transfers between devices with their start and end apart: 21 -> 21, of which waited for: 16 -> 9; matrix products, arithmetic and copies ran while one was open for 15% -> 16% of each run, Pallas kernels for 0% -> 22%
where the time goes in v6:
time: 140 us
  Pallas kernels  45 us (32%)
  waiting for transfers between devices  23.1 us (16%)
  starting transfers between devices  22.5 us (16%)
  matrix products  17.5 us (12%)
  local copies, waits for them, and re-layouts  13.4 us (10%)
  other arithmetic  13.3 us (10%)
  between operations  4.75 us (3%)
    pallas_call x6, Pallas kernels, attend(): pl.pallas_call(kernel, grid=(req_local, head_count), in_specs=[pl.BlockSp...  45 us
    dot_general x1, matrix products, on_device(): lax.dot_general(normed, head, (((1,), (1,)), ((), ())), preferred_element...  17.3 us
    ppermute x8, starting transfers between devices, butterfly_gather(): other = lax.ppermute(x, axis, xor_pairs(count, bit))  14.3 us
    ppermute x2, waiting for transfers between devices, exchange_pieces(): other = lax.ppermute(held, axis, xor_pairs(count, bit))  8.03 us
    ppermute x5, waiting for transfers between devices, butterfly_stats(): other = lax.ppermute(packed, axis, xor_pairs(count, bit))  6.46 us
    ppermute x8, waiting for transfers between devices, butterfly_gather(): other = lax.ppermute(x, axis, xor_pairs(count, bit))  5.58 us
    gather x1, local copies, waits for them, and re-layouts, on_device(): from_cache = jnp.take_along_axis(cache_keys, cache_row[:, :, None], axis=1)  3.9 us
    unnamed x40, local copies, waits for them, and re-layouts  3.88 us
  transfers between devices with their start and end apart: 21, of which 9 were waited for; matrix products, arithmetic and copies ran while one was open for 16% of the time, Pallas kernels for 22%

profile of v6, /device:TPU:0, one launch (start us, length us, event | category | flops | bytes accessed | tf_op | source)
XLA Modules:
  0.0 139.5 jit_solution(14909676006369578127)
XLA Ops:
  0.6 3.0 %collective-permute-start.4 = (bf16[1,192,512]{2,1,0:T(8,128)(2,1)}, bf16[1,192,512]{2,1,0:T(8,128)(2,1)S(1)}, u32[]{:S(2)}, u32[]{:S(2)}) collective-permute-start(bf16[1,192,512]{2,1,0:T(8,128)(2,1)} %refs_18_.11), channel_id=1, source_target_pairs={{0,2},{1,3},{2,0},{3,1},{4,6},{5,7},{6,4},{7,5},{8,10},{9,11},{10,... | collective-permute-start | bytes 589832 | tf_op jit(solution)/shard_map/ppermute | solution.py:81
  12.0 8.0 %collective-permute-done.1.refs_15_.refs_16_ = bf16[1,512,512]{2,1,0:T(8,128)(2,1)S(1)} collective-permute-done((bf16[1,512,512]{2,1,0:T(8,128)(2,1)}, bf16[1,512,512]{2,1,0:T(8,128)(2,1)S(1)}, u32[]{:S(2)}, u32[]{:S(2)}) %collective-permute-start.1) | collective-permute-done | bytes 524320 | tf_op jit(solution)/shard_map/ppermute | solution.py:81
  24.5 14.7 %shard_map.235 = bf16[1,8,2560]{2,1,0:T(8,128)(2,1)} custom-call(s32[192,1]{1,0:T(8,128)} %iota_add_fusion.qpos_ref, s32[1,1,512]{2,1,0:T(1,128)} %get-tuple-element.84.refs_0_, s32[1,1,512]{2,1,0:T(1,128)} %get-tuple-element.83.refs_1_, s32[1,1,512]{2,1,0:T(1,128)} %get-tuple-element.82.refs_2_, s32[1,1,512]{2,1,0:T(1,128)} %get-tuple-element.81.refs_3_, ...), custom_call_target="tpu_custom_call" | custom-call | tf_op jit(solution)/shard_map/pallas_call | solution.py:150
  40.4 2.6 %compare_select_fusion.3 = (s32[512,1]{0,1:T(1,128)S(1)}, s32[1,512]{1,0:T(1,128)S(1)}, s32[512,1]{0,1:T(1,128)S(1)}) fusion(s32[]{:T(128)} %axis_index.14, s32[]{:T(128)} %bitcast.19, s32[]{:T(128)} %bitcast.18, s32[]{:T(128)} %bitcast.17, s32[]{:T(128)} %bitcast.16, s32[]{:T(128)} %bitcast.15), kind=kLoop, calls=%fused_computation.36 | loop fusion | flops 55296 | bytes 6168 | tf_op jit(solution)/shard_map/jit(take_along_axis)/select_n | solution.py:229
  43.9 1.8 %collective-permute-start.7 = (bf16[1,2560]{1,0:T(2,128)(2,1)S(1)}, bf16[1,2560]{1,0:T(2,128)(2,1)S(1)}, u32[]{:S(2)}, u32[]{:S(2)}) collective-permute-start(bf16[1,2560]{1,0:T(2,128)(2,1)S(1)} %fusion.47), channel_id=1, source_target_pairs={{0,2},{1,3},{2,0},{3,1},{4,6},{5,7},{6,4},{7,5},{8,10},{9,11},{10,... | collective-permute-start | bytes 15368 | tf_op jit(solution)/shard_map/ppermute | solution.py:25
  45.7 1.9 %collective-permute-done.7 = bf16[1,2560]{1,0:T(2,128)(2,1)S(1)} collective-permute-done((bf16[1,2560]{1,0:T(2,128)(2,1)S(1)}, bf16[1,2560]{1,0:T(2,128)(2,1)S(1)}, u32[]{:S(2)}, u32[]{:S(2)}) %collective-permute-start.7) | collective-permute-done | bytes 5152 | tf_op jit(solution)/shard_map/ppermute | solution.py:25
  47.6 1.8 %collective-permute-start.8 = (bf16[1,2560]{1,0:T(2,128)(2,1)S(1)}, bf16[1,2560]{1,0:T(2,128)(2,1)S(1)}, u32[]{:S(2)}, u32[]{:S(2)}) collective-permute-start(bf16[1,2560]{1,0:T(2,128)(2,1)S(1)} %add.615), channel_id=1, source_target_pairs={{0,4},{4,0},{8,12},{12,8},{16,20},{20,16},{24,28},{28,24},{1,5},{5... | collective-permute-start | bytes 15368 | tf_op jit(solution)/shard_map/ppermute | solution.py:37
  49.5 1.9 %collective-permute-done.8 = bf16[1,2560]{1,0:T(2,128)(2,1)S(1)} collective-permute-done((bf16[1,2560]{1,0:T(2,128)(2,1)S(1)}, bf16[1,2560]{1,0:T(2,128)(2,1)S(1)}, u32[]{:S(2)}, u32[]{:S(2)}) %collective-permute-start.8) | collective-permute-done | bytes 5152 | tf_op jit(solution)/shard_map/ppermute | solution.py:37
  51.4 1.9 %collective-permute-start.9 = (bf16[2,2560]{1,0:T(2,128)(2,1)S(1)}, bf16[2,2560]{1,0:T(2,128)(2,1)S(1)}, u32[]{:S(2)}, u32[]{:S(2)}) collective-permute-start(bf16[2,2560]{1,0:T(2,128)(2,1)S(1)} %broadcast_select_fusion.1), channel_id=1, source_target_pairs={{0,8},{4,12},{8,0},{12,4},{16,24},{20,28},{24,16},{28,20},{1,9},{5... | collective-permute-start | bytes 30728 | tf_op jit(solution)/shard_map/ppermute | solution.py:37
  53.3 1.8 %collective-permute-done.9 = bf16[2,2560]{1,0:T(2,128)(2,1)S(1)} collective-permute-done((bf16[2,2560]{1,0:T(2,128)(2,1)S(1)}, bf16[2,2560]{1,0:T(2,128)(2,1)S(1)}, u32[]{:S(2)}, u32[]{:S(2)}) %collective-permute-start.9) | collective-permute-done | bytes 10272 | tf_op jit(solution)/shard_map/ppermute | solution.py:37
  55.2 2.9 %collective-permute-start.10 = (bf16[4,2560]{1,0:T(4,128)(2,1)S(1)}, bf16[4,2560]{1,0:T(4,128)(2,1)S(1)}, u32[]{:S(2)}, u32[]{:S(2)}) collective-permute-start(bf16[4,2560]{1,0:T(4,128)(2,1)S(1)} %maximum_select_fusion.3), channel_id=1, source_target_pairs={{0,16},{4,20},{8,24},{12,28},{16,0},{20,4},{24,8},{28,12},{1,17},{... | collective-permute-start | bytes 61448 | tf_op jit(solution)/shard_map/ppermute | solution.py:37
  58.1 1.8 %collective-permute-done.10 = bf16[4,2560]{1,0:T(4,128)(2,1)S(1)} collective-permute-done((bf16[4,2560]{1,0:T(4,128)(2,1)S(1)}, bf16[4,2560]{1,0:T(4,128)(2,1)S(1)}, u32[]{:S(2)}, u32[]{:S(2)}) %collective-permute-start.10) | collective-permute-done | bytes 20512 | tf_op jit(solution)/shard_map/ppermute | solution.py:37
  61.4 2.6 %gather_fusion.1 = bf16[512,512]{1,0:T(8,128)(2,1)} fusion(bf16[768,512]{1,0:T(8,128)(2,1)S(1)} %maximum_bitcast_fusion.1, s32[1024]{0:T(1024)S(1)} %pad_clamp_fusion), kind=kCustom, calls=%fused_computation.1 | custom fusion | bytes 1050624 | tf_op jit(solution)/shard_map/jit(take_along_axis)/gather | solution.py:230
  64.1 1.7 %collective-permute-start.12 = (bf16[8,160]{1,0:T(8,128)(2,1)S(1)}, bf16[8,160]{1,0:T(8,128)(2,1)S(1)}, u32[]{:S(2)}, u32[]{:S(2)}) collective-permute-start(bf16[8,160]{1,0:T(8,128)(2,1)S(1)} %maximum_select_fusion.8), channel_id=1, source_target_pairs={{0,2},{1,3},{2,0},{3,1},{4,6},{5,7},{6,4},{7,5},{8,10},{9,11},{10,... | collective-permute-start | bytes 7688 | tf_op jit(solution)/shard_map/ppermute | solution.py:37
  67.4 3.9 %gather_fusion = bf16[512,512]{1,0:T(8,128)(2,1)S(1)} fusion(bf16[2048,512]{1,0:T(8,128)(2,1)} %maximum_bitcast_fusion, s32[1024]{0:T(1024)S(1)} %pad_clamp_fusion.1), kind=kCustom, calls=%fused_computation | custom fusion | bytes 1050624 | tf_op jit(solution)/shard_map/jit(take_along_axis)/gather | solution.py:229
  74.0 6.0 %shard_map.230 = bf16[1,192,512]{2,1,0:T(8,128)(2,1)} custom-call(s32[192,1]{1,0:T(8,128)} %iota_add_fusion.qpos_ref, s32[1,1,512]{2,1,0:T(1,128)} %get-tuple-element.84.refs_0_, s32[1,1,512]{2,1,0:T(1,128)} %get-tuple-element.83.refs_1_, s32[1,1,512]{2,1,0:T(1,128)} %get-tuple-element.82.refs_2_, s32[1,1,512]{2,1,0:T(1,128)} %get-tuple-element.81.refs_3_, ...), custom_call_target="tpu_custom_call" | custom-call | tf_op jit(solution)/shard_map/pallas_call | solution.py:150
  82.6 6.0 %shard_map.231 = bf16[1,192,512]{2,1,0:T(8,128)(2,1)} custom-call(s32[192,1]{1,0:T(8,128)} %iota_add_fusion.qpos_ref, s32[1,1,512]{2,1,0:T(1,128)} %get-tuple-element.84.refs_0_, s32[1,1,512]{2,1,0:T(1,128)} %get-tuple-element.83.refs_1_, s32[1,1,512]{2,1,0:T(1,128)} %get-tuple-element.82.refs_2_, s32[1,1,512]{2,1,0:T(1,128)} %get-tuple-element.81.refs_3_, ...), custom_call_target="tpu_custom_call" | custom-call | tf_op jit(solution)/shard_map/pallas_call | solution.py:150
  88.7 2.8 %collective-permute-start.15 = (bf16[8,1280]{1,0:T(8,128)(2,1)S(1)}, bf16[8,1280]{1,0:T(8,128)(2,1)S(1)}, u32[]{:S(2)}, u32[]{:S(2)}) collective-permute-start(bf16[8,1280]{1,0:T(8,128)(2,1)S(1)} %maximum_select_fusion.4), channel_id=1, source_target_pairs={{0,16},{4,20},{8,24},{12,28},{16,0},{20,4},{24,8},{28,12},{1,17},{... | collective-permute-start | bytes 61448 | tf_op jit(solution)/shard_map/ppermute | solution.py:37
  92.4 6.0 %shard_map.232 = bf16[1,192,512]{2,1,0:T(8,128)(2,1)} custom-call(s32[192,1]{1,0:T(8,128)} %iota_add_fusion.qpos_ref, s32[1,1,512]{2,1,0:T(1,128)} %get-tuple-element.84.refs_0_, s32[1,1,512]{2,1,0:T(1,128)} %get-tuple-element.83.refs_1_, s32[1,1,512]{2,1,0:T(1,128)} %get-tuple-element.82.refs_2_, s32[1,1,512]{2,1,0:T(1,128)} %get-tuple-element.81.refs_3_, ...), custom_call_target="tpu_custom_call" | custom-call | tf_op jit(solution)/shard_map/pallas_call | solution.py:150
  98.6 17.3 %fusion.44 = (f32[8]{0:T(128)S(1)}, f32[8,8000]{1,0:T(8,128)S(1)}) fusion(bf16[8000,2560]{1,0:T(8,128)(2,1)} %param.30, f32[2560]{0:T(1024)S(1)} %convert_element_type.18, f32[8]{0:T(128)S(1)} %add_rsqrt_fusion, bf16[8,1280]{1,0:T(8,128)(2,1)S(1)} %maximum_select_fusion.4, bf16[8,1280]{1,0:T(8,128)(2,1)S(1)} %collective-permute-done.15, pred[]{:T(512)S(6)} %eq.61), kind=kOutput, calls=%fused_computation.154 | convolution fusion | flops 328010240 | bytes 41267264 | tf_op jit(solution)/shard_map/dot_general | solution.py:250
  118.0 6.2 %shard_map.233 = bf16[1,192,512]{2,1,0:T(8,128)(2,1)} custom-call(s32[192,1]{1,0:T(8,128)} %iota_add_fusion.qpos_ref, s32[1,1,512]{2,1,0:T(1,128)} %get-tuple-element.84.refs_0_, s32[1,1,512]{2,1,0:T(1,128)} %get-tuple-element.83.refs_1_, s32[1,1,512]{2,1,0:T(1,128)} %get-tuple-element.82.refs_2_, s32[1,1,512]{2,1,0:T(1,128)} %get-tuple-element.81.refs_3_, ...), custom_call_target="tpu_custom_call" | custom-call | tf_op jit(solution)/shard_map/pallas_call | solution.py:150
  125.8 2.1 %collective-permute-done.18 = f32[3,8]{1,0:T(4,128)S(1)} collective-permute-done((f32[3,8]{1,0:T(4,128)S(1)}, f32[3,8]{1,0:T(4,128)S(1)}, u32[]{:S(2)}, u32[]{:S(2)}) %collective-permute-start.18) | collective-permute-done | bytes 128 | tf_op jit(solution)/shard_map/ppermute | solution.py:64
  128.4 6.0 %shard_map.234 = bf16[1,192,512]{2,1,0:T(8,128)(2,1)} custom-call(s32[192,1]{1,0:T(8,128)} %iota_add_fusion.qpos_ref, s32[1,1,512]{2,1,0:T(1,128)} %get-tuple-element.84.refs_0_, s32[1,1,512]{2,1,0:T(1,128)} %get-tuple-element.83.refs_1_, s32[1,1,512]{2,1,0:T(1,128)} %get-tuple-element.82.refs_2_, s32[1,1,512]{2,1,0:T(1,128)} %get-tuple-element.81.refs_3_, ...), custom_call_target="tpu_custom_call" | custom-call | tf_op jit(solution)/shard_map/pallas_call | solution.py:150
  135.8 3.2 %collective-permute-done.20 = f32[3,8]{1,0:T(4,128)S(1)} collective-permute-done((f32[3,8]{1,0:T(4,128)S(1)}, f32[3,8]{1,0:T(4,128)S(1)}, u32[]{:S(2)}, u32[]{:S(2)}) %collective-permute-start.20) | collective-permute-done | bytes 128 | tf_op jit(solution)/shard_map/ppermute | solution.py:64
  (110 shorter events, 26.6 us)
Async XLA Ops:
  0.6 59.3 %copy-start = (bf16[2560,80]{0,1:T(8,128)(2,1)S(1)}, bf16[2560,80]{0,1:T(8,128)(2,1)}, u32[]{:S(2)}) copy-start(bf16[2560,80]{0,1:T(8,128)(2,1)} %param.27) | copy-start | bytes 1228804
  0.6 21.3 %collective-permute-start.4 = (bf16[1,192,512]{2,1,0:T(8,128)(2,1)}, bf16[1,192,512]{2,1,0:T(8,128)(2,1)S(1)}, u32[]{:S(2)}, u32[]{:S(2)}) collective-permute-start(bf16[1,192,512]{2,1,0:T(8,128)(2,1)} %refs_18_.11), channel_id=1, source_target_pairs={{0,2},{1,3},{2,0},{3,1},{4,6},{5,7},{6,4},{7,5},{8,10},{9,11},{10,... | collective-permute-start | bytes 589832 | tf_op jit(solution)/shard_map/ppermute | solution.py:81
  3.7 18.7 %collective-permute-start.3 = (bf16[1,192,512]{2,1,0:T(8,128)(2,1)}, bf16[1,192,512]{2,1,0:T(8,128)(2,1)S(1)}, u32[]{:S(2)}, u32[]{:S(2)}) collective-permute-start(bf16[1,192,512]{2,1,0:T(8,128)(2,1)} %refs_18_.11), channel_id=1, source_target_pairs={{0,1},{1,0},{2,3},{3,2},{4,5},{5,4},{6,7},{7,6},{8,9},{9,8},{10,11... | collective-permute-start | bytes 589832 | tf_op jit(solution)/shard_map/ppermute | solution.py:77
  3.7 16.3 %collective-permute-start.1 = (bf16[1,512,512]{2,1,0:T(8,128)(2,1)}, bf16[1,512,512]{2,1,0:T(8,128)(2,1)S(1)}, u32[]{:S(2)}, u32[]{:S(2)}) collective-permute-start(bf16[1,512,512]{2,1,0:T(8,128)(2,1)} %refs_10_.11), channel_id=1, source_target_pairs={{0,2},{1,3},{2,0},{3,1},{4,6},{5,7},{6,4},{7,5},{8,10},{9,11},{10,... | collective-permute-start | bytes 1572872 | tf_op jit(solution)/shard_map/ppermute | solution.py:81
  3.8 19.6 %collective-permute-start = (bf16[1,512,512]{2,1,0:T(8,128)(2,1)}, bf16[1,512,512]{2,1,0:T(8,128)(2,1)S(1)}, u32[]{:S(2)}, u32[]{:S(2)}) collective-permute-start(bf16[1,512,512]{2,1,0:T(8,128)(2,1)} %refs_10_.11), channel_id=1, source_target_pairs={{0,1},{1,0},{2,3},{3,2},{4,5},{5,4},{6,7},{7,6},{8,9},{9,8},{10,11... | collective-permute-start | bytes 1572872 | tf_op jit(solution)/shard_map/ppermute | solution.py:77
  20.0 3.4 %collective-permute-start.2 = (bf16[1,512,512]{2,1,0:T(8,128)(2,1)S(1)}, bf16[1,512,512]{2,1,0:T(8,128)(2,1)S(1)}, u32[]{:S(2)}, u32[]{:S(2)}) collective-permute-start(bf16[1,512,512]{2,1,0:T(8,128)(2,1)S(1)} %collective-permute-done.1.refs_15_.refs_16_), channel_id=1, source_target_pairs={{0,1},{1,0},{2,3},{3,2},{4,5},{5,4},{6,7},{7,6},{8,9},{9,8},{10,11... | collective-permute-start | bytes 1572872 | tf_op jit(solution)/shard_map/ppermute | solution.py:91
  21.9 1.5 %collective-permute-start.5 = (bf16[1,192,512]{2,1,0:T(8,128)(2,1)S(1)}, bf16[1,192,512]{2,1,0:T(8,128)(2,1)S(1)}, u32[]{:S(2)}, u32[]{:S(2)}) collective-permute-start(bf16[1,192,512]{2,1,0:T(8,128)(2,1)S(1)} %collective-permute-done.4.refs_23_.refs_24_), channel_id=1, source_target_pairs={{0,1},{1,0},{2,3},{3,2},{4,5},{5,4},{6,7},{7,6},{8,9},{9,8},{10,11... | collective-permute-start | bytes 589832 | tf_op jit(solution)/shard_map/ppermute | solution.py:91
  24.5 35.5 %copy-start.16 = (bf16[8,80]{1,0:T(8,128)(2,1)S(1)}, bf16[8,80]{1,0:T(8,128)(2,1)}, u32[]{:S(2)}) copy-start(bf16[8,80]{1,0:T(8,128)(2,1)} %param.28) | copy-start | bytes 3844
  24.5 35.7 %copy-start.8 = (bf16[1,192,512]{2,1,0:T(8,128)(2,1)S(1)}, bf16[1,192,512]{2,1,0:T(8,128)(2,1)}, u32[]{:S(2)}) copy-start(bf16[1,192,512]{2,1,0:T(8,128)(2,1)} %refs_18_.11) | copy-start | bytes 589828
  40.0 3.1 %collective-permute-start.6 = (bf16[1,2560]{1,0:T(2,128)(2,1)S(1)}, bf16[1,2560]{1,0:T(2,128)(2,1)S(1)}, u32[]{:S(2)}, u32[]{:S(2)}) collective-permute-start(bf16[1,2560]{1,0:T(2,128)(2,1)S(1)} %fusion.15), channel_id=1, source_target_pairs={{0,1},{1,0},{2,3},{3,2},{4,5},{5,4},{6,7},{7,6},{8,9},{9,8},{10,11... | collective-permute-start | bytes 15368 | tf_op jit(solution)/shard_map/ppermute | solution.py:25
  43.9 3.7 %collective-permute-start.7 = (bf16[1,2560]{1,0:T(2,128)(2,1)S(1)}, bf16[1,2560]{1,0:T(2,128)(2,1)S(1)}, u32[]{:S(2)}, u32[]{:S(2)}) collective-permute-start(bf16[1,2560]{1,0:T(2,128)(2,1)S(1)} %fusion.47), channel_id=1, source_target_pairs={{0,2},{1,3},{2,0},{3,1},{4,6},{5,7},{6,4},{7,5},{8,10},{9,11},{10,... | collective-permute-start | bytes 15368 | tf_op jit(solution)/shard_map/ppermute | solution.py:25
  47.6 3.7 %collective-permute-start.8 = (bf16[1,2560]{1,0:T(2,128)(2,1)S(1)}, bf16[1,2560]{1,0:T(2,128)(2,1)S(1)}, u32[]{:S(2)}, u32[]{:S(2)}) collective-permute-start(bf16[1,2560]{1,0:T(2,128)(2,1)S(1)} %add.615), channel_id=1, source_target_pairs={{0,4},{4,0},{8,12},{12,8},{16,20},{20,16},{24,28},{28,24},{1,5},{5... | collective-permute-start | bytes 15368 | tf_op jit(solution)/shard_map/ppermute | solution.py:37
  51.4 3.7 %collective-permute-start.9 = (bf16[2,2560]{1,0:T(2,128)(2,1)S(1)}, bf16[2,2560]{1,0:T(2,128)(2,1)S(1)}, u32[]{:S(2)}, u32[]{:S(2)}) collective-permute-start(bf16[2,2560]{1,0:T(2,128)(2,1)S(1)} %broadcast_select_fusion.1), channel_id=1, source_target_pairs={{0,8},{4,12},{8,0},{12,4},{16,24},{20,28},{24,16},{28,20},{1,9},{5... | collective-permute-start | bytes 30728 | tf_op jit(solution)/shard_map/ppermute | solution.py:37
  55.2 4.7 %collective-permute-start.10 = (bf16[4,2560]{1,0:T(4,128)(2,1)S(1)}, bf16[4,2560]{1,0:T(4,128)(2,1)S(1)}, u32[]{:S(2)}, u32[]{:S(2)}) collective-permute-start(bf16[4,2560]{1,0:T(4,128)(2,1)S(1)} %maximum_select_fusion.3), channel_id=1, source_target_pairs={{0,16},{4,20},{8,24},{12,28},{16,0},{20,4},{24,8},{28,12},{1,17},{... | collective-permute-start | bytes 61448 | tf_op jit(solution)/shard_map/ppermute | solution.py:37
  60.2 3.9 %collective-permute-start.11 = (bf16[8,80]{1,0:T(8,128)(2,1)S(1)}, bf16[8,80]{1,0:T(8,128)(2,1)S(1)}, u32[]{:S(2)}, u32[]{:S(2)}) collective-permute-start(bf16[8,80]{1,0:T(8,128)(2,1)S(1)} %fusion), channel_id=1, source_target_pairs={{0,1},{1,0},{2,3},{3,2},{4,5},{5,4},{6,7},{7,6},{8,9},{9,8},{10,11... | collective-permute-start | bytes 3848 | tf_op jit(solution)/shard_map/ppermute | solution.py:37
  64.1 7.2 %collective-permute-start.12 = (bf16[8,160]{1,0:T(8,128)(2,1)S(1)}, bf16[8,160]{1,0:T(8,128)(2,1)S(1)}, u32[]{:S(2)}, u32[]{:S(2)}) collective-permute-start(bf16[8,160]{1,0:T(8,128)(2,1)S(1)} %maximum_select_fusion.8), channel_id=1, source_target_pairs={{0,2},{1,3},{2,0},{3,1},{4,6},{5,7},{6,4},{7,5},{8,10},{9,11},{10,... | collective-permute-start | bytes 7688 | tf_op jit(solution)/shard_map/ppermute | solution.py:37
  71.4 8.6 %collective-permute-start.13 = (bf16[8,320]{1,0:T(8,128)(2,1)S(1)}, bf16[8,320]{1,0:T(8,128)(2,1)S(1)}, u32[]{:S(2)}, u32[]{:S(2)}) collective-permute-start(bf16[8,320]{1,0:T(8,128)(2,1)S(1)} %maximum_select_fusion.7), channel_id=1, source_target_pairs={{0,4},{4,0},{8,12},{12,8},{16,20},{20,16},{24,28},{28,24},{1,5},{5... | collective-permute-start | bytes 15368 | tf_op jit(solution)/shard_map/ppermute | solution.py:37
  80.1 8.6 %collective-permute-start.14 = (bf16[8,640]{1,0:T(8,128)(2,1)S(1)}, bf16[8,640]{1,0:T(8,128)(2,1)S(1)}, u32[]{:S(2)}, u32[]{:S(2)}) collective-permute-start(bf16[8,640]{1,0:T(8,128)(2,1)S(1)} %maximum_select_fusion.5), channel_id=1, source_target_pairs={{0,8},{4,12},{8,0},{12,4},{16,24},{20,28},{24,16},{28,20},{1,9},{5... | collective-permute-start | bytes 30728 | tf_op jit(solution)/shard_map/ppermute | solution.py:37
  88.7 9.8 %collective-permute-start.15 = (bf16[8,1280]{1,0:T(8,128)(2,1)S(1)}, bf16[8,1280]{1,0:T(8,128)(2,1)S(1)}, u32[]{:S(2)}, u32[]{:S(2)}) collective-permute-start(bf16[8,1280]{1,0:T(8,128)(2,1)S(1)} %maximum_select_fusion.4), channel_id=1, source_target_pairs={{0,16},{4,20},{8,24},{12,28},{16,0},{20,4},{24,8},{28,12},{1,17},{... | collective-permute-start | bytes 61448 | tf_op jit(solution)/shard_map/ppermute | solution.py:37
  116.2 1.2 collective-permute-start.16
  117.4 6.8 %collective-permute-start.17 = (f32[3,8]{1,0:T(4,128)S(1)}, f32[3,8]{1,0:T(4,128)S(1)}, u32[]{:S(2)}, u32[]{:S(2)}) collective-permute-start(f32[3,8]{1,0:T(4,128)S(1)} %pad_maximum_fusion.1), channel_id=1, source_target_pairs={{0,2},{1,3},{2,0},{3,1},{4,6},{5,7},{6,4},{7,5},{8,10},{9,11},{10,... | collective-permute-start | bytes 296 | tf_op jit(solution)/shard_map/ppermute | solution.py:64
  124.3 3.7 %collective-permute-start.18 = (f32[3,8]{1,0:T(4,128)S(1)}, f32[3,8]{1,0:T(4,128)S(1)}, u32[]{:S(2)}, u32[]{:S(2)}) collective-permute-start(f32[3,8]{1,0:T(4,128)S(1)} %pad_maximum_fusion.2), channel_id=1, source_target_pairs={{0,4},{4,0},{8,12},{12,8},{16,20},{20,16},{24,28},{28,24},{1,5},{5... | collective-permute-start | bytes 296 | tf_op jit(solution)/shard_map/ppermute | solution.py:64
  128.0 6.4 %collective-permute-start.19 = (f32[3,8]{1,0:T(4,128)S(1)}, f32[3,8]{1,0:T(4,128)S(1)}, u32[]{:S(2)}, u32[]{:S(2)}) collective-permute-start(f32[3,8]{1,0:T(4,128)S(1)} %pad_maximum_fusion.3), channel_id=1, source_target_pairs={{0,8},{4,12},{8,0},{12,4},{16,24},{20,28},{24,16},{28,20},{1,9},{5... | collective-permute-start | bytes 296 | tf_op jit(solution)/shard_map/ppermute | solution.py:64
  134.4 4.5 %collective-permute-start.20 = (f32[3,8]{1,0:T(4,128)S(1)}, f32[3,8]{1,0:T(4,128)S(1)}, u32[]{:S(2)}, u32[]{:S(2)}) collective-permute-start(f32[3,8]{1,0:T(4,128)S(1)} %pad_maximum_fusion.4), channel_id=1, source_target_pairs={{0,16},{4,20},{8,24},{12,28},{16,0},{20,4},{24,8},{28,12},{1,17},{... | collective-permute-start | bytes 296 | tf_op jit(solution)/shard_map/ppermute | solution.py:64
  (15 other events, 112.2 us)

commit v7 on v6

--- a/solution.py
+++ b/solution.py
@@ -98,7 +98,7 @@
     return jnp.bitwise_xor(masks, my_index) if by_xor else masks
 
 
-def attention_kernel(qpos_ref, *refs, kinds, scale):
+def attention_kernel(qpos_ref, *refs, kinds, scale, stacked, head_dim):
     count = len(kinds)
     bound_refs = refs[:count]
     q_ref = refs[count]
@@ -106,6 +106,11 @@
     out_ref = refs[-1]
     query = q_ref[0]
     position = qpos_ref[...]
+    if stacked > 1:
+        query = jnp.concatenate(
+            [query[:, i * head_dim : (i + 1) * head_dim] for i in range(stacked)], axis=0
+        )
+        position = jnp.concatenate([position] * stacked, axis=0)
     dims = (((1,), (1,)), ((), ()))
     masked = []
     for i, kind in enumerate(kinds):
@@ -126,10 +131,16 @@
             for i, w in enumerate(weights)
         ],
     )
-    out_ref[0] = (mixed / total).astype(out_ref.dtype)
-
-
-def attend(queries, query_pos, pieces, head_dim, first_head=0, head_count=None, rows=None):
+    result = (mixed / total).astype(out_ref.dtype)
+    if stacked > 1:
+        rows = result.shape[0] // stacked
+        for i in range(stacked):
+            out_ref[0, :, i * head_dim : (i + 1) * head_dim] = result[i * rows : (i + 1) * rows]
+    else:
+        out_ref[0] = result
+
+
+def attend(queries, query_pos, pieces, head_dim, first_head=0, head_count=None, rows=None, stacked=1):
     req_local, new_local, model_cols = queries.shape
     if head_count is None:
         head_count = model_cols // head_dim
@@ -137,7 +148,14 @@
         new_local = rows
     row_block = (new_local - 1) // new_local if rows is None else (queries.shape[1] // rows - 1)
     kinds = [kind for kind, _, _ in pieces]
-    kernel = functools.partial(attention_kernel, kinds=kinds, scale=1.0 / math.sqrt(head_dim))
+    kernel = functools.partial(
+        attention_kernel,
+        kinds=kinds,
+        scale=1.0 / math.sqrt(head_dim),
+        stacked=stacked,
+        head_dim=head_dim,
+    )
+    width = head_dim * stacked
     bound_specs = [
         pl.BlockSpec((1, 1, rows.shape[1]), lambda r, h: (r, 0, 0)) for _, rows, _ in pieces
     ]
@@ -149,12 +167,12 @@
         kv_args.extend([rows, rows])
     return pl.pallas_call(
         kernel,
-        grid=(req_local, head_count),
+        grid=(req_local, head_count // stacked),
         in_specs=[pl.BlockSpec((new_local, 1), lambda r, h: (row_block, 0))]
         + bound_specs
-        + [pl.BlockSpec((1, new_local, head_dim), lambda r, h: (r, row_block, h + first_head))]
+        + [pl.BlockSpec((1, new_local, width), lambda r, h: (r, row_block, h + first_head // stacked))]
         + kv_specs,
-        out_specs=pl.BlockSpec((1, new_local, head_dim), lambda r, h: (r, 0, h)),
+        out_specs=pl.BlockSpec((1, new_local, width), lambda r, h: (r, 0, h)),
         out_shape=jax.ShapeDtypeStruct(
             (req_local, new_local, head_count * head_dim), queries.dtype
         ),
@@ -198,8 +216,8 @@
         pieces.append(("lo", rows, new_lo))
     head_count = model_cols // head_dim
     tail_rows = 8 if new_local % 8 == 0 else new_local
-    last_rows = attend(queries, query_pos, pieces, head_dim, rows=tail_rows)
-    group = 2 if head_count % 2 == 0 else 1
+    last_rows = attend(queries, query_pos, pieces, head_dim, rows=tail_rows, stacked=head_count)
+    group = head_count // 2 if head_count % 2 == 0 else head_count
     mixed_out = jnp.concatenate(
         [
             attend(queries, query_pos, pieces, head_dim, first, group)

time: 140 us -> 124 us (0.89)
  Pallas kernels: 45 us -> 26.6 us
  local copies, waits for them, and re-layouts: 13.4 us -> 7 us
  other arithmetic: 13.3 us -> 18.6 us
  starting transfers between devices: 22.5 us -> 24.8 us
  waiting for transfers between devices: 23.1 us -> 24.8 us
    pallas_call x6 -> x3, Pallas kernels: 45 us -> 26.6 us  [attend(): pl.pallas_call(kernel, grid=(req_local, head_count // stacked), in_specs=...]
    ppermute x5, starting transfers between devices: 2.05 us -> 5.65 us  [butterfly_stats(): other = lax.ppermute(packed, axis, xor_pairs(count, bit))]
    ppermute x8, waiting for transfers between devices: 5.58 us -> 8.9 us  [butterfly_gather(): other = lax.ppermute(x, axis, xor_pairs(count, bit))]
    ppermute x5, waiting for transfers between devices: 6.46 us -> 4.1 us  [butterfly_stats(): other = lax.ppermute(packed, axis, xor_pairs(count, bit))]
    unnamed x40 -> x52, local copies, waits for them, and re-layouts: 3.88 us -> 1.68 us
    concatenate x0 -> x1, other arithmetic: none -> 2.04 us  [on_device(): jnp.concatenate([attend(queries, query_pos, pieces, head_dim, first, grou...]
    gather x1, local copies, waits for them, and re-layouts: 3.9 us -> 2.1 us  [on_device(): from_cache = jnp.take_along_axis(cache_keys, cache_row[:, :, None], axis=1)]
    ppermute x2, waiting for transfers between devices: 8.03 us -> 9.52 us  [exchange_pieces(): other = lax.ppermute(held, axis, xor_pairs(count, bit))]
  transfers between devices with their start and end apart: 21 -> 21, of which waited for: 9 -> 15; matrix products, arithmetic and copies ran while one was open for 16% -> 15% of each run, Pallas kernels for 22% -> 18%
where the time goes in v7:
time: 124 us
  Pallas kernels  26.6 us (21%)
  starting transfers between devices  24.8 us (20%)
  waiting for transfers between devices  24.8 us (20%)
  other arithmetic  18.6 us (15%)
  matrix products  17.4 us (14%)
  local copies, waits for them, and re-layouts  7 us (6%)
  between operations  4.74 us (4%)
    pallas_call x3, Pallas kernels, attend(): pl.pallas_call(kernel, grid=(req_local, head_count // stacked), in_specs=...  26.6 us
    dot_general x1, matrix products, on_device(): lax.dot_general(normed, head, (((1,), (1,)), ((), ())), preferred_element...  17.2 us
    ppermute x8, starting transfers between devices, butterfly_gather(): other = lax.ppermute(x, axis, xor_pairs(count, bit))  13.4 us
    ppermute x2, waiting for transfers between devices, exchange_pieces(): other = lax.ppermute(held, axis, xor_pairs(count, bit))  9.52 us
    ppermute x8, waiting for transfers between devices, butterfly_gather(): other = lax.ppermute(x, axis, xor_pairs(count, bit))  8.9 us
    ppermute x5, starting transfers between devices, butterfly_stats(): other = lax.ppermute(packed, axis, xor_pairs(count, bit))  5.65 us
    ppermute x5, waiting for transfers between devices, butterfly_stats(): other = lax.ppermute(packed, axis, xor_pairs(count, bit))  4.1 us
    ppermute x2, starting transfers between devices, exchange_pieces(): other = lax.ppermute(held, axis, xor_pairs(count, bit))  3.16 us
  transfers between devices with their start and end apart: 21, of which 15 were waited for; matrix products, arithmetic and copies ran while one was open for 15% of the time, Pallas kernels for 18%

profile of v7, /device:TPU:0, one launch (start us, length us, event | category | flops | bytes accessed | tf_op | source)
XLA Modules:
  0.0 123.9 jit_solution(10328833595722127)
XLA Ops:
  0.6 3.0 %collective-permute-start.1 = (bf16[1,512,512]{2,1,0:T(8,128)(2,1)}, bf16[1,512,512]{2,1,0:T(8,128)(2,1)S(1)}, u32[]{:S(2)}, u32[]{:S(2)}) collective-permute-start(bf16[1,512,512]{2,1,0:T(8,128)(2,1)} %refs_10_.5), channel_id=1, source_target_pairs={{0,2},{1,3},{2,0},{3,1},{4,6},{5,7},{6,4},{7,5},{8,10},{9,11},{10,... | collective-permute-start | bytes 1572872 | tf_op jit(solution)/shard_map/ppermute | solution.py:81
  8.6 8.0 %collective-permute-done.1.refs_15_.refs_16_ = bf16[1,512,512]{2,1,0:T(8,128)(2,1)S(1)} collective-permute-done((bf16[1,512,512]{2,1,0:T(8,128)(2,1)}, bf16[1,512,512]{2,1,0:T(8,128)(2,1)S(1)}, u32[]{:S(2)}, u32[]{:S(2)}) %collective-permute-start.1) | collective-permute-done | bytes 524320 | tf_op jit(solution)/shard_map/ppermute | solution.py:81
  22.5 3.8 %shard_map.232 = bf16[1,8,2560]{2,1,0:T(8,128)(2,1)} custom-call(s32[192,1]{1,0:T(8,128)} %iota_add_fusion.qpos_ref, s32[1,1,512]{2,1,0:T(1,128)} %get-tuple-element.84.refs_0_, s32[1,1,512]{2,1,0:T(1,128)} %get-tuple-element.83.refs_1_, s32[1,1,512]{2,1,0:T(1,128)} %get-tuple-element.82.refs_2_, s32[1,1,512]{2,1,0:T(1,128)} %get-tuple-element.81.refs_3_, ...), custom_call_target="tpu_custom_call" | custom-call | tf_op jit(solution)/shard_map/pallas_call | solution.py:168
  29.2 1.8 %collective-permute-start.7 = (bf16[1,2560]{1,0:T(2,128)(2,1)S(1)}, bf16[1,2560]{1,0:T(2,128)(2,1)S(1)}, u32[]{:S(2)}, u32[]{:S(2)}) collective-permute-start(bf16[1,2560]{1,0:T(2,128)(2,1)S(1)} %fusion.47), channel_id=1, source_target_pairs={{0,2},{1,3},{2,0},{3,1},{4,6},{5,7},{6,4},{7,5},{8,10},{9,11},{10,... | collective-permute-start | bytes 15368 | tf_op jit(solution)/shard_map/ppermute | solution.py:25
  31.1 1.9 %collective-permute-done.7 = bf16[1,2560]{1,0:T(2,128)(2,1)S(1)} collective-permute-done((bf16[1,2560]{1,0:T(2,128)(2,1)S(1)}, bf16[1,2560]{1,0:T(2,128)(2,1)S(1)}, u32[]{:S(2)}, u32[]{:S(2)}) %collective-permute-start.7) | collective-permute-done | bytes 5152 | tf_op jit(solution)/shard_map/ppermute | solution.py:25
  33.0 1.8 %collective-permute-start.8 = (bf16[1,2560]{1,0:T(2,128)(2,1)S(1)}, bf16[1,2560]{1,0:T(2,128)(2,1)S(1)}, u32[]{:S(2)}, u32[]{:S(2)}) collective-permute-start(bf16[1,2560]{1,0:T(2,128)(2,1)S(1)} %add.615), channel_id=1, source_target_pairs={{0,4},{4,0},{8,12},{12,8},{16,20},{20,16},{24,28},{28,24},{1,5},{5... | collective-permute-start | bytes 15368 | tf_op jit(solution)/shard_map/ppermute | solution.py:37
  36.8 1.9 %collective-permute-start.9 = (bf16[2,2560]{1,0:T(2,128)(2,1)S(1)}, bf16[2,2560]{1,0:T(2,128)(2,1)S(1)}, u32[]{:S(2)}, u32[]{:S(2)}) collective-permute-start(bf16[2,2560]{1,0:T(2,128)(2,1)S(1)} %broadcast_select_fusion.1), channel_id=1, source_target_pairs={{0,8},{4,12},{8,0},{12,4},{16,24},{20,28},{24,16},{28,20},{1,9},{5... | collective-permute-start | bytes 30728 | tf_op jit(solution)/shard_map/ppermute | solution.py:37
  40.6 2.9 %collective-permute-start.10 = (bf16[4,2560]{1,0:T(4,128)(2,1)S(1)}, bf16[4,2560]{1,0:T(4,128)(2,1)S(1)}, u32[]{:S(2)}, u32[]{:S(2)}) collective-permute-start(bf16[4,2560]{1,0:T(4,128)(2,1)S(1)} %maximum_select_fusion.3), channel_id=1, source_target_pairs={{0,16},{4,20},{8,24},{12,28},{16,0},{20,4},{24,8},{28,12},{1,17},{... | collective-permute-start | bytes 61448 | tf_op jit(solution)/shard_map/ppermute | solution.py:37
  43.5 2.6 %compare_select_fusion.3 = (s32[512,1]{0,1:T(1,128)S(1)}, s32[1,512]{1,0:T(1,128)S(1)}, s32[512,1]{0,1:T(1,128)S(1)}) fusion(s32[]{:T(128)} %axis_index.14, s32[]{:T(128)} %bitcast.19, s32[]{:T(128)} %bitcast.18, s32[]{:T(128)} %bitcast.17, s32[]{:T(128)} %bitcast.16, s32[]{:T(128)} %bitcast.15), kind=kLoop, calls=%fused_computation.37 | loop fusion | flops 55296 | bytes 6168 | tf_op jit(solution)/shard_map/jit(take_along_axis)/select_n | solution.py:247
  49.1 2.1 %collective-permute-done.12 = bf16[8,160]{1,0:T(8,128)(2,1)S(1)} collective-permute-done((bf16[8,160]{1,0:T(8,128)(2,1)S(1)}, bf16[8,160]{1,0:T(8,128)(2,1)S(1)}, u32[]{:S(2)}, u32[]{:S(2)}) %collective-permute-start.12) | collective-permute-done | bytes 2592 | tf_op jit(solution)/shard_map/ppermute | solution.py:37
  55.0 1.6 %collective-permute-start.14 = (bf16[8,640]{1,0:T(8,128)(2,1)S(1)}, bf16[8,640]{1,0:T(8,128)(2,1)S(1)}, u32[]{:S(2)}, u32[]{:S(2)}) collective-permute-start(bf16[8,640]{1,0:T(8,128)(2,1)S(1)} %maximum_select_fusion.5), channel_id=1, source_target_pairs={{0,8},{4,12},{8,0},{12,4},{16,24},{20,28},{24,16},{28,20},{1,9},{5... | collective-permute-start | bytes 30728 | tf_op jit(solution)/shard_map/ppermute | solution.py:37
  56.6 2.1 %collective-permute-done.14 = bf16[8,640]{1,0:T(8,128)(2,1)S(1)} collective-permute-done((bf16[8,640]{1,0:T(8,128)(2,1)S(1)}, bf16[8,640]{1,0:T(8,128)(2,1)S(1)}, u32[]{:S(2)}, u32[]{:S(2)}) %collective-permute-start.14) | collective-permute-done | bytes 10272 | tf_op jit(solution)/shard_map/ppermute | solution.py:37
  58.7 2.1 %collective-permute-start.15 = (bf16[8,1280]{1,0:T(8,128)(2,1)S(1)}, bf16[8,1280]{1,0:T(8,128)(2,1)S(1)}, u32[]{:S(2)}, u32[]{:S(2)}) collective-permute-start(bf16[8,1280]{1,0:T(8,128)(2,1)S(1)} %maximum_select_fusion.4), channel_id=1, source_target_pairs={{0,16},{4,20},{8,24},{12,28},{16,0},{20,4},{24,8},{28,12},{1,17},{... | collective-permute-start | bytes 61448 | tf_op jit(solution)/shard_map/ppermute | solution.py:37
  62.0 2.0 %gather_fusion.1 = bf16[512,512]{1,0:T(8,128)(2,1)S(1)} fusion(bf16[768,512]{1,0:T(8,128)(2,1)S(1)} %maximum_bitcast_fusion.1, s32[1024]{0:T(1024)S(1)} %pad_clamp_fusion), kind=kCustom, calls=%fused_computation.1 | custom fusion | bytes 1050624 | tf_op jit(solution)/shard_map/jit(take_along_axis)/gather | solution.py:248
  64.0 11.3 %shard_map.230 = bf16[1,192,1280]{2,1,0:T(8,128)(2,1)} custom-call(s32[192,1]{1,0:T(8,128)} %iota_add_fusion.qpos_ref, s32[1,1,512]{2,1,0:T(1,128)} %get-tuple-element.84.refs_0_, s32[1,1,512]{2,1,0:T(1,128)} %get-tuple-element.83.refs_1_, s32[1,1,512]{2,1,0:T(1,128)} %get-tuple-element.82.refs_2_, s32[1,1,512]{2,1,0:T(1,128)} %get-tuple-element.81.refs_3_, ...), custom_call_target="tpu_custom_call" | custom-call | tf_op jit(solution)/shard_map/pallas_call | solution.py:168
  75.5 17.2 %fusion.44 = (f32[8]{0:T(128)S(1)}, f32[8,8000]{1,0:T(8,128)S(1)}) fusion(bf16[8000,2560]{1,0:T(8,128)(2,1)} %param.30, f32[2560]{0:T(1024)S(1)} %convert_element_type.18, f32[8]{0:T(128)S(1)} %add_rsqrt_fusion, bf16[8,1280]{1,0:T(8,128)(2,1)S(1)} %maximum_select_fusion.4, bf16[8,1280]{1,0:T(8,128)(2,1)S(1)} %collective-permute-done.15, pred[]{:T(512)S(6)} %eq.61), kind=kOutput, calls=%fused_computation.150 | convolution fusion | flops 328010240 | bytes 41267264 | tf_op jit(solution)/shard_map/dot_general | solution.py:268
  93.1 11.4 %shard_map.231 = bf16[1,192,1280]{2,1,0:T(8,128)(2,1)} custom-call(s32[192,1]{1,0:T(8,128)} %iota_add_fusion.qpos_ref, s32[1,1,512]{2,1,0:T(1,128)} %get-tuple-element.84.refs_0_, s32[1,1,512]{2,1,0:T(1,128)} %get-tuple-element.83.refs_1_, s32[1,1,512]{2,1,0:T(1,128)} %get-tuple-element.82.refs_2_, s32[1,1,512]{2,1,0:T(1,128)} %get-tuple-element.81.refs_3_, ...), custom_call_target="tpu_custom_call" | custom-call | tf_op jit(solution)/shard_map/pallas_call | solution.py:168
  104.7 1.6 %collective-permute-start.17 = (f32[3,8]{1,0:T(4,128)S(1)}, f32[3,8]{1,0:T(4,128)S(1)}, u32[]{:S(2)}, u32[]{:S(2)}) collective-permute-start(f32[3,8]{1,0:T(4,128)S(1)} %pad_maximum_fusion.2), channel_id=1, source_target_pairs={{0,2},{1,3},{2,0},{3,1},{4,6},{5,7},{6,4},{7,5},{8,10},{9,11},{10,... | collective-permute-start | bytes 296 | tf_op jit(solution)/shard_map/ppermute | solution.py:64
  106.3 2.0 %pad_maximum_fusion = bf16[1,192,2560]{2,1,0:T(8,128)(2,1)} fusion(bf16[1,192,1280]{2,1,0:T(8,128)(2,1)} %shard_map.231, bf16[1,192,1280]{2,1,0:T(8,128)(2,1)S(1)} %copy-done.12), kind=kLoop, calls=%fused_computation.5 | loop fusion | flops 1966080 | bytes 1966080 | tf_op jit(solution)/shard_map/concatenate | solution.py:221
  110.6 1.9 %collective-permute-done.18 = f32[3,8]{1,0:T(4,128)S(1)} collective-permute-done((f32[3,8]{1,0:T(4,128)S(1)}, f32[3,8]{1,0:T(4,128)S(1)}, u32[]{:S(2)}, u32[]{:S(2)}) %collective-permute-start.18) | collective-permute-done | bytes 128 | tf_op jit(solution)/shard_map/ppermute | solution.py:64
  113.2 1.6 %collective-permute-start.19 = (f32[3,8]{1,0:T(4,128)}, f32[3,8]{1,0:T(4,128)}, u32[]{:S(2)}, u32[]{:S(2)}) collective-permute-start(f32[3,8]{1,0:T(4,128)} %pad_maximum_fusion.4), channel_id=1, source_target_pairs={{0,8},{4,12},{8,0},{12,4},{16,24},{20,28},{24,16},{28,20},{1,9},{5... | collective-permute-start | bytes 296 | tf_op jit(solution)/shard_map/ppermute | solution.py:64
  114.8 2.1 %gather_fusion = bf16[512,512]{1,0:T(8,128)(2,1)S(1)} fusion(bf16[2048,512]{1,0:T(8,128)(2,1)S(1)} %maximum_bitcast_fusion, s32[1024]{0:T(1024)} %pad_clamp_fusion.1), kind=kCustom, calls=%fused_computation | custom fusion | bytes 1050624 | tf_op jit(solution)/shard_map/jit(take_along_axis)/gather | solution.py:247
  118.8 1.8 %fusion.1 = bf16[1,512,512]{2,1,0:T(8,128)(2,1)} fusion(bf16[512,512]{1,0:T(8,128)(2,1)S(1)} %gather_fusion.1, bf16[512,512]{1,0:T(8,128)(2,1)S(1)} %gather_fusion, pred[512]{0:T(512)(128)(4,1)} %get-tuple-element.90, pred[512]{0:T(512)(128)(4,1)} %compare_and_fusion.1, pred[512]{0:T(512)(128)(4,1)} %get-tuple-element.89), kind=kLoop, calls=%fused_computation.8 | loop fusion | flops 786432 | bytes 1574400 | tf_op jit(solution)/shard_map/jit(_where)/select_n | solution.py:249
  120.6 1.9 %collective-permute-done.20 = f32[3,8]{1,0:T(4,128)S(1)} collective-permute-done((f32[3,8]{1,0:T(4,128)S(1)}, f32[3,8]{1,0:T(4,128)S(1)}, u32[]{:S(2)}, u32[]{:S(2)}) %collective-permute-start.20) | collective-permute-done | bytes 128 | tf_op jit(solution)/shard_map/ppermute | solution.py:64
  (119 shorter events, 28.6 us)
Async XLA Ops:
  0.6 45.5 %copy-start = (bf16[2560,80]{0,1:T(8,128)(2,1)S(1)}, bf16[2560,80]{0,1:T(8,128)(2,1)}, u32[]{:S(2)}) copy-start(bf16[2560,80]{0,1:T(8,128)(2,1)} %param.27) | copy-start | bytes 1228804
  0.6 16.0 %collective-permute-start.1 = (bf16[1,512,512]{2,1,0:T(8,128)(2,1)}, bf16[1,512,512]{2,1,0:T(8,128)(2,1)S(1)}, u32[]{:S(2)}, u32[]{:S(2)}) collective-permute-start(bf16[1,512,512]{2,1,0:T(8,128)(2,1)} %refs_10_.5), channel_id=1, source_target_pairs={{0,2},{1,3},{2,0},{3,1},{4,6},{5,7},{6,4},{7,5},{8,10},{9,11},{10,... | collective-permute-start | bytes 1572872 | tf_op jit(solution)/shard_map/ppermute | solution.py:81
  3.6 17.8 %collective-permute-start = (bf16[1,512,512]{2,1,0:T(8,128)(2,1)}, bf16[1,512,512]{2,1,0:T(8,128)(2,1)S(1)}, u32[]{:S(2)}, u32[]{:S(2)}) collective-permute-start(bf16[1,512,512]{2,1,0:T(8,128)(2,1)} %refs_10_.5), channel_id=1, source_target_pairs={{0,1},{1,0},{2,3},{3,2},{4,5},{5,4},{6,7},{7,6},{8,9},{9,8},{10,11... | collective-permute-start | bytes 1572872 | tf_op jit(solution)/shard_map/ppermute | solution.py:77
  3.7 16.3 %collective-permute-start.4 = (bf16[1,192,512]{2,1,0:T(8,128)(2,1)}, bf16[1,192,512]{2,1,0:T(8,128)(2,1)S(1)}, u32[]{:S(2)}, u32[]{:S(2)}) collective-permute-start(bf16[1,192,512]{2,1,0:T(8,128)(2,1)} %refs_18_.5), channel_id=1, source_target_pairs={{0,2},{1,3},{2,0},{3,1},{4,6},{5,7},{6,4},{7,5},{8,10},{9,11},{10,... | collective-permute-start | bytes 589832 | tf_op jit(solution)/shard_map/ppermute | solution.py:81
  3.8 17.5 %collective-permute-start.3 = (bf16[1,192,512]{2,1,0:T(8,128)(2,1)}, bf16[1,192,512]{2,1,0:T(8,128)(2,1)S(1)}, u32[]{:S(2)}, u32[]{:S(2)}) collective-permute-start(bf16[1,192,512]{2,1,0:T(8,128)(2,1)} %refs_18_.5), channel_id=1, source_target_pairs={{0,1},{1,0},{2,3},{3,2},{4,5},{5,4},{6,7},{7,6},{8,9},{9,8},{10,11... | collective-permute-start | bytes 589832 | tf_op jit(solution)/shard_map/ppermute | solution.py:77
  16.6 4.8 %collective-permute-start.2 = (bf16[1,512,512]{2,1,0:T(8,128)(2,1)S(1)}, bf16[1,512,512]{2,1,0:T(8,128)(2,1)S(1)}, u32[]{:S(2)}, u32[]{:S(2)}) collective-permute-start(bf16[1,512,512]{2,1,0:T(8,128)(2,1)S(1)} %collective-permute-done.1.refs_15_.refs_16_), channel_id=1, source_target_pairs={{0,1},{1,0},{2,3},{3,2},{4,5},{5,4},{6,7},{7,6},{8,9},{9,8},{10,11... | collective-permute-start | bytes 1572872 | tf_op jit(solution)/shard_map/ppermute | solution.py:91
  20.0 1.4 %collective-permute-start.5 = (bf16[1,192,512]{2,1,0:T(8,128)(2,1)S(1)}, bf16[1,192,512]{2,1,0:T(8,128)(2,1)S(1)}, u32[]{:S(2)}, u32[]{:S(2)}) collective-permute-start(bf16[1,192,512]{2,1,0:T(8,128)(2,1)S(1)} %collective-permute-done.4.refs_23_.refs_24_), channel_id=1, source_target_pairs={{0,1},{1,0},{2,3},{3,2},{4,5},{5,4},{6,7},{7,6},{8,9},{9,8},{10,11... | collective-permute-start | bytes 589832 | tf_op jit(solution)/shard_map/ppermute | solution.py:91
  22.5 34.1 %copy-start.17 = (bf16[2560]{0:T(1024)(128)(2,1)S(1)}, bf16[2560]{0:T(1024)(128)(2,1)}, u32[]{:S(2)}) copy-start(bf16[2560]{0:T(1024)(128)(2,1)} %param.29) | copy-start | bytes 15364
  22.5 38.3 %copy-start.8 = (bf16[1,192,512]{2,1,0:T(8,128)(2,1)S(1)}, bf16[1,192,512]{2,1,0:T(8,128)(2,1)}, u32[]{:S(2)}) copy-start(bf16[1,192,512]{2,1,0:T(8,128)(2,1)} %refs_18_.5) | copy-start | bytes 589828
  27.2 1.3 %collective-permute-start.6 = (bf16[1,2560]{1,0:T(2,128)(2,1)S(1)}, bf16[1,2560]{1,0:T(2,128)(2,1)S(1)}, u32[]{:S(2)}, u32[]{:S(2)}) collective-permute-start(bf16[1,2560]{1,0:T(2,128)(2,1)S(1)} %fusion.15), channel_id=1, source_target_pairs={{0,1},{1,0},{2,3},{3,2},{4,5},{5,4},{6,7},{7,6},{8,9},{9,8},{10,11... | collective-permute-start | bytes 15368 | tf_op jit(solution)/shard_map/ppermute | solution.py:25
  29.2 3.7 %collective-permute-start.7 = (bf16[1,2560]{1,0:T(2,128)(2,1)S(1)}, bf16[1,2560]{1,0:T(2,128)(2,1)S(1)}, u32[]{:S(2)}, u32[]{:S(2)}) collective-permute-start(bf16[1,2560]{1,0:T(2,128)(2,1)S(1)} %fusion.47), channel_id=1, source_target_pairs={{0,2},{1,3},{2,0},{3,1},{4,6},{5,7},{6,4},{7,5},{8,10},{9,11},{10,... | collective-permute-start | bytes 15368 | tf_op jit(solution)/shard_map/ppermute | solution.py:25
  33.0 3.7 %collective-permute-start.8 = (bf16[1,2560]{1,0:T(2,128)(2,1)S(1)}, bf16[1,2560]{1,0:T(2,128)(2,1)S(1)}, u32[]{:S(2)}, u32[]{:S(2)}) collective-permute-start(bf16[1,2560]{1,0:T(2,128)(2,1)S(1)} %add.615), channel_id=1, source_target_pairs={{0,4},{4,0},{8,12},{12,8},{16,20},{20,16},{24,28},{28,24},{1,5},{5... | collective-permute-start | bytes 15368 | tf_op jit(solution)/shard_map/ppermute | solution.py:37
  36.8 3.7 %collective-permute-start.9 = (bf16[2,2560]{1,0:T(2,128)(2,1)S(1)}, bf16[2,2560]{1,0:T(2,128)(2,1)S(1)}, u32[]{:S(2)}, u32[]{:S(2)}) collective-permute-start(bf16[2,2560]{1,0:T(2,128)(2,1)S(1)} %broadcast_select_fusion.1), channel_id=1, source_target_pairs={{0,8},{4,12},{8,0},{12,4},{16,24},{20,28},{24,16},{28,20},{1,9},{5... | collective-permute-start | bytes 30728 | tf_op jit(solution)/shard_map/ppermute | solution.py:37
  40.6 5.5 %collective-permute-start.10 = (bf16[4,2560]{1,0:T(4,128)(2,1)S(1)}, bf16[4,2560]{1,0:T(4,128)(2,1)S(1)}, u32[]{:S(2)}, u32[]{:S(2)}) collective-permute-start(bf16[4,2560]{1,0:T(4,128)(2,1)S(1)} %maximum_select_fusion.3), channel_id=1, source_target_pairs={{0,16},{4,20},{8,24},{12,28},{16,0},{20,4},{24,8},{28,12},{1,17},{... | collective-permute-start | bytes 61448 | tf_op jit(solution)/shard_map/ppermute | solution.py:37
  46.4 1.2 collective-permute-start.11
  47.6 3.6 %collective-permute-start.12 = (bf16[8,160]{1,0:T(8,128)(2,1)S(1)}, bf16[8,160]{1,0:T(8,128)(2,1)S(1)}, u32[]{:S(2)}, u32[]{:S(2)}) collective-permute-start(bf16[8,160]{1,0:T(8,128)(2,1)S(1)} %maximum_select_fusion.8), channel_id=1, source_target_pairs={{0,2},{1,3},{2,0},{3,1},{4,6},{5,7},{6,4},{7,5},{8,10},{9,11},{10,... | collective-permute-start | bytes 7688 | tf_op jit(solution)/shard_map/ppermute | solution.py:37
  51.3 3.6 %collective-permute-start.13 = (bf16[8,320]{1,0:T(8,128)(2,1)S(1)}, bf16[8,320]{1,0:T(8,128)(2,1)S(1)}, u32[]{:S(2)}, u32[]{:S(2)}) collective-permute-start(bf16[8,320]{1,0:T(8,128)(2,1)S(1)} %maximum_select_fusion.7), channel_id=1, source_target_pairs={{0,4},{4,0},{8,12},{12,8},{16,20},{20,16},{24,28},{28,24},{1,5},{5... | collective-permute-start | bytes 15368 | tf_op jit(solution)/shard_map/ppermute | solution.py:37
  55.0 3.7 %collective-permute-start.14 = (bf16[8,640]{1,0:T(8,128)(2,1)S(1)}, bf16[8,640]{1,0:T(8,128)(2,1)S(1)}, u32[]{:S(2)}, u32[]{:S(2)}) collective-permute-start(bf16[8,640]{1,0:T(8,128)(2,1)S(1)} %maximum_select_fusion.5), channel_id=1, source_target_pairs={{0,8},{4,12},{8,0},{12,4},{16,24},{20,28},{24,16},{28,20},{1,9},{5... | collective-permute-start | bytes 30728 | tf_op jit(solution)/shard_map/ppermute | solution.py:37
  58.7 16.6 %collective-permute-start.15 = (bf16[8,1280]{1,0:T(8,128)(2,1)S(1)}, bf16[8,1280]{1,0:T(8,128)(2,1)S(1)}, u32[]{:S(2)}, u32[]{:S(2)}) collective-permute-start(bf16[8,1280]{1,0:T(8,128)(2,1)S(1)} %maximum_select_fusion.4), channel_id=1, source_target_pairs={{0,16},{4,20},{8,24},{12,28},{16,0},{20,4},{24,8},{28,12},{1,17},{... | collective-permute-start | bytes 61448 | tf_op jit(solution)/shard_map/ppermute | solution.py:37
  93.1 11.6 %collective-permute-start.16 = (f32[3,8]{1,0:T(4,128)S(1)}, f32[3,8]{1,0:T(4,128)S(1)}, u32[]{:S(2)}, u32[]{:S(2)}) collective-permute-start(f32[3,8]{1,0:T(4,128)S(1)} %pad_maximum_fusion.1), channel_id=1, source_target_pairs={{0,1},{1,0},{2,3},{3,2},{4,5},{5,4},{6,7},{7,6},{8,9},{9,8},{10,11... | collective-permute-start | bytes 296 | tf_op jit(solution)/shard_map/ppermute | solution.py:64
  104.7 3.7 %collective-permute-start.17 = (f32[3,8]{1,0:T(4,128)S(1)}, f32[3,8]{1,0:T(4,128)S(1)}, u32[]{:S(2)}, u32[]{:S(2)}) collective-permute-start(f32[3,8]{1,0:T(4,128)S(1)} %pad_maximum_fusion.2), channel_id=1, source_target_pairs={{0,2},{1,3},{2,0},{3,1},{4,6},{5,7},{6,4},{7,5},{8,10},{9,11},{10,... | collective-permute-start | bytes 296 | tf_op jit(solution)/shard_map/ppermute | solution.py:64
  109.0 3.6 %collective-permute-start.18 = (f32[3,8]{1,0:T(4,128)S(1)}, f32[3,8]{1,0:T(4,128)S(1)}, u32[]{:S(2)}, u32[]{:S(2)}) collective-permute-start(f32[3,8]{1,0:T(4,128)S(1)} %pad_maximum_fusion.3), channel_id=1, source_target_pairs={{0,4},{4,0},{8,12},{12,8},{16,20},{20,16},{24,28},{28,24},{1,5},{5... | collective-permute-start | bytes 296 | tf_op jit(solution)/shard_map/ppermute | solution.py:64
  113.2 4.0 %collective-permute-start.19 = (f32[3,8]{1,0:T(4,128)}, f32[3,8]{1,0:T(4,128)}, u32[]{:S(2)}, u32[]{:S(2)}) collective-permute-start(f32[3,8]{1,0:T(4,128)} %pad_maximum_fusion.4), channel_id=1, source_target_pairs={{0,8},{4,12},{8,0},{12,4},{16,24},{20,28},{24,16},{28,20},{1,9},{5... | collective-permute-start | bytes 296 | tf_op jit(solution)/shard_map/ppermute | solution.py:64
  118.0 4.5 %collective-permute-start.20 = (f32[3,8]{1,0:T(4,128)S(1)}, f32[3,8]{1,0:T(4,128)S(1)}, u32[]{:S(2)}, u32[]{:S(2)}) collective-permute-start(f32[3,8]{1,0:T(4,128)S(1)} %pad_maximum_fusion.5), channel_id=1, source_target_pairs={{0,16},{4,20},{8,24},{12,28},{16,0},{20,4},{24,8},{28,12},{1,17},{... | collective-permute-start | bytes 296 | tf_op jit(solution)/shard_map/ppermute | solution.py:64
  (23 other events, 166.3 us)

commit v8 on v7

--- a/solution.py
+++ b/solution.py
@@ -215,16 +215,8 @@
         new_lo = jnp.broadcast_to(new_pos[None, None, :], (req_local, 1, new_pos.shape[0]))
         pieces.append(("lo", rows, new_lo))
     head_count = model_cols // head_dim
-    tail_rows = 8 if new_local % 8 == 0 else new_local
-    last_rows = attend(queries, query_pos, pieces, head_dim, rows=tail_rows, stacked=head_count)
-    group = head_count // 2 if head_count % 2 == 0 else head_count
-    mixed_out = jnp.concatenate(
-        [
-            attend(queries, query_pos, pieces, head_dim, first, group)
-            for first in range(0, head_count, group)
-        ],
-        axis=2,
-    )
+    stacked = 5 if head_count % 5 == 0 else 1
+    mixed_out = attend(queries, query_pos, pieces, head_dim, stacked=stacked)
 
     cache_masks = [m for _, masks in cache_pieces for m in masks]
     new_masks = [m for _, masks in new_pieces for m in masks]
@@ -248,7 +240,7 @@
     from_new = jnp.take_along_axis(new_keys, new_row[:, :, None], axis=1)
     fresh_block = jnp.where(from_old[:, :, None], from_cache, from_new)
 
-    last_local = last_rows[:, tail_rows - 1, :]
+    last_local = mixed_out[:, new_local - 1, :]
     group_req = lax.axis_size("gx")
     holder = my_index == group_pos - 1
     last_local = jnp.where(holder, last_local, jnp.zeros_like(last_local))

time: 124 us -> 117 us (0.944)
  Pallas kernels: 26.6 us -> 16.3 us
  starting transfers between devices: 24.8 us -> 28.4 us
  other arithmetic: 18.6 us -> 16.6 us
  local copies, waits for them, and re-layouts: 7 us -> 8.29 us
    pallas_call x3 -> x1, Pallas kernels: 26.6 us -> 16.3 us  [attend(): pl.pallas_call(kernel, grid=(req_local, head_count // stacked), in_specs=...]
    ppermute x5, starting transfers between devices: 5.65 us -> 7.7 us  [butterfly_stats(): other = lax.ppermute(packed, axis, xor_pairs(count, bit))]
    concatenate x1 -> x0, other arithmetic: 2.04 us -> none  [on_device(): jnp.concatenate([attend(queries, query_pos, pieces, head_dim, first, grou...]
    ppermute x5, waiting for transfers between devices: 4.1 us -> 2.12 us  [butterfly_stats(): other = lax.ppermute(packed, axis, xor_pairs(count, bit))]
    ppermute x8, waiting for transfers between devices: 8.9 us -> 10.6 us  [butterfly_gather(): other = lax.ppermute(x, axis, xor_pairs(count, bit))]
    ppermute x8, starting transfers between devices: 13.4 us -> 14.8 us  [butterfly_gather(): other = lax.ppermute(x, axis, xor_pairs(count, bit))]
  transfers between devices with their start and end apart: 21 -> 21, of which waited for: 15 -> 16; matrix products, arithmetic and copies ran while one was open for 15% -> 15% of each run, Pallas kernels for 18% -> 0%
where the time goes in v8:
time: 117 us; the launch traced here: 116 us
  starting transfers between devices  28.4 us (24%)
  waiting for transfers between devices  24.3 us (21%)
  matrix products  17.5 us (15%)
  other arithmetic  16.6 us (14%)
  Pallas kernels  16.3 us (14%)
  local copies, waits for them, and re-layouts  8.29 us (7%)
  between operations  4.84 us (4%)
    dot_general x1, matrix products, on_device(): lax.dot_general(normed, head, (((1,), (1,)), ((), ())), preferred_element...  17.3 us
    pallas_call x1, Pallas kernels, attend(): pl.pallas_call(kernel, grid=(req_local, head_count // stacked), in_specs=...  16.3 us
    ppermute x8, starting transfers between devices, butterfly_gather(): other = lax.ppermute(x, axis, xor_pairs(count, bit))  14.8 us
    ppermute x8, waiting for transfers between devices, butterfly_gather(): other = lax.ppermute(x, axis, xor_pairs(count, bit))  10.6 us
    ppermute x2, waiting for transfers between devices, exchange_pieces(): other = lax.ppermute(held, axis, xor_pairs(count, bit))  9.35 us
    ppermute x5, starting transfers between devices, butterfly_stats(): other = lax.ppermute(packed, axis, xor_pairs(count, bit))  7.7 us
    ppermute x2, starting transfers between devices, exchange_pieces(): other = lax.ppermute(held, axis, xor_pairs(count, bit))  3.08 us
    select_n x1, other arithmetic, on_device(): from_cache = jnp.take_along_axis(cache_keys, cache_row[:, :, None], axis=1)  2.68 us
  transfers between devices with their start and end apart: 21, of which 16 were waited for; matrix products, arithmetic and copies ran while one was open for 15% of the time, Pallas kernels for 0%

profile of v8, /device:TPU:0, one launch (start us, length us, event | category | flops | bytes accessed | tf_op | source)
XLA Modules:
  0.0 116.2 jit_solution(16458104243359855625)
XLA Ops:
  0.6 3.0 %collective-permute-start.1 = (bf16[1,512,512]{2,1,0:T(8,128)(2,1)}, bf16[1,512,512]{2,1,0:T(8,128)(2,1)S(1)}, u32[]{:S(2)}, u32[]{:S(2)}) collective-permute-start(bf16[1,512,512]{2,1,0:T(8,128)(2,1)} %refs_10_.1), channel_id=1, source_target_pairs={{0,2},{1,3},{2,0},{3,1},{4,6},{5,7},{6,4},{7,5},{8,10},{9,11},{10,... | collective-permute-start | bytes 1572872 | tf_op jit(solution)/shard_map/ppermute | solution.py:81
  8.8 7.8 %collective-permute-done.1.refs_15_.refs_16_ = bf16[1,512,512]{2,1,0:T(8,128)(2,1)S(1)} collective-permute-done((bf16[1,512,512]{2,1,0:T(8,128)(2,1)}, bf16[1,512,512]{2,1,0:T(8,128)(2,1)S(1)}, u32[]{:S(2)}, u32[]{:S(2)}) %collective-permute-start.1) | collective-permute-done | bytes 524320 | tf_op jit(solution)/shard_map/ppermute | solution.py:81
  18.4 1.6 %collective-permute-done.4.refs_23_.refs_24_ = bf16[1,192,512]{2,1,0:T(8,128)(2,1)S(1)} collective-permute-done((bf16[1,192,512]{2,1,0:T(8,128)(2,1)}, bf16[1,192,512]{2,1,0:T(8,128)(2,1)S(1)}, u32[]{:S(2)}, u32[]{:S(2)}) %collective-permute-start.4) | collective-permute-done | bytes 196640 | tf_op jit(solution)/shard_map/ppermute | solution.py:81
  22.5 16.3 %shard_map.230 = bf16[1,192,2560]{2,1,0:T(8,128)(2,1)} custom-call(s32[192,1]{1,0:T(8,128)} %iota_add_fusion.qpos_ref, s32[1,1,512]{2,1,0:T(1,128)} %get-tuple-element.84.refs_0_, s32[1,1,512]{2,1,0:T(1,128)} %get-tuple-element.83.refs_1_, s32[1,1,512]{2,1,0:T(1,128)} %get-tuple-element.82.refs_2_, s32[1,1,512]{2,1,0:T(1,128)} %get-tuple-element.81.refs_3_, ...), custom_call_target="tpu_custom_call" | custom-call | tf_op jit(solution)/shard_map/pallas_call | solution.py:168
  41.7 1.8 %collective-permute-start.7 = (bf16[1,2560]{1,0:T(2,128)(2,1)S(1)}, bf16[1,2560]{1,0:T(2,128)(2,1)S(1)}, u32[]{:S(2)}, u32[]{:S(2)}) collective-permute-start(bf16[1,2560]{1,0:T(2,128)(2,1)S(1)} %fusion.47), channel_id=1, source_target_pairs={{0,2},{1,3},{2,0},{3,1},{4,6},{5,7},{6,4},{7,5},{8,10},{9,11},{10,... | collective-permute-start | bytes 15368 | tf_op jit(solution)/shard_map/ppermute | solution.py:25
  45.5 1.8 %collective-permute-start.8 = (bf16[1,2560]{1,0:T(2,128)(2,1)S(1)}, bf16[1,2560]{1,0:T(2,128)(2,1)S(1)}, u32[]{:S(2)}, u32[]{:S(2)}) collective-permute-start(bf16[1,2560]{1,0:T(2,128)(2,1)S(1)} %add.615), channel_id=1, source_target_pairs={{0,4},{4,0},{8,12},{12,8},{16,20},{20,16},{24,28},{28,24},{1,5},{5... | collective-permute-start | bytes 15368 | tf_op jit(solution)/shard_map/ppermute | solution.py:37
  47.3 1.9 %collective-permute-done.8 = bf16[1,2560]{1,0:T(2,128)(2,1)S(1)} collective-permute-done((bf16[1,2560]{1,0:T(2,128)(2,1)S(1)}, bf16[1,2560]{1,0:T(2,128)(2,1)S(1)}, u32[]{:S(2)}, u32[]{:S(2)}) %collective-permute-start.8) | collective-permute-done | bytes 5152 | tf_op jit(solution)/shard_map/ppermute | solution.py:37
  49.2 1.9 %collective-permute-start.9 = (bf16[2,2560]{1,0:T(2,128)(2,1)S(1)}, bf16[2,2560]{1,0:T(2,128)(2,1)S(1)}, u32[]{:S(2)}, u32[]{:S(2)}) collective-permute-start(bf16[2,2560]{1,0:T(2,128)(2,1)S(1)} %broadcast_select_fusion.1), channel_id=1, source_target_pairs={{0,8},{4,12},{8,0},{12,4},{16,24},{20,28},{24,16},{28,20},{1,9},{5... | collective-permute-start | bytes 30728 | tf_op jit(solution)/shard_map/ppermute | solution.py:37
  53.0 2.9 %collective-permute-start.10 = (bf16[4,2560]{1,0:T(4,128)(2,1)S(1)}, bf16[4,2560]{1,0:T(4,128)(2,1)S(1)}, u32[]{:S(2)}, u32[]{:S(2)}) collective-permute-start(bf16[4,2560]{1,0:T(4,128)(2,1)S(1)} %maximum_select_fusion.3), channel_id=1, source_target_pairs={{0,16},{4,20},{8,24},{12,28},{16,0},{20,4},{24,8},{28,12},{1,17},{... | collective-permute-start | bytes 61448 | tf_op jit(solution)/shard_map/ppermute | solution.py:37
  58.0 2.7 %compare_select_fusion.3 = (s32[512,1]{0,1:T(1,128)S(1)}, s32[1,512]{1,0:T(1,128)S(1)}, s32[512,1]{0,1:T(1,128)S(1)}) fusion(s32[]{:T(128)} %axis_index.14, s32[]{:T(128)} %bitcast.19, s32[]{:T(128)} %bitcast.18, s32[]{:T(128)} %bitcast.17, s32[]{:T(128)} %bitcast.16, s32[]{:T(128)} %bitcast.15), kind=kLoop, calls=%fused_computation.36 | loop fusion | flops 55296 | bytes 6168 | tf_op jit(solution)/shard_map/jit(take_along_axis)/select_n | solution.py:239
  60.8 1.7 %collective-permute-start.12 = (bf16[8,160]{1,0:T(8,128)(2,1)S(1)}, bf16[8,160]{1,0:T(8,128)(2,1)S(1)}, u32[]{:S(2)}, u32[]{:S(2)}) collective-permute-start(bf16[8,160]{1,0:T(8,128)(2,1)S(1)} %maximum_select_fusion.8), channel_id=1, source_target_pairs={{0,2},{1,3},{2,0},{3,1},{4,6},{5,7},{6,4},{7,5},{8,10},{9,11},{10,... | collective-permute-start | bytes 7688 | tf_op jit(solution)/shard_map/ppermute | solution.py:37
  64.5 1.8 %collective-permute-start.13 = (bf16[8,320]{1,0:T(8,128)(2,1)S(1)}, bf16[8,320]{1,0:T(8,128)(2,1)S(1)}, u32[]{:S(2)}, u32[]{:S(2)}) collective-permute-start(bf16[8,320]{1,0:T(8,128)(2,1)S(1)} %maximum_select_fusion.7), channel_id=1, source_target_pairs={{0,4},{4,0},{8,12},{12,8},{16,20},{20,16},{24,28},{28,24},{1,5},{5... | collective-permute-start | bytes 15368 | tf_op jit(solution)/shard_map/ppermute | solution.py:37
  66.3 1.9 %collective-permute-done.13 = bf16[8,320]{1,0:T(8,128)(2,1)S(1)} collective-permute-done((bf16[8,320]{1,0:T(8,128)(2,1)S(1)}, bf16[8,320]{1,0:T(8,128)(2,1)S(1)}, u32[]{:S(2)}, u32[]{:S(2)}) %collective-permute-start.13) | collective-permute-done | bytes 5152 | tf_op jit(solution)/shard_map/ppermute | solution.py:37
  68.2 1.8 %collective-permute-start.14 = (bf16[8,640]{1,0:T(8,128)(2,1)S(1)}, bf16[8,640]{1,0:T(8,128)(2,1)S(1)}, u32[]{:S(2)}, u32[]{:S(2)}) collective-permute-start(bf16[8,640]{1,0:T(8,128)(2,1)S(1)} %maximum_select_fusion.5), channel_id=1, source_target_pairs={{0,8},{4,12},{8,0},{12,4},{16,24},{20,28},{24,16},{28,20},{1,9},{5... | collective-permute-start | bytes 30728 | tf_op jit(solution)/shard_map/ppermute | solution.py:37
  70.0 1.8 %collective-permute-done.14 = bf16[8,640]{1,0:T(8,128)(2,1)S(1)} collective-permute-done((bf16[8,640]{1,0:T(8,128)(2,1)S(1)}, bf16[8,640]{1,0:T(8,128)(2,1)S(1)}, u32[]{:S(2)}, u32[]{:S(2)}) %collective-permute-start.14) | collective-permute-done | bytes 10272 | tf_op jit(solution)/shard_map/ppermute | solution.py:37
  71.9 2.8 %collective-permute-start.15 = (bf16[8,1280]{1,0:T(8,128)(2,1)S(1)}, bf16[8,1280]{1,0:T(8,128)(2,1)S(1)}, u32[]{:S(2)}, u32[]{:S(2)}) collective-permute-start(bf16[8,1280]{1,0:T(8,128)(2,1)S(1)} %maximum_select_fusion.4), channel_id=1, source_target_pairs={{0,16},{4,20},{8,24},{12,28},{16,0},{20,4},{24,8},{28,12},{1,17},{... | collective-permute-start | bytes 61448 | tf_op jit(solution)/shard_map/ppermute | solution.py:37
  76.7 17.3 %fusion.44 = (f32[8]{0:T(128)S(1)}, f32[8,8000]{1,0:T(8,128)S(1)}) fusion(bf16[8000,2560]{1,0:T(8,128)(2,1)} %param.30, f32[2560]{0:T(1024)S(1)} %convert_element_type.18, f32[8]{0:T(128)S(1)} %add_rsqrt_fusion, bf16[8,1280]{1,0:T(8,128)(2,1)S(1)} %maximum_select_fusion.4, bf16[8,1280]{1,0:T(8,128)(2,1)S(1)} %collective-permute-done.15, pred[]{:T(512)S(6)} %eq.61), kind=kOutput, calls=%fused_computation.149 | convolution fusion | flops 328010240 | bytes 41267264 | tf_op jit(solution)/shard_map/dot_general | solution.py:260
  96.2 1.8 %collective-permute-start.17 = (f32[3,8]{1,0:T(4,128)S(1)}, f32[3,8]{1,0:T(4,128)S(1)}, u32[]{:S(2)}, u32[]{:S(2)}) collective-permute-start(f32[3,8]{1,0:T(4,128)S(1)} %pad_maximum_fusion.1), channel_id=1, source_target_pairs={{0,2},{1,3},{2,0},{3,1},{4,6},{5,7},{6,4},{7,5},{8,10},{9,11},{10,... | collective-permute-start | bytes 296 | tf_op jit(solution)/shard_map/ppermute | solution.py:64
  98.0 2.7 %gather_fusion.1 = bf16[512,512]{1,0:T(8,128)(2,1)} fusion(bf16[768,512]{1,0:T(8,128)(2,1)S(1)} %maximum_bitcast_fusion.1, s32[1024]{0:T(1024)S(1)} %pad_clamp_fusion), kind=kCustom, calls=%fused_computation.1 | custom fusion | bytes 1050624 | tf_op jit(solution)/shard_map/jit(take_along_axis)/gather | solution.py:240
  101.3 1.5 %collective-permute-start.18 = (f32[3,8]{1,0:T(4,128)S(1)}, f32[3,8]{1,0:T(4,128)S(1)}, u32[]{:S(2)}, u32[]{:S(2)}) collective-permute-start(f32[3,8]{1,0:T(4,128)S(1)} %pad_maximum_fusion.2), channel_id=1, source_target_pairs={{0,4},{4,0},{8,12},{12,8},{16,20},{20,16},{24,28},{28,24},{1,5},{5... | collective-permute-start | bytes 296 | tf_op jit(solution)/shard_map/ppermute | solution.py:64
  105.5 1.6 %collective-permute-start.19 = (f32[3,8]{1,0:T(4,128)}, f32[3,8]{1,0:T(4,128)}, u32[]{:S(2)}, u32[]{:S(2)}) collective-permute-start(f32[3,8]{1,0:T(4,128)} %pad_maximum_fusion.3), channel_id=1, source_target_pairs={{0,8},{4,12},{8,0},{12,4},{16,24},{20,28},{24,16},{28,20},{1,9},{5... | collective-permute-start | bytes 296 | tf_op jit(solution)/shard_map/ppermute | solution.py:64
  107.2 2.1 %gather_fusion = bf16[512,512]{1,0:T(8,128)(2,1)S(1)} fusion(bf16[2048,512]{1,0:T(8,128)(2,1)S(1)} %maximum_bitcast_fusion, s32[1024]{0:T(1024)} %pad_clamp_fusion.1), kind=kCustom, calls=%fused_computation | custom fusion | bytes 1050624 | tf_op jit(solution)/shard_map/jit(take_along_axis)/gather | solution.py:239
  110.3 2.7 %collective-permute-start.20 = (f32[3,8]{1,0:T(4,128)S(1)}, f32[3,8]{1,0:T(4,128)S(1)}, u32[]{:S(2)}, u32[]{:S(2)}) collective-permute-start(f32[3,8]{1,0:T(4,128)S(1)} %pad_maximum_fusion.4), channel_id=1, source_target_pairs={{0,16},{4,20},{8,24},{12,28},{16,0},{20,4},{24,8},{28,12},{1,17},{... | collective-permute-start | bytes 296 | tf_op jit(solution)/shard_map/ppermute | solution.py:64
  113.0 1.8 %fusion.1 = bf16[1,512,512]{2,1,0:T(8,128)(2,1)} fusion(bf16[512,512]{1,0:T(8,128)(2,1)S(1)} %copy-done.6, bf16[512,512]{1,0:T(8,128)(2,1)S(1)} %gather_fusion, pred[512]{0:T(512)(128)(4,1)} %get-tuple-element.90, pred[512]{0:T(512)(128)(4,1)} %compare_and_fusion.1, pred[512]{0:T(512)(128)(4,1)} %get-tuple-element.89), kind=kLoop, calls=%fused_computation.7 | loop fusion | flops 786432 | bytes 1574400 | tf_op jit(solution)/shard_map/jit(_where)/select_n | solution.py:241
  (118 shorter events, 26.5 us)
Async XLA Ops:
  0.6 57.1 %copy-start = (bf16[2560,80]{0,1:T(8,128)(2,1)S(1)}, bf16[2560,80]{0,1:T(8,128)(2,1)}, u32[]{:S(2)}) copy-start(bf16[2560,80]{0,1:T(8,128)(2,1)} %param.27) | copy-start | bytes 1228804
  0.6 16.0 %collective-permute-start.1 = (bf16[1,512,512]{2,1,0:T(8,128)(2,1)}, bf16[1,512,512]{2,1,0:T(8,128)(2,1)S(1)}, u32[]{:S(2)}, u32[]{:S(2)}) collective-permute-start(bf16[1,512,512]{2,1,0:T(8,128)(2,1)} %refs_10_.1), channel_id=1, source_target_pairs={{0,2},{1,3},{2,0},{3,1},{4,6},{5,7},{6,4},{7,5},{8,10},{9,11},{10,... | collective-permute-start | bytes 1572872 | tf_op jit(solution)/shard_map/ppermute | solution.py:81
  3.7 17.8 %collective-permute-start = (bf16[1,512,512]{2,1,0:T(8,128)(2,1)}, bf16[1,512,512]{2,1,0:T(8,128)(2,1)S(1)}, u32[]{:S(2)}, u32[]{:S(2)}) collective-permute-start(bf16[1,512,512]{2,1,0:T(8,128)(2,1)} %refs_10_.1), channel_id=1, source_target_pairs={{0,1},{1,0},{2,3},{3,2},{4,5},{5,4},{6,7},{7,6},{8,9},{9,8},{10,11... | collective-permute-start | bytes 1572872 | tf_op jit(solution)/shard_map/ppermute | solution.py:77
  3.7 17.6 %collective-permute-start.3 = (bf16[1,192,512]{2,1,0:T(8,128)(2,1)}, bf16[1,192,512]{2,1,0:T(8,128)(2,1)S(1)}, u32[]{:S(2)}, u32[]{:S(2)}) collective-permute-start(bf16[1,192,512]{2,1,0:T(8,128)(2,1)} %refs_18_.1), channel_id=1, source_target_pairs={{0,1},{1,0},{2,3},{3,2},{4,5},{5,4},{6,7},{7,6},{8,9},{9,8},{10,11... | collective-permute-start | bytes 589832 | tf_op jit(solution)/shard_map/ppermute | solution.py:77
  4.2 15.8 %collective-permute-start.4 = (bf16[1,192,512]{2,1,0:T(8,128)(2,1)}, bf16[1,192,512]{2,1,0:T(8,128)(2,1)S(1)}, u32[]{:S(2)}, u32[]{:S(2)}) collective-permute-start(bf16[1,192,512]{2,1,0:T(8,128)(2,1)} %refs_18_.1), channel_id=1, source_target_pairs={{0,2},{1,3},{2,0},{3,1},{4,6},{5,7},{6,4},{7,5},{8,10},{9,11},{10,... | collective-permute-start | bytes 589832 | tf_op jit(solution)/shard_map/ppermute | solution.py:81
  16.6 4.8 %collective-permute-start.2 = (bf16[1,512,512]{2,1,0:T(8,128)(2,1)S(1)}, bf16[1,512,512]{2,1,0:T(8,128)(2,1)S(1)}, u32[]{:S(2)}, u32[]{:S(2)}) collective-permute-start(bf16[1,512,512]{2,1,0:T(8,128)(2,1)S(1)} %collective-permute-done.1.refs_15_.refs_16_), channel_id=1, source_target_pairs={{0,1},{1,0},{2,3},{3,2},{4,5},{5,4},{6,7},{7,6},{8,9},{9,8},{10,11... | collective-permute-start | bytes 1572872 | tf_op jit(solution)/shard_map/ppermute | solution.py:91
  20.0 1.4 %collective-permute-start.5 = (bf16[1,192,512]{2,1,0:T(8,128)(2,1)S(1)}, bf16[1,192,512]{2,1,0:T(8,128)(2,1)S(1)}, u32[]{:S(2)}, u32[]{:S(2)}) collective-permute-start(bf16[1,192,512]{2,1,0:T(8,128)(2,1)S(1)} %collective-permute-done.4.refs_23_.refs_24_), channel_id=1, source_target_pairs={{0,1},{1,0},{2,3},{3,2},{4,5},{5,4},{6,7},{7,6},{8,9},{9,8},{10,11... | collective-permute-start | bytes 589832 | tf_op jit(solution)/shard_map/ppermute | solution.py:91
  22.5 43.8 %copy-start.26 = (s32[8]{0:T(128)S(1)}, s32[8]{0:T(128)}, u32[]{:S(2)}) copy-start(s32[8]{0:T(128)} %param.31) | copy-start | bytes 100
  22.5 52.8 %copy-start.18 = (bf16[2560]{0:T(1024)(128)(2,1)S(1)}, bf16[2560]{0:T(1024)(128)(2,1)}, u32[]{:S(2)}) copy-start(bf16[2560]{0:T(1024)(128)(2,1)} %param.29) | copy-start | bytes 15364
  39.6 1.3 %collective-permute-start.6 = (bf16[1,2560]{1,0:T(2,128)(2,1)S(1)}, bf16[1,2560]{1,0:T(2,128)(2,1)S(1)}, u32[]{:S(2)}, u32[]{:S(2)}) collective-permute-start(bf16[1,2560]{1,0:T(2,128)(2,1)S(1)} %fusion.15), channel_id=1, source_target_pairs={{0,1},{1,0},{2,3},{3,2},{4,5},{5,4},{6,7},{7,6},{8,9},{9,8},{10,11... | collective-permute-start | bytes 15368 | tf_op jit(solution)/shard_map/ppermute | solution.py:25
  41.7 3.7 %collective-permute-start.7 = (bf16[1,2560]{1,0:T(2,128)(2,1)S(1)}, bf16[1,2560]{1,0:T(2,128)(2,1)S(1)}, u32[]{:S(2)}, u32[]{:S(2)}) collective-permute-start(bf16[1,2560]{1,0:T(2,128)(2,1)S(1)} %fusion.47), channel_id=1, source_target_pairs={{0,2},{1,3},{2,0},{3,1},{4,6},{5,7},{6,4},{7,5},{8,10},{9,11},{10,... | collective-permute-start | bytes 15368 | tf_op jit(solution)/shard_map/ppermute | solution.py:25
  45.5 3.7 %collective-permute-start.8 = (bf16[1,2560]{1,0:T(2,128)(2,1)S(1)}, bf16[1,2560]{1,0:T(2,128)(2,1)S(1)}, u32[]{:S(2)}, u32[]{:S(2)}) collective-permute-start(bf16[1,2560]{1,0:T(2,128)(2,1)S(1)} %add.615), channel_id=1, source_target_pairs={{0,4},{4,0},{8,12},{12,8},{16,20},{20,16},{24,28},{28,24},{1,5},{5... | collective-permute-start | bytes 15368 | tf_op jit(solution)/shard_map/ppermute | solution.py:37
  49.2 3.7 %collective-permute-start.9 = (bf16[2,2560]{1,0:T(2,128)(2,1)S(1)}, bf16[2,2560]{1,0:T(2,128)(2,1)S(1)}, u32[]{:S(2)}, u32[]{:S(2)}) collective-permute-start(bf16[2,2560]{1,0:T(2,128)(2,1)S(1)} %broadcast_select_fusion.1), channel_id=1, source_target_pairs={{0,8},{4,12},{8,0},{12,4},{16,24},{20,28},{24,16},{28,20},{1,9},{5... | collective-permute-start | bytes 30728 | tf_op jit(solution)/shard_map/ppermute | solution.py:37
  53.0 4.7 %collective-permute-start.10 = (bf16[4,2560]{1,0:T(4,128)(2,1)S(1)}, bf16[4,2560]{1,0:T(4,128)(2,1)S(1)}, u32[]{:S(2)}, u32[]{:S(2)}) collective-permute-start(bf16[4,2560]{1,0:T(4,128)(2,1)S(1)} %maximum_select_fusion.3), channel_id=1, source_target_pairs={{0,16},{4,20},{8,24},{12,28},{16,0},{20,4},{24,8},{28,12},{1,17},{... | collective-permute-start | bytes 61448 | tf_op jit(solution)/shard_map/ppermute | solution.py:37
  58.0 2.7 %collective-permute-start.11 = (bf16[8,80]{1,0:T(8,128)(2,1)S(1)}, bf16[8,80]{1,0:T(8,128)(2,1)S(1)}, u32[]{:S(2)}, u32[]{:S(2)}) collective-permute-start(bf16[8,80]{1,0:T(8,128)(2,1)S(1)} %fusion), channel_id=1, source_target_pairs={{0,1},{1,0},{2,3},{3,2},{4,5},{5,4},{6,7},{7,6},{8,9},{9,8},{10,11... | collective-permute-start | bytes 3848 | tf_op jit(solution)/shard_map/ppermute | solution.py:37
  60.8 3.6 %collective-permute-start.12 = (bf16[8,160]{1,0:T(8,128)(2,1)S(1)}, bf16[8,160]{1,0:T(8,128)(2,1)S(1)}, u32[]{:S(2)}, u32[]{:S(2)}) collective-permute-start(bf16[8,160]{1,0:T(8,128)(2,1)S(1)} %maximum_select_fusion.8), channel_id=1, source_target_pairs={{0,2},{1,3},{2,0},{3,1},{4,6},{5,7},{6,4},{7,5},{8,10},{9,11},{10,... | collective-permute-start | bytes 7688 | tf_op jit(solution)/shard_map/ppermute | solution.py:37
  64.5 3.6 %collective-permute-start.13 = (bf16[8,320]{1,0:T(8,128)(2,1)S(1)}, bf16[8,320]{1,0:T(8,128)(2,1)S(1)}, u32[]{:S(2)}, u32[]{:S(2)}) collective-permute-start(bf16[8,320]{1,0:T(8,128)(2,1)S(1)} %maximum_select_fusion.7), channel_id=1, source_target_pairs={{0,4},{4,0},{8,12},{12,8},{16,20},{20,16},{24,28},{28,24},{1,5},{5... | collective-permute-start | bytes 15368 | tf_op jit(solution)/shard_map/ppermute | solution.py:37
  68.2 3.7 %collective-permute-start.14 = (bf16[8,640]{1,0:T(8,128)(2,1)S(1)}, bf16[8,640]{1,0:T(8,128)(2,1)S(1)}, u32[]{:S(2)}, u32[]{:S(2)}) collective-permute-start(bf16[8,640]{1,0:T(8,128)(2,1)S(1)} %maximum_select_fusion.5), channel_id=1, source_target_pairs={{0,8},{4,12},{8,0},{12,4},{16,24},{20,28},{24,16},{28,20},{1,9},{5... | collective-permute-start | bytes 30728 | tf_op jit(solution)/shard_map/ppermute | solution.py:37
  71.9 4.7 %collective-permute-start.15 = (bf16[8,1280]{1,0:T(8,128)(2,1)S(1)}, bf16[8,1280]{1,0:T(8,128)(2,1)S(1)}, u32[]{:S(2)}, u32[]{:S(2)}) collective-permute-start(bf16[8,1280]{1,0:T(8,128)(2,1)S(1)} %maximum_select_fusion.4), channel_id=1, source_target_pairs={{0,16},{4,20},{8,24},{12,28},{16,0},{20,4},{24,8},{28,12},{1,17},{... | collective-permute-start | bytes 61448 | tf_op jit(solution)/shard_map/ppermute | solution.py:37
  94.4 1.2 %collective-permute-start.16 = (f32[3,8]{1,0:T(4,128)S(1)}, f32[3,8]{1,0:T(4,128)S(1)}, u32[]{:S(2)}, u32[]{:S(2)}) collective-permute-start(f32[3,8]{1,0:T(4,128)S(1)} %pad_maximum_fusion), channel_id=1, source_target_pairs={{0,1},{1,0},{2,3},{3,2},{4,5},{5,4},{6,7},{7,6},{8,9},{9,8},{10,11... | collective-permute-start | bytes 296 | tf_op jit(solution)/shard_map/ppermute | solution.py:64
  96.2 4.5 %collective-permute-start.17 = (f32[3,8]{1,0:T(4,128)S(1)}, f32[3,8]{1,0:T(4,128)S(1)}, u32[]{:S(2)}, u32[]{:S(2)}) collective-permute-start(f32[3,8]{1,0:T(4,128)S(1)} %pad_maximum_fusion.1), channel_id=1, source_target_pairs={{0,2},{1,3},{2,0},{3,1},{4,6},{5,7},{6,4},{7,5},{8,10},{9,11},{10,... | collective-permute-start | bytes 296 | tf_op jit(solution)/shard_map/ppermute | solution.py:64
  101.3 3.6 %collective-permute-start.18 = (f32[3,8]{1,0:T(4,128)S(1)}, f32[3,8]{1,0:T(4,128)S(1)}, u32[]{:S(2)}, u32[]{:S(2)}) collective-permute-start(f32[3,8]{1,0:T(4,128)S(1)} %pad_maximum_fusion.2), channel_id=1, source_target_pairs={{0,4},{4,0},{8,12},{12,8},{16,20},{20,16},{24,28},{28,24},{1,5},{5... | collective-permute-start | bytes 296 | tf_op jit(solution)/shard_map/ppermute | solution.py:64
  105.5 4.0 %collective-permute-start.19 = (f32[3,8]{1,0:T(4,128)}, f32[3,8]{1,0:T(4,128)}, u32[]{:S(2)}, u32[]{:S(2)}) collective-permute-start(f32[3,8]{1,0:T(4,128)} %pad_maximum_fusion.3), channel_id=1, source_target_pairs={{0,8},{4,12},{8,0},{12,4},{16,24},{20,28},{24,16},{28,20},{1,9},{5... | collective-permute-start | bytes 296 | tf_op jit(solution)/shard_map/ppermute | solution.py:64
  110.3 4.5 %collective-permute-start.20 = (f32[3,8]{1,0:T(4,128)S(1)}, f32[3,8]{1,0:T(4,128)S(1)}, u32[]{:S(2)}, u32[]{:S(2)}) collective-permute-start(f32[3,8]{1,0:T(4,128)S(1)} %pad_maximum_fusion.4), channel_id=1, source_target_pairs={{0,16},{4,20},{8,24},{12,28},{16,0},{20,4},{24,8},{28,12},{1,17},{... | collective-permute-start | bytes 296 | tf_op jit(solution)/shard_map/ppermute | solution.py:64
  (24 other events, 183.5 us)

commit v9 on v8

--- a/solution.py
+++ b/solution.py
@@ -215,7 +215,7 @@
         new_lo = jnp.broadcast_to(new_pos[None, None, :], (req_local, 1, new_pos.shape[0]))
         pieces.append(("lo", rows, new_lo))
     head_count = model_cols // head_dim
-    stacked = 5 if head_count % 5 == 0 else 1
+    stacked = head_count
     mixed_out = attend(queries, query_pos, pieces, head_dim, stacked=stacked)
 
     cache_masks = [m for _, masks in cache_pieces for m in masks]

time: 117 us -> 117 us (level)
  no operation moved by 1% of the time
where the time goes in v9:
time: 117 us
  starting transfers between devices  28.4 us (24%)
  waiting for transfers between devices  24.3 us (21%)
  matrix products  17.5 us (15%)
  other arithmetic  16.6 us (14%)
  Pallas kernels  16.6 us (14%)
  local copies, waits for them, and re-layouts  8.29 us (7%)
  between operations  4.84 us (4%)
    dot_general x1, matrix products, on_device(): lax.dot_general(normed, head, (((1,), (1,)), ((), ())), preferred_element...  17.3 us
    pallas_call x1, Pallas kernels, attend(): pl.pallas_call(kernel, grid=(req_local, head_count // stacked), in_specs=...  16.6 us
    ppermute x8, starting transfers between devices, butterfly_gather(): other = lax.ppermute(x, axis, xor_pairs(count, bit))  14.8 us
    ppermute x8, waiting for transfers between devices, butterfly_gather(): other = lax.ppermute(x, axis, xor_pairs(count, bit))  10.6 us
    ppermute x2, waiting for transfers between devices, exchange_pieces(): other = lax.ppermute(held, axis, xor_pairs(count, bit))  9.35 us
    ppermute x5, starting transfers between devices, butterfly_stats(): other = lax.ppermute(packed, axis, xor_pairs(count, bit))  7.7 us
    ppermute x2, starting transfers between devices, exchange_pieces(): other = lax.ppermute(held, axis, xor_pairs(count, bit))  3.08 us
    select_n x1, other arithmetic, on_device(): from_cache = jnp.take_along_axis(cache_keys, cache_row[:, :, None], axis=1)  2.68 us
  transfers between devices with their start and end apart: 21, of which 16 were waited for; matrix products, arithmetic and copies ran while one was open for 15% of the time, Pallas kernels for 0%

profile of v9, /device:TPU:0, one launch (start us, length us, event | category | flops | bytes accessed | tf_op | source)
XLA Modules:
  0.0 116.5 jit_solution(11319609630620483291)
XLA Ops:
  0.6 3.0 %collective-permute-start.1 = (bf16[1,512,512]{2,1,0:T(8,128)(2,1)}, bf16[1,512,512]{2,1,0:T(8,128)(2,1)S(1)}, u32[]{:S(2)}, u32[]{:S(2)}) collective-permute-start(bf16[1,512,512]{2,1,0:T(8,128)(2,1)} %refs_10_.1), channel_id=1, source_target_pairs={{0,2},{1,3},{2,0},{3,1},{4,6},{5,7},{6,4},{7,5},{8,10},{9,11},{10,... | collective-permute-start | bytes 1572872 | tf_op jit(solution)/shard_map/ppermute | solution.py:81
  8.8 7.8 %collective-permute-done.1.refs_15_.refs_16_ = bf16[1,512,512]{2,1,0:T(8,128)(2,1)S(1)} collective-permute-done((bf16[1,512,512]{2,1,0:T(8,128)(2,1)}, bf16[1,512,512]{2,1,0:T(8,128)(2,1)S(1)}, u32[]{:S(2)}, u32[]{:S(2)}) %collective-permute-start.1) | collective-permute-done | bytes 524320 | tf_op jit(solution)/shard_map/ppermute | solution.py:81
  18.4 1.6 %collective-permute-done.4.refs_23_.refs_24_ = bf16[1,192,512]{2,1,0:T(8,128)(2,1)S(1)} collective-permute-done((bf16[1,192,512]{2,1,0:T(8,128)(2,1)}, bf16[1,192,512]{2,1,0:T(8,128)(2,1)S(1)}, u32[]{:S(2)}, u32[]{:S(2)}) %collective-permute-start.4) | collective-permute-done | bytes 196640 | tf_op jit(solution)/shard_map/ppermute | solution.py:81
  22.5 16.6 %shard_map.230 = bf16[1,192,2560]{2,1,0:T(8,128)(2,1)} custom-call(s32[192,1]{1,0:T(8,128)} %iota_add_fusion.qpos_ref, s32[1,1,512]{2,1,0:T(1,128)} %get-tuple-element.84.refs_0_, s32[1,1,512]{2,1,0:T(1,128)} %get-tuple-element.83.refs_1_, s32[1,1,512]{2,1,0:T(1,128)} %get-tuple-element.82.refs_2_, s32[1,1,512]{2,1,0:T(1,128)} %get-tuple-element.81.refs_3_, ...), custom_call_target="tpu_custom_call" | custom-call | tf_op jit(solution)/shard_map/pallas_call | solution.py:168
  42.0 1.8 %collective-permute-start.7 = (bf16[1,2560]{1,0:T(2,128)(2,1)S(1)}, bf16[1,2560]{1,0:T(2,128)(2,1)S(1)}, u32[]{:S(2)}, u32[]{:S(2)}) collective-permute-start(bf16[1,2560]{1,0:T(2,128)(2,1)S(1)} %fusion.47), channel_id=1, source_target_pairs={{0,2},{1,3},{2,0},{3,1},{4,6},{5,7},{6,4},{7,5},{8,10},{9,11},{10,... | collective-permute-start | bytes 15368 | tf_op jit(solution)/shard_map/ppermute | solution.py:25
  45.7 1.8 %collective-permute-start.8 = (bf16[1,2560]{1,0:T(2,128)(2,1)S(1)}, bf16[1,2560]{1,0:T(2,128)(2,1)S(1)}, u32[]{:S(2)}, u32[]{:S(2)}) collective-permute-start(bf16[1,2560]{1,0:T(2,128)(2,1)S(1)} %add.615), channel_id=1, source_target_pairs={{0,4},{4,0},{8,12},{12,8},{16,20},{20,16},{24,28},{28,24},{1,5},{5... | collective-permute-start | bytes 15368 | tf_op jit(solution)/shard_map/ppermute | solution.py:37
  47.6 1.9 %collective-permute-done.8 = bf16[1,2560]{1,0:T(2,128)(2,1)S(1)} collective-permute-done((bf16[1,2560]{1,0:T(2,128)(2,1)S(1)}, bf16[1,2560]{1,0:T(2,128)(2,1)S(1)}, u32[]{:S(2)}, u32[]{:S(2)}) %collective-permute-start.8) | collective-permute-done | bytes 5152 | tf_op jit(solution)/shard_map/ppermute | solution.py:37
  49.5 1.9 %collective-permute-start.9 = (bf16[2,2560]{1,0:T(2,128)(2,1)S(1)}, bf16[2,2560]{1,0:T(2,128)(2,1)S(1)}, u32[]{:S(2)}, u32[]{:S(2)}) collective-permute-start(bf16[2,2560]{1,0:T(2,128)(2,1)S(1)} %broadcast_select_fusion.1), channel_id=1, source_target_pairs={{0,8},{4,12},{8,0},{12,4},{16,24},{20,28},{24,16},{28,20},{1,9},{5... | collective-permute-start | bytes 30728 | tf_op jit(solution)/shard_map/ppermute | solution.py:37
  53.3 2.9 %collective-permute-start.10 = (bf16[4,2560]{1,0:T(4,128)(2,1)S(1)}, bf16[4,2560]{1,0:T(4,128)(2,1)S(1)}, u32[]{:S(2)}, u32[]{:S(2)}) collective-permute-start(bf16[4,2560]{1,0:T(4,128)(2,1)S(1)} %maximum_select_fusion.3), channel_id=1, source_target_pairs={{0,16},{4,20},{8,24},{12,28},{16,0},{20,4},{24,8},{28,12},{1,17},{... | collective-permute-start | bytes 61448 | tf_op jit(solution)/shard_map/ppermute | solution.py:37
  58.3 2.7 %compare_select_fusion.3 = (s32[512,1]{0,1:T(1,128)S(1)}, s32[1,512]{1,0:T(1,128)S(1)}, s32[512,1]{0,1:T(1,128)S(1)}) fusion(s32[]{:T(128)} %axis_index.14, s32[]{:T(128)} %bitcast.19, s32[]{:T(128)} %bitcast.18, s32[]{:T(128)} %bitcast.17, s32[]{:T(128)} %bitcast.16, s32[]{:T(128)} %bitcast.15), kind=kLoop, calls=%fused_computation.36 | loop fusion | flops 55296 | bytes 6168 | tf_op jit(solution)/shard_map/jit(take_along_axis)/select_n | solution.py:239
  61.1 1.7 %collective-permute-start.12 = (bf16[8,160]{1,0:T(8,128)(2,1)S(1)}, bf16[8,160]{1,0:T(8,128)(2,1)S(1)}, u32[]{:S(2)}, u32[]{:S(2)}) collective-permute-start(bf16[8,160]{1,0:T(8,128)(2,1)S(1)} %maximum_select_fusion.8), channel_id=1, source_target_pairs={{0,2},{1,3},{2,0},{3,1},{4,6},{5,7},{6,4},{7,5},{8,10},{9,11},{10,... | collective-permute-start | bytes 7688 | tf_op jit(solution)/shard_map/ppermute | solution.py:37
  64.8 1.8 %collective-permute-start.13 = (bf16[8,320]{1,0:T(8,128)(2,1)S(1)}, bf16[8,320]{1,0:T(8,128)(2,1)S(1)}, u32[]{:S(2)}, u32[]{:S(2)}) collective-permute-start(bf16[8,320]{1,0:T(8,128)(2,1)S(1)} %maximum_select_fusion.7), channel_id=1, source_target_pairs={{0,4},{4,0},{8,12},{12,8},{16,20},{20,16},{24,28},{28,24},{1,5},{5... | collective-permute-start | bytes 15368 | tf_op jit(solution)/shard_map/ppermute | solution.py:37
  66.6 1.9 %collective-permute-done.13 = bf16[8,320]{1,0:T(8,128)(2,1)S(1)} collective-permute-done((bf16[8,320]{1,0:T(8,128)(2,1)S(1)}, bf16[8,320]{1,0:T(8,128)(2,1)S(1)}, u32[]{:S(2)}, u32[]{:S(2)}) %collective-permute-start.13) | collective-permute-done | bytes 5152 | tf_op jit(solution)/shard_map/ppermute | solution.py:37
  68.5 1.8 %collective-permute-start.14 = (bf16[8,640]{1,0:T(8,128)(2,1)S(1)}, bf16[8,640]{1,0:T(8,128)(2,1)S(1)}, u32[]{:S(2)}, u32[]{:S(2)}) collective-permute-start(bf16[8,640]{1,0:T(8,128)(2,1)S(1)} %maximum_select_fusion.5), channel_id=1, source_target_pairs={{0,8},{4,12},{8,0},{12,4},{16,24},{20,28},{24,16},{28,20},{1,9},{5... | collective-permute-start | bytes 30728 | tf_op jit(solution)/shard_map/ppermute | solution.py:37
  70.3 1.8 %collective-permute-done.14 = bf16[8,640]{1,0:T(8,128)(2,1)S(1)} collective-permute-done((bf16[8,640]{1,0:T(8,128)(2,1)S(1)}, bf16[8,640]{1,0:T(8,128)(2,1)S(1)}, u32[]{:S(2)}, u32[]{:S(2)}) %collective-permute-start.14) | collective-permute-done | bytes 10272 | tf_op jit(solution)/shard_map/ppermute | solution.py:37
  72.2 2.8 %collective-permute-start.15 = (bf16[8,1280]{1,0:T(8,128)(2,1)S(1)}, bf16[8,1280]{1,0:T(8,128)(2,1)S(1)}, u32[]{:S(2)}, u32[]{:S(2)}) collective-permute-start(bf16[8,1280]{1,0:T(8,128)(2,1)S(1)} %maximum_select_fusion.4), channel_id=1, source_target_pairs={{0,16},{4,20},{8,24},{12,28},{16,0},{20,4},{24,8},{28,12},{1,17},{... | collective-permute-start | bytes 61448 | tf_op jit(solution)/shard_map/ppermute | solution.py:37
  77.0 17.3 %fusion.44 = (f32[8]{0:T(128)S(1)}, f32[8,8000]{1,0:T(8,128)S(1)}) fusion(bf16[8000,2560]{1,0:T(8,128)(2,1)} %param.30, f32[2560]{0:T(1024)S(1)} %convert_element_type.18, f32[8]{0:T(128)S(1)} %add_rsqrt_fusion, bf16[8,1280]{1,0:T(8,128)(2,1)S(1)} %maximum_select_fusion.4, bf16[8,1280]{1,0:T(8,128)(2,1)S(1)} %collective-permute-done.15, pred[]{:T(512)S(6)} %eq.61), kind=kOutput, calls=%fused_computation.149 | convolution fusion | flops 328010240 | bytes 41267264 | tf_op jit(solution)/shard_map/dot_general | solution.py:260
  96.5 1.8 %collective-permute-start.17 = (f32[3,8]{1,0:T(4,128)S(1)}, f32[3,8]{1,0:T(4,128)S(1)}, u32[]{:S(2)}, u32[]{:S(2)}) collective-permute-start(f32[3,8]{1,0:T(4,128)S(1)} %pad_maximum_fusion.1), channel_id=1, source_target_pairs={{0,2},{1,3},{2,0},{3,1},{4,6},{5,7},{6,4},{7,5},{8,10},{9,11},{10,... | collective-permute-start | bytes 296 | tf_op jit(solution)/shard_map/ppermute | solution.py:64
  98.3 2.7 %gather_fusion.1 = bf16[512,512]{1,0:T(8,128)(2,1)} fusion(bf16[768,512]{1,0:T(8,128)(2,1)S(1)} %maximum_bitcast_fusion.1, s32[1024]{0:T(1024)S(1)} %pad_clamp_fusion), kind=kCustom, calls=%fused_computation.1 | custom fusion | bytes 1050624 | tf_op jit(solution)/shard_map/jit(take_along_axis)/gather | solution.py:240
  101.6 1.5 %collective-permute-start.18 = (f32[3,8]{1,0:T(4,128)S(1)}, f32[3,8]{1,0:T(4,128)S(1)}, u32[]{:S(2)}, u32[]{:S(2)}) collective-permute-start(f32[3,8]{1,0:T(4,128)S(1)} %pad_maximum_fusion.2), channel_id=1, source_target_pairs={{0,4},{4,0},{8,12},{12,8},{16,20},{20,16},{24,28},{28,24},{1,5},{5... | collective-permute-start | bytes 296 | tf_op jit(solution)/shard_map/ppermute | solution.py:64
  105.8 1.6 %collective-permute-start.19 = (f32[3,8]{1,0:T(4,128)}, f32[3,8]{1,0:T(4,128)}, u32[]{:S(2)}, u32[]{:S(2)}) collective-permute-start(f32[3,8]{1,0:T(4,128)} %pad_maximum_fusion.3), channel_id=1, source_target_pairs={{0,8},{4,12},{8,0},{12,4},{16,24},{20,28},{24,16},{28,20},{1,9},{5... | collective-permute-start | bytes 296 | tf_op jit(solution)/shard_map/ppermute | solution.py:64
  107.5 2.1 %gather_fusion = bf16[512,512]{1,0:T(8,128)(2,1)S(1)} fusion(bf16[2048,512]{1,0:T(8,128)(2,1)S(1)} %maximum_bitcast_fusion, s32[1024]{0:T(1024)} %pad_clamp_fusion.1), kind=kCustom, calls=%fused_computation | custom fusion | bytes 1050624 | tf_op jit(solution)/shard_map/jit(take_along_axis)/gather | solution.py:239
  110.6 2.7 %collective-permute-start.20 = (f32[3,8]{1,0:T(4,128)S(1)}, f32[3,8]{1,0:T(4,128)S(1)}, u32[]{:S(2)}, u32[]{:S(2)}) collective-permute-start(f32[3,8]{1,0:T(4,128)S(1)} %pad_maximum_fusion.4), channel_id=1, source_target_pairs={{0,16},{4,20},{8,24},{12,28},{16,0},{20,4},{24,8},{28,12},{1,17},{... | collective-permute-start | bytes 296 | tf_op jit(solution)/shard_map/ppermute | solution.py:64
  113.3 1.8 %fusion.1 = bf16[1,512,512]{2,1,0:T(8,128)(2,1)} fusion(bf16[512,512]{1,0:T(8,128)(2,1)S(1)} %copy-done.6, bf16[512,512]{1,0:T(8,128)(2,1)S(1)} %gather_fusion, pred[512]{0:T(512)(128)(4,1)} %get-tuple-element.90, pred[512]{0:T(512)(128)(4,1)} %compare_and_fusion.1, pred[512]{0:T(512)(128)(4,1)} %get-tuple-element.89), kind=kLoop, calls=%fused_computation.7 | loop fusion | flops 786432 | bytes 1574400 | tf_op jit(solution)/shard_map/jit(_where)/select_n | solution.py:241
  (118 shorter events, 26.5 us)
Async XLA Ops:
  0.6 57.4 %copy-start = (bf16[2560,80]{0,1:T(8,128)(2,1)S(1)}, bf16[2560,80]{0,1:T(8,128)(2,1)}, u32[]{:S(2)}) copy-start(bf16[2560,80]{0,1:T(8,128)(2,1)} %param.27) | copy-start | bytes 1228804
  0.6 16.0 %collective-permute-start.1 = (bf16[1,512,512]{2,1,0:T(8,128)(2,1)}, bf16[1,512,512]{2,1,0:T(8,128)(2,1)S(1)}, u32[]{:S(2)}, u32[]{:S(2)}) collective-permute-start(bf16[1,512,512]{2,1,0:T(8,128)(2,1)} %refs_10_.1), channel_id=1, source_target_pairs={{0,2},{1,3},{2,0},{3,1},{4,6},{5,7},{6,4},{7,5},{8,10},{9,11},{10,... | collective-permute-start | bytes 1572872 | tf_op jit(solution)/shard_map/ppermute | solution.py:81
  3.7 17.8 %collective-permute-start = (bf16[1,512,512]{2,1,0:T(8,128)(2,1)}, bf16[1,512,512]{2,1,0:T(8,128)(2,1)S(1)}, u32[]{:S(2)}, u32[]{:S(2)}) collective-permute-start(bf16[1,512,512]{2,1,0:T(8,128)(2,1)} %refs_10_.1), channel_id=1, source_target_pairs={{0,1},{1,0},{2,3},{3,2},{4,5},{5,4},{6,7},{7,6},{8,9},{9,8},{10,11... | collective-permute-start | bytes 1572872 | tf_op jit(solution)/shard_map/ppermute | solution.py:77
  3.7 17.6 %collective-permute-start.3 = (bf16[1,192,512]{2,1,0:T(8,128)(2,1)}, bf16[1,192,512]{2,1,0:T(8,128)(2,1)S(1)}, u32[]{:S(2)}, u32[]{:S(2)}) collective-permute-start(bf16[1,192,512]{2,1,0:T(8,128)(2,1)} %refs_18_.1), channel_id=1, source_target_pairs={{0,1},{1,0},{2,3},{3,2},{4,5},{5,4},{6,7},{7,6},{8,9},{9,8},{10,11... | collective-permute-start | bytes 589832 | tf_op jit(solution)/shard_map/ppermute | solution.py:77
  4.2 15.8 %collective-permute-start.4 = (bf16[1,192,512]{2,1,0:T(8,128)(2,1)}, bf16[1,192,512]{2,1,0:T(8,128)(2,1)S(1)}, u32[]{:S(2)}, u32[]{:S(2)}) collective-permute-start(bf16[1,192,512]{2,1,0:T(8,128)(2,1)} %refs_18_.1), channel_id=1, source_target_pairs={{0,2},{1,3},{2,0},{3,1},{4,6},{5,7},{6,4},{7,5},{8,10},{9,11},{10,... | collective-permute-start | bytes 589832 | tf_op jit(solution)/shard_map/ppermute | solution.py:81
  16.6 4.8 %collective-permute-start.2 = (bf16[1,512,512]{2,1,0:T(8,128)(2,1)S(1)}, bf16[1,512,512]{2,1,0:T(8,128)(2,1)S(1)}, u32[]{:S(2)}, u32[]{:S(2)}) collective-permute-start(bf16[1,512,512]{2,1,0:T(8,128)(2,1)S(1)} %collective-permute-done.1.refs_15_.refs_16_), channel_id=1, source_target_pairs={{0,1},{1,0},{2,3},{3,2},{4,5},{5,4},{6,7},{7,6},{8,9},{9,8},{10,11... | collective-permute-start | bytes 1572872 | tf_op jit(solution)/shard_map/ppermute | solution.py:91
  20.0 1.4 %collective-permute-start.5 = (bf16[1,192,512]{2,1,0:T(8,128)(2,1)S(1)}, bf16[1,192,512]{2,1,0:T(8,128)(2,1)S(1)}, u32[]{:S(2)}, u32[]{:S(2)}) collective-permute-start(bf16[1,192,512]{2,1,0:T(8,128)(2,1)S(1)} %collective-permute-done.4.refs_23_.refs_24_), channel_id=1, source_target_pairs={{0,1},{1,0},{2,3},{3,2},{4,5},{5,4},{6,7},{7,6},{8,9},{9,8},{10,11... | collective-permute-start | bytes 589832 | tf_op jit(solution)/shard_map/ppermute | solution.py:91
  22.5 44.0 %copy-start.26 = (s32[8]{0:T(128)S(1)}, s32[8]{0:T(128)}, u32[]{:S(2)}) copy-start(s32[8]{0:T(128)} %param.31) | copy-start | bytes 100
  22.5 53.1 %copy-start.18 = (bf16[2560]{0:T(1024)(128)(2,1)S(1)}, bf16[2560]{0:T(1024)(128)(2,1)}, u32[]{:S(2)}) copy-start(bf16[2560]{0:T(1024)(128)(2,1)} %param.29) | copy-start | bytes 15364
  39.9 1.3 %collective-permute-start.6 = (bf16[1,2560]{1,0:T(2,128)(2,1)S(1)}, bf16[1,2560]{1,0:T(2,128)(2,1)S(1)}, u32[]{:S(2)}, u32[]{:S(2)}) collective-permute-start(bf16[1,2560]{1,0:T(2,128)(2,1)S(1)} %fusion.15), channel_id=1, source_target_pairs={{0,1},{1,0},{2,3},{3,2},{4,5},{5,4},{6,7},{7,6},{8,9},{9,8},{10,11... | collective-permute-start | bytes 15368 | tf_op jit(solution)/shard_map/ppermute | solution.py:25
  42.0 3.7 %collective-permute-start.7 = (bf16[1,2560]{1,0:T(2,128)(2,1)S(1)}, bf16[1,2560]{1,0:T(2,128)(2,1)S(1)}, u32[]{:S(2)}, u32[]{:S(2)}) collective-permute-start(bf16[1,2560]{1,0:T(2,128)(2,1)S(1)} %fusion.47), channel_id=1, source_target_pairs={{0,2},{1,3},{2,0},{3,1},{4,6},{5,7},{6,4},{7,5},{8,10},{9,11},{10,... | collective-permute-start | bytes 15368 | tf_op jit(solution)/shard_map/ppermute | solution.py:25
  45.7 3.7 %collective-permute-start.8 = (bf16[1,2560]{1,0:T(2,128)(2,1)S(1)}, bf16[1,2560]{1,0:T(2,128)(2,1)S(1)}, u32[]{:S(2)}, u32[]{:S(2)}) collective-permute-start(bf16[1,2560]{1,0:T(2,128)(2,1)S(1)} %add.615), channel_id=1, source_target_pairs={{0,4},{4,0},{8,12},{12,8},{16,20},{20,16},{24,28},{28,24},{1,5},{5... | collective-permute-start | bytes 15368 | tf_op jit(solution)/shard_map/ppermute | solution.py:37
  49.5 3.7 %collective-permute-start.9 = (bf16[2,2560]{1,0:T(2,128)(2,1)S(1)}, bf16[2,2560]{1,0:T(2,128)(2,1)S(1)}, u32[]{:S(2)}, u32[]{:S(2)}) collective-permute-start(bf16[2,2560]{1,0:T(2,128)(2,1)S(1)} %broadcast_select_fusion.1), channel_id=1, source_target_pairs={{0,8},{4,12},{8,0},{12,4},{16,24},{20,28},{24,16},{28,20},{1,9},{5... | collective-permute-start | bytes 30728 | tf_op jit(solution)/shard_map/ppermute | solution.py:37
  53.3 4.7 %collective-permute-start.10 = (bf16[4,2560]{1,0:T(4,128)(2,1)S(1)}, bf16[4,2560]{1,0:T(4,128)(2,1)S(1)}, u32[]{:S(2)}, u32[]{:S(2)}) collective-permute-start(bf16[4,2560]{1,0:T(4,128)(2,1)S(1)} %maximum_select_fusion.3), channel_id=1, source_target_pairs={{0,16},{4,20},{8,24},{12,28},{16,0},{20,4},{24,8},{28,12},{1,17},{... | collective-permute-start | bytes 61448 | tf_op jit(solution)/shard_map/ppermute | solution.py:37
  58.3 2.7 %collective-permute-start.11 = (bf16[8,80]{1,0:T(8,128)(2,1)S(1)}, bf16[8,80]{1,0:T(8,128)(2,1)S(1)}, u32[]{:S(2)}, u32[]{:S(2)}) collective-permute-start(bf16[8,80]{1,0:T(8,128)(2,1)S(1)} %fusion), channel_id=1, source_target_pairs={{0,1},{1,0},{2,3},{3,2},{4,5},{5,4},{6,7},{7,6},{8,9},{9,8},{10,11... | collective-permute-start | bytes 3848 | tf_op jit(solution)/shard_map/ppermute | solution.py:37
  61.1 3.6 %collective-permute-start.12 = (bf16[8,160]{1,0:T(8,128)(2,1)S(1)}, bf16[8,160]{1,0:T(8,128)(2,1)S(1)}, u32[]{:S(2)}, u32[]{:S(2)}) collective-permute-start(bf16[8,160]{1,0:T(8,128)(2,1)S(1)} %maximum_select_fusion.8), channel_id=1, source_target_pairs={{0,2},{1,3},{2,0},{3,1},{4,6},{5,7},{6,4},{7,5},{8,10},{9,11},{10,... | collective-permute-start | bytes 7688 | tf_op jit(solution)/shard_map/ppermute | solution.py:37
  64.8 3.6 %collective-permute-start.13 = (bf16[8,320]{1,0:T(8,128)(2,1)S(1)}, bf16[8,320]{1,0:T(8,128)(2,1)S(1)}, u32[]{:S(2)}, u32[]{:S(2)}) collective-permute-start(bf16[8,320]{1,0:T(8,128)(2,1)S(1)} %maximum_select_fusion.7), channel_id=1, source_target_pairs={{0,4},{4,0},{8,12},{12,8},{16,20},{20,16},{24,28},{28,24},{1,5},{5... | collective-permute-start | bytes 15368 | tf_op jit(solution)/shard_map/ppermute | solution.py:37
  68.5 3.7 %collective-permute-start.14 = (bf16[8,640]{1,0:T(8,128)(2,1)S(1)}, bf16[8,640]{1,0:T(8,128)(2,1)S(1)}, u32[]{:S(2)}, u32[]{:S(2)}) collective-permute-start(bf16[8,640]{1,0:T(8,128)(2,1)S(1)} %maximum_select_fusion.5), channel_id=1, source_target_pairs={{0,8},{4,12},{8,0},{12,4},{16,24},{20,28},{24,16},{28,20},{1,9},{5... | collective-permute-start | bytes 30728 | tf_op jit(solution)/shard_map/ppermute | solution.py:37
  72.2 4.7 %collective-permute-start.15 = (bf16[8,1280]{1,0:T(8,128)(2,1)S(1)}, bf16[8,1280]{1,0:T(8,128)(2,1)S(1)}, u32[]{:S(2)}, u32[]{:S(2)}) collective-permute-start(bf16[8,1280]{1,0:T(8,128)(2,1)S(1)} %maximum_select_fusion.4), channel_id=1, source_target_pairs={{0,16},{4,20},{8,24},{12,28},{16,0},{20,4},{24,8},{28,12},{1,17},{... | collective-permute-start | bytes 61448 | tf_op jit(solution)/shard_map/ppermute | solution.py:37
  94.7 1.2 %collective-permute-start.16 = (f32[3,8]{1,0:T(4,128)S(1)}, f32[3,8]{1,0:T(4,128)S(1)}, u32[]{:S(2)}, u32[]{:S(2)}) collective-permute-start(f32[3,8]{1,0:T(4,128)S(1)} %pad_maximum_fusion), channel_id=1, source_target_pairs={{0,1},{1,0},{2,3},{3,2},{4,5},{5,4},{6,7},{7,6},{8,9},{9,8},{10,11... | collective-permute-start | bytes 296 | tf_op jit(solution)/shard_map/ppermute | solution.py:64
  96.5 4.5 %collective-permute-start.17 = (f32[3,8]{1,0:T(4,128)S(1)}, f32[3,8]{1,0:T(4,128)S(1)}, u32[]{:S(2)}, u32[]{:S(2)}) collective-permute-start(f32[3,8]{1,0:T(4,128)S(1)} %pad_maximum_fusion.1), channel_id=1, source_target_pairs={{0,2},{1,3},{2,0},{3,1},{4,6},{5,7},{6,4},{7,5},{8,10},{9,11},{10,... | collective-permute-start | bytes 296 | tf_op jit(solution)/shard_map/ppermute | solution.py:64
  101.6 3.6 %collective-permute-start.18 = (f32[3,8]{1,0:T(4,128)S(1)}, f32[3,8]{1,0:T(4,128)S(1)}, u32[]{:S(2)}, u32[]{:S(2)}) collective-permute-start(f32[3,8]{1,0:T(4,128)S(1)} %pad_maximum_fusion.2), channel_id=1, source_target_pairs={{0,4},{4,0},{8,12},{12,8},{16,20},{20,16},{24,28},{28,24},{1,5},{5... | collective-permute-start | bytes 296 | tf_op jit(solution)/shard_map/ppermute | solution.py:64
  105.8 4.0 %collective-permute-start.19 = (f32[3,8]{1,0:T(4,128)}, f32[3,8]{1,0:T(4,128)}, u32[]{:S(2)}, u32[]{:S(2)}) collective-permute-start(f32[3,8]{1,0:T(4,128)} %pad_maximum_fusion.3), channel_id=1, source_target_pairs={{0,8},{4,12},{8,0},{12,4},{16,24},{20,28},{24,16},{28,20},{1,9},{5... | collective-permute-start | bytes 296 | tf_op jit(solution)/shard_map/ppermute | solution.py:64
  110.6 4.5 %collective-permute-start.20 = (f32[3,8]{1,0:T(4,128)S(1)}, f32[3,8]{1,0:T(4,128)S(1)}, u32[]{:S(2)}, u32[]{:S(2)}) collective-permute-start(f32[3,8]{1,0:T(4,128)S(1)} %pad_maximum_fusion.4), channel_id=1, source_target_pairs={{0,16},{4,20},{8,24},{12,28},{16,0},{20,4},{24,8},{28,12},{1,17},{... | collective-permute-start | bytes 296 | tf_op jit(solution)/shard_map/ppermute | solution.py:64
  (24 other events, 184.0 us)

commit v10 on v8

--- a/solution.py
+++ b/solution.py
@@ -245,6 +245,7 @@
     holder = my_index == group_pos - 1
     last_local = jnp.where(holder, last_local, jnp.zeros_like(last_local))
     last_mixed = butterfly_gather(butterfly_sum(last_local, "gy"), "gx", 0)
+    last_mixed, fresh_block = lax.optimization_barrier((last_mixed, fresh_block))
     last_hidden = (
         last_residual.astype(jnp.float32)
         + jnp.dot(last_mixed, w_out, preferred_element_type=jnp.float32)

time: 117 us -> 116 us (level)
  starting transfers between devices: 28.4 us -> 21.4 us
  waiting for transfers between devices: 24.3 us -> 30.3 us
    ppermute x5, waiting for transfers between devices: 2.12 us -> 11.7 us  [butterfly_stats(): other = lax.ppermute(packed, axis, xor_pairs(count, bit))]
    ppermute x2, waiting for transfers between devices: 9.35 us -> 2.94 us  [exchange_pieces(): other = lax.ppermute(held, axis, xor_pairs(count, bit))]
    ppermute x8, starting transfers between devices: 14.8 us -> 10.8 us  [butterfly_gather(): other = lax.ppermute(x, axis, xor_pairs(count, bit))]
    ppermute x5, starting transfers between devices: 7.7 us -> 5.05 us  [butterfly_stats(): other = lax.ppermute(packed, axis, xor_pairs(count, bit))]
    ppermute x8, waiting for transfers between devices: 10.6 us -> 12.4 us  [butterfly_gather(): other = lax.ppermute(x, axis, xor_pairs(count, bit))]
    select_n x6 -> x7, other arithmetic: 0.33 us -> 1.75 us  [butterfly_gather(): jnp.where(low, jnp.concatenate([x, other], dim), jnp.concatenate([other,...]
    unnamed x54 -> x26, local copies, waits for them, and re-layouts: 2.23 us -> 1.04 us
  transfers between devices with their start and end apart: 21 -> 21, of which waited for: 16 -> 16; matrix products, arithmetic and copies ran while one was open for 15% -> 17% of each run, Pallas kernels for 0% -> 0%
where the time goes in v10:
time: 116 us
  waiting for transfers between devices  30.3 us (26%)
  starting transfers between devices  21.4 us (18%)
  matrix products  18.1 us (16%)
  other arithmetic  16.9 us (15%)
  Pallas kernels  16.3 us (14%)
  local copies, waits for them, and re-layouts  7.95 us (7%)
  between operations  4.63 us (4%)
    dot_general x1, matrix products, on_device(): lax.dot_general(normed, head, (((1,), (1,)), ((), ())), preferred_element...  17.2 us
    pallas_call x1, Pallas kernels, attend(): pl.pallas_call(kernel, grid=(req_local, head_count // stacked), in_specs=...  16.3 us
    ppermute x8, waiting for transfers between devices, butterfly_gather(): other = lax.ppermute(x, axis, xor_pairs(count, bit))  12.4 us
    ppermute x5, waiting for transfers between devices, butterfly_stats(): other = lax.ppermute(packed, axis, xor_pairs(count, bit))  11.7 us
    ppermute x8, starting transfers between devices, butterfly_gather(): other = lax.ppermute(x, axis, xor_pairs(count, bit))  10.8 us
    ppermute x5, starting transfers between devices, butterfly_stats(): other = lax.ppermute(packed, axis, xor_pairs(count, bit))  5.05 us
    ppermute x2, starting transfers between devices, exchange_pieces(): other = lax.ppermute(held, axis, xor_pairs(count, bit))  3.16 us
    ppermute x2, waiting for transfers between devices, exchange_pieces(): other = lax.ppermute(held, axis, xor_pairs(count, bit))  2.94 us
  transfers between devices with their start and end apart: 21, of which 16 were waited for; matrix products, arithmetic and copies ran while one was open for 17% of the time, Pallas kernels for 0%

profile of v10, /device:TPU:0, one launch (start us, length us, event | category | flops | bytes accessed | tf_op | source)
XLA Modules:
  0.0 115.6 jit_solution(8913113604667098370)
XLA Ops:
  0.6 3.0 %collective-permute-start.1 = (bf16[1,512,512]{2,1,0:T(8,128)(2,1)}, bf16[1,512,512]{2,1,0:T(8,128)(2,1)S(1)}, u32[]{:S(2)}, u32[]{:S(2)}) collective-permute-start(bf16[1,512,512]{2,1,0:T(8,128)(2,1)} %refs_10_.1), channel_id=1, source_target_pairs={{0,2},{1,3},{2,0},{3,1},{4,6},{5,7},{6,4},{7,5},{8,10},{9,11},{10,... | collective-permute-start | bytes 1572872 | tf_op jit(solution)/shard_map/ppermute | solution.py:81
  12.6 2.7 %compare_select_fusion.3 = (s32[512,1]{0,1:T(1,128)S(1)}, s32[1,512]{1,0:T(1,128)S(1)}, s32[512,1]{0,1:T(1,128)S(1)}) fusion(s32[]{:T(128)} %axis_index.14, s32[]{:T(128)} %bitcast.20, s32[]{:T(128)} %bitcast.19, s32[]{:T(128)} %bitcast.18, s32[]{:T(128)} %bitcast.17, s32[]{:T(128)} %bitcast.16), kind=kLoop, calls=%fused_computation.30 | loop fusion | flops 55296 | bytes 6168 | tf_op jit(solution)/shard_map/jit(take_along_axis)/select_n | solution.py:239
  17.8 2.2 %collective-permute-done.4.refs_23_.refs_24_ = bf16[1,192,512]{2,1,0:T(8,128)(2,1)S(1)} collective-permute-done((bf16[1,192,512]{2,1,0:T(8,128)(2,1)}, bf16[1,192,512]{2,1,0:T(8,128)(2,1)S(1)}, u32[]{:S(2)}, u32[]{:S(2)}) %collective-permute-start.4) | collective-permute-done | bytes 196640 | tf_op jit(solution)/shard_map/ppermute | solution.py:81
  22.5 16.3 %shard_map.230 = bf16[1,192,2560]{2,1,0:T(8,128)(2,1)} custom-call(s32[192,1]{1,0:T(8,128)} %iota_add_fusion.qpos_ref, s32[1,1,512]{2,1,0:T(1,128)} %get-tuple-element.88.refs_0_, s32[1,1,512]{2,1,0:T(1,128)} %get-tuple-element.87.refs_1_, s32[1,1,512]{2,1,0:T(1,128)} %get-tuple-element.86.refs_2_, s32[1,1,512]{2,1,0:T(1,128)} %get-tuple-element.85.refs_3_, ...), custom_call_target="tpu_custom_call" | custom-call | tf_op jit(solution)/shard_map/pallas_call | solution.py:168
  41.6 1.8 %collective-permute-start.7 = (bf16[1,2560]{1,0:T(2,128)(2,1)S(1)}, bf16[1,2560]{1,0:T(2,128)(2,1)S(1)}, u32[]{:S(2)}, u32[]{:S(2)}) collective-permute-start(bf16[1,2560]{1,0:T(2,128)(2,1)S(1)} %fusion.41), channel_id=1, source_target_pairs={{0,2},{1,3},{2,0},{3,1},{4,6},{5,7},{6,4},{7,5},{8,10},{9,11},{10,... | collective-permute-start | bytes 15368 | tf_op jit(solution)/shard_map/ppermute | solution.py:25
  43.4 1.9 %collective-permute-done.7 = bf16[1,2560]{1,0:T(2,128)(2,1)S(1)} collective-permute-done((bf16[1,2560]{1,0:T(2,128)(2,1)S(1)}, bf16[1,2560]{1,0:T(2,128)(2,1)S(1)}, u32[]{:S(2)}, u32[]{:S(2)}) %collective-permute-start.7) | collective-permute-done | bytes 5152 | tf_op jit(solution)/shard_map/ppermute | solution.py:25
  45.4 1.8 %collective-permute-start.8 = (bf16[1,2560]{1,0:T(2,128)(2,1)S(1)}, bf16[1,2560]{1,0:T(2,128)(2,1)S(1)}, u32[]{:S(2)}, u32[]{:S(2)}) collective-permute-start(bf16[1,2560]{1,0:T(2,128)(2,1)S(1)} %add.588), channel_id=1, source_target_pairs={{0,4},{4,0},{8,12},{12,8},{16,20},{20,16},{24,28},{28,24},{1,5},{5... | collective-permute-start | bytes 15368 | tf_op jit(solution)/shard_map/ppermute | solution.py:37
  48.4 2.6 %gather_fusion.1 = bf16[512,512]{1,0:T(8,128)(2,1)} fusion(bf16[768,512]{1,0:T(8,128)(2,1)S(1)} %maximum_bitcast_fusion.1, s32[1024]{0:T(1024)S(1)} %pad_clamp_fusion), kind=kCustom, calls=%fused_computation.1 | custom fusion | bytes 1050624 | tf_op jit(solution)/shard_map/jit(take_along_axis)/gather | solution.py:240
  51.7 1.6 %collective-permute-start.9 = (bf16[2,2560]{1,0:T(2,128)(2,1)}, bf16[2,2560]{1,0:T(2,128)(2,1)}, u32[]{:S(2)}, u32[]{:S(2)}) collective-permute-start(bf16[2,2560]{1,0:T(2,128)(2,1)} %broadcast_select_fusion.1), channel_id=1, source_target_pairs={{0,8},{4,12},{8,0},{12,4},{16,24},{20,28},{24,16},{28,20},{1,9},{5... | collective-permute-start | bytes 30728 | tf_op jit(solution)/shard_map/ppermute | solution.py:37
  54.6 2.2 %gather_fusion = bf16[512,512]{1,0:T(8,128)(2,1)S(1)} fusion(bf16[2048,512]{1,0:T(8,128)(2,1)S(1)} %maximum_bitcast_fusion, s32[1024]{0:T(1024)} %pad_clamp_fusion.1), kind=kCustom, calls=%fused_computation | custom fusion | bytes 1050624 | tf_op jit(solution)/shard_map/jit(take_along_axis)/gather | solution.py:239
  57.7 2.7 %collective-permute-start.10 = (bf16[4,2560]{1,0:T(4,128)(2,1)S(1)}, bf16[4,2560]{1,0:T(4,128)(2,1)S(1)}, u32[]{:S(2)}, u32[]{:S(2)}) collective-permute-start(bf16[4,2560]{1,0:T(4,128)(2,1)S(1)} %maximum_select_fusion.2), channel_id=1, source_target_pairs={{0,16},{4,20},{8,24},{12,28},{16,0},{20,4},{24,8},{28,12},{1,17},{... | collective-permute-start | bytes 61448 | tf_op jit(solution)/shard_map/ppermute | solution.py:37
  60.4 1.7 %fusion.1 = bf16[1,512,512]{2,1,0:T(8,128)(2,1)} fusion(bf16[512,512]{1,0:T(8,128)(2,1)S(1)} %copy-done.6, bf16[512,512]{1,0:T(8,128)(2,1)S(1)} %gather_fusion, pred[512]{0:T(512)(128)(4,1)} %get-tuple-element.94, pred[512]{0:T(512)(128)(4,1)} %compare_and_fusion.1, pred[512]{0:T(512)(128)(4,1)} %get-tuple-element.93), kind=kLoop, calls=%fused_computation.7 | loop fusion | flops 786432 | bytes 1574400 | tf_op jit(solution)/shard_map/jit(_where)/select_n | solution.py:241
  66.3 2.1 %collective-permute-done.12 = bf16[8,160]{1,0:T(8,128)(2,1)S(1)} collective-permute-done((bf16[8,160]{1,0:T(8,128)(2,1)S(1)}, bf16[8,160]{1,0:T(8,128)(2,1)S(1)}, u32[]{:S(2)}, u32[]{:S(2)}) %collective-permute-start.12) | collective-permute-done | bytes 2592 | tf_op jit(solution)/shard_map/ppermute | solution.py:37
  68.9 3.2 %collective-permute-done.13 = bf16[8,320]{1,0:T(8,128)(2,1)S(1)} collective-permute-done((bf16[8,320]{1,0:T(8,128)(2,1)S(1)}, bf16[8,320]{1,0:T(8,128)(2,1)S(1)}, u32[]{:S(2)}, u32[]{:S(2)}) %collective-permute-start.13) | collective-permute-done | bytes 5152 | tf_op jit(solution)/shard_map/ppermute | solution.py:37
  72.5 3.3 %collective-permute-done.14 = bf16[8,640]{1,0:T(8,128)(2,1)S(1)} collective-permute-done((bf16[8,640]{1,0:T(8,128)(2,1)S(1)}, bf16[8,640]{1,0:T(8,128)(2,1)S(1)}, u32[]{:S(2)}, u32[]{:S(2)}) %collective-permute-start.14) | collective-permute-done | bytes 10272 | tf_op jit(solution)/shard_map/ppermute | solution.py:37
  75.9 2.5 %collective-permute-start.15 = (bf16[8,1280]{1,0:T(8,128)(2,1)S(1)}, bf16[8,1280]{1,0:T(8,128)(2,1)S(1)}, u32[]{:S(2)}, u32[]{:S(2)}) collective-permute-start(bf16[8,1280]{1,0:T(8,128)(2,1)S(1)} %maximum_select_fusion.3), channel_id=1, source_target_pairs={{0,16},{4,20},{8,24},{12,28},{16,0},{20,4},{24,8},{28,12},{1,17},{... | collective-permute-start | bytes 61448 | tf_op jit(solution)/shard_map/ppermute | solution.py:37
  78.4 2.2 %collective-permute-done.15 = bf16[8,1280]{1,0:T(8,128)(2,1)S(1)} collective-permute-done((bf16[8,1280]{1,0:T(8,128)(2,1)S(1)}, bf16[8,1280]{1,0:T(8,128)(2,1)S(1)}, u32[]{:S(2)}, u32[]{:S(2)}) %collective-permute-start.15) | collective-permute-done | bytes 20512 | tf_op jit(solution)/shard_map/ppermute | solution.py:37
  80.7 17.2 %fusion.37 = (f32[8]{0:T(128)S(1)}, f32[8,8000]{1,0:T(8,128)S(1)}) fusion(bf16[8000,2560]{1,0:T(8,128)(2,1)} %param.30, f32[2560]{0:T(1024)S(1)} %convert_element_type.18, f32[8]{0:T(128)S(1)} %add_rsqrt_fusion, bf16[8,1280]{1,0:T(8,128)(2,1)S(1)} %maximum_select_fusion.3, bf16[8,1280]{1,0:T(8,128)(2,1)S(1)} %collective-permute-done.15, pred[]{:T(512)S(6)} %eq.61), kind=kOutput, calls=%fused_computation.142 | convolution fusion | flops 328010240 | bytes 41267264 | tf_op jit(solution)/shard_map/dot_general | solution.py:261
  99.5 1.6 %collective-permute-start.17 = (f32[3,8]{1,0:T(4,128)S(1)}, f32[3,8]{1,0:T(4,128)S(1)}, u32[]{:S(2)}, u32[]{:S(2)}) collective-permute-start(f32[3,8]{1,0:T(4,128)S(1)} %pad_maximum_fusion.1), channel_id=1, source_target_pairs={{0,2},{1,3},{2,0},{3,1},{4,6},{5,7},{6,4},{7,5},{8,10},{9,11},{10,... | collective-permute-start | bytes 296 | tf_op jit(solution)/shard_map/ppermute | solution.py:64
  101.1 2.1 %collective-permute-done.17 = f32[3,8]{1,0:T(4,128)S(1)} collective-permute-done((f32[3,8]{1,0:T(4,128)S(1)}, f32[3,8]{1,0:T(4,128)S(1)}, u32[]{:S(2)}, u32[]{:S(2)}) %collective-permute-start.17) | collective-permute-done | bytes 128 | tf_op jit(solution)/shard_map/ppermute | solution.py:64
  103.6 3.2 %collective-permute-done.18 = f32[3,8]{1,0:T(4,128)S(1)} collective-permute-done((f32[3,8]{1,0:T(4,128)S(1)}, f32[3,8]{1,0:T(4,128)S(1)}, u32[]{:S(2)}, u32[]{:S(2)}) %collective-permute-start.18) | collective-permute-done | bytes 128 | tf_op jit(solution)/shard_map/ppermute | solution.py:64
  107.3 3.2 %collective-permute-done.19 = f32[3,8]{1,0:T(4,128)S(1)} collective-permute-done((f32[3,8]{1,0:T(4,128)S(1)}, f32[3,8]{1,0:T(4,128)S(1)}, u32[]{:S(2)}, u32[]{:S(2)}) %collective-permute-start.19) | collective-permute-done | bytes 128 | tf_op jit(solution)/shard_map/ppermute | solution.py:64
  110.5 2.5 %collective-permute-start.20 = (f32[3,8]{1,0:T(4,128)S(1)}, f32[3,8]{1,0:T(4,128)S(1)}, u32[]{:S(2)}, u32[]{:S(2)}) collective-permute-start(f32[3,8]{1,0:T(4,128)S(1)} %pad_maximum_fusion.4), channel_id=1, source_target_pairs={{0,16},{4,20},{8,24},{12,28},{16,0},{20,4},{24,8},{28,12},{1,17},{... | collective-permute-start | bytes 296 | tf_op jit(solution)/shard_map/ppermute | solution.py:64
  113.1 2.0 %collective-permute-done.20 = f32[3,8]{1,0:T(4,128)S(1)} collective-permute-done((f32[3,8]{1,0:T(4,128)S(1)}, f32[3,8]{1,0:T(4,128)S(1)}, u32[]{:S(2)}, u32[]{:S(2)}) %collective-permute-start.20) | collective-permute-done | bytes 128 | tf_op jit(solution)/shard_map/ppermute | solution.py:64
  (91 shorter events, 25.3 us)
Async XLA Ops:
  0.6 62.0 %copy-start = (bf16[2560,80]{0,1:T(8,128)(2,1)S(1)}, bf16[2560,80]{0,1:T(8,128)(2,1)}, u32[]{:S(2)}) copy-start(bf16[2560,80]{0,1:T(8,128)(2,1)} %param.27) | copy-start | bytes 1228804
  0.6 16.0 %collective-permute-start.1 = (bf16[1,512,512]{2,1,0:T(8,128)(2,1)}, bf16[1,512,512]{2,1,0:T(8,128)(2,1)S(1)}, u32[]{:S(2)}, u32[]{:S(2)}) collective-permute-start(bf16[1,512,512]{2,1,0:T(8,128)(2,1)} %refs_10_.1), channel_id=1, source_target_pairs={{0,2},{1,3},{2,0},{3,1},{4,6},{5,7},{6,4},{7,5},{8,10},{9,11},{10,... | collective-permute-start | bytes 1572872 | tf_op jit(solution)/shard_map/ppermute | solution.py:81
  3.6 17.8 %collective-permute-start = (bf16[1,512,512]{2,1,0:T(8,128)(2,1)}, bf16[1,512,512]{2,1,0:T(8,128)(2,1)S(1)}, u32[]{:S(2)}, u32[]{:S(2)}) collective-permute-start(bf16[1,512,512]{2,1,0:T(8,128)(2,1)} %refs_10_.1), channel_id=1, source_target_pairs={{0,1},{1,0},{2,3},{3,2},{4,5},{5,4},{6,7},{7,6},{8,9},{9,8},{10,11... | collective-permute-start | bytes 1572872 | tf_op jit(solution)/shard_map/ppermute | solution.py:77
  3.7 16.3 %collective-permute-start.4 = (bf16[1,192,512]{2,1,0:T(8,128)(2,1)}, bf16[1,192,512]{2,1,0:T(8,128)(2,1)S(1)}, u32[]{:S(2)}, u32[]{:S(2)}) collective-permute-start(bf16[1,192,512]{2,1,0:T(8,128)(2,1)} %refs_18_.1), channel_id=1, source_target_pairs={{0,2},{1,3},{2,0},{3,1},{4,6},{5,7},{6,4},{7,5},{8,10},{9,11},{10,... | collective-permute-start | bytes 589832 | tf_op jit(solution)/shard_map/ppermute | solution.py:81
  3.8 16.7 %collective-permute-start.3 = (bf16[1,192,512]{2,1,0:T(8,128)(2,1)}, bf16[1,192,512]{2,1,0:T(8,128)(2,1)S(1)}, u32[]{:S(2)}, u32[]{:S(2)}) collective-permute-start(bf16[1,192,512]{2,1,0:T(8,128)(2,1)} %refs_18_.1), channel_id=1, source_target_pairs={{0,1},{1,0},{2,3},{3,2},{4,5},{5,4},{6,7},{7,6},{8,9},{9,8},{10,11... | collective-permute-start | bytes 589832 | tf_op jit(solution)/shard_map/ppermute | solution.py:77
  16.6 4.8 %collective-permute-start.2 = (bf16[1,512,512]{2,1,0:T(8,128)(2,1)S(1)}, bf16[1,512,512]{2,1,0:T(8,128)(2,1)S(1)}, u32[]{:S(2)}, u32[]{:S(2)}) collective-permute-start(bf16[1,512,512]{2,1,0:T(8,128)(2,1)S(1)} %collective-permute-done.1.refs_15_.refs_16_), channel_id=1, source_target_pairs={{0,1},{1,0},{2,3},{3,2},{4,5},{5,4},{6,7},{7,6},{8,9},{9,8},{10,11... | collective-permute-start | bytes 1572872 | tf_op jit(solution)/shard_map/ppermute | solution.py:91
  20.0 1.4 %collective-permute-start.5 = (bf16[1,192,512]{2,1,0:T(8,128)(2,1)S(1)}, bf16[1,192,512]{2,1,0:T(8,128)(2,1)S(1)}, u32[]{:S(2)}, u32[]{:S(2)}) collective-permute-start(bf16[1,192,512]{2,1,0:T(8,128)(2,1)S(1)} %collective-permute-done.4.refs_23_.refs_24_), channel_id=1, source_target_pairs={{0,1},{1,0},{2,3},{3,2},{4,5},{5,4},{6,7},{7,6},{8,9},{9,8},{10,11... | collective-permute-start | bytes 589832 | tf_op jit(solution)/shard_map/ppermute | solution.py:91
  22.5 24.7 %copy-start.7 = (bf16[1,192,512]{2,1,0:T(8,128)(2,1)S(1)}, bf16[1,192,512]{2,1,0:T(8,128)(2,1)}, u32[]{:S(2)}) copy-start(bf16[1,192,512]{2,1,0:T(8,128)(2,1)} %refs_18_.1) | copy-start | bytes 589828
  39.6 1.2 %collective-permute-start.6 = (bf16[1,2560]{1,0:T(2,128)(2,1)S(1)}, bf16[1,2560]{1,0:T(2,128)(2,1)S(1)}, u32[]{:S(2)}, u32[]{:S(2)}) collective-permute-start(bf16[1,2560]{1,0:T(2,128)(2,1)S(1)} %fusion.9), channel_id=1, source_target_pairs={{0,1},{1,0},{2,3},{3,2},{4,5},{5,4},{6,7},{7,6},{8,9},{9,8},{10,11... | collective-permute-start | bytes 15368 | tf_op jit(solution)/shard_map/ppermute | solution.py:25
  41.6 3.7 %collective-permute-start.7 = (bf16[1,2560]{1,0:T(2,128)(2,1)S(1)}, bf16[1,2560]{1,0:T(2,128)(2,1)S(1)}, u32[]{:S(2)}, u32[]{:S(2)}) collective-permute-start(bf16[1,2560]{1,0:T(2,128)(2,1)S(1)} %fusion.41), channel_id=1, source_target_pairs={{0,2},{1,3},{2,0},{3,1},{4,6},{5,7},{6,4},{7,5},{8,10},{9,11},{10,... | collective-permute-start | bytes 15368 | tf_op jit(solution)/shard_map/ppermute | solution.py:25
  45.4 5.6 %collective-permute-start.8 = (bf16[1,2560]{1,0:T(2,128)(2,1)S(1)}, bf16[1,2560]{1,0:T(2,128)(2,1)S(1)}, u32[]{:S(2)}, u32[]{:S(2)}) collective-permute-start(bf16[1,2560]{1,0:T(2,128)(2,1)S(1)} %add.588), channel_id=1, source_target_pairs={{0,4},{4,0},{8,12},{12,8},{16,20},{20,16},{24,28},{28,24},{1,5},{5... | collective-permute-start | bytes 15368 | tf_op jit(solution)/shard_map/ppermute | solution.py:37
  51.7 5.2 %collective-permute-start.9 = (bf16[2,2560]{1,0:T(2,128)(2,1)}, bf16[2,2560]{1,0:T(2,128)(2,1)}, u32[]{:S(2)}, u32[]{:S(2)}) collective-permute-start(bf16[2,2560]{1,0:T(2,128)(2,1)} %broadcast_select_fusion.1), channel_id=1, source_target_pairs={{0,8},{4,12},{8,0},{12,4},{16,24},{20,28},{24,16},{28,20},{1,9},{5... | collective-permute-start | bytes 30728 | tf_op jit(solution)/shard_map/ppermute | solution.py:37
  56.9 21.5 %copy-start.12 = (s32[8]{0:T(128)S(1)}, s32[8]{0:T(128)}, u32[]{:S(2)}) copy-start(s32[8]{0:T(128)} %param.31) | copy-start | bytes 100
  57.7 4.9 %collective-permute-start.10 = (bf16[4,2560]{1,0:T(4,128)(2,1)S(1)}, bf16[4,2560]{1,0:T(4,128)(2,1)S(1)}, u32[]{:S(2)}, u32[]{:S(2)}) collective-permute-start(bf16[4,2560]{1,0:T(4,128)(2,1)S(1)} %maximum_select_fusion.2), channel_id=1, source_target_pairs={{0,16},{4,20},{8,24},{12,28},{16,0},{20,4},{24,8},{28,12},{1,17},{... | collective-permute-start | bytes 61448 | tf_op jit(solution)/shard_map/ppermute | solution.py:37
  63.5 1.2 %collective-permute-start.11 = (bf16[8,80]{1,0:T(8,128)(2,1)S(1)}, bf16[8,80]{1,0:T(8,128)(2,1)S(1)}, u32[]{:S(2)}, u32[]{:S(2)}) collective-permute-start(bf16[8,80]{1,0:T(8,128)(2,1)S(1)} %fusion), channel_id=1, source_target_pairs={{0,1},{1,0},{2,3},{3,2},{4,5},{5,4},{6,7},{7,6},{8,9},{9,8},{10,11... | collective-permute-start | bytes 3848 | tf_op jit(solution)/shard_map/ppermute | solution.py:37
  64.8 3.6 %collective-permute-start.12 = (bf16[8,160]{1,0:T(8,128)(2,1)S(1)}, bf16[8,160]{1,0:T(8,128)(2,1)S(1)}, u32[]{:S(2)}, u32[]{:S(2)}) collective-permute-start(bf16[8,160]{1,0:T(8,128)(2,1)S(1)} %maximum_select_fusion.7), channel_id=1, source_target_pairs={{0,2},{1,3},{2,0},{3,1},{4,6},{5,7},{6,4},{7,5},{8,10},{9,11},{10,... | collective-permute-start | bytes 7688 | tf_op jit(solution)/shard_map/ppermute | solution.py:37
  68.5 3.6 %collective-permute-start.13 = (bf16[8,320]{1,0:T(8,128)(2,1)S(1)}, bf16[8,320]{1,0:T(8,128)(2,1)S(1)}, u32[]{:S(2)}, u32[]{:S(2)}) collective-permute-start(bf16[8,320]{1,0:T(8,128)(2,1)S(1)} %maximum_select_fusion.6), channel_id=1, source_target_pairs={{0,4},{4,0},{8,12},{12,8},{16,20},{20,16},{24,28},{28,24},{1,5},{5... | collective-permute-start | bytes 15368 | tf_op jit(solution)/shard_map/ppermute | solution.py:37
  72.2 3.7 %collective-permute-start.14 = (bf16[8,640]{1,0:T(8,128)(2,1)S(1)}, bf16[8,640]{1,0:T(8,128)(2,1)S(1)}, u32[]{:S(2)}, u32[]{:S(2)}) collective-permute-start(bf16[8,640]{1,0:T(8,128)(2,1)S(1)} %maximum_select_fusion.4), channel_id=1, source_target_pairs={{0,8},{4,12},{8,0},{12,4},{16,24},{20,28},{24,16},{28,20},{1,9},{5... | collective-permute-start | bytes 30728 | tf_op jit(solution)/shard_map/ppermute | solution.py:37
  75.9 4.7 %collective-permute-start.15 = (bf16[8,1280]{1,0:T(8,128)(2,1)S(1)}, bf16[8,1280]{1,0:T(8,128)(2,1)S(1)}, u32[]{:S(2)}, u32[]{:S(2)}) collective-permute-start(bf16[8,1280]{1,0:T(8,128)(2,1)S(1)} %maximum_select_fusion.3), channel_id=1, source_target_pairs={{0,16},{4,20},{8,24},{12,28},{16,0},{20,4},{24,8},{28,12},{1,17},{... | collective-permute-start | bytes 61448 | tf_op jit(solution)/shard_map/ppermute | solution.py:37
  98.2 1.2 %collective-permute-start.16 = (f32[3,8]{1,0:T(4,128)S(1)}, f32[3,8]{1,0:T(4,128)S(1)}, u32[]{:S(2)}, u32[]{:S(2)}) collective-permute-start(f32[3,8]{1,0:T(4,128)S(1)} %pad_maximum_fusion), channel_id=1, source_target_pairs={{0,1},{1,0},{2,3},{3,2},{4,5},{5,4},{6,7},{7,6},{8,9},{9,8},{10,11... | collective-permute-start | bytes 296 | tf_op jit(solution)/shard_map/ppermute | solution.py:64
  99.5 3.7 %collective-permute-start.17 = (f32[3,8]{1,0:T(4,128)S(1)}, f32[3,8]{1,0:T(4,128)S(1)}, u32[]{:S(2)}, u32[]{:S(2)}) collective-permute-start(f32[3,8]{1,0:T(4,128)S(1)} %pad_maximum_fusion.1), channel_id=1, source_target_pairs={{0,2},{1,3},{2,0},{3,1},{4,6},{5,7},{6,4},{7,5},{8,10},{9,11},{10,... | collective-permute-start | bytes 296 | tf_op jit(solution)/shard_map/ppermute | solution.py:64
  103.2 3.7 %collective-permute-start.18 = (f32[3,8]{1,0:T(4,128)S(1)}, f32[3,8]{1,0:T(4,128)S(1)}, u32[]{:S(2)}, u32[]{:S(2)}) collective-permute-start(f32[3,8]{1,0:T(4,128)S(1)} %pad_maximum_fusion.2), channel_id=1, source_target_pairs={{0,4},{4,0},{8,12},{12,8},{16,20},{20,16},{24,28},{28,24},{1,5},{5... | collective-permute-start | bytes 296 | tf_op jit(solution)/shard_map/ppermute | solution.py:64
  106.9 3.7 %collective-permute-start.19 = (f32[3,8]{1,0:T(4,128)S(1)}, f32[3,8]{1,0:T(4,128)S(1)}, u32[]{:S(2)}, u32[]{:S(2)}) collective-permute-start(f32[3,8]{1,0:T(4,128)S(1)} %pad_maximum_fusion.3), channel_id=1, source_target_pairs={{0,8},{4,12},{8,0},{12,4},{16,24},{20,28},{24,16},{28,20},{1,9},{5... | collective-permute-start | bytes 296 | tf_op jit(solution)/shard_map/ppermute | solution.py:64
  110.5 4.5 %collective-permute-start.20 = (f32[3,8]{1,0:T(4,128)S(1)}, f32[3,8]{1,0:T(4,128)S(1)}, u32[]{:S(2)}, u32[]{:S(2)}) collective-permute-start(f32[3,8]{1,0:T(4,128)S(1)} %pad_maximum_fusion.4), channel_id=1, source_target_pairs={{0,16},{4,20},{8,24},{12,28},{16,0},{20,4},{24,8},{28,12},{1,17},{... | collective-permute-start | bytes 296 | tf_op jit(solution)/shard_map/ppermute | solution.py:64
  (10 other events, 46.8 us)

commit v11 on v10

--- a/solution.py
+++ b/solution.py
@@ -179,6 +179,30 @@
     )(query_pos, *[bound for _, _, bound in pieces], queries, *kv_args)
 
 
+def logits_kernel(head_ref, normed_ref, out_ref):
+    out_ref[...] = jnp.dot(head_ref[...], normed_ref[...], preferred_element_type=jnp.float32)
+
+
+def vocab_logits(head, normed_t):
+    vocab_local, model_cols = head.shape
+    rows = normed_t.shape[1]
+    block = vocab_local
+    for size in range(min(2000, vocab_local), 7, -1):
+        if vocab_local % size == 0 and size % 8 == 0:
+            block = size
+            break
+    return pl.pallas_call(
+        logits_kernel,
+        grid=(vocab_local // block,),
+        in_specs=[
+            pl.BlockSpec((block, model_cols), lambda i: (i, 0)),
+            pl.BlockSpec((model_cols, rows), lambda i: (0, 0)),
+        ],
+        out_specs=pl.BlockSpec((block, rows), lambda i: (i, 0)),
+        out_shape=jax.ShapeDtypeStruct((vocab_local, rows), jnp.float32),
+    )(head, normed_t)
+
+
 def on_device(
     queries, new_kv, cache_pool, lengths, owner, w_out, last_residual, norm_gain, head, targets
 ):
@@ -258,15 +282,13 @@
         * lax.rsqrt(jnp.mean(full_hidden * full_hidden, axis=1, keepdims=True) + 1e-06)
         * norm_gain.astype(jnp.float32)
     ).astype(jnp.bfloat16)
-    logits = lax.dot_general(
-        normed, head, (((1,), (1,)), ((), ())), preferred_element_type=jnp.float32
-    )
+    logits = vocab_logits(head, normed.T)
     vocab_local = head.shape[0]
     local_target = targets - lax.axis_index(("gx", "gy")) * vocab_local
-    target_hit = jnp.arange(vocab_local, dtype=jnp.int32)[None, :] == local_target[:, None]
-    picked = jnp.sum(jnp.where(target_hit, logits, 0.0), axis=1)
-    local_top = jnp.max(logits, axis=1)
-    local_total = jnp.sum(jnp.exp(logits - local_top[:, None]), axis=1)
+    target_hit = jnp.arange(vocab_local, dtype=jnp.int32)[:, None] == local_target[None, :]
+    picked = jnp.sum(jnp.where(target_hit, logits, 0.0), axis=0)
+    local_top = jnp.max(logits, axis=0)
+    local_total = jnp.sum(jnp.exp(logits - local_top[None, :]), axis=0)
     top_logit, exp_total, picked = butterfly_stats(local_top, local_total, picked)
     log_norm = top_logit + jnp.log(exp_total)
     return (mixed_out, fresh_block, log_norm, top_logit, picked - log_norm)

time: 116 us -> 126 us (1.086)
  Pallas kernels: 16.3 us -> 34.7 us
  matrix products: 18.1 us -> 0.21 us
  other arithmetic: 16.9 us -> 23.9 us
    pallas_call x0 -> x1, Pallas kernels: none -> 18.4 us  [vocab_logits(): pl.pallas_call(logits_kernel, grid=(vocab_local // block,), in_specs=[pl....]
    dot_general x1 -> x0, matrix products: 17.2 us -> none  [on_device(): lax.dot_general(normed, head, (((1,), (1,)), ((), ())), preferred_element...]
    reduce_max x0 -> x1, other arithmetic: none -> 3.23 us  [on_device(): local_top = jnp.max(logits, axis=0)]
    reduce_sum x1, other arithmetic: 0.3 us -> 3.5 us  [on_device(): local_total = jnp.sum(jnp.exp(logits - local_top[None, :]), axis=0)]
  transfers between devices with their start and end apart: 21 -> 21, of which waited for: 16 -> 15; matrix products, arithmetic and copies ran while one was open for 17% -> 16% of each run, Pallas kernels for 0% -> 0%
where the time goes in v11:
time: 126 us; the launch traced here: 125 us
  Pallas kernels  34.7 us (28%)
  waiting for transfers between devices  30.3 us (24%)
  other arithmetic  23.9 us (19%)
  starting transfers between devices  22.2 us (18%)
  local copies, waits for them, and re-layouts  9.08 us (7%)
  between operations  4.73 us (4%)
    pallas_call x1, Pallas kernels, vocab_logits(): pl.pallas_call(logits_kernel, grid=(vocab_local // block,), in_specs=[pl....  18.4 us
    pallas_call x1, Pallas kernels, attend(): pl.pallas_call(kernel, grid=(req_local, head_count // stacked), in_specs=...  16.3 us
    ppermute x8, waiting for transfers between devices, butterfly_gather(): other = lax.ppermute(x, axis, xor_pairs(count, bit))  12 us
    ppermute x5, waiting for transfers between devices, butterfly_stats(): other = lax.ppermute(packed, axis, xor_pairs(count, bit))  11.6 us
    ppermute x8, starting transfers between devices, butterfly_gather(): other = lax.ppermute(x, axis, xor_pairs(count, bit))  10.9 us
    ppermute x5, starting transfers between devices, butterfly_stats(): other = lax.ppermute(packed, axis, xor_pairs(count, bit))  5.12 us
    ppermute x2, waiting for transfers between devices, exchange_pieces(): other = lax.ppermute(held, axis, xor_pairs(count, bit))  4.02 us
    reduce_sum x1, other arithmetic, on_device(): local_total = jnp.sum(jnp.exp(logits - local_top[None, :]), axis=0)  3.5 us
  transfers between devices with their start and end apart: 21, of which 15 were waited for; matrix products, arithmetic and copies ran while one was open for 16% of the time, Pallas kernels for 0%

profile of v11, /device:TPU:0, one launch (start us, length us, event | category | flops | bytes accessed | tf_op | source)
XLA Modules:
  0.0 125.2 jit_solution(17529763439248732103)
XLA Ops:
  0.6 3.0 %collective-permute-start.4 = (bf16[1,192,512]{2,1,0:T(8,128)(2,1)}, bf16[1,192,512]{2,1,0:T(8,128)(2,1)S(1)}, u32[]{:S(2)}, u32[]{:S(2)}) collective-permute-start(bf16[1,192,512]{2,1,0:T(8,128)(2,1)} %refs_18_.1), channel_id=1, source_target_pairs={{0,2},{1,3},{2,0},{3,1},{4,6},{5,7},{6,4},{7,5},{8,10},{9,11},{10,... | collective-permute-start | bytes 589832 | tf_op jit(solution)/shard_map/ppermute | solution.py:81
  12.7 2.7 %compare_select_fusion.3 = (s32[512,1]{0,1:T(1,128)S(1)}, s32[1,512]{1,0:T(1,128)S(1)}, s32[512,1]{0,1:T(1,128)S(1)}) fusion(s32[]{:T(128)} %axis_index.14, s32[]{:T(128)} %bitcast.20, s32[]{:T(128)} %bitcast.19, s32[]{:T(128)} %bitcast.18, s32[]{:T(128)} %bitcast.17, s32[]{:T(128)} %bitcast.16), kind=kLoop, calls=%fused_computation.27 | loop fusion | flops 55296 | bytes 6168 | tf_op jit(solution)/shard_map/jit(take_along_axis)/select_n | solution.py:263
  16.0 4.0 %collective-permute-done.1.refs_15_.refs_16_ = bf16[1,512,512]{2,1,0:T(8,128)(2,1)S(1)} collective-permute-done((bf16[1,512,512]{2,1,0:T(8,128)(2,1)}, bf16[1,512,512]{2,1,0:T(8,128)(2,1)S(1)}, u32[]{:S(2)}, u32[]{:S(2)}) %collective-permute-start.1) | collective-permute-done | bytes 524320 | tf_op jit(solution)/shard_map/ppermute | solution.py:81
  23.8 16.3 %shard_map.230 = bf16[1,192,2560]{2,1,0:T(8,128)(2,1)} custom-call(s32[192,1]{1,0:T(8,128)} %iota_add_fusion.qpos_ref, s32[1,1,512]{2,1,0:T(1,128)} %get-tuple-element.86.refs_0_, s32[1,1,512]{2,1,0:T(1,128)} %get-tuple-element.85.refs_1_, s32[1,1,512]{2,1,0:T(1,128)} %get-tuple-element.84.refs_2_, s32[1,1,512]{2,1,0:T(1,128)} %get-tuple-element.83.refs_3_, ...), custom_call_target="tpu_custom_call" | custom-call | tf_op jit(solution)/shard_map/pallas_call | solution.py:168
  43.0 1.8 %collective-permute-start.7 = (bf16[1,2560]{1,0:T(2,128)(2,1)S(1)}, bf16[1,2560]{1,0:T(2,128)(2,1)S(1)}, u32[]{:S(2)}, u32[]{:S(2)}) collective-permute-start(bf16[1,2560]{1,0:T(2,128)(2,1)S(1)} %fusion.34), channel_id=1, source_target_pairs={{0,2},{1,3},{2,0},{3,1},{4,6},{5,7},{6,4},{7,5},{8,10},{9,11},{10,... | collective-permute-start | bytes 15368 | tf_op jit(solution)/shard_map/ppermute | solution.py:25
  44.8 1.9 %collective-permute-done.7 = bf16[1,2560]{1,0:T(2,128)(2,1)S(1)} collective-permute-done((bf16[1,2560]{1,0:T(2,128)(2,1)S(1)}, bf16[1,2560]{1,0:T(2,128)(2,1)S(1)}, u32[]{:S(2)}, u32[]{:S(2)}) %collective-permute-start.7) | collective-permute-done | bytes 5152 | tf_op jit(solution)/shard_map/ppermute | solution.py:25
  46.8 1.8 %collective-permute-start.8 = (bf16[1,2560]{1,0:T(2,128)(2,1)S(1)}, bf16[1,2560]{1,0:T(2,128)(2,1)S(1)}, u32[]{:S(2)}, u32[]{:S(2)}) collective-permute-start(bf16[1,2560]{1,0:T(2,128)(2,1)S(1)} %add.588), channel_id=1, source_target_pairs={{0,4},{4,0},{8,12},{12,8},{16,20},{20,16},{24,28},{28,24},{1,5},{5... | collective-permute-start | bytes 15368 | tf_op jit(solution)/shard_map/ppermute | solution.py:37
  49.8 2.6 %gather_fusion.1 = bf16[512,512]{1,0:T(8,128)(2,1)} fusion(bf16[768,512]{1,0:T(8,128)(2,1)S(1)} %maximum_bitcast_fusion.1, s32[1024]{0:T(1024)S(1)} %pad_clamp_fusion), kind=kCustom, calls=%fused_computation.1 | custom fusion | bytes 1050624 | tf_op jit(solution)/shard_map/jit(take_along_axis)/gather | solution.py:264
  56.0 2.2 %gather_fusion = bf16[512,512]{1,0:T(8,128)(2,1)S(1)} fusion(bf16[2048,512]{1,0:T(8,128)(2,1)S(1)} %maximum_bitcast_fusion, s32[1024]{0:T(1024)} %pad_clamp_fusion.1), kind=kCustom, calls=%fused_computation | custom fusion | bytes 1050624 | tf_op jit(solution)/shard_map/jit(take_along_axis)/gather | solution.py:263
  59.1 2.7 %collective-permute-start.10 = (bf16[4,2560]{1,0:T(4,128)(2,1)S(1)}, bf16[4,2560]{1,0:T(4,128)(2,1)S(1)}, u32[]{:S(2)}, u32[]{:S(2)}) collective-permute-start(bf16[4,2560]{1,0:T(4,128)(2,1)S(1)} %maximum_select_fusion.2), channel_id=1, source_target_pairs={{0,16},{4,20},{8,24},{12,28},{16,0},{20,4},{24,8},{28,12},{1,17},{... | collective-permute-start | bytes 61448 | tf_op jit(solution)/shard_map/ppermute | solution.py:37
  61.7 2.1 %fusion.1 = bf16[1,512,512]{2,1,0:T(8,128)(2,1)} fusion(bf16[512,512]{1,0:T(8,128)(2,1)} %gather_fusion.1, bf16[512,512]{1,0:T(8,128)(2,1)S(1)} %gather_fusion, pred[512]{0:T(512)(128)(4,1)} %get-tuple-element.92, pred[512]{0:T(512)(128)(4,1)} %compare_and_fusion.1, pred[512]{0:T(512)(128)(4,1)} %get-tuple-element.91), kind=kLoop, calls=%fused_computation.10 | loop fusion | flops 786432 | bytes 1574400 | tf_op jit(solution)/shard_map/jit(_where)/select_n | solution.py:265
  67.0 2.1 %collective-permute-done.12 = bf16[8,160]{1,0:T(8,128)(2,1)S(1)} collective-permute-done((bf16[8,160]{1,0:T(8,128)(2,1)S(1)}, bf16[8,160]{1,0:T(8,128)(2,1)S(1)}, u32[]{:S(2)}, u32[]{:S(2)}) %collective-permute-start.12) | collective-permute-done | bytes 2592 | tf_op jit(solution)/shard_map/ppermute | solution.py:37
  69.6 3.2 %collective-permute-done.13 = bf16[8,320]{1,0:T(8,128)(2,1)S(1)} collective-permute-done((bf16[8,320]{1,0:T(8,128)(2,1)S(1)}, bf16[8,320]{1,0:T(8,128)(2,1)S(1)}, u32[]{:S(2)}, u32[]{:S(2)}) %collective-permute-start.13) | collective-permute-done | bytes 5152 | tf_op jit(solution)/shard_map/ppermute | solution.py:37
  73.3 3.3 %collective-permute-done.14 = bf16[8,640]{1,0:T(8,128)(2,1)S(1)} collective-permute-done((bf16[8,640]{1,0:T(8,128)(2,1)S(1)}, bf16[8,640]{1,0:T(8,128)(2,1)S(1)}, u32[]{:S(2)}, u32[]{:S(2)}) %collective-permute-start.14) | collective-permute-done | bytes 10272 | tf_op jit(solution)/shard_map/ppermute | solution.py:37
  76.6 2.5 %collective-permute-start.15 = (bf16[8,1280]{1,0:T(8,128)(2,1)S(1)}, bf16[8,1280]{1,0:T(8,128)(2,1)S(1)}, u32[]{:S(2)}, u32[]{:S(2)}) collective-permute-start(bf16[8,1280]{1,0:T(8,128)(2,1)S(1)} %maximum_select_fusion.3), channel_id=1, source_target_pairs={{0,16},{4,20},{8,24},{12,28},{16,0},{20,4},{24,8},{28,12},{1,17},{... | collective-permute-start | bytes 61448 | tf_op jit(solution)/shard_map/ppermute | solution.py:37
  79.1 2.2 %collective-permute-done.15 = bf16[8,1280]{1,0:T(8,128)(2,1)S(1)} collective-permute-done((bf16[8,1280]{1,0:T(8,128)(2,1)S(1)}, bf16[8,1280]{1,0:T(8,128)(2,1)S(1)}, u32[]{:S(2)}, u32[]{:S(2)}) %collective-permute-start.15) | collective-permute-done | bytes 20512 | tf_op jit(solution)/shard_map/ppermute | solution.py:37
  82.6 18.4 %shard_map.231 = f32[8000,8]{1,0:T(8,128)} custom-call(bf16[8000,2560]{1,0:T(8,128)(2,1)} %head_ref.1, bf16[2560,8]{1,0:T(8,128)(2,1)} %bitcast.188), custom_call_target="tpu_custom_call" | custom-call | tf_op jit(solution)/shard_map/pallas_call | solution.py:194
  101.0 3.2 %reduce_max.9 = f32[8]{0:T(128)S(1)} reduce(f32[8000,8]{1,0:T(8,128)} %shard_map.231, f32[]{:T(128)} %constant.196.clone.1), dimensions={0}, to_apply=%region_2.4 | reduce | flops 63992 | bytes 256036 | tf_op jit(solution)/shard_map/reduce_max | solution.py:290
  104.3 3.5 %exponential_reduce_fusion = (f32[8]{0:T(128)S(1)}, f32[8]{0:T(128)S(1)}) fusion(f32[8000,8]{1,0:T(8,128)} %shard_map.231, f32[8]{0:T(128)S(1)} %reduce_max.9, s32[8]{0:T(128)S(1)} %broadcast_subtract_fusion), kind=kLoop, calls=%fused_computation.4 | loop fusion | flops 319984 | bytes 256128 | tf_op jit(solution)/shard_map/reduce_sum | solution.py:291
  110.6 2.1 %collective-permute-done.17 = f32[3,8]{1,0:T(4,128)S(1)} collective-permute-done((f32[3,8]{1,0:T(4,128)S(1)}, f32[3,8]{1,0:T(4,128)S(1)}, u32[]{:S(2)}, u32[]{:S(2)}) %collective-permute-start.17) | collective-permute-done | bytes 128 | tf_op jit(solution)/shard_map/ppermute | solution.py:64
  113.3 3.1 %collective-permute-done.18 = f32[3,8]{1,0:T(4,128)S(1)} collective-permute-done((f32[3,8]{1,0:T(4,128)S(1)}, f32[3,8]{1,0:T(4,128)S(1)}, u32[]{:S(2)}, u32[]{:S(2)}) %collective-permute-start.18) | collective-permute-done | bytes 128 | tf_op jit(solution)/shard_map/ppermute | solution.py:64
  116.8 3.2 %collective-permute-done.19 = f32[3,8]{1,0:T(4,128)S(1)} collective-permute-done((f32[3,8]{1,0:T(4,128)S(1)}, f32[3,8]{1,0:T(4,128)S(1)}, u32[]{:S(2)}, u32[]{:S(2)}) %collective-permute-start.19) | collective-permute-done | bytes 128 | tf_op jit(solution)/shard_map/ppermute | solution.py:64
  120.1 2.5 %collective-permute-start.20 = (f32[3,8]{1,0:T(4,128)S(1)}, f32[3,8]{1,0:T(4,128)S(1)}, u32[]{:S(2)}, u32[]{:S(2)}) collective-permute-start(f32[3,8]{1,0:T(4,128)S(1)} %pad_maximum_fusion.4), channel_id=1, source_target_pairs={{0,16},{4,20},{8,24},{12,28},{16,0},{20,4},{24,8},{28,12},{1,17},{... | collective-permute-start | bytes 296 | tf_op jit(solution)/shard_map/ppermute | solution.py:64
  122.6 2.0 %collective-permute-done.20 = f32[3,8]{1,0:T(4,128)S(1)} collective-permute-done((f32[3,8]{1,0:T(4,128)S(1)}, f32[3,8]{1,0:T(4,128)S(1)}, u32[]{:S(2)}, u32[]{:S(2)}) %collective-permute-start.20) | collective-permute-done | bytes 128 | tf_op jit(solution)/shard_map/ppermute | solution.py:64
  (94 shorter events, 27.9 us)
Async XLA Ops:
  0.6 63.4 %copy-start = (bf16[2560,80]{0,1:T(8,128)(2,1)S(1)}, bf16[2560,80]{0,1:T(8,128)(2,1)}, u32[]{:S(2)}) copy-start(bf16[2560,80]{0,1:T(8,128)(2,1)} %param.27) | copy-start | bytes 1228804
  0.6 20.5 %collective-permute-start.4 = (bf16[1,192,512]{2,1,0:T(8,128)(2,1)}, bf16[1,192,512]{2,1,0:T(8,128)(2,1)S(1)}, u32[]{:S(2)}, u32[]{:S(2)}) collective-permute-start(bf16[1,192,512]{2,1,0:T(8,128)(2,1)} %refs_18_.1), channel_id=1, source_target_pairs={{0,2},{1,3},{2,0},{3,1},{4,6},{5,7},{6,4},{7,5},{8,10},{9,11},{10,... | collective-permute-start | bytes 589832 | tf_op jit(solution)/shard_map/ppermute | solution.py:81
  3.7 18.6 %collective-permute-start.3 = (bf16[1,192,512]{2,1,0:T(8,128)(2,1)}, bf16[1,192,512]{2,1,0:T(8,128)(2,1)S(1)}, u32[]{:S(2)}, u32[]{:S(2)}) collective-permute-start(bf16[1,192,512]{2,1,0:T(8,128)(2,1)} %refs_18_.1), channel_id=1, source_target_pairs={{0,1},{1,0},{2,3},{3,2},{4,5},{5,4},{6,7},{7,6},{8,9},{9,8},{10,11... | collective-permute-start | bytes 589832 | tf_op jit(solution)/shard_map/ppermute | solution.py:77
  3.7 16.3 %collective-permute-start.1 = (bf16[1,512,512]{2,1,0:T(8,128)(2,1)}, bf16[1,512,512]{2,1,0:T(8,128)(2,1)S(1)}, u32[]{:S(2)}, u32[]{:S(2)}) collective-permute-start(bf16[1,512,512]{2,1,0:T(8,128)(2,1)} %refs_10_.1), channel_id=1, source_target_pairs={{0,2},{1,3},{2,0},{3,1},{4,6},{5,7},{6,4},{7,5},{8,10},{9,11},{10,... | collective-permute-start | bytes 1572872 | tf_op jit(solution)/shard_map/ppermute | solution.py:81
  3.8 18.9 %collective-permute-start = (bf16[1,512,512]{2,1,0:T(8,128)(2,1)}, bf16[1,512,512]{2,1,0:T(8,128)(2,1)S(1)}, u32[]{:S(2)}, u32[]{:S(2)}) collective-permute-start(bf16[1,512,512]{2,1,0:T(8,128)(2,1)} %refs_10_.1), channel_id=1, source_target_pairs={{0,1},{1,0},{2,3},{3,2},{4,5},{5,4},{6,7},{7,6},{8,9},{9,8},{10,11... | collective-permute-start | bytes 1572872 | tf_op jit(solution)/shard_map/ppermute | solution.py:77
  6.2 42.4 %copy-start.6 = (bf16[1,192,512]{2,1,0:T(8,128)(2,1)S(1)}, bf16[1,192,512]{2,1,0:T(8,128)(2,1)}, u32[]{:S(2)}) copy-start(bf16[1,192,512]{2,1,0:T(8,128)(2,1)} %refs_18_.1) | copy-start | bytes 589828
  20.0 2.7 %collective-permute-start.2 = (bf16[1,512,512]{2,1,0:T(8,128)(2,1)S(1)}, bf16[1,512,512]{2,1,0:T(8,128)(2,1)S(1)}, u32[]{:S(2)}, u32[]{:S(2)}) collective-permute-start(bf16[1,512,512]{2,1,0:T(8,128)(2,1)S(1)} %collective-permute-done.1.refs_15_.refs_16_), channel_id=1, source_target_pairs={{0,1},{1,0},{2,3},{3,2},{4,5},{5,4},{6,7},{7,6},{8,9},{9,8},{10,11... | collective-permute-start | bytes 1572872 | tf_op jit(solution)/shard_map/ppermute | solution.py:91
  21.2 1.5 %collective-permute-start.5 = (bf16[1,192,512]{2,1,0:T(8,128)(2,1)S(1)}, bf16[1,192,512]{2,1,0:T(8,128)(2,1)S(1)}, u32[]{:S(2)}, u32[]{:S(2)}) collective-permute-start(bf16[1,192,512]{2,1,0:T(8,128)(2,1)S(1)} %collective-permute-done.4.refs_23_.refs_24_), channel_id=1, source_target_pairs={{0,1},{1,0},{2,3},{3,2},{4,5},{5,4},{6,7},{7,6},{8,9},{9,8},{10,11... | collective-permute-start | bytes 589832 | tf_op jit(solution)/shard_map/ppermute | solution.py:91
  40.9 1.3 %collective-permute-start.6 = (bf16[1,2560]{1,0:T(2,128)(2,1)S(1)}, bf16[1,2560]{1,0:T(2,128)(2,1)S(1)}, u32[]{:S(2)}, u32[]{:S(2)}) collective-permute-start(bf16[1,2560]{1,0:T(2,128)(2,1)S(1)} %fusion.5), channel_id=1, source_target_pairs={{0,1},{1,0},{2,3},{3,2},{4,5},{5,4},{6,7},{7,6},{8,9},{9,8},{10,11... | collective-permute-start | bytes 15368 | tf_op jit(solution)/shard_map/ppermute | solution.py:25
  43.0 3.7 %collective-permute-start.7 = (bf16[1,2560]{1,0:T(2,128)(2,1)S(1)}, bf16[1,2560]{1,0:T(2,128)(2,1)S(1)}, u32[]{:S(2)}, u32[]{:S(2)}) collective-permute-start(bf16[1,2560]{1,0:T(2,128)(2,1)S(1)} %fusion.34), channel_id=1, source_target_pairs={{0,2},{1,3},{2,0},{3,1},{4,6},{5,7},{6,4},{7,5},{8,10},{9,11},{10,... | collective-permute-start | bytes 15368 | tf_op jit(solution)/shard_map/ppermute | solution.py:25
  46.8 5.6 %collective-permute-start.8 = (bf16[1,2560]{1,0:T(2,128)(2,1)S(1)}, bf16[1,2560]{1,0:T(2,128)(2,1)S(1)}, u32[]{:S(2)}, u32[]{:S(2)}) collective-permute-start(bf16[1,2560]{1,0:T(2,128)(2,1)S(1)} %add.588), channel_id=1, source_target_pairs={{0,4},{4,0},{8,12},{12,8},{16,20},{20,16},{24,28},{28,24},{1,5},{5... | collective-permute-start | bytes 15368 | tf_op jit(solution)/shard_map/ppermute | solution.py:37
  53.0 5.2 %collective-permute-start.9 = (bf16[2,2560]{1,0:T(2,128)(2,1)}, bf16[2,2560]{1,0:T(2,128)(2,1)}, u32[]{:S(2)}, u32[]{:S(2)}) collective-permute-start(bf16[2,2560]{1,0:T(2,128)(2,1)} %broadcast_select_fusion.1), channel_id=1, source_target_pairs={{0,8},{4,12},{8,0},{12,4},{16,24},{20,28},{24,16},{28,20},{1,9},{5... | collective-permute-start | bytes 30728 | tf_op jit(solution)/shard_map/ppermute | solution.py:37
  56.0 23.1 %copy-start.12 = (s32[8]{0:T(128)S(1)}, s32[8]{0:T(128)}, u32[]{:S(2)}) copy-start(s32[8]{0:T(128)} %param.31) | copy-start | bytes 100
  59.1 4.9 %collective-permute-start.10 = (bf16[4,2560]{1,0:T(4,128)(2,1)S(1)}, bf16[4,2560]{1,0:T(4,128)(2,1)S(1)}, u32[]{:S(2)}, u32[]{:S(2)}) collective-permute-start(bf16[4,2560]{1,0:T(4,128)(2,1)S(1)} %maximum_select_fusion.2), channel_id=1, source_target_pairs={{0,16},{4,20},{8,24},{12,28},{16,0},{20,4},{24,8},{28,12},{1,17},{... | collective-permute-start | bytes 61448 | tf_op jit(solution)/shard_map/ppermute | solution.py:37
  64.2 1.2 collective-permute-start.11
  65.5 3.6 %collective-permute-start.12 = (bf16[8,160]{1,0:T(8,128)(2,1)S(1)}, bf16[8,160]{1,0:T(8,128)(2,1)S(1)}, u32[]{:S(2)}, u32[]{:S(2)}) collective-permute-start(bf16[8,160]{1,0:T(8,128)(2,1)S(1)} %maximum_select_fusion.6), channel_id=1, source_target_pairs={{0,2},{1,3},{2,0},{3,1},{4,6},{5,7},{6,4},{7,5},{8,10},{9,11},{10,... | collective-permute-start | bytes 7688 | tf_op jit(solution)/shard_map/ppermute | solution.py:37
  69.2 3.6 %collective-permute-start.13 = (bf16[8,320]{1,0:T(8,128)(2,1)S(1)}, bf16[8,320]{1,0:T(8,128)(2,1)S(1)}, u32[]{:S(2)}, u32[]{:S(2)}) collective-permute-start(bf16[8,320]{1,0:T(8,128)(2,1)S(1)} %maximum_select_fusion.5), channel_id=1, source_target_pairs={{0,4},{4,0},{8,12},{12,8},{16,20},{20,16},{24,28},{28,24},{1,5},{5... | collective-permute-start | bytes 15368 | tf_op jit(solution)/shard_map/ppermute | solution.py:37
  72.9 3.7 %collective-permute-start.14 = (bf16[8,640]{1,0:T(8,128)(2,1)S(1)}, bf16[8,640]{1,0:T(8,128)(2,1)S(1)}, u32[]{:S(2)}, u32[]{:S(2)}) collective-permute-start(bf16[8,640]{1,0:T(8,128)(2,1)S(1)} %maximum_select_fusion.4), channel_id=1, source_target_pairs={{0,8},{4,12},{8,0},{12,4},{16,24},{20,28},{24,16},{28,20},{1,9},{5... | collective-permute-start | bytes 30728 | tf_op jit(solution)/shard_map/ppermute | solution.py:37
  76.6 4.7 %collective-permute-start.15 = (bf16[8,1280]{1,0:T(8,128)(2,1)S(1)}, bf16[8,1280]{1,0:T(8,128)(2,1)S(1)}, u32[]{:S(2)}, u32[]{:S(2)}) collective-permute-start(bf16[8,1280]{1,0:T(8,128)(2,1)S(1)} %maximum_select_fusion.3), channel_id=1, source_target_pairs={{0,16},{4,20},{8,24},{12,28},{16,0},{20,4},{24,8},{28,12},{1,17},{... | collective-permute-start | bytes 61448 | tf_op jit(solution)/shard_map/ppermute | solution.py:37
  107.8 1.2 collective-permute-start.16
  109.0 3.7 %collective-permute-start.17 = (f32[3,8]{1,0:T(4,128)S(1)}, f32[3,8]{1,0:T(4,128)S(1)}, u32[]{:S(2)}, u32[]{:S(2)}) collective-permute-start(f32[3,8]{1,0:T(4,128)S(1)} %pad_maximum_fusion.1), channel_id=1, source_target_pairs={{0,2},{1,3},{2,0},{3,1},{4,6},{5,7},{6,4},{7,5},{8,10},{9,11},{10,... | collective-permute-start | bytes 296 | tf_op jit(solution)/shard_map/ppermute | solution.py:64
  112.7 3.7 %collective-permute-start.18 = (f32[3,8]{1,0:T(4,128)S(1)}, f32[3,8]{1,0:T(4,128)S(1)}, u32[]{:S(2)}, u32[]{:S(2)}) collective-permute-start(f32[3,8]{1,0:T(4,128)S(1)} %pad_maximum_fusion.2), channel_id=1, source_target_pairs={{0,4},{4,0},{8,12},{12,8},{16,20},{20,16},{24,28},{28,24},{1,5},{5... | collective-permute-start | bytes 296 | tf_op jit(solution)/shard_map/ppermute | solution.py:64
  116.4 3.7 %collective-permute-start.19 = (f32[3,8]{1,0:T(4,128)S(1)}, f32[3,8]{1,0:T(4,128)S(1)}, u32[]{:S(2)}, u32[]{:S(2)}) collective-permute-start(f32[3,8]{1,0:T(4,128)S(1)} %pad_maximum_fusion.3), channel_id=1, source_target_pairs={{0,8},{4,12},{8,0},{12,4},{16,24},{20,28},{24,16},{28,20},{1,9},{5... | collective-permute-start | bytes 296 | tf_op jit(solution)/shard_map/ppermute | solution.py:64
  120.1 4.5 %collective-permute-start.20 = (f32[3,8]{1,0:T(4,128)S(1)}, f32[3,8]{1,0:T(4,128)S(1)}, u32[]{:S(2)}, u32[]{:S(2)}) collective-permute-start(f32[3,8]{1,0:T(4,128)S(1)} %pad_maximum_fusion.4), channel_id=1, source_target_pairs={{0,16},{4,20},{8,24},{12,28},{16,0},{20,4},{24,8},{28,12},{1,17},{... | collective-permute-start | bytes 296 | tf_op jit(solution)/shard_map/ppermute | solution.py:64
  (10 other events, 67.8 us)

commit v12 on v10

--- a/solution.py
+++ b/solution.py
@@ -34,6 +34,20 @@
     index = lax.axis_index(axis)
     bit = 1
     while bit < count:
+        other = lax.ppermute(x, axis, xor_pairs(count, bit))
+        low = (index & bit) == 0
+        x = jnp.where(
+            low, jnp.concatenate([x, other], dim), jnp.concatenate([other, x], dim)
+        )
+        bit *= 2
+    return x
+
+
+def butterfly_gather_below(x, axis, dim, stop):
+    count = lax.axis_size(axis)
+    index = lax.axis_index(axis)
+    bit = 1
+    while bit < stop:
         other = lax.ppermute(x, axis, xor_pairs(count, bit))
         low = (index & bit) == 0
         x = jnp.where(
@@ -250,17 +264,42 @@
         last_residual.astype(jnp.float32)
         + jnp.dot(last_mixed, w_out, preferred_element_type=jnp.float32)
     ).astype(jnp.bfloat16)
-    full_hidden = butterfly_gather(butterfly_gather(last_hidden, "gy", 1), "gx", 1).astype(
-        jnp.float32
-    )
-    normed = (
-        full_hidden
-        * lax.rsqrt(jnp.mean(full_hidden * full_hidden, axis=1, keepdims=True) + 1e-06)
-        * norm_gain.astype(jnp.float32)
-    ).astype(jnp.bfloat16)
-    logits = lax.dot_general(
-        normed, head, (((1,), (1,)), ((), ())), preferred_element_type=jnp.float32
-    )
+    gy_hidden = butterfly_gather(last_hidden, "gy", 1)
+    gx_count = lax.axis_size("gx")
+    if is_pow2(gx_count) and gx_count > 1:
+        half_bit = gx_count // 2
+        held = butterfly_gather_below(gy_hidden, "gx", 1, half_bit)
+        other = lax.ppermute(held, "gx", xor_pairs(gx_count, half_bit))
+        upper = (lax.axis_index("gx") & half_bit) != 0
+        half = held.shape[1]
+        gain = norm_gain.astype(jnp.float32)
+
+        def part(rows, first):
+            scaled = (rows.astype(jnp.float32) * gain[first : first + half]).astype(jnp.bfloat16)
+            return lax.dot_general(
+                scaled,
+                head[:, first : first + half],
+                (((1,), (1,)), ((), ())),
+                preferred_element_type=jnp.float32,
+            )
+
+        held_part = lax.cond(upper, lambda x: part(x, half), lambda x: part(x, 0), held)
+        other_part = lax.cond(upper, lambda x: part(x, 0), lambda x: part(x, half), other)
+        full_hidden = jnp.where(
+            upper, jnp.concatenate([other, held], 1), jnp.concatenate([held, other], 1)
+        ).astype(jnp.float32)
+        scale = lax.rsqrt(jnp.mean(full_hidden * full_hidden, axis=1, keepdims=True) + 1e-06)
+        logits = (held_part + other_part) * scale
+    else:
+        full_hidden = butterfly_gather(gy_hidden, "gx", 1).astype(jnp.float32)
+        normed = (
+            full_hidden
+            * lax.rsqrt(jnp.mean(full_hidden * full_hidden, axis=1, keepdims=True) + 1e-06)
+            * norm_gain.astype(jnp.float32)
+        ).astype(jnp.bfloat16)
+        logits = lax.dot_general(
+            normed, head, (((1,), (1,)), ((), ())), preferred_element_type=jnp.float32
+        )
     vocab_local = head.shape[0]
     local_target = targets - lax.axis_index(("gx", "gy")) * vocab_local
     target_hit = jnp.arange(vocab_local, dtype=jnp.int32)[None, :] == local_target[:, None]

time: 116 us -> 116 us (level)
  starting transfers between devices: 21.4 us -> 19.7 us
  matrix products: 18.1 us -> 19.5 us
    ppermute x8 -> x5, waiting for transfers between devices: 12.4 us -> 3.33 us  [butterfly_gather(): other = lax.ppermute(x, axis, xor_pairs(count, bit))]
    ppermute x0 -> x3, waiting for transfers between devices: none -> 6.48 us  [the longest x2 6.48 us: butterfly_gather_below(): other = lax.ppermute(x, axis, xor_pairs(count, bit))]
    ppermute x0 -> x3, starting transfers between devices: none -> 3.31 us  [the longest x1 2.48 us: on_device(): other = lax.ppermute(held, 'gx', xor_pairs(gx_count, half_bit))]
    ppermute x8 -> x5, starting transfers between devices: 10.8 us -> 7.58 us  [butterfly_gather(): other = lax.ppermute(x, axis, xor_pairs(count, bit))]
    dot_general x1 -> x2, matrix products: 17.2 us -> 19.3 us  [part(): lax.dot_general(scaled, head[:, first:first + half], (((1,), (1,)), ((),...]
    ppermute x5, waiting for transfers between devices: 11.7 us -> 13.4 us  [butterfly_stats(): other = lax.ppermute(packed, axis, xor_pairs(count, bit))]
    ppermute x5, starting transfers between devices: 5.05 us -> 3.29 us  [butterfly_stats(): other = lax.ppermute(packed, axis, xor_pairs(count, bit))]
  transfers between devices with their start and end apart: 21 -> 21, of which waited for: 16 -> 15; matrix products, arithmetic and copies ran while one was open for 17% -> 25% of each run, Pallas kernels for 0% -> 0%
where the time goes in v12:
time: 116 us; the launch traced here: 115 us
  waiting for transfers between devices  29.5 us (25%)
  starting transfers between devices  19.7 us (17%)
  matrix products  19.5 us (17%)
  other arithmetic  17.7 us (15%)
  Pallas kernels  16.3 us (14%)
  local copies, waits for them, and re-layouts  7.96 us (7%)
  between operations  4.6 us (4%)
    dot_general x2, matrix products, part(): lax.dot_general(scaled, head[:, first:first + half], (((1,), (1,)), ((),...  19.3 us
    pallas_call x1, Pallas kernels, attend(): pl.pallas_call(kernel, grid=(req_local, head_count // stacked), in_specs=...  16.3 us
    ppermute x5, waiting for transfers between devices, butterfly_stats(): other = lax.ppermute(packed, axis, xor_pairs(count, bit))  13.4 us
    ppermute x5, starting transfers between devices, butterfly_gather(): other = lax.ppermute(x, axis, xor_pairs(count, bit))  7.58 us
    ppermute x2, waiting for transfers between devices, butterfly_gather_below(): other = lax.ppermute(x, axis, xor_pairs(count, bit))  6.48 us
    ppermute x5, waiting for transfers between devices, butterfly_gather(): other = lax.ppermute(x, axis, xor_pairs(count, bit))  3.33 us
    ppermute x5, starting transfers between devices, butterfly_stats(): other = lax.ppermute(packed, axis, xor_pairs(count, bit))  3.29 us
    ppermute x2, starting transfers between devices, exchange_pieces(): other = lax.ppermute(held, axis, xor_pairs(count, bit))  3.16 us
  transfers between devices with their start and end apart: 21, of which 15 were waited for; matrix products, arithmetic and copies ran while one was open for 25% of the time, Pallas kernels for 0%

profile of v12, /device:TPU:0, one launch (start us, length us, event | category | flops | bytes accessed | tf_op | source)
XLA Modules:
  0.0 115.4 jit_solution(17034304922060380565)
XLA Ops:
  0.7 3.0 %collective-permute-start.1 = (bf16[1,512,512]{2,1,0:T(8,128)(2,1)}, bf16[1,512,512]{2,1,0:T(8,128)(2,1)S(1)}, u32[]{:S(2)}, u32[]{:S(2)}) collective-permute-start(bf16[1,512,512]{2,1,0:T(8,128)(2,1)} %refs_10_.1), channel_id=1, source_target_pairs={{0,2},{1,3},{2,0},{3,1},{4,6},{5,7},{6,4},{7,5},{8,10},{9,11},{10,... | collective-permute-start | bytes 1572872 | tf_op jit(solution)/shard_map/ppermute | solution.py:95
  12.5 2.7 %compare_select_fusion.3 = (s32[512,1]{0,1:T(1,128)S(1)}, s32[1,512]{1,0:T(1,128)S(1)}, s32[512,1]{0,1:T(1,128)S(1)}) fusion(s32[]{:T(128)} %axis_index.14, s32[]{:T(128)} %bitcast.20, s32[]{:T(128)} %bitcast.19, s32[]{:T(128)} %bitcast.18, s32[]{:T(128)} %bitcast.17, s32[]{:T(128)} %bitcast.16), kind=kLoop, calls=%fused_computation.40 | loop fusion | flops 55296 | bytes 6168 | tf_op jit(solution)/shard_map/jit(take_along_axis)/select_n | solution.py:253
  17.8 2.2 %collective-permute-done.4.refs_23_.refs_24_ = bf16[1,192,512]{2,1,0:T(8,128)(2,1)S(1)} collective-permute-done((bf16[1,192,512]{2,1,0:T(8,128)(2,1)}, bf16[1,192,512]{2,1,0:T(8,128)(2,1)S(1)}, u32[]{:S(2)}, u32[]{:S(2)}) %collective-permute-start.4) | collective-permute-done | bytes 196640 | tf_op jit(solution)/shard_map/ppermute | solution.py:95
  22.5 16.3 %shard_map.230 = bf16[1,192,2560]{2,1,0:T(8,128)(2,1)} custom-call(s32[192,1]{1,0:T(8,128)} %iota_add_fusion.qpos_ref, s32[1,1,512]{2,1,0:T(1,128)} %get-tuple-element.130.refs_0_, s32[1,1,512]{2,1,0:T(1,128)} %get-tuple-element.129.refs_1_, s32[1,1,512]{2,1,0:T(1,128)} %get-tuple-element.128.refs_2_, s32[1,1,512]{2,1,0:T(1,128)} %get-tuple-element.127.refs_3_, ...), custom_call_target="tpu_custom_call" | custom-call | tf_op jit(solution)/shard_map/pallas_call | solution.py:182
  41.7 1.8 %collective-permute-start.7 = (bf16[1,2560]{1,0:T(2,128)(2,1)S(1)}, bf16[1,2560]{1,0:T(2,128)(2,1)S(1)}, u32[]{:S(2)}, u32[]{:S(2)}) collective-permute-start(bf16[1,2560]{1,0:T(2,128)(2,1)S(1)} %fusion.44), channel_id=1, source_target_pairs={{0,2},{1,3},{2,0},{3,1},{4,6},{5,7},{6,4},{7,5},{8,10},{9,11},{10,... | collective-permute-start | bytes 15368 | tf_op jit(solution)/shard_map/ppermute | solution.py:25
  43.5 1.9 %collective-permute-done.7 = bf16[1,2560]{1,0:T(2,128)(2,1)S(1)} collective-permute-done((bf16[1,2560]{1,0:T(2,128)(2,1)S(1)}, bf16[1,2560]{1,0:T(2,128)(2,1)S(1)}, u32[]{:S(2)}, u32[]{:S(2)}) %collective-permute-start.7) | collective-permute-done | bytes 5152 | tf_op jit(solution)/shard_map/ppermute | solution.py:25
  45.5 1.8 %collective-permute-start.8 = (bf16[1,2560]{1,0:T(2,128)(2,1)S(1)}, bf16[1,2560]{1,0:T(2,128)(2,1)S(1)}, u32[]{:S(2)}, u32[]{:S(2)}) collective-permute-start(bf16[1,2560]{1,0:T(2,128)(2,1)S(1)} %add.591), channel_id=1, source_target_pairs={{0,4},{4,0},{8,12},{12,8},{16,20},{20,16},{24,28},{28,24},{1,5},{5... | collective-permute-start | bytes 15368 | tf_op jit(solution)/shard_map/ppermute | solution.py:37
  48.5 2.6 %gather_fusion.1 = bf16[512,512]{1,0:T(8,128)(2,1)} fusion(bf16[768,512]{1,0:T(8,128)(2,1)S(1)} %maximum_bitcast_fusion.1, s32[1024]{0:T(1024)S(1)} %pad_clamp_fusion), kind=kCustom, calls=%fused_computation.1 | custom fusion | bytes 1050624 | tf_op jit(solution)/shard_map/jit(take_along_axis)/gather | solution.py:254
  51.8 1.6 %collective-permute-start.9 = (bf16[2,2560]{1,0:T(2,128)(2,1)}, bf16[2,2560]{1,0:T(2,128)(2,1)}, u32[]{:S(2)}, u32[]{:S(2)}) collective-permute-start(bf16[2,2560]{1,0:T(2,128)(2,1)} %broadcast_select_fusion.1), channel_id=1, source_target_pairs={{0,8},{4,12},{8,0},{12,4},{16,24},{20,28},{24,16},{28,20},{1,9},{5... | collective-permute-start | bytes 30728 | tf_op jit(solution)/shard_map/ppermute | solution.py:37
  54.7 2.2 %gather_fusion = bf16[512,512]{1,0:T(8,128)(2,1)S(1)} fusion(bf16[2048,512]{1,0:T(8,128)(2,1)S(1)} %maximum_bitcast_fusion, s32[1024]{0:T(1024)} %pad_clamp_fusion.1), kind=kCustom, calls=%fused_computation | custom fusion | bytes 1050624 | tf_op jit(solution)/shard_map/jit(take_along_axis)/gather | solution.py:253
  57.8 2.7 %collective-permute-start.10 = (bf16[4,2560]{1,0:T(4,128)(2,1)S(1)}, bf16[4,2560]{1,0:T(4,128)(2,1)S(1)}, u32[]{:S(2)}, u32[]{:S(2)}) collective-permute-start(bf16[4,2560]{1,0:T(4,128)(2,1)S(1)} %maximum_select_fusion.2), channel_id=1, source_target_pairs={{0,16},{4,20},{8,24},{12,28},{16,0},{20,4},{24,8},{28,12},{1,17},{... | collective-permute-start | bytes 61448 | tf_op jit(solution)/shard_map/ppermute | solution.py:37
  60.5 2.1 %fusion.13 = bf16[1,512,512]{2,1,0:T(8,128)(2,1)} fusion(bf16[512,512]{1,0:T(8,128)(2,1)} %gather_fusion.1, bf16[512,512]{1,0:T(8,128)(2,1)S(1)} %gather_fusion, pred[512]{0:T(512)(128)(4,1)} %get-tuple-element.136, pred[512]{0:T(512)(128)(4,1)} %compare_and_fusion.1, pred[512]{0:T(512)(128)(4,1)} %get-tuple-element.135), kind=kLoop, calls=%fused_computation.23 | loop fusion | flops 786432 | bytes 1574400 | tf_op jit(solution)/shard_map/jit(_where)/select_n | solution.py:255
  65.7 2.1 %collective-permute-done.12 = bf16[8,160]{1,0:T(8,128)(2,1)S(1)} collective-permute-done((bf16[8,160]{1,0:T(8,128)(2,1)S(1)}, bf16[8,160]{1,0:T(8,128)(2,1)S(1)}, u32[]{:S(2)}, u32[]{:S(2)}) %collective-permute-start.12) | collective-permute-done | bytes 2592 | tf_op jit(solution)/shard_map/ppermute | solution.py:37
  68.3 3.2 %collective-permute-done.13 = bf16[8,320]{1,0:T(8,128)(2,1)S(1)} collective-permute-done((bf16[8,320]{1,0:T(8,128)(2,1)S(1)}, bf16[8,320]{1,0:T(8,128)(2,1)S(1)}, u32[]{:S(2)}, u32[]{:S(2)}) %collective-permute-start.13) | collective-permute-done | bytes 5152 | tf_op jit(solution)/shard_map/ppermute | solution.py:51
  72.0 3.3 %collective-permute-done.14 = bf16[8,640]{1,0:T(8,128)(2,1)S(1)} collective-permute-done((bf16[8,640]{1,0:T(8,128)(2,1)S(1)}, bf16[8,640]{1,0:T(8,128)(2,1)S(1)}, u32[]{:S(2)}, u32[]{:S(2)}) %collective-permute-start.14) | collective-permute-done | bytes 10272 | tf_op jit(solution)/shard_map/ppermute | solution.py:51
  75.3 2.5 %collective-permute-start.15 = (bf16[8,1280]{1,0:T(8,128)(2,1)S(1)}, bf16[8,1280]{1,0:T(8,128)(2,1)S(1)}, u32[]{:S(2)}, u32[]{:S(2)}) collective-permute-start(bf16[8,1280]{1,0:T(8,128)(2,1)S(1)} %maximum_select_fusion.3), channel_id=1, source_target_pairs={{0,16},{4,20},{8,24},{12,28},{16,0},{20,4},{24,8},{28,12},{1,17},{... | collective-permute-start | bytes 61448 | tf_op jit(solution)/shard_map/ppermute | solution.py:272
  77.8 9.7 %conditional.2 = (f32[8,8000]{1,0:T(8,128)S(1)}) conditional(s32[]{:T(128)} %convert_element_type.40, (bf16[8,1280]{1,0:T(8,128)(2,1)S(1)}, f32[2560]{0:T(1024)S(1)}, bf16[8000,2560]{1,0:T(8,128)(2,1)}) %tuple.23, (bf16[8,1280]{1,0:T(8,128)(2,1)S(1)}, f32[2560]{0:T(1024)S(1)}, bf16[8000,2560]{1,0:T(8,128)(2,1)}) %tuple.23), branch_computations={%region_1.3_spmd, %region_2.4_spmd} | conditional | flops 163870720 | bytes 20771848 | solution.py:286
  77.8 9.6 %fusion = f32[8,8000]{1,0:T(8,128)S(1)} fusion(bf16[8000,2560]{1,0:T(8,128)(2,1)} %get-tuple-element.29, bf16[8,1280]{1,0:T(8,128)(2,1)S(1)} %get-tuple-element.27, f32[1280]{0:T(1024)S(1)} %slice.48), kind=kOutput, calls=%fused_computation.2 | convolution fusion | flops 163870720 | bytes 20761600 | tf_op jit(solution)/shard_map/cond/branch_0_fun/dot_general | solution.py:279
  87.5 9.7 %conditional.3 = (f32[8,8000]{1,0:T(8,128)S(1)}) conditional(s32[]{:T(128)} %convert_element_type.40, (bf16[8,1280]{1,0:T(8,128)(2,1)S(1)}, f32[2560]{0:T(1024)S(1)}, bf16[8000,2560]{1,0:T(8,128)(2,1)}) %tuple.24, (bf16[8,1280]{1,0:T(8,128)(2,1)S(1)}, f32[2560]{0:T(1024)S(1)}, bf16[8000,2560]{1,0:T(8,128)(2,1)}) %tuple.24), branch_computations={%region_3.5_spmd, %region_4.6_spmd} | conditional | flops 163870720 | bytes 20771848 | solution.py:287
  87.5 9.7 %fusion.6 = f32[8,8000]{1,0:T(8,128)S(1)} fusion(bf16[8000,2560]{1,0:T(8,128)(2,1)} %get-tuple-element.39, bf16[8,1280]{1,0:T(8,128)(2,1)S(1)} %get-tuple-element.37, f32[1280]{0:T(1024)S(1)} %slice.52), kind=kOutput, calls=%fused_computation.10 | convolution fusion | flops 163870720 | bytes 20761600 | tf_op jit(solution)/shard_map/cond/branch_0_fun/dot_general | solution.py:279
  100.8 2.1 %collective-permute-done.17 = f32[3,8]{1,0:T(4,128)S(1)} collective-permute-done((f32[3,8]{1,0:T(4,128)S(1)}, f32[3,8]{1,0:T(4,128)S(1)}, u32[]{:S(2)}, u32[]{:S(2)}) %collective-permute-start.17) | collective-permute-done | bytes 128 | tf_op jit(solution)/shard_map/ppermute | solution.py:78
  103.5 3.1 %collective-permute-done.18 = f32[3,8]{1,0:T(4,128)S(1)} collective-permute-done((f32[3,8]{1,0:T(4,128)S(1)}, f32[3,8]{1,0:T(4,128)S(1)}, u32[]{:S(2)}, u32[]{:S(2)}) %collective-permute-start.18) | collective-permute-done | bytes 128 | tf_op jit(solution)/shard_map/ppermute | solution.py:78
  107.1 3.1 %collective-permute-done.19 = f32[3,8]{1,0:T(4,128)S(1)} collective-permute-done((f32[3,8]{1,0:T(4,128)S(1)}, f32[3,8]{1,0:T(4,128)S(1)}, u32[]{:S(2)}, u32[]{:S(2)}) %collective-permute-start.19) | collective-permute-done | bytes 128 | tf_op jit(solution)/shard_map/ppermute | solution.py:78
  110.8 4.0 %collective-permute-done.20 = f32[3,8]{1,0:T(4,128)S(1)} collective-permute-done((f32[3,8]{1,0:T(4,128)S(1)}, f32[3,8]{1,0:T(4,128)S(1)}, u32[]{:S(2)}, u32[]{:S(2)}) %collective-permute-start.20) | collective-permute-done | bytes 128 | tf_op jit(solution)/shard_map/ppermute | solution.py:78
  (97 shorter events, 27.0 us)
Async XLA Ops:
  0.6 62.1 %copy-start = (bf16[2560,80]{0,1:T(8,128)(2,1)S(1)}, bf16[2560,80]{0,1:T(8,128)(2,1)}, u32[]{:S(2)}) copy-start(bf16[2560,80]{0,1:T(8,128)(2,1)} %param.31) | copy-start | bytes 1228804
  0.6 46.7 %copy-start.6 = (bf16[1,192,512]{2,1,0:T(8,128)(2,1)S(1)}, bf16[1,192,512]{2,1,0:T(8,128)(2,1)}, u32[]{:S(2)}) copy-start(bf16[1,192,512]{2,1,0:T(8,128)(2,1)} %refs_18_.1) | copy-start | bytes 589828
  0.7 16.0 %collective-permute-start.1 = (bf16[1,512,512]{2,1,0:T(8,128)(2,1)}, bf16[1,512,512]{2,1,0:T(8,128)(2,1)S(1)}, u32[]{:S(2)}, u32[]{:S(2)}) collective-permute-start(bf16[1,512,512]{2,1,0:T(8,128)(2,1)} %refs_10_.1), channel_id=1, source_target_pairs={{0,2},{1,3},{2,0},{3,1},{4,6},{5,7},{6,4},{7,5},{8,10},{9,11},{10,... | collective-permute-start | bytes 1572872 | tf_op jit(solution)/shard_map/ppermute | solution.py:95
  3.7 17.8 %collective-permute-start = (bf16[1,512,512]{2,1,0:T(8,128)(2,1)}, bf16[1,512,512]{2,1,0:T(8,128)(2,1)S(1)}, u32[]{:S(2)}, u32[]{:S(2)}) collective-permute-start(bf16[1,512,512]{2,1,0:T(8,128)(2,1)} %refs_10_.1), channel_id=1, source_target_pairs={{0,1},{1,0},{2,3},{3,2},{4,5},{5,4},{6,7},{7,6},{8,9},{9,8},{10,11... | collective-permute-start | bytes 1572872 | tf_op jit(solution)/shard_map/ppermute | solution.py:91
  3.7 16.3 %collective-permute-start.4 = (bf16[1,192,512]{2,1,0:T(8,128)(2,1)}, bf16[1,192,512]{2,1,0:T(8,128)(2,1)S(1)}, u32[]{:S(2)}, u32[]{:S(2)}) collective-permute-start(bf16[1,192,512]{2,1,0:T(8,128)(2,1)} %refs_18_.1), channel_id=1, source_target_pairs={{0,2},{1,3},{2,0},{3,1},{4,6},{5,7},{6,4},{7,5},{8,10},{9,11},{10,... | collective-permute-start | bytes 589832 | tf_op jit(solution)/shard_map/ppermute | solution.py:95
  3.8 16.8 %collective-permute-start.3 = (bf16[1,192,512]{2,1,0:T(8,128)(2,1)}, bf16[1,192,512]{2,1,0:T(8,128)(2,1)S(1)}, u32[]{:S(2)}, u32[]{:S(2)}) collective-permute-start(bf16[1,192,512]{2,1,0:T(8,128)(2,1)} %refs_18_.1), channel_id=1, source_target_pairs={{0,1},{1,0},{2,3},{3,2},{4,5},{5,4},{6,7},{7,6},{8,9},{9,8},{10,11... | collective-permute-start | bytes 589832 | tf_op jit(solution)/shard_map/ppermute | solution.py:91
  16.6 4.8 %collective-permute-start.2 = (bf16[1,512,512]{2,1,0:T(8,128)(2,1)S(1)}, bf16[1,512,512]{2,1,0:T(8,128)(2,1)S(1)}, u32[]{:S(2)}, u32[]{:S(2)}) collective-permute-start(bf16[1,512,512]{2,1,0:T(8,128)(2,1)S(1)} %collective-permute-done.1.refs_15_.refs_16_), channel_id=1, source_target_pairs={{0,1},{1,0},{2,3},{3,2},{4,5},{5,4},{6,7},{7,6},{8,9},{9,8},{10,11... | collective-permute-start | bytes 1572872 | tf_op jit(solution)/shard_map/ppermute | solution.py:105
  20.0 1.4 %collective-permute-start.5 = (bf16[1,192,512]{2,1,0:T(8,128)(2,1)S(1)}, bf16[1,192,512]{2,1,0:T(8,128)(2,1)S(1)}, u32[]{:S(2)}, u32[]{:S(2)}) collective-permute-start(bf16[1,192,512]{2,1,0:T(8,128)(2,1)S(1)} %collective-permute-done.4.refs_23_.refs_24_), channel_id=1, source_target_pairs={{0,1},{1,0},{2,3},{3,2},{4,5},{5,4},{6,7},{7,6},{8,9},{9,8},{10,11... | collective-permute-start | bytes 589832 | tf_op jit(solution)/shard_map/ppermute | solution.py:105
  39.7 1.2 %collective-permute-start.6 = (bf16[1,2560]{1,0:T(2,128)(2,1)S(1)}, bf16[1,2560]{1,0:T(2,128)(2,1)S(1)}, u32[]{:S(2)}, u32[]{:S(2)}) collective-permute-start(bf16[1,2560]{1,0:T(2,128)(2,1)S(1)} %fusion.14), channel_id=1, source_target_pairs={{0,1},{1,0},{2,3},{3,2},{4,5},{5,4},{6,7},{7,6},{8,9},{9,8},{10,11... | collective-permute-start | bytes 15368 | tf_op jit(solution)/shard_map/ppermute | solution.py:25
  41.7 3.7 %collective-permute-start.7 = (bf16[1,2560]{1,0:T(2,128)(2,1)S(1)}, bf16[1,2560]{1,0:T(2,128)(2,1)S(1)}, u32[]{:S(2)}, u32[]{:S(2)}) collective-permute-start(bf16[1,2560]{1,0:T(2,128)(2,1)S(1)} %fusion.44), channel_id=1, source_target_pairs={{0,2},{1,3},{2,0},{3,1},{4,6},{5,7},{6,4},{7,5},{8,10},{9,11},{10,... | collective-permute-start | bytes 15368 | tf_op jit(solution)/shard_map/ppermute | solution.py:25
  45.5 5.6 %collective-permute-start.8 = (bf16[1,2560]{1,0:T(2,128)(2,1)S(1)}, bf16[1,2560]{1,0:T(2,128)(2,1)S(1)}, u32[]{:S(2)}, u32[]{:S(2)}) collective-permute-start(bf16[1,2560]{1,0:T(2,128)(2,1)S(1)} %add.591), channel_id=1, source_target_pairs={{0,4},{4,0},{8,12},{12,8},{16,20},{20,16},{24,28},{28,24},{1,5},{5... | collective-permute-start | bytes 15368 | tf_op jit(solution)/shard_map/ppermute | solution.py:37
  51.8 5.2 %collective-permute-start.9 = (bf16[2,2560]{1,0:T(2,128)(2,1)}, bf16[2,2560]{1,0:T(2,128)(2,1)}, u32[]{:S(2)}, u32[]{:S(2)}) collective-permute-start(bf16[2,2560]{1,0:T(2,128)(2,1)} %broadcast_select_fusion.1), channel_id=1, source_target_pairs={{0,8},{4,12},{8,0},{12,4},{16,24},{20,28},{24,16},{28,20},{1,9},{5... | collective-permute-start | bytes 30728 | tf_op jit(solution)/shard_map/ppermute | solution.py:37
  54.7 23.1 %copy-start.12 = (s32[8]{0:T(128)S(1)}, s32[8]{0:T(128)}, u32[]{:S(2)}) copy-start(s32[8]{0:T(128)} %param.35) | copy-start | bytes 100
  57.8 4.9 %collective-permute-start.10 = (bf16[4,2560]{1,0:T(4,128)(2,1)S(1)}, bf16[4,2560]{1,0:T(4,128)(2,1)S(1)}, u32[]{:S(2)}, u32[]{:S(2)}) collective-permute-start(bf16[4,2560]{1,0:T(4,128)(2,1)S(1)} %maximum_select_fusion.2), channel_id=1, source_target_pairs={{0,16},{4,20},{8,24},{12,28},{16,0},{20,4},{24,8},{28,12},{1,17},{... | collective-permute-start | bytes 61448 | tf_op jit(solution)/shard_map/ppermute | solution.py:37
  62.9 1.2 %collective-permute-start.11 = (bf16[8,80]{1,0:T(8,128)(2,1)S(1)}, bf16[8,80]{1,0:T(8,128)(2,1)S(1)}, u32[]{:S(2)}, u32[]{:S(2)}) collective-permute-start(bf16[8,80]{1,0:T(8,128)(2,1)S(1)} %fusion.12), channel_id=1, source_target_pairs={{0,1},{1,0},{2,3},{3,2},{4,5},{5,4},{6,7},{7,6},{8,9},{9,8},{10,11... | collective-permute-start | bytes 3848 | tf_op jit(solution)/shard_map/ppermute | solution.py:37
  64.2 3.6 %collective-permute-start.12 = (bf16[8,160]{1,0:T(8,128)(2,1)S(1)}, bf16[8,160]{1,0:T(8,128)(2,1)S(1)}, u32[]{:S(2)}, u32[]{:S(2)}) collective-permute-start(bf16[8,160]{1,0:T(8,128)(2,1)S(1)} %maximum_select_fusion.6), channel_id=1, source_target_pairs={{0,2},{1,3},{2,0},{3,1},{4,6},{5,7},{6,4},{7,5},{8,10},{9,11},{10,... | collective-permute-start | bytes 7688 | tf_op jit(solution)/shard_map/ppermute | solution.py:37
  67.9 3.6 %collective-permute-start.13 = (bf16[8,320]{1,0:T(8,128)(2,1)S(1)}, bf16[8,320]{1,0:T(8,128)(2,1)S(1)}, u32[]{:S(2)}, u32[]{:S(2)}) collective-permute-start(bf16[8,320]{1,0:T(8,128)(2,1)S(1)} %maximum_select_fusion.5), channel_id=1, source_target_pairs={{0,4},{4,0},{8,12},{12,8},{16,20},{20,16},{24,28},{28,24},{1,5},{5... | collective-permute-start | bytes 15368 | tf_op jit(solution)/shard_map/ppermute | solution.py:51
  71.6 3.7 %collective-permute-start.14 = (bf16[8,640]{1,0:T(8,128)(2,1)S(1)}, bf16[8,640]{1,0:T(8,128)(2,1)S(1)}, u32[]{:S(2)}, u32[]{:S(2)}) collective-permute-start(bf16[8,640]{1,0:T(8,128)(2,1)S(1)} %maximum_select_fusion.4), channel_id=1, source_target_pairs={{0,8},{4,12},{8,0},{12,4},{16,24},{20,28},{24,16},{28,20},{1,9},{5... | collective-permute-start | bytes 30728 | tf_op jit(solution)/shard_map/ppermute | solution.py:51
  75.3 12.2 %collective-permute-start.15 = (bf16[8,1280]{1,0:T(8,128)(2,1)S(1)}, bf16[8,1280]{1,0:T(8,128)(2,1)S(1)}, u32[]{:S(2)}, u32[]{:S(2)}) collective-permute-start(bf16[8,1280]{1,0:T(8,128)(2,1)S(1)} %maximum_select_fusion.3), channel_id=1, source_target_pairs={{0,16},{4,20},{8,24},{12,28},{16,0},{20,4},{24,8},{28,12},{1,17},{... | collective-permute-start | bytes 61448 | tf_op jit(solution)/shard_map/ppermute | solution.py:272
  98.0 1.2 %collective-permute-start.16 = (f32[3,8]{1,0:T(4,128)S(1)}, f32[3,8]{1,0:T(4,128)S(1)}, u32[]{:S(2)}, u32[]{:S(2)}) collective-permute-start(f32[3,8]{1,0:T(4,128)S(1)} %pad_maximum_fusion), channel_id=1, source_target_pairs={{0,1},{1,0},{2,3},{3,2},{4,5},{5,4},{6,7},{7,6},{8,9},{9,8},{10,11... | collective-permute-start | bytes 296 | tf_op jit(solution)/shard_map/ppermute | solution.py:78
  99.2 3.7 %collective-permute-start.17 = (f32[3,8]{1,0:T(4,128)S(1)}, f32[3,8]{1,0:T(4,128)S(1)}, u32[]{:S(2)}, u32[]{:S(2)}) collective-permute-start(f32[3,8]{1,0:T(4,128)S(1)} %pad_maximum_fusion.1), channel_id=1, source_target_pairs={{0,2},{1,3},{2,0},{3,1},{4,6},{5,7},{6,4},{7,5},{8,10},{9,11},{10,... | collective-permute-start | bytes 296 | tf_op jit(solution)/shard_map/ppermute | solution.py:78
  102.9 3.7 %collective-permute-start.18 = (f32[3,8]{1,0:T(4,128)S(1)}, f32[3,8]{1,0:T(4,128)S(1)}, u32[]{:S(2)}, u32[]{:S(2)}) collective-permute-start(f32[3,8]{1,0:T(4,128)S(1)} %pad_maximum_fusion.2), channel_id=1, source_target_pairs={{0,4},{4,0},{8,12},{12,8},{16,20},{20,16},{24,28},{28,24},{1,5},{5... | collective-permute-start | bytes 296 | tf_op jit(solution)/shard_map/ppermute | solution.py:78
  106.6 3.7 %collective-permute-start.19 = (f32[3,8]{1,0:T(4,128)S(1)}, f32[3,8]{1,0:T(4,128)S(1)}, u32[]{:S(2)}, u32[]{:S(2)}) collective-permute-start(f32[3,8]{1,0:T(4,128)S(1)} %pad_maximum_fusion.3), channel_id=1, source_target_pairs={{0,8},{4,12},{8,0},{12,4},{16,24},{20,28},{24,16},{28,20},{1,9},{5... | collective-permute-start | bytes 296 | tf_op jit(solution)/shard_map/ppermute | solution.py:78
  110.3 4.5 %collective-permute-start.20 = (f32[3,8]{1,0:T(4,128)S(1)}, f32[3,8]{1,0:T(4,128)S(1)}, u32[]{:S(2)}, u32[]{:S(2)}) collective-permute-start(f32[3,8]{1,0:T(4,128)S(1)} %pad_maximum_fusion.4), channel_id=1, source_target_pairs={{0,16},{4,20},{8,24},{12,28},{16,0},{20,4},{24,8},{28,12},{1,17},{... | collective-permute-start | bytes 296 | tf_op jit(solution)/shard_map/ppermute | solution.py:78
  (10 other events, 70.0 us)

commit v13 on v12

--- a/solution.py
+++ b/solution.py
@@ -258,12 +258,35 @@
     group_req = lax.axis_size("gx")
     holder = my_index == group_pos - 1
     last_local = jnp.where(holder, last_local, jnp.zeros_like(last_local))
-    last_mixed = butterfly_gather(butterfly_sum(last_local, "gy"), "gx", 0)
-    last_mixed, fresh_block = lax.optimization_barrier((last_mixed, fresh_block))
-    last_hidden = (
-        last_residual.astype(jnp.float32)
-        + jnp.dot(last_mixed, w_out, preferred_element_type=jnp.float32)
-    ).astype(jnp.bfloat16)
+    row_sum = butterfly_sum(last_local, "gy")
+    gx_count = lax.axis_size("gx")
+
+    def hidden_rows(mixed_rows, residual_rows):
+        return (
+            residual_rows.astype(jnp.float32)
+            + jnp.dot(mixed_rows, w_out, preferred_element_type=jnp.float32)
+        ).astype(jnp.bfloat16)
+
+    if is_pow2(gx_count) and gx_count > 1:
+        half_bit = gx_count // 2
+        held_rows = butterfly_gather_below(row_sum, "gx", 0, half_bit)
+        held_rows, fresh_block = lax.optimization_barrier((held_rows, fresh_block))
+        other_rows = lax.ppermute(held_rows, "gx", xor_pairs(gx_count, half_bit))
+        row_upper = (lax.axis_index("gx") & half_bit) != 0
+        row_half = held_rows.shape[0]
+        low_res = last_residual[:row_half]
+        high_res = last_residual[row_half:]
+        held_hidden = hidden_rows(held_rows, jnp.where(row_upper, high_res, low_res))
+        other_hidden = hidden_rows(other_rows, jnp.where(row_upper, low_res, high_res))
+        last_hidden = jnp.where(
+            row_upper,
+            jnp.concatenate([other_hidden, held_hidden], 0),
+            jnp.concatenate([held_hidden, other_hidden], 0),
+        )
+    else:
+        last_mixed = butterfly_gather(row_sum, "gx", 0)
+        last_mixed, fresh_block = lax.optimization_barrier((last_mixed, fresh_block))
+        last_hidden = hidden_rows(last_mixed, last_residual)
     gy_hidden = butterfly_gather(last_hidden, "gy", 1)
     gx_count = lax.axis_size("gx")
     if is_pow2(gx_count) and gx_count > 1:

time: 116 us -> 116 us (level)
    ppermute x5 -> x2, starting transfers between devices: 7.58 us -> 0.61 us  [butterfly_gather(): other = lax.ppermute(x, axis, xor_pairs(count, bit))]
    ppermute x2 -> x4, starting transfers between devices: 0.83 us -> 5.22 us  [butterfly_gather_below(): other = lax.ppermute(x, axis, xor_pairs(count, bit))]
    ppermute x0 -> x1, starting transfers between devices: none -> 2.66 us  [on_device(): other_rows = lax.ppermute(held_rows, 'gx', xor_pairs(gx_count, half_bit))]
    ppermute x0 -> x1, waiting for transfers between devices: none -> 1.87 us  [on_device(): other_rows = lax.ppermute(held_rows, 'gx', xor_pairs(gx_count, half_bit))]
    select_n x5 -> x2, other arithmetic: 1.66 us -> 0.15 us  [butterfly_gather(): jnp.where(low, jnp.concatenate([x, other], dim), jnp.concatenate([other,...]
    ppermute x2, waiting for transfers between devices: 2.37 us -> 1.03 us  [butterfly_sum(): x = x + lax.ppermute(x, axis, xor_pairs(count, bit))]
    ppermute x2 -> x4, waiting for transfers between devices: 6.48 us -> 5.26 us  [butterfly_gather_below(): other = lax.ppermute(x, axis, xor_pairs(count, bit))]
    ppermute x5 -> x2, waiting for transfers between devices: 3.33 us -> 4.21 us  [butterfly_gather(): other = lax.ppermute(x, axis, xor_pairs(count, bit))]
  transfers between devices with their start and end apart: 21 -> 21, of which waited for: 15 -> 14; matrix products, arithmetic and copies ran while one was open for 25% -> 26% of each run, Pallas kernels for 0% -> 0%
where the time goes in v13:
time: 116 us; the launch traced here: 115 us
  waiting for transfers between devices  29 us (25%)
  starting transfers between devices  20 us (17%)
  matrix products  19.7 us (17%)
  other arithmetic  17.5 us (15%)
  Pallas kernels  16.3 us (14%)
  local copies, waits for them, and re-layouts  8.02 us (7%)
  between operations  4.58 us (4%)
    dot_general x2, matrix products, part(): lax.dot_general(scaled, head[:, first:first + half], (((1,), (1,)), ((),...  19.3 us
    pallas_call x1, Pallas kernels, attend(): pl.pallas_call(kernel, grid=(req_local, head_count // stacked), in_specs=...  16.3 us
    ppermute x5, waiting for transfers between devices, butterfly_stats(): other = lax.ppermute(packed, axis, xor_pairs(count, bit))  13.3 us
    ppermute x4, waiting for transfers between devices, butterfly_gather_below(): other = lax.ppermute(x, axis, xor_pairs(count, bit))  5.26 us
    ppermute x4, starting transfers between devices, butterfly_gather_below(): other = lax.ppermute(x, axis, xor_pairs(count, bit))  5.22 us
    ppermute x2, waiting for transfers between devices, butterfly_gather(): other = lax.ppermute(x, axis, xor_pairs(count, bit))  4.21 us
    ppermute x5, starting transfers between devices, butterfly_stats(): other = lax.ppermute(packed, axis, xor_pairs(count, bit))  3.42 us
    ppermute x2, starting transfers between devices, exchange_pieces(): other = lax.ppermute(held, axis, xor_pairs(count, bit))  3.16 us
  transfers between devices with their start and end apart: 21, of which 14 were waited for; matrix products, arithmetic and copies ran while one was open for 26% of the time, Pallas kernels for 0%

profile of v13, /device:TPU:0, one launch (start us, length us, event | category | flops | bytes accessed | tf_op | source)
XLA Modules:
  0.0 115.3 jit_solution(9945255561688673553)
XLA Ops:
  0.7 3.0 %collective-permute-start.1 = (bf16[1,512,512]{2,1,0:T(8,128)(2,1)}, bf16[1,512,512]{2,1,0:T(8,128)(2,1)S(1)}, u32[]{:S(2)}, u32[]{:S(2)}) collective-permute-start(bf16[1,512,512]{2,1,0:T(8,128)(2,1)} %refs_10_.1), channel_id=1, source_target_pairs={{0,2},{1,3},{2,0},{3,1},{4,6},{5,7},{6,4},{7,5},{8,10},{9,11},{10,... | collective-permute-start | bytes 1572872 | tf_op jit(solution)/shard_map/ppermute | solution.py:95
  10.8 2.5 %compare_select_fusion.3 = (s32[512,1]{0,1:T(1,128)S(1)}, s32[1,512]{1,0:T(1,128)S(1)}, s32[512,1]{0,1:T(1,128)S(1)}) fusion(s32[]{:T(128)} %axis_index.14, s32[]{:T(128)} %bitcast.20, s32[]{:T(128)} %bitcast.19, s32[]{:T(128)} %bitcast.18, s32[]{:T(128)} %bitcast.17, s32[]{:T(128)} %bitcast.16), kind=kLoop, calls=%fused_computation.41 | loop fusion | flops 55296 | bytes 6168 | tf_op jit(solution)/shard_map/jit(take_along_axis)/select_n | solution.py:253
  17.8 2.2 %collective-permute-done.4.refs_23_.refs_24_ = bf16[1,192,512]{2,1,0:T(8,128)(2,1)S(1)} collective-permute-done((bf16[1,192,512]{2,1,0:T(8,128)(2,1)}, bf16[1,192,512]{2,1,0:T(8,128)(2,1)S(1)}, u32[]{:S(2)}, u32[]{:S(2)}) %collective-permute-start.4) | collective-permute-done | bytes 196640 | tf_op jit(solution)/shard_map/ppermute | solution.py:95
  22.5 16.3 %shard_map.230 = bf16[1,192,2560]{2,1,0:T(8,128)(2,1)} custom-call(s32[192,1]{1,0:T(8,128)} %iota_add_fusion.qpos_ref, s32[1,1,512]{2,1,0:T(1,128)} %get-tuple-element.130.refs_0_, s32[1,1,512]{2,1,0:T(1,128)} %get-tuple-element.129.refs_1_, s32[1,1,512]{2,1,0:T(1,128)} %get-tuple-element.128.refs_2_, s32[1,1,512]{2,1,0:T(1,128)} %get-tuple-element.127.refs_3_, ...), custom_call_target="tpu_custom_call" | custom-call | tf_op jit(solution)/shard_map/pallas_call | solution.py:182
  41.7 1.8 %collective-permute-start.7 = (bf16[1,2560]{1,0:T(2,128)(2,1)S(1)}, bf16[1,2560]{1,0:T(2,128)(2,1)S(1)}, u32[]{:S(2)}, u32[]{:S(2)}) collective-permute-start(bf16[1,2560]{1,0:T(2,128)(2,1)S(1)} %fusion.47), channel_id=1, source_target_pairs={{0,2},{1,3},{2,0},{3,1},{4,6},{5,7},{6,4},{7,5},{8,10},{9,11},{10,... | collective-permute-start | bytes 15368 | tf_op jit(solution)/shard_map/ppermute | solution.py:25
  44.7 2.6 %gather_fusion.1 = bf16[512,512]{1,0:T(8,128)(2,1)} fusion(bf16[768,512]{1,0:T(8,128)(2,1)S(1)} %maximum_bitcast_fusion.1, s32[1024]{0:T(1024)S(1)} %pad_clamp_fusion), kind=kCustom, calls=%fused_computation.1 | custom fusion | bytes 1050624 | tf_op jit(solution)/shard_map/jit(take_along_axis)/gather | solution.py:254
  50.8 2.2 %gather_fusion = bf16[512,512]{1,0:T(8,128)(2,1)S(1)} fusion(bf16[2048,512]{1,0:T(8,128)(2,1)S(1)} %maximum_bitcast_fusion, s32[1024]{0:T(1024)} %pad_clamp_fusion.1), kind=kCustom, calls=%fused_computation | custom fusion | bytes 1050624 | tf_op jit(solution)/shard_map/jit(take_along_axis)/gather | solution.py:253
  53.9 1.6 %collective-permute-start.9 = (bf16[2,2560]{1,0:T(2,128)(2,1)S(1)}, bf16[2,2560]{1,0:T(2,128)(2,1)S(1)}, u32[]{:S(2)}, u32[]{:S(2)}) collective-permute-start(bf16[2,2560]{1,0:T(2,128)(2,1)S(1)} %broadcast_select_fusion.1), channel_id=1, source_target_pairs={{0,8},{4,12},{8,0},{12,4},{16,24},{20,28},{24,16},{28,20},{1,9},{5... | collective-permute-start | bytes 30728 | tf_op jit(solution)/shard_map/ppermute | solution.py:51
  55.6 2.1 %fusion.14 = bf16[1,512,512]{2,1,0:T(8,128)(2,1)} fusion(bf16[512,512]{1,0:T(8,128)(2,1)} %gather_fusion.1, bf16[512,512]{1,0:T(8,128)(2,1)S(1)} %gather_fusion, pred[512]{0:T(512)(128)(4,1)} %get-tuple-element.136, pred[512]{0:T(512)(128)(4,1)} %compare_and_fusion.1, pred[512]{0:T(512)(128)(4,1)} %get-tuple-element.135), kind=kLoop, calls=%fused_computation.25 | loop fusion | flops 786432 | bytes 1574400 | tf_op jit(solution)/shard_map/jit(_where)/select_n | solution.py:255
  57.7 2.7 %collective-permute-start.10 = (bf16[4,2560]{1,0:T(4,128)(2,1)S(1)}, bf16[4,2560]{1,0:T(4,128)(2,1)S(1)}, u32[]{:S(2)}, u32[]{:S(2)}) collective-permute-start(bf16[4,2560]{1,0:T(4,128)(2,1)S(1)} %maximum_select_fusion.1), channel_id=1, source_target_pairs={{0,16},{4,20},{8,24},{12,28},{16,0},{20,4},{24,8},{28,12},{1,17},{... | collective-permute-start | bytes 61448 | tf_op jit(solution)/shard_map/ppermute | solution.py:274
  60.6 1.9 %collective-permute-done.10 = bf16[4,2560]{1,0:T(4,128)(2,1)S(1)} collective-permute-done((bf16[4,2560]{1,0:T(4,128)(2,1)S(1)}, bf16[4,2560]{1,0:T(4,128)(2,1)S(1)}, u32[]{:S(2)}, u32[]{:S(2)}) %collective-permute-start.10) | collective-permute-done | bytes 20512 | tf_op jit(solution)/shard_map/ppermute | solution.py:274
  64.6 3.1 %collective-permute-done.12 = bf16[8,160]{1,0:T(8,128)(2,1)S(1)} collective-permute-done((bf16[8,160]{1,0:T(8,128)(2,1)S(1)}, bf16[8,160]{1,0:T(8,128)(2,1)S(1)}, u32[]{:S(2)}, u32[]{:S(2)}) %collective-permute-start.12) | collective-permute-done | bytes 2592 | tf_op jit(solution)/shard_map/ppermute | solution.py:37
  68.2 3.1 %collective-permute-done.13 = bf16[8,320]{1,0:T(8,128)(2,1)S(1)} collective-permute-done((bf16[8,320]{1,0:T(8,128)(2,1)S(1)}, bf16[8,320]{1,0:T(8,128)(2,1)S(1)}, u32[]{:S(2)}, u32[]{:S(2)}) %collective-permute-start.13) | collective-permute-done | bytes 5152 | tf_op jit(solution)/shard_map/ppermute | solution.py:51
  73.0 2.1 %collective-permute-done.14 = bf16[8,640]{1,0:T(8,128)(2,1)S(1)} collective-permute-done((bf16[8,640]{1,0:T(8,128)(2,1)S(1)}, bf16[8,640]{1,0:T(8,128)(2,1)S(1)}, u32[]{:S(2)}, u32[]{:S(2)}) %collective-permute-start.14) | collective-permute-done | bytes 10272 | tf_op jit(solution)/shard_map/ppermute | solution.py:51
  75.1 2.6 %collective-permute-start.15 = (bf16[8,1280]{1,0:T(8,128)(2,1)S(1)}, bf16[8,1280]{1,0:T(8,128)(2,1)S(1)}, u32[]{:S(2)}, u32[]{:S(2)}) collective-permute-start(bf16[8,1280]{1,0:T(8,128)(2,1)S(1)} %maximum_select_fusion.2), channel_id=1, source_target_pairs={{0,16},{4,20},{8,24},{12,28},{16,0},{20,4},{24,8},{28,12},{1,17},{... | collective-permute-start | bytes 61448 | tf_op jit(solution)/shard_map/ppermute | solution.py:295
  77.7 9.7 %conditional.2 = (f32[8,8000]{1,0:T(8,128)S(1)}) conditional(s32[]{:T(128)} %convert_element_type.46, (bf16[8,1280]{1,0:T(8,128)(2,1)S(1)}, f32[2560]{0:T(1024)S(1)}, bf16[8000,2560]{1,0:T(8,128)(2,1)}) %tuple.23, (bf16[8,1280]{1,0:T(8,128)(2,1)S(1)}, f32[2560]{0:T(1024)S(1)}, bf16[8000,2560]{1,0:T(8,128)(2,1)}) %tuple.23), branch_computations={%region_1.3_spmd, %region_2.4_spmd} | conditional | flops 163870720 | bytes 20771848 | solution.py:309
  77.8 9.6 %fusion = f32[8,8000]{1,0:T(8,128)S(1)} fusion(bf16[8000,2560]{1,0:T(8,128)(2,1)} %get-tuple-element.29, bf16[8,1280]{1,0:T(8,128)(2,1)S(1)} %get-tuple-element.27, f32[1280]{0:T(1024)S(1)} %slice.52), kind=kOutput, calls=%fused_computation.2 | convolution fusion | flops 163870720 | bytes 20761600 | tf_op jit(solution)/shard_map/cond/branch_0_fun/dot_general | solution.py:302
  87.5 9.7 %conditional.3 = (f32[8,8000]{1,0:T(8,128)S(1)}) conditional(s32[]{:T(128)} %convert_element_type.46, (bf16[8,1280]{1,0:T(8,128)(2,1)S(1)}, f32[2560]{0:T(1024)S(1)}, bf16[8000,2560]{1,0:T(8,128)(2,1)}) %tuple.24, (bf16[8,1280]{1,0:T(8,128)(2,1)S(1)}, f32[2560]{0:T(1024)S(1)}, bf16[8000,2560]{1,0:T(8,128)(2,1)}) %tuple.24), branch_computations={%region_3.5_spmd, %region_4.6_spmd} | conditional | flops 163870720 | bytes 20771848 | solution.py:310
  87.5 9.7 %fusion.6 = f32[8,8000]{1,0:T(8,128)S(1)} fusion(bf16[8000,2560]{1,0:T(8,128)(2,1)} %get-tuple-element.39, bf16[8,1280]{1,0:T(8,128)(2,1)S(1)} %get-tuple-element.37, f32[1280]{0:T(1024)S(1)} %slice.56), kind=kOutput, calls=%fused_computation.10 | convolution fusion | flops 163870720 | bytes 20761600 | tf_op jit(solution)/shard_map/cond/branch_0_fun/dot_general | solution.py:302
  99.8 3.1 %collective-permute-done.17 = f32[3,8]{1,0:T(4,128)S(1)} collective-permute-done((f32[3,8]{1,0:T(4,128)S(1)}, f32[3,8]{1,0:T(4,128)S(1)}, u32[]{:S(2)}, u32[]{:S(2)}) %collective-permute-start.17) | collective-permute-done | bytes 128 | tf_op jit(solution)/shard_map/ppermute | solution.py:78
  103.4 3.1 %collective-permute-done.18 = f32[3,8]{1,0:T(4,128)S(1)} collective-permute-done((f32[3,8]{1,0:T(4,128)S(1)}, f32[3,8]{1,0:T(4,128)S(1)}, u32[]{:S(2)}, u32[]{:S(2)}) %collective-permute-start.18) | collective-permute-done | bytes 128 | tf_op jit(solution)/shard_map/ppermute | solution.py:78
  106.5 1.7 %collective-permute-start.19 = (f32[3,8]{1,0:T(4,128)S(1)}, f32[3,8]{1,0:T(4,128)S(1)}, u32[]{:S(2)}, u32[]{:S(2)}) collective-permute-start(f32[3,8]{1,0:T(4,128)S(1)} %pad_maximum_fusion.3), channel_id=1, source_target_pairs={{0,8},{4,12},{8,0},{12,4},{16,24},{20,28},{24,16},{28,20},{1,9},{5... | collective-permute-start | bytes 296 | tf_op jit(solution)/shard_map/ppermute | solution.py:78
  108.3 1.9 %collective-permute-done.19 = f32[3,8]{1,0:T(4,128)S(1)} collective-permute-done((f32[3,8]{1,0:T(4,128)S(1)}, f32[3,8]{1,0:T(4,128)S(1)}, u32[]{:S(2)}, u32[]{:S(2)}) %collective-permute-start.19) | collective-permute-done | bytes 128 | tf_op jit(solution)/shard_map/ppermute | solution.py:78
  110.7 4.1 %collective-permute-done.20 = f32[3,8]{1,0:T(4,128)S(1)} collective-permute-done((f32[3,8]{1,0:T(4,128)S(1)}, f32[3,8]{1,0:T(4,128)S(1)}, u32[]{:S(2)}, u32[]{:S(2)}) %collective-permute-start.20) | collective-permute-done | bytes 128 | tf_op jit(solution)/shard_map/ppermute | solution.py:78
  (98 shorter events, 27.5 us)
Async XLA Ops:
  0.6 59.8 %copy-start = (bf16[2560,80]{0,1:T(8,128)(2,1)S(1)}, bf16[2560,80]{0,1:T(8,128)(2,1)}, u32[]{:S(2)}) copy-start(bf16[2560,80]{0,1:T(8,128)(2,1)} %param.31) | copy-start | bytes 1228804
  0.6 42.9 %copy-start.6 = (bf16[1,192,512]{2,1,0:T(8,128)(2,1)S(1)}, bf16[1,192,512]{2,1,0:T(8,128)(2,1)}, u32[]{:S(2)}) copy-start(bf16[1,192,512]{2,1,0:T(8,128)(2,1)} %refs_18_.1) | copy-start | bytes 589828
  0.7 16.0 %collective-permute-start.1 = (bf16[1,512,512]{2,1,0:T(8,128)(2,1)}, bf16[1,512,512]{2,1,0:T(8,128)(2,1)S(1)}, u32[]{:S(2)}, u32[]{:S(2)}) collective-permute-start(bf16[1,512,512]{2,1,0:T(8,128)(2,1)} %refs_10_.1), channel_id=1, source_target_pairs={{0,2},{1,3},{2,0},{3,1},{4,6},{5,7},{6,4},{7,5},{8,10},{9,11},{10,... | collective-permute-start | bytes 1572872 | tf_op jit(solution)/shard_map/ppermute | solution.py:95
  3.7 17.8 %collective-permute-start = (bf16[1,512,512]{2,1,0:T(8,128)(2,1)}, bf16[1,512,512]{2,1,0:T(8,128)(2,1)S(1)}, u32[]{:S(2)}, u32[]{:S(2)}) collective-permute-start(bf16[1,512,512]{2,1,0:T(8,128)(2,1)} %refs_10_.1), channel_id=1, source_target_pairs={{0,1},{1,0},{2,3},{3,2},{4,5},{5,4},{6,7},{7,6},{8,9},{9,8},{10,11... | collective-permute-start | bytes 1572872 | tf_op jit(solution)/shard_map/ppermute | solution.py:91
  3.7 16.3 %collective-permute-start.4 = (bf16[1,192,512]{2,1,0:T(8,128)(2,1)}, bf16[1,192,512]{2,1,0:T(8,128)(2,1)S(1)}, u32[]{:S(2)}, u32[]{:S(2)}) collective-permute-start(bf16[1,192,512]{2,1,0:T(8,128)(2,1)} %refs_18_.1), channel_id=1, source_target_pairs={{0,2},{1,3},{2,0},{3,1},{4,6},{5,7},{6,4},{7,5},{8,10},{9,11},{10,... | collective-permute-start | bytes 589832 | tf_op jit(solution)/shard_map/ppermute | solution.py:95
  3.8 16.8 %collective-permute-start.3 = (bf16[1,192,512]{2,1,0:T(8,128)(2,1)}, bf16[1,192,512]{2,1,0:T(8,128)(2,1)S(1)}, u32[]{:S(2)}, u32[]{:S(2)}) collective-permute-start(bf16[1,192,512]{2,1,0:T(8,128)(2,1)} %refs_18_.1), channel_id=1, source_target_pairs={{0,1},{1,0},{2,3},{3,2},{4,5},{5,4},{6,7},{7,6},{8,9},{9,8},{10,11... | collective-permute-start | bytes 589832 | tf_op jit(solution)/shard_map/ppermute | solution.py:91
  16.6 4.8 %collective-permute-start.2 = (bf16[1,512,512]{2,1,0:T(8,128)(2,1)S(1)}, bf16[1,512,512]{2,1,0:T(8,128)(2,1)S(1)}, u32[]{:S(2)}, u32[]{:S(2)}) collective-permute-start(bf16[1,512,512]{2,1,0:T(8,128)(2,1)S(1)} %collective-permute-done.1.refs_15_.refs_16_), channel_id=1, source_target_pairs={{0,1},{1,0},{2,3},{3,2},{4,5},{5,4},{6,7},{7,6},{8,9},{9,8},{10,11... | collective-permute-start | bytes 1572872 | tf_op jit(solution)/shard_map/ppermute | solution.py:105
  20.0 1.4 %collective-permute-start.5 = (bf16[1,192,512]{2,1,0:T(8,128)(2,1)S(1)}, bf16[1,192,512]{2,1,0:T(8,128)(2,1)S(1)}, u32[]{:S(2)}, u32[]{:S(2)}) collective-permute-start(bf16[1,192,512]{2,1,0:T(8,128)(2,1)S(1)} %collective-permute-done.4.refs_23_.refs_24_), channel_id=1, source_target_pairs={{0,1},{1,0},{2,3},{3,2},{4,5},{5,4},{6,7},{7,6},{8,9},{9,8},{10,11... | collective-permute-start | bytes 589832 | tf_op jit(solution)/shard_map/ppermute | solution.py:105
  39.7 1.2 %collective-permute-start.6 = (bf16[1,2560]{1,0:T(2,128)(2,1)S(1)}, bf16[1,2560]{1,0:T(2,128)(2,1)S(1)}, u32[]{:S(2)}, u32[]{:S(2)}) collective-permute-start(bf16[1,2560]{1,0:T(2,128)(2,1)S(1)} %fusion.15), channel_id=1, source_target_pairs={{0,1},{1,0},{2,3},{3,2},{4,5},{5,4},{6,7},{7,6},{8,9},{9,8},{10,11... | collective-permute-start | bytes 15368 | tf_op jit(solution)/shard_map/ppermute | solution.py:25
  41.7 5.6 %collective-permute-start.7 = (bf16[1,2560]{1,0:T(2,128)(2,1)S(1)}, bf16[1,2560]{1,0:T(2,128)(2,1)S(1)}, u32[]{:S(2)}, u32[]{:S(2)}) collective-permute-start(bf16[1,2560]{1,0:T(2,128)(2,1)S(1)} %fusion.47), channel_id=1, source_target_pairs={{0,2},{1,3},{2,0},{3,1},{4,6},{5,7},{6,4},{7,5},{8,10},{9,11},{10,... | collective-permute-start | bytes 15368 | tf_op jit(solution)/shard_map/ppermute | solution.py:25
  47.9 5.2 %collective-permute-start.8 = (bf16[1,2560]{1,0:T(2,128)(2,1)}, bf16[1,2560]{1,0:T(2,128)(2,1)}, u32[]{:S(2)}, u32[]{:S(2)}) collective-permute-start(bf16[1,2560]{1,0:T(2,128)(2,1)} %add.594), channel_id=1, source_target_pairs={{0,4},{4,0},{8,12},{12,8},{16,20},{20,16},{24,28},{28,24},{1,5},{5... | collective-permute-start | bytes 15368 | tf_op jit(solution)/shard_map/ppermute | solution.py:51
  50.8 26.9 %copy-start.12 = (s32[8]{0:T(128)S(1)}, s32[8]{0:T(128)}, u32[]{:S(2)}) copy-start(s32[8]{0:T(128)} %param.35) | copy-start | bytes 100
  53.9 3.8 %collective-permute-start.9 = (bf16[2,2560]{1,0:T(2,128)(2,1)S(1)}, bf16[2,2560]{1,0:T(2,128)(2,1)S(1)}, u32[]{:S(2)}, u32[]{:S(2)}) collective-permute-start(bf16[2,2560]{1,0:T(2,128)(2,1)S(1)} %broadcast_select_fusion.1), channel_id=1, source_target_pairs={{0,8},{4,12},{8,0},{12,4},{16,24},{20,28},{24,16},{28,20},{1,9},{5... | collective-permute-start | bytes 30728 | tf_op jit(solution)/shard_map/ppermute | solution.py:51
  57.7 4.7 %collective-permute-start.10 = (bf16[4,2560]{1,0:T(4,128)(2,1)S(1)}, bf16[4,2560]{1,0:T(4,128)(2,1)S(1)}, u32[]{:S(2)}, u32[]{:S(2)}) collective-permute-start(bf16[4,2560]{1,0:T(4,128)(2,1)S(1)} %maximum_select_fusion.1), channel_id=1, source_target_pairs={{0,16},{4,20},{8,24},{12,28},{16,0},{20,4},{24,8},{28,12},{1,17},{... | collective-permute-start | bytes 61448 | tf_op jit(solution)/shard_map/ppermute | solution.py:274
  62.7 1.2 %collective-permute-start.11 = (bf16[8,80]{1,0:T(8,128)(2,1)S(1)}, bf16[8,80]{1,0:T(8,128)(2,1)S(1)}, u32[]{:S(2)}, u32[]{:S(2)}) collective-permute-start(bf16[8,80]{1,0:T(8,128)(2,1)S(1)} %maximum_select_fusion.6), channel_id=1, source_target_pairs={{0,1},{1,0},{2,3},{3,2},{4,5},{5,4},{6,7},{7,6},{8,9},{9,8},{10,11... | collective-permute-start | bytes 3848 | tf_op jit(solution)/shard_map/ppermute | solution.py:37
  64.0 3.6 %collective-permute-start.12 = (bf16[8,160]{1,0:T(8,128)(2,1)S(1)}, bf16[8,160]{1,0:T(8,128)(2,1)S(1)}, u32[]{:S(2)}, u32[]{:S(2)}) collective-permute-start(bf16[8,160]{1,0:T(8,128)(2,1)S(1)} %maximum_select_fusion.5), channel_id=1, source_target_pairs={{0,2},{1,3},{2,0},{3,1},{4,6},{5,7},{6,4},{7,5},{8,10},{9,11},{10,... | collective-permute-start | bytes 7688 | tf_op jit(solution)/shard_map/ppermute | solution.py:37
  67.7 3.6 %collective-permute-start.13 = (bf16[8,320]{1,0:T(8,128)(2,1)S(1)}, bf16[8,320]{1,0:T(8,128)(2,1)S(1)}, u32[]{:S(2)}, u32[]{:S(2)}) collective-permute-start(bf16[8,320]{1,0:T(8,128)(2,1)S(1)} %maximum_select_fusion.4), channel_id=1, source_target_pairs={{0,4},{4,0},{8,12},{12,8},{16,20},{20,16},{24,28},{28,24},{1,5},{5... | collective-permute-start | bytes 15368 | tf_op jit(solution)/shard_map/ppermute | solution.py:51
  71.4 3.7 %collective-permute-start.14 = (bf16[8,640]{1,0:T(8,128)(2,1)S(1)}, bf16[8,640]{1,0:T(8,128)(2,1)S(1)}, u32[]{:S(2)}, u32[]{:S(2)}) collective-permute-start(bf16[8,640]{1,0:T(8,128)(2,1)S(1)} %maximum_select_fusion.3), channel_id=1, source_target_pairs={{0,8},{4,12},{8,0},{12,4},{16,24},{20,28},{24,16},{28,20},{1,9},{5... | collective-permute-start | bytes 30728 | tf_op jit(solution)/shard_map/ppermute | solution.py:51
  75.1 12.4 %collective-permute-start.15 = (bf16[8,1280]{1,0:T(8,128)(2,1)S(1)}, bf16[8,1280]{1,0:T(8,128)(2,1)S(1)}, u32[]{:S(2)}, u32[]{:S(2)}) collective-permute-start(bf16[8,1280]{1,0:T(8,128)(2,1)S(1)} %maximum_select_fusion.2), channel_id=1, source_target_pairs={{0,16},{4,20},{8,24},{12,28},{16,0},{20,4},{24,8},{28,12},{1,17},{... | collective-permute-start | bytes 61448 | tf_op jit(solution)/shard_map/ppermute | solution.py:295
  97.9 1.2 %collective-permute-start.16 = (f32[3,8]{1,0:T(4,128)S(1)}, f32[3,8]{1,0:T(4,128)S(1)}, u32[]{:S(2)}, u32[]{:S(2)}) collective-permute-start(f32[3,8]{1,0:T(4,128)S(1)} %pad_maximum_fusion), channel_id=1, source_target_pairs={{0,1},{1,0},{2,3},{3,2},{4,5},{5,4},{6,7},{7,6},{8,9},{9,8},{10,11... | collective-permute-start | bytes 296 | tf_op jit(solution)/shard_map/ppermute | solution.py:78
  99.2 3.7 %collective-permute-start.17 = (f32[3,8]{1,0:T(4,128)S(1)}, f32[3,8]{1,0:T(4,128)S(1)}, u32[]{:S(2)}, u32[]{:S(2)}) collective-permute-start(f32[3,8]{1,0:T(4,128)S(1)} %pad_maximum_fusion.1), channel_id=1, source_target_pairs={{0,2},{1,3},{2,0},{3,1},{4,6},{5,7},{6,4},{7,5},{8,10},{9,11},{10,... | collective-permute-start | bytes 296 | tf_op jit(solution)/shard_map/ppermute | solution.py:78
  102.9 3.7 %collective-permute-start.18 = (f32[3,8]{1,0:T(4,128)S(1)}, f32[3,8]{1,0:T(4,128)S(1)}, u32[]{:S(2)}, u32[]{:S(2)}) collective-permute-start(f32[3,8]{1,0:T(4,128)S(1)} %pad_maximum_fusion.2), channel_id=1, source_target_pairs={{0,4},{4,0},{8,12},{12,8},{16,20},{20,16},{24,28},{28,24},{1,5},{5... | collective-permute-start | bytes 296 | tf_op jit(solution)/shard_map/ppermute | solution.py:78
  106.5 3.7 %collective-permute-start.19 = (f32[3,8]{1,0:T(4,128)S(1)}, f32[3,8]{1,0:T(4,128)S(1)}, u32[]{:S(2)}, u32[]{:S(2)}) collective-permute-start(f32[3,8]{1,0:T(4,128)S(1)} %pad_maximum_fusion.3), channel_id=1, source_target_pairs={{0,8},{4,12},{8,0},{12,4},{16,24},{20,28},{24,16},{28,20},{1,9},{5... | collective-permute-start | bytes 296 | tf_op jit(solution)/shard_map/ppermute | solution.py:78
  110.2 4.5 %collective-permute-start.20 = (f32[3,8]{1,0:T(4,128)S(1)}, f32[3,8]{1,0:T(4,128)S(1)}, u32[]{:S(2)}, u32[]{:S(2)}) collective-permute-start(f32[3,8]{1,0:T(4,128)S(1)} %pad_maximum_fusion.4), channel_id=1, source_target_pairs={{0,16},{4,20},{8,24},{12,28},{16,0},{20,4},{24,8},{28,12},{1,17},{... | collective-permute-start | bytes 296 | tf_op jit(solution)/shard_map/ppermute | solution.py:78
  (10 other events, 67.7 us)

commit v14 on v10

--- a/solution.py
+++ b/solution.py
@@ -111,12 +111,12 @@
             [query[:, i * head_dim : (i + 1) * head_dim] for i in range(stacked)], axis=0
         )
         position = jnp.concatenate([position] * stacked, axis=0)
+    query = query * jnp.asarray(scale, query.dtype)
     dims = (((1,), (1,)), ((), ()))
     masked = []
     for i, kind in enumerate(kinds):
-        score = (
-            lax.dot_general(query, kv_refs[2 * i][0], dims, preferred_element_type=jnp.float32)
-            * scale
+        score = lax.dot_general(
+            query, kv_refs[2 * i][0], dims, preferred_element_type=jnp.float32
         )
         bound = bound_refs[i][0]
         seen = position <= bound if kind == "hi" else bound <= position

time: 116 us -> 116 us (level)
  no operation moved by 1% of the time
where the time goes in v14:
time: 116 us; the launch traced here: 115 us
  waiting for transfers between devices  30.3 us (26%)
  starting transfers between devices  21.4 us (18%)
  matrix products  18.1 us (16%)
  other arithmetic  16.9 us (15%)
  Pallas kernels  16.1 us (14%)
  local copies, waits for them, and re-layouts  7.95 us (7%)
  between operations  4.63 us (4%)
    dot_general x1, matrix products, on_device(): lax.dot_general(normed, head, (((1,), (1,)), ((), ())), preferred_element...  17.2 us
    pallas_call x1, Pallas kernels, attend(): pl.pallas_call(kernel, grid=(req_local, head_count // stacked), in_specs=...  16.1 us
    ppermute x8, waiting for transfers between devices, butterfly_gather(): other = lax.ppermute(x, axis, xor_pairs(count, bit))  12.4 us
    ppermute x5, waiting for transfers between devices, butterfly_stats(): other = lax.ppermute(packed, axis, xor_pairs(count, bit))  11.7 us
    ppermute x8, starting transfers between devices, butterfly_gather(): other = lax.ppermute(x, axis, xor_pairs(count, bit))  10.8 us
    ppermute x5, starting transfers between devices, butterfly_stats(): other = lax.ppermute(packed, axis, xor_pairs(count, bit))  5.04 us
    ppermute x2, starting transfers between devices, exchange_pieces(): other = lax.ppermute(held, axis, xor_pairs(count, bit))  3.16 us
    ppermute x2, waiting for transfers between devices, exchange_pieces(): other = lax.ppermute(held, axis, xor_pairs(count, bit))  2.94 us
  transfers between devices with their start and end apart: 21, of which 16 were waited for; matrix products, arithmetic and copies ran while one was open for 17% of the time, Pallas kernels for 0%

profile of v14, /device:TPU:0, one launch (start us, length us, event | category | flops | bytes accessed | tf_op | source)
XLA Modules:
  0.0 115.4 jit_solution(6184014107850485573)
XLA Ops:
  0.6 3.0 %collective-permute-start.1 = (bf16[1,512,512]{2,1,0:T(8,128)(2,1)}, bf16[1,512,512]{2,1,0:T(8,128)(2,1)S(1)}, u32[]{:S(2)}, u32[]{:S(2)}) collective-permute-start(bf16[1,512,512]{2,1,0:T(8,128)(2,1)} %refs_10_.1), channel_id=1, source_target_pairs={{0,2},{1,3},{2,0},{3,1},{4,6},{5,7},{6,4},{7,5},{8,10},{9,11},{10,... | collective-permute-start | bytes 1572872 | tf_op jit(solution)/shard_map/ppermute | solution.py:81
  12.6 2.7 %compare_select_fusion.3 = (s32[512,1]{0,1:T(1,128)S(1)}, s32[1,512]{1,0:T(1,128)S(1)}, s32[512,1]{0,1:T(1,128)S(1)}) fusion(s32[]{:T(128)} %axis_index.14, s32[]{:T(128)} %bitcast.20, s32[]{:T(128)} %bitcast.19, s32[]{:T(128)} %bitcast.18, s32[]{:T(128)} %bitcast.17, s32[]{:T(128)} %bitcast.16), kind=kLoop, calls=%fused_computation.30 | loop fusion | flops 55296 | bytes 6168 | tf_op jit(solution)/shard_map/jit(take_along_axis)/select_n | solution.py:239
  17.8 2.2 %collective-permute-done.4.refs_23_.refs_24_ = bf16[1,192,512]{2,1,0:T(8,128)(2,1)S(1)} collective-permute-done((bf16[1,192,512]{2,1,0:T(8,128)(2,1)}, bf16[1,192,512]{2,1,0:T(8,128)(2,1)S(1)}, u32[]{:S(2)}, u32[]{:S(2)}) %collective-permute-start.4) | collective-permute-done | bytes 196640 | tf_op jit(solution)/shard_map/ppermute | solution.py:81
  22.5 16.1 %shard_map.230 = bf16[1,192,2560]{2,1,0:T(8,128)(2,1)} custom-call(s32[192,1]{1,0:T(8,128)} %iota_add_fusion.qpos_ref, s32[1,1,512]{2,1,0:T(1,128)} %get-tuple-element.88.refs_0_, s32[1,1,512]{2,1,0:T(1,128)} %get-tuple-element.87.refs_1_, s32[1,1,512]{2,1,0:T(1,128)} %get-tuple-element.86.refs_2_, s32[1,1,512]{2,1,0:T(1,128)} %get-tuple-element.85.refs_3_, ...), custom_call_target="tpu_custom_call" | custom-call | tf_op jit(solution)/shard_map/pallas_call | solution.py:168
  41.4 1.8 %collective-permute-start.7 = (bf16[1,2560]{1,0:T(2,128)(2,1)S(1)}, bf16[1,2560]{1,0:T(2,128)(2,1)S(1)}, u32[]{:S(2)}, u32[]{:S(2)}) collective-permute-start(bf16[1,2560]{1,0:T(2,128)(2,1)S(1)} %fusion.41), channel_id=1, source_target_pairs={{0,2},{1,3},{2,0},{3,1},{4,6},{5,7},{6,4},{7,5},{8,10},{9,11},{10,... | collective-permute-start | bytes 15368 | tf_op jit(solution)/shard_map/ppermute | solution.py:25
  43.2 1.9 %collective-permute-done.7 = bf16[1,2560]{1,0:T(2,128)(2,1)S(1)} collective-permute-done((bf16[1,2560]{1,0:T(2,128)(2,1)S(1)}, bf16[1,2560]{1,0:T(2,128)(2,1)S(1)}, u32[]{:S(2)}, u32[]{:S(2)}) %collective-permute-start.7) | collective-permute-done | bytes 5152 | tf_op jit(solution)/shard_map/ppermute | solution.py:25
  45.2 1.8 %collective-permute-start.8 = (bf16[1,2560]{1,0:T(2,128)(2,1)S(1)}, bf16[1,2560]{1,0:T(2,128)(2,1)S(1)}, u32[]{:S(2)}, u32[]{:S(2)}) collective-permute-start(bf16[1,2560]{1,0:T(2,128)(2,1)S(1)} %add.588), channel_id=1, source_target_pairs={{0,4},{4,0},{8,12},{12,8},{16,20},{20,16},{24,28},{28,24},{1,5},{5... | collective-permute-start | bytes 15368 | tf_op jit(solution)/shard_map/ppermute | solution.py:37
  48.2 2.6 %gather_fusion.1 = bf16[512,512]{1,0:T(8,128)(2,1)} fusion(bf16[768,512]{1,0:T(8,128)(2,1)S(1)} %maximum_bitcast_fusion.1, s32[1024]{0:T(1024)S(1)} %pad_clamp_fusion), kind=kCustom, calls=%fused_computation.1 | custom fusion | bytes 1050624 | tf_op jit(solution)/shard_map/jit(take_along_axis)/gather | solution.py:240
  51.5 1.6 %collective-permute-start.9 = (bf16[2,2560]{1,0:T(2,128)(2,1)}, bf16[2,2560]{1,0:T(2,128)(2,1)}, u32[]{:S(2)}, u32[]{:S(2)}) collective-permute-start(bf16[2,2560]{1,0:T(2,128)(2,1)} %broadcast_select_fusion.1), channel_id=1, source_target_pairs={{0,8},{4,12},{8,0},{12,4},{16,24},{20,28},{24,16},{28,20},{1,9},{5... | collective-permute-start | bytes 30728 | tf_op jit(solution)/shard_map/ppermute | solution.py:37
  54.4 2.2 %gather_fusion = bf16[512,512]{1,0:T(8,128)(2,1)S(1)} fusion(bf16[2048,512]{1,0:T(8,128)(2,1)S(1)} %maximum_bitcast_fusion, s32[1024]{0:T(1024)} %pad_clamp_fusion.1), kind=kCustom, calls=%fused_computation | custom fusion | bytes 1050624 | tf_op jit(solution)/shard_map/jit(take_along_axis)/gather | solution.py:239
  57.5 2.6 %collective-permute-start.10 = (bf16[4,2560]{1,0:T(4,128)(2,1)S(1)}, bf16[4,2560]{1,0:T(4,128)(2,1)S(1)}, u32[]{:S(2)}, u32[]{:S(2)}) collective-permute-start(bf16[4,2560]{1,0:T(4,128)(2,1)S(1)} %maximum_select_fusion.2), channel_id=1, source_target_pairs={{0,16},{4,20},{8,24},{12,28},{16,0},{20,4},{24,8},{28,12},{1,17},{... | collective-permute-start | bytes 61448 | tf_op jit(solution)/shard_map/ppermute | solution.py:37
  60.2 1.7 %fusion.1 = bf16[1,512,512]{2,1,0:T(8,128)(2,1)} fusion(bf16[512,512]{1,0:T(8,128)(2,1)S(1)} %copy-done.6, bf16[512,512]{1,0:T(8,128)(2,1)S(1)} %gather_fusion, pred[512]{0:T(512)(128)(4,1)} %get-tuple-element.94, pred[512]{0:T(512)(128)(4,1)} %compare_and_fusion.1, pred[512]{0:T(512)(128)(4,1)} %get-tuple-element.93), kind=kLoop, calls=%fused_computation.7 | loop fusion | flops 786432 | bytes 1574400 | tf_op jit(solution)/shard_map/jit(_where)/select_n | solution.py:241
  66.1 2.1 %collective-permute-done.12 = bf16[8,160]{1,0:T(8,128)(2,1)S(1)} collective-permute-done((bf16[8,160]{1,0:T(8,128)(2,1)S(1)}, bf16[8,160]{1,0:T(8,128)(2,1)S(1)}, u32[]{:S(2)}, u32[]{:S(2)}) %collective-permute-start.12) | collective-permute-done | bytes 2592 | tf_op jit(solution)/shard_map/ppermute | solution.py:37
  68.7 3.2 %collective-permute-done.13 = bf16[8,320]{1,0:T(8,128)(2,1)S(1)} collective-permute-done((bf16[8,320]{1,0:T(8,128)(2,1)S(1)}, bf16[8,320]{1,0:T(8,128)(2,1)S(1)}, u32[]{:S(2)}, u32[]{:S(2)}) %collective-permute-start.13) | collective-permute-done | bytes 5152 | tf_op jit(solution)/shard_map/ppermute | solution.py:37
  72.3 3.3 %collective-permute-done.14 = bf16[8,640]{1,0:T(8,128)(2,1)S(1)} collective-permute-done((bf16[8,640]{1,0:T(8,128)(2,1)S(1)}, bf16[8,640]{1,0:T(8,128)(2,1)S(1)}, u32[]{:S(2)}, u32[]{:S(2)}) %collective-permute-start.14) | collective-permute-done | bytes 10272 | tf_op jit(solution)/shard_map/ppermute | solution.py:37
  75.7 2.5 %collective-permute-start.15 = (bf16[8,1280]{1,0:T(8,128)(2,1)S(1)}, bf16[8,1280]{1,0:T(8,128)(2,1)S(1)}, u32[]{:S(2)}, u32[]{:S(2)}) collective-permute-start(bf16[8,1280]{1,0:T(8,128)(2,1)S(1)} %maximum_select_fusion.3), channel_id=1, source_target_pairs={{0,16},{4,20},{8,24},{12,28},{16,0},{20,4},{24,8},{28,12},{1,17},{... | collective-permute-start | bytes 61448 | tf_op jit(solution)/shard_map/ppermute | solution.py:37
  78.2 2.2 %collective-permute-done.15 = bf16[8,1280]{1,0:T(8,128)(2,1)S(1)} collective-permute-done((bf16[8,1280]{1,0:T(8,128)(2,1)S(1)}, bf16[8,1280]{1,0:T(8,128)(2,1)S(1)}, u32[]{:S(2)}, u32[]{:S(2)}) %collective-permute-start.15) | collective-permute-done | bytes 20512 | tf_op jit(solution)/shard_map/ppermute | solution.py:37
  80.5 17.2 %fusion.37 = (f32[8]{0:T(128)S(1)}, f32[8,8000]{1,0:T(8,128)S(1)}) fusion(bf16[8000,2560]{1,0:T(8,128)(2,1)} %param.30, f32[2560]{0:T(1024)S(1)} %convert_element_type.18, f32[8]{0:T(128)S(1)} %add_rsqrt_fusion, bf16[8,1280]{1,0:T(8,128)(2,1)S(1)} %maximum_select_fusion.3, bf16[8,1280]{1,0:T(8,128)(2,1)S(1)} %collective-permute-done.15, pred[]{:T(512)S(6)} %eq.61), kind=kOutput, calls=%fused_computation.142 | convolution fusion | flops 328010240 | bytes 41267264 | tf_op jit(solution)/shard_map/dot_general | solution.py:261
  99.3 1.6 %collective-permute-start.17 = (f32[3,8]{1,0:T(4,128)S(1)}, f32[3,8]{1,0:T(4,128)S(1)}, u32[]{:S(2)}, u32[]{:S(2)}) collective-permute-start(f32[3,8]{1,0:T(4,128)S(1)} %pad_maximum_fusion.1), channel_id=1, source_target_pairs={{0,2},{1,3},{2,0},{3,1},{4,6},{5,7},{6,4},{7,5},{8,10},{9,11},{10,... | collective-permute-start | bytes 296 | tf_op jit(solution)/shard_map/ppermute | solution.py:64
  100.9 2.1 %collective-permute-done.17 = f32[3,8]{1,0:T(4,128)S(1)} collective-permute-done((f32[3,8]{1,0:T(4,128)S(1)}, f32[3,8]{1,0:T(4,128)S(1)}, u32[]{:S(2)}, u32[]{:S(2)}) %collective-permute-start.17) | collective-permute-done | bytes 128 | tf_op jit(solution)/shard_map/ppermute | solution.py:64
  103.4 3.2 %collective-permute-done.18 = f32[3,8]{1,0:T(4,128)S(1)} collective-permute-done((f32[3,8]{1,0:T(4,128)S(1)}, f32[3,8]{1,0:T(4,128)S(1)}, u32[]{:S(2)}, u32[]{:S(2)}) %collective-permute-start.18) | collective-permute-done | bytes 128 | tf_op jit(solution)/shard_map/ppermute | solution.py:64
  107.1 3.2 %collective-permute-done.19 = f32[3,8]{1,0:T(4,128)S(1)} collective-permute-done((f32[3,8]{1,0:T(4,128)S(1)}, f32[3,8]{1,0:T(4,128)S(1)}, u32[]{:S(2)}, u32[]{:S(2)}) %collective-permute-start.19) | collective-permute-done | bytes 128 | tf_op jit(solution)/shard_map/ppermute | solution.py:64
  110.3 2.5 %collective-permute-start.20 = (f32[3,8]{1,0:T(4,128)S(1)}, f32[3,8]{1,0:T(4,128)S(1)}, u32[]{:S(2)}, u32[]{:S(2)}) collective-permute-start(f32[3,8]{1,0:T(4,128)S(1)} %pad_maximum_fusion.4), channel_id=1, source_target_pairs={{0,16},{4,20},{8,24},{12,28},{16,0},{20,4},{24,8},{28,12},{1,17},{... | collective-permute-start | bytes 296 | tf_op jit(solution)/shard_map/ppermute | solution.py:64
  112.9 2.0 %collective-permute-done.20 = f32[3,8]{1,0:T(4,128)S(1)} collective-permute-done((f32[3,8]{1,0:T(4,128)S(1)}, f32[3,8]{1,0:T(4,128)S(1)}, u32[]{:S(2)}, u32[]{:S(2)}) %collective-permute-start.20) | collective-permute-done | bytes 128 | tf_op jit(solution)/shard_map/ppermute | solution.py:64
  (91 shorter events, 25.3 us)
Async XLA Ops:
  0.6 61.8 %copy-start = (bf16[2560,80]{0,1:T(8,128)(2,1)S(1)}, bf16[2560,80]{0,1:T(8,128)(2,1)}, u32[]{:S(2)}) copy-start(bf16[2560,80]{0,1:T(8,128)(2,1)} %param.27) | copy-start | bytes 1228804
  0.6 16.0 %collective-permute-start.1 = (bf16[1,512,512]{2,1,0:T(8,128)(2,1)}, bf16[1,512,512]{2,1,0:T(8,128)(2,1)S(1)}, u32[]{:S(2)}, u32[]{:S(2)}) collective-permute-start(bf16[1,512,512]{2,1,0:T(8,128)(2,1)} %refs_10_.1), channel_id=1, source_target_pairs={{0,2},{1,3},{2,0},{3,1},{4,6},{5,7},{6,4},{7,5},{8,10},{9,11},{10,... | collective-permute-start | bytes 1572872 | tf_op jit(solution)/shard_map/ppermute | solution.py:81
  3.6 17.8 %collective-permute-start = (bf16[1,512,512]{2,1,0:T(8,128)(2,1)}, bf16[1,512,512]{2,1,0:T(8,128)(2,1)S(1)}, u32[]{:S(2)}, u32[]{:S(2)}) collective-permute-start(bf16[1,512,512]{2,1,0:T(8,128)(2,1)} %refs_10_.1), channel_id=1, source_target_pairs={{0,1},{1,0},{2,3},{3,2},{4,5},{5,4},{6,7},{7,6},{8,9},{9,8},{10,11... | collective-permute-start | bytes 1572872 | tf_op jit(solution)/shard_map/ppermute | solution.py:77
  3.7 16.3 %collective-permute-start.4 = (bf16[1,192,512]{2,1,0:T(8,128)(2,1)}, bf16[1,192,512]{2,1,0:T(8,128)(2,1)S(1)}, u32[]{:S(2)}, u32[]{:S(2)}) collective-permute-start(bf16[1,192,512]{2,1,0:T(8,128)(2,1)} %refs_18_.1), channel_id=1, source_target_pairs={{0,2},{1,3},{2,0},{3,1},{4,6},{5,7},{6,4},{7,5},{8,10},{9,11},{10,... | collective-permute-start | bytes 589832 | tf_op jit(solution)/shard_map/ppermute | solution.py:81
  3.8 16.7 %collective-permute-start.3 = (bf16[1,192,512]{2,1,0:T(8,128)(2,1)}, bf16[1,192,512]{2,1,0:T(8,128)(2,1)S(1)}, u32[]{:S(2)}, u32[]{:S(2)}) collective-permute-start(bf16[1,192,512]{2,1,0:T(8,128)(2,1)} %refs_18_.1), channel_id=1, source_target_pairs={{0,1},{1,0},{2,3},{3,2},{4,5},{5,4},{6,7},{7,6},{8,9},{9,8},{10,11... | collective-permute-start | bytes 589832 | tf_op jit(solution)/shard_map/ppermute | solution.py:77
  16.6 4.8 %collective-permute-start.2 = (bf16[1,512,512]{2,1,0:T(8,128)(2,1)S(1)}, bf16[1,512,512]{2,1,0:T(8,128)(2,1)S(1)}, u32[]{:S(2)}, u32[]{:S(2)}) collective-permute-start(bf16[1,512,512]{2,1,0:T(8,128)(2,1)S(1)} %collective-permute-done.1.refs_15_.refs_16_), channel_id=1, source_target_pairs={{0,1},{1,0},{2,3},{3,2},{4,5},{5,4},{6,7},{7,6},{8,9},{9,8},{10,11... | collective-permute-start | bytes 1572872 | tf_op jit(solution)/shard_map/ppermute | solution.py:91
  20.0 1.4 %collective-permute-start.5 = (bf16[1,192,512]{2,1,0:T(8,128)(2,1)S(1)}, bf16[1,192,512]{2,1,0:T(8,128)(2,1)S(1)}, u32[]{:S(2)}, u32[]{:S(2)}) collective-permute-start(bf16[1,192,512]{2,1,0:T(8,128)(2,1)S(1)} %collective-permute-done.4.refs_23_.refs_24_), channel_id=1, source_target_pairs={{0,1},{1,0},{2,3},{3,2},{4,5},{5,4},{6,7},{7,6},{8,9},{9,8},{10,11... | collective-permute-start | bytes 589832 | tf_op jit(solution)/shard_map/ppermute | solution.py:91
  22.5 24.5 %copy-start.7 = (bf16[1,192,512]{2,1,0:T(8,128)(2,1)S(1)}, bf16[1,192,512]{2,1,0:T(8,128)(2,1)}, u32[]{:S(2)}) copy-start(bf16[1,192,512]{2,1,0:T(8,128)(2,1)} %refs_18_.1) | copy-start | bytes 589828
  39.4 1.2 %collective-permute-start.6 = (bf16[1,2560]{1,0:T(2,128)(2,1)S(1)}, bf16[1,2560]{1,0:T(2,128)(2,1)S(1)}, u32[]{:S(2)}, u32[]{:S(2)}) collective-permute-start(bf16[1,2560]{1,0:T(2,128)(2,1)S(1)} %fusion.9), channel_id=1, source_target_pairs={{0,1},{1,0},{2,3},{3,2},{4,5},{5,4},{6,7},{7,6},{8,9},{9,8},{10,11... | collective-permute-start | bytes 15368 | tf_op jit(solution)/shard_map/ppermute | solution.py:25
  41.4 3.7 %collective-permute-start.7 = (bf16[1,2560]{1,0:T(2,128)(2,1)S(1)}, bf16[1,2560]{1,0:T(2,128)(2,1)S(1)}, u32[]{:S(2)}, u32[]{:S(2)}) collective-permute-start(bf16[1,2560]{1,0:T(2,128)(2,1)S(1)} %fusion.41), channel_id=1, source_target_pairs={{0,2},{1,3},{2,0},{3,1},{4,6},{5,7},{6,4},{7,5},{8,10},{9,11},{10,... | collective-permute-start | bytes 15368 | tf_op jit(solution)/shard_map/ppermute | solution.py:25
  45.2 5.6 %collective-permute-start.8 = (bf16[1,2560]{1,0:T(2,128)(2,1)S(1)}, bf16[1,2560]{1,0:T(2,128)(2,1)S(1)}, u32[]{:S(2)}, u32[]{:S(2)}) collective-permute-start(bf16[1,2560]{1,0:T(2,128)(2,1)S(1)} %add.588), channel_id=1, source_target_pairs={{0,4},{4,0},{8,12},{12,8},{16,20},{20,16},{24,28},{28,24},{1,5},{5... | collective-permute-start | bytes 15368 | tf_op jit(solution)/shard_map/ppermute | solution.py:37
  51.5 5.2 %collective-permute-start.9 = (bf16[2,2560]{1,0:T(2,128)(2,1)}, bf16[2,2560]{1,0:T(2,128)(2,1)}, u32[]{:S(2)}, u32[]{:S(2)}) collective-permute-start(bf16[2,2560]{1,0:T(2,128)(2,1)} %broadcast_select_fusion.1), channel_id=1, source_target_pairs={{0,8},{4,12},{8,0},{12,4},{16,24},{20,28},{24,16},{28,20},{1,9},{5... | collective-permute-start | bytes 30728 | tf_op jit(solution)/shard_map/ppermute | solution.py:37
  56.7 21.5 %copy-start.12 = (s32[8]{0:T(128)S(1)}, s32[8]{0:T(128)}, u32[]{:S(2)}) copy-start(s32[8]{0:T(128)} %param.31) | copy-start | bytes 100
  57.5 4.9 %collective-permute-start.10 = (bf16[4,2560]{1,0:T(4,128)(2,1)S(1)}, bf16[4,2560]{1,0:T(4,128)(2,1)S(1)}, u32[]{:S(2)}, u32[]{:S(2)}) collective-permute-start(bf16[4,2560]{1,0:T(4,128)(2,1)S(1)} %maximum_select_fusion.2), channel_id=1, source_target_pairs={{0,16},{4,20},{8,24},{12,28},{16,0},{20,4},{24,8},{28,12},{1,17},{... | collective-permute-start | bytes 61448 | tf_op jit(solution)/shard_map/ppermute | solution.py:37
  63.3 1.2 %collective-permute-start.11 = (bf16[8,80]{1,0:T(8,128)(2,1)S(1)}, bf16[8,80]{1,0:T(8,128)(2,1)S(1)}, u32[]{:S(2)}, u32[]{:S(2)}) collective-permute-start(bf16[8,80]{1,0:T(8,128)(2,1)S(1)} %fusion), channel_id=1, source_target_pairs={{0,1},{1,0},{2,3},{3,2},{4,5},{5,4},{6,7},{7,6},{8,9},{9,8},{10,11... | collective-permute-start | bytes 3848 | tf_op jit(solution)/shard_map/ppermute | solution.py:37
  64.6 3.6 %collective-permute-start.12 = (bf16[8,160]{1,0:T(8,128)(2,1)S(1)}, bf16[8,160]{1,0:T(8,128)(2,1)S(1)}, u32[]{:S(2)}, u32[]{:S(2)}) collective-permute-start(bf16[8,160]{1,0:T(8,128)(2,1)S(1)} %maximum_select_fusion.7), channel_id=1, source_target_pairs={{0,2},{1,3},{2,0},{3,1},{4,6},{5,7},{6,4},{7,5},{8,10},{9,11},{10,... | collective-permute-start | bytes 7688 | tf_op jit(solution)/shard_map/ppermute | solution.py:37
  68.3 3.6 %collective-permute-start.13 = (bf16[8,320]{1,0:T(8,128)(2,1)S(1)}, bf16[8,320]{1,0:T(8,128)(2,1)S(1)}, u32[]{:S(2)}, u32[]{:S(2)}) collective-permute-start(bf16[8,320]{1,0:T(8,128)(2,1)S(1)} %maximum_select_fusion.6), channel_id=1, source_target_pairs={{0,4},{4,0},{8,12},{12,8},{16,20},{20,16},{24,28},{28,24},{1,5},{5... | collective-permute-start | bytes 15368 | tf_op jit(solution)/shard_map/ppermute | solution.py:37
  72.0 3.7 %collective-permute-start.14 = (bf16[8,640]{1,0:T(8,128)(2,1)S(1)}, bf16[8,640]{1,0:T(8,128)(2,1)S(1)}, u32[]{:S(2)}, u32[]{:S(2)}) collective-permute-start(bf16[8,640]{1,0:T(8,128)(2,1)S(1)} %maximum_select_fusion.4), channel_id=1, source_target_pairs={{0,8},{4,12},{8,0},{12,4},{16,24},{20,28},{24,16},{28,20},{1,9},{5... | collective-permute-start | bytes 30728 | tf_op jit(solution)/shard_map/ppermute | solution.py:37
  75.7 4.7 %collective-permute-start.15 = (bf16[8,1280]{1,0:T(8,128)(2,1)S(1)}, bf16[8,1280]{1,0:T(8,128)(2,1)S(1)}, u32[]{:S(2)}, u32[]{:S(2)}) collective-permute-start(bf16[8,1280]{1,0:T(8,128)(2,1)S(1)} %maximum_select_fusion.3), channel_id=1, source_target_pairs={{0,16},{4,20},{8,24},{12,28},{16,0},{20,4},{24,8},{28,12},{1,17},{... | collective-permute-start | bytes 61448 | tf_op jit(solution)/shard_map/ppermute | solution.py:37
  98.1 1.2 %collective-permute-start.16 = (f32[3,8]{1,0:T(4,128)S(1)}, f32[3,8]{1,0:T(4,128)S(1)}, u32[]{:S(2)}, u32[]{:S(2)}) collective-permute-start(f32[3,8]{1,0:T(4,128)S(1)} %pad_maximum_fusion), channel_id=1, source_target_pairs={{0,1},{1,0},{2,3},{3,2},{4,5},{5,4},{6,7},{7,6},{8,9},{9,8},{10,11... | collective-permute-start | bytes 296 | tf_op jit(solution)/shard_map/ppermute | solution.py:64
  99.3 3.7 %collective-permute-start.17 = (f32[3,8]{1,0:T(4,128)S(1)}, f32[3,8]{1,0:T(4,128)S(1)}, u32[]{:S(2)}, u32[]{:S(2)}) collective-permute-start(f32[3,8]{1,0:T(4,128)S(1)} %pad_maximum_fusion.1), channel_id=1, source_target_pairs={{0,2},{1,3},{2,0},{3,1},{4,6},{5,7},{6,4},{7,5},{8,10},{9,11},{10,... | collective-permute-start | bytes 296 | tf_op jit(solution)/shard_map/ppermute | solution.py:64
  103.0 3.7 %collective-permute-start.18 = (f32[3,8]{1,0:T(4,128)S(1)}, f32[3,8]{1,0:T(4,128)S(1)}, u32[]{:S(2)}, u32[]{:S(2)}) collective-permute-start(f32[3,8]{1,0:T(4,128)S(1)} %pad_maximum_fusion.2), channel_id=1, source_target_pairs={{0,4},{4,0},{8,12},{12,8},{16,20},{20,16},{24,28},{28,24},{1,5},{5... | collective-permute-start | bytes 296 | tf_op jit(solution)/shard_map/ppermute | solution.py:64
  106.7 3.7 %collective-permute-start.19 = (f32[3,8]{1,0:T(4,128)S(1)}, f32[3,8]{1,0:T(4,128)S(1)}, u32[]{:S(2)}, u32[]{:S(2)}) collective-permute-start(f32[3,8]{1,0:T(4,128)S(1)} %pad_maximum_fusion.3), channel_id=1, source_target_pairs={{0,8},{4,12},{8,0},{12,4},{16,24},{20,28},{24,16},{28,20},{1,9},{5... | collective-permute-start | bytes 296 | tf_op jit(solution)/shard_map/ppermute | solution.py:64
  110.3 4.5 %collective-permute-start.20 = (f32[3,8]{1,0:T(4,128)S(1)}, f32[3,8]{1,0:T(4,128)S(1)}, u32[]{:S(2)}, u32[]{:S(2)}) collective-permute-start(f32[3,8]{1,0:T(4,128)S(1)} %pad_maximum_fusion.4), channel_id=1, source_target_pairs={{0,16},{4,20},{8,24},{12,28},{16,0},{20,4},{24,8},{28,12},{1,17},{... | collective-permute-start | bytes 296 | tf_op jit(solution)/shard_map/ppermute | solution.py:64
  (10 other events, 46.8 us)

commit v15 on v14

--- a/solution.py
+++ b/solution.py
@@ -34,6 +34,20 @@
     index = lax.axis_index(axis)
     bit = 1
     while bit < count:
+        other = lax.ppermute(x, axis, xor_pairs(count, bit))
+        low = (index & bit) == 0
+        x = jnp.where(
+            low, jnp.concatenate([x, other], dim), jnp.concatenate([other, x], dim)
+        )
+        bit *= 2
+    return x
+
+
+def butterfly_gather_below(x, axis, dim, stop):
+    count = lax.axis_size(axis)
+    index = lax.axis_index(axis)
+    bit = 1
+    while bit < stop:
         other = lax.ppermute(x, axis, xor_pairs(count, bit))
         low = (index & bit) == 0
         x = jnp.where(
@@ -244,12 +258,35 @@
     group_req = lax.axis_size("gx")
     holder = my_index == group_pos - 1
     last_local = jnp.where(holder, last_local, jnp.zeros_like(last_local))
-    last_mixed = butterfly_gather(butterfly_sum(last_local, "gy"), "gx", 0)
-    last_mixed, fresh_block = lax.optimization_barrier((last_mixed, fresh_block))
-    last_hidden = (
-        last_residual.astype(jnp.float32)
-        + jnp.dot(last_mixed, w_out, preferred_element_type=jnp.float32)
-    ).astype(jnp.bfloat16)
+    row_sum = butterfly_sum(last_local, "gy")
+    gx_count = lax.axis_size("gx")
+
+    def hidden_rows(mixed_rows, residual_rows):
+        return (
+            residual_rows.astype(jnp.float32)
+            + jnp.dot(mixed_rows, w_out, preferred_element_type=jnp.float32)
+        ).astype(jnp.bfloat16)
+
+    if is_pow2(gx_count) and gx_count > 1:
+        half_bit = gx_count // 2
+        held_rows = butterfly_gather_below(row_sum, "gx", 0, half_bit)
+        held_rows, fresh_block = lax.optimization_barrier((held_rows, fresh_block))
+        other_rows = lax.ppermute(held_rows, "gx", xor_pairs(gx_count, half_bit))
+        row_upper = (lax.axis_index("gx") & half_bit) != 0
+        row_half = held_rows.shape[0]
+        low_res = last_residual[:row_half]
+        high_res = last_residual[row_half:]
+        held_hidden = hidden_rows(held_rows, jnp.where(row_upper, high_res, low_res))
+        other_hidden = hidden_rows(other_rows, jnp.where(row_upper, low_res, high_res))
+        last_hidden = jnp.where(
+            row_upper,
+            jnp.concatenate([other_hidden, held_hidden], 0),
+            jnp.concatenate([held_hidden, other_hidden], 0),
+        )
+    else:
+        last_mixed = butterfly_gather(row_sum, "gx", 0)
+        last_mixed, fresh_block = lax.optimization_barrier((last_mixed, fresh_block))
+        last_hidden = hidden_rows(last_mixed, last_residual)
     full_hidden = butterfly_gather(butterfly_gather(last_hidden, "gy", 1), "gx", 1).astype(
         jnp.float32
     )

time: 116 us -> 116 us (level)
  waiting for transfers between devices: 30.3 us -> 28.4 us
    ppermute x0 -> x3, starting transfers between devices: none -> 5.81 us  [the longest x2 3.16 us: butterfly_gather_below(): other = lax.ppermute(x, axis, xor_pairs(count, bit))]
    ppermute x8 -> x5, starting transfers between devices: 10.8 us -> 5.28 us  [butterfly_gather(): other = lax.ppermute(x, axis, xor_pairs(count, bit))]
    select_n x7 -> x4, other arithmetic: 1.75 us -> 0.24 us  [butterfly_gather(): jnp.where(low, jnp.concatenate([x, other], dim), jnp.concatenate([other,...]
    ppermute x0 -> x3, waiting for transfers between devices: none -> 1.48 us  [the longest x1 1.13 us: on_device(): other_rows = lax.ppermute(held_rows, 'gx', xor_pairs(gx_count, half_bit))]
    ppermute x2, waiting for transfers between devices: 2.38 us -> 1.03 us  [butterfly_sum(): x = x + lax.ppermute(x, axis, xor_pairs(count, bit))]
    ppermute x8 -> x5, waiting for transfers between devices: 12.4 us -> 11.5 us  [butterfly_gather(): other = lax.ppermute(x, axis, xor_pairs(count, bit))]
  transfers between devices with their start and end apart: 21 -> 21, of which waited for: 16 -> 16; matrix products, arithmetic and copies ran while one was open for 17% -> 18% of each run, Pallas kernels for 0% -> 0%
where the time goes in v15:
time: 116 us; the launch traced here: 115 us
  waiting for transfers between devices  28.4 us (24%)
  starting transfers between devices  22.2 us (19%)
  matrix products  19.2 us (17%)
  other arithmetic  16.9 us (15%)
  Pallas kernels  16.1 us (14%)
  local copies, waits for them, and re-layouts  8.01 us (7%)
  between operations  4.63 us (4%)
    dot_general x1, matrix products, on_device(): lax.dot_general(normed, head, (((1,), (1,)), ((), ())), preferred_element...  17.2 us
    pallas_call x1, Pallas kernels, attend(): pl.pallas_call(kernel, grid=(req_local, head_count // stacked), in_specs=...  16.1 us
    ppermute x5, waiting for transfers between devices, butterfly_gather(): other = lax.ppermute(x, axis, xor_pairs(count, bit))  11.5 us
    ppermute x5, waiting for transfers between devices, butterfly_stats(): other = lax.ppermute(packed, axis, xor_pairs(count, bit))  11.2 us
    ppermute x5, starting transfers between devices, butterfly_stats(): other = lax.ppermute(packed, axis, xor_pairs(count, bit))  5.53 us
    ppermute x5, starting transfers between devices, butterfly_gather(): other = lax.ppermute(x, axis, xor_pairs(count, bit))  5.28 us
    ppermute x2, starting transfers between devices, exchange_pieces(): other = lax.ppermute(held, axis, xor_pairs(count, bit))  3.16 us
    ppermute x2, starting transfers between devices, butterfly_gather_below(): other = lax.ppermute(x, axis, xor_pairs(count, bit))  3.16 us
  transfers between devices with their start and end apart: 21, of which 16 were waited for; matrix products, arithmetic and copies ran while one was open for 18% of the time, Pallas kernels for 0%

profile of v15, /device:TPU:0, one launch (start us, length us, event | category | flops | bytes accessed | tf_op | source)
XLA Modules:
  0.0 115.3 jit_solution(5848727645439720191)
XLA Ops:
  0.6 3.0 %collective-permute-start.1 = (bf16[1,512,512]{2,1,0:T(8,128)(2,1)}, bf16[1,512,512]{2,1,0:T(8,128)(2,1)S(1)}, u32[]{:S(2)}, u32[]{:S(2)}) collective-permute-start(bf16[1,512,512]{2,1,0:T(8,128)(2,1)} %refs_10_.1), channel_id=1, source_target_pairs={{0,2},{1,3},{2,0},{3,1},{4,6},{5,7},{6,4},{7,5},{8,10},{9,11},{10,... | collective-permute-start | bytes 1572872 | tf_op jit(solution)/shard_map/ppermute | solution.py:95
  10.8 2.6 %compare_select_fusion.3 = (s32[512,1]{0,1:T(1,128)S(1)}, s32[1,512]{1,0:T(1,128)S(1)}, s32[512,1]{0,1:T(1,128)S(1)}) fusion(s32[]{:T(128)} %axis_index.14, s32[]{:T(128)} %bitcast.20, s32[]{:T(128)} %bitcast.19, s32[]{:T(128)} %bitcast.18, s32[]{:T(128)} %bitcast.17, s32[]{:T(128)} %bitcast.16), kind=kLoop, calls=%fused_computation.31 | loop fusion | flops 55296 | bytes 6168 | tf_op jit(solution)/shard_map/jit(take_along_axis)/select_n | solution.py:253
  17.8 2.2 %collective-permute-done.4.refs_23_.refs_24_ = bf16[1,192,512]{2,1,0:T(8,128)(2,1)S(1)} collective-permute-done((bf16[1,192,512]{2,1,0:T(8,128)(2,1)}, bf16[1,192,512]{2,1,0:T(8,128)(2,1)S(1)}, u32[]{:S(2)}, u32[]{:S(2)}) %collective-permute-start.4) | collective-permute-done | bytes 196640 | tf_op jit(solution)/shard_map/ppermute | solution.py:95
  22.5 16.1 %shard_map.230 = bf16[1,192,2560]{2,1,0:T(8,128)(2,1)} custom-call(s32[192,1]{1,0:T(8,128)} %iota_add_fusion.qpos_ref, s32[1,1,512]{2,1,0:T(1,128)} %get-tuple-element.88.refs_0_, s32[1,1,512]{2,1,0:T(1,128)} %get-tuple-element.87.refs_1_, s32[1,1,512]{2,1,0:T(1,128)} %get-tuple-element.86.refs_2_, s32[1,1,512]{2,1,0:T(1,128)} %get-tuple-element.85.refs_3_, ...), custom_call_target="tpu_custom_call" | custom-call | tf_op jit(solution)/shard_map/pallas_call | solution.py:182
  41.4 1.8 %collective-permute-start.7 = (bf16[1,2560]{1,0:T(2,128)(2,1)S(1)}, bf16[1,2560]{1,0:T(2,128)(2,1)S(1)}, u32[]{:S(2)}, u32[]{:S(2)}) collective-permute-start(bf16[1,2560]{1,0:T(2,128)(2,1)S(1)} %fusion.44), channel_id=1, source_target_pairs={{0,2},{1,3},{2,0},{3,1},{4,6},{5,7},{6,4},{7,5},{8,10},{9,11},{10,... | collective-permute-start | bytes 15368 | tf_op jit(solution)/shard_map/ppermute | solution.py:25
  44.4 2.6 %gather_fusion.1 = bf16[512,512]{1,0:T(8,128)(2,1)} fusion(bf16[768,512]{1,0:T(8,128)(2,1)S(1)} %maximum_bitcast_fusion.1, s32[1024]{0:T(1024)S(1)} %pad_clamp_fusion), kind=kCustom, calls=%fused_computation.1 | custom fusion | bytes 1050624 | tf_op jit(solution)/shard_map/jit(take_along_axis)/gather | solution.py:254
  47.7 1.5 %collective-permute-start.8 = (bf16[1,2560]{1,0:T(2,128)(2,1)}, bf16[1,2560]{1,0:T(2,128)(2,1)}, u32[]{:S(2)}, u32[]{:S(2)}) collective-permute-start(bf16[1,2560]{1,0:T(2,128)(2,1)} %add.591), channel_id=1, source_target_pairs={{0,4},{4,0},{8,12},{12,8},{16,20},{20,16},{24,28},{28,24},{1,5},{5... | collective-permute-start | bytes 15368 | tf_op jit(solution)/shard_map/ppermute | solution.py:51
  50.5 2.2 %gather_fusion = bf16[512,512]{1,0:T(8,128)(2,1)S(1)} fusion(bf16[2048,512]{1,0:T(8,128)(2,1)S(1)} %maximum_bitcast_fusion, s32[1024]{0:T(1024)} %pad_clamp_fusion.1), kind=kCustom, calls=%fused_computation | custom fusion | bytes 1050624 | tf_op jit(solution)/shard_map/jit(take_along_axis)/gather | solution.py:253
  53.7 1.6 %collective-permute-start.9 = (bf16[2,2560]{1,0:T(2,128)(2,1)S(1)}, bf16[2,2560]{1,0:T(2,128)(2,1)S(1)}, u32[]{:S(2)}, u32[]{:S(2)}) collective-permute-start(bf16[2,2560]{1,0:T(2,128)(2,1)S(1)} %broadcast_select_fusion.1), channel_id=1, source_target_pairs={{0,8},{4,12},{8,0},{12,4},{16,24},{20,28},{24,16},{28,20},{1,9},{5... | collective-permute-start | bytes 30728 | tf_op jit(solution)/shard_map/ppermute | solution.py:51
  55.3 1.7 %fusion.2 = bf16[1,512,512]{2,1,0:T(8,128)(2,1)} fusion(bf16[512,512]{1,0:T(8,128)(2,1)S(1)} %copy-done.6, bf16[512,512]{1,0:T(8,128)(2,1)S(1)} %gather_fusion, pred[512]{0:T(512)(128)(4,1)} %get-tuple-element.94, pred[512]{0:T(512)(128)(4,1)} %compare_and_fusion.1, pred[512]{0:T(512)(128)(4,1)} %get-tuple-element.93), kind=kLoop, calls=%fused_computation.9 | loop fusion | flops 786432 | bytes 1574400 | tf_op jit(solution)/shard_map/jit(_where)/select_n | solution.py:255
  57.4 2.7 %collective-permute-start.10 = (bf16[4,2560]{1,0:T(4,128)(2,1)S(1)}, bf16[4,2560]{1,0:T(4,128)(2,1)S(1)}, u32[]{:S(2)}, u32[]{:S(2)}) collective-permute-start(bf16[4,2560]{1,0:T(4,128)(2,1)S(1)} %maximum_select_fusion.1), channel_id=1, source_target_pairs={{0,16},{4,20},{8,24},{12,28},{16,0},{20,4},{24,8},{28,12},{1,17},{... | collective-permute-start | bytes 61448 | tf_op jit(solution)/shard_map/ppermute | solution.py:274
  65.0 3.1 %collective-permute-done.12 = bf16[8,160]{1,0:T(8,128)(2,1)S(1)} collective-permute-done((bf16[8,160]{1,0:T(8,128)(2,1)S(1)}, bf16[8,160]{1,0:T(8,128)(2,1)S(1)}, u32[]{:S(2)}, u32[]{:S(2)}) %collective-permute-start.12) | collective-permute-done | bytes 2592 | tf_op jit(solution)/shard_map/ppermute | solution.py:37
  68.7 3.1 %collective-permute-done.13 = bf16[8,320]{1,0:T(8,128)(2,1)S(1)} collective-permute-done((bf16[8,320]{1,0:T(8,128)(2,1)S(1)}, bf16[8,320]{1,0:T(8,128)(2,1)S(1)}, u32[]{:S(2)}, u32[]{:S(2)}) %collective-permute-start.13) | collective-permute-done | bytes 5152 | tf_op jit(solution)/shard_map/ppermute | solution.py:37
  71.9 1.6 %collective-permute-start.14 = (bf16[8,640]{1,0:T(8,128)(2,1)S(1)}, bf16[8,640]{1,0:T(8,128)(2,1)S(1)}, u32[]{:S(2)}, u32[]{:S(2)}) collective-permute-start(bf16[8,640]{1,0:T(8,128)(2,1)S(1)} %maximum_select_fusion.3), channel_id=1, source_target_pairs={{0,8},{4,12},{8,0},{12,4},{16,24},{20,28},{24,16},{28,20},{1,9},{5... | collective-permute-start | bytes 30728 | tf_op jit(solution)/shard_map/ppermute | solution.py:37
  73.5 2.1 %collective-permute-done.14 = bf16[8,640]{1,0:T(8,128)(2,1)S(1)} collective-permute-done((bf16[8,640]{1,0:T(8,128)(2,1)S(1)}, bf16[8,640]{1,0:T(8,128)(2,1)S(1)}, u32[]{:S(2)}, u32[]{:S(2)}) %collective-permute-start.14) | collective-permute-done | bytes 10272 | tf_op jit(solution)/shard_map/ppermute | solution.py:37
  75.6 2.6 %collective-permute-start.15 = (bf16[8,1280]{1,0:T(8,128)(2,1)S(1)}, bf16[8,1280]{1,0:T(8,128)(2,1)S(1)}, u32[]{:S(2)}, u32[]{:S(2)}) collective-permute-start(bf16[8,1280]{1,0:T(8,128)(2,1)S(1)} %maximum_select_fusion.2), channel_id=1, source_target_pairs={{0,16},{4,20},{8,24},{12,28},{16,0},{20,4},{24,8},{28,12},{1,17},{... | collective-permute-start | bytes 61448 | tf_op jit(solution)/shard_map/ppermute | solution.py:37
  78.2 2.1 %collective-permute-done.15 = bf16[8,1280]{1,0:T(8,128)(2,1)S(1)} collective-permute-done((bf16[8,1280]{1,0:T(8,128)(2,1)S(1)}, bf16[8,1280]{1,0:T(8,128)(2,1)S(1)}, u32[]{:S(2)}, u32[]{:S(2)}) %collective-permute-start.15) | collective-permute-done | bytes 20512 | tf_op jit(solution)/shard_map/ppermute | solution.py:37
  80.4 17.2 %fusion.38 = (f32[8]{0:T(128)S(1)}, f32[8,8000]{1,0:T(8,128)S(1)}) fusion(bf16[8000,2560]{1,0:T(8,128)(2,1)} %param.30, f32[2560]{0:T(1024)S(1)} %convert_element_type.26, f32[8]{0:T(128)S(1)} %add_rsqrt_fusion, bf16[8,1280]{1,0:T(8,128)(2,1)S(1)} %maximum_select_fusion.2, bf16[8,1280]{1,0:T(8,128)(2,1)S(1)} %collective-permute-done.15, pred[]{:T(512)S(6)} %eq.63), kind=kOutput, calls=%fused_computation.144 | convolution fusion | flops 328010240 | bytes 41267264 | tf_op jit(solution)/shard_map/dot_general | solution.py:298
  99.8 3.1 %collective-permute-done.17 = f32[3,8]{1,0:T(4,128)S(1)} collective-permute-done((f32[3,8]{1,0:T(4,128)S(1)}, f32[3,8]{1,0:T(4,128)S(1)}, u32[]{:S(2)}, u32[]{:S(2)}) %collective-permute-start.17) | collective-permute-done | bytes 128 | tf_op jit(solution)/shard_map/ppermute | solution.py:78
  103.4 3.1 %collective-permute-done.18 = f32[3,8]{1,0:T(4,128)S(1)} collective-permute-done((f32[3,8]{1,0:T(4,128)S(1)}, f32[3,8]{1,0:T(4,128)S(1)}, u32[]{:S(2)}, u32[]{:S(2)}) %collective-permute-start.18) | collective-permute-done | bytes 128 | tf_op jit(solution)/shard_map/ppermute | solution.py:78
  106.5 1.6 %collective-permute-start.19 = (f32[3,8]{1,0:T(4,128)S(1)}, f32[3,8]{1,0:T(4,128)S(1)}, u32[]{:S(2)}, u32[]{:S(2)}) collective-permute-start(f32[3,8]{1,0:T(4,128)S(1)} %pad_maximum_fusion.3), channel_id=1, source_target_pairs={{0,8},{4,12},{8,0},{12,4},{16,24},{20,28},{24,16},{28,20},{1,9},{5... | collective-permute-start | bytes 296 | tf_op jit(solution)/shard_map/ppermute | solution.py:78
  108.2 2.0 %collective-permute-done.19 = f32[3,8]{1,0:T(4,128)S(1)} collective-permute-done((f32[3,8]{1,0:T(4,128)S(1)}, f32[3,8]{1,0:T(4,128)S(1)}, u32[]{:S(2)}, u32[]{:S(2)}) %collective-permute-start.19) | collective-permute-done | bytes 128 | tf_op jit(solution)/shard_map/ppermute | solution.py:78
  110.2 2.7 %collective-permute-start.20 = (f32[3,8]{1,0:T(4,128)S(1)}, f32[3,8]{1,0:T(4,128)S(1)}, u32[]{:S(2)}, u32[]{:S(2)}) collective-permute-start(f32[3,8]{1,0:T(4,128)S(1)} %pad_maximum_fusion.4), channel_id=1, source_target_pairs={{0,16},{4,20},{8,24},{12,28},{16,0},{20,4},{24,8},{28,12},{1,17},{... | collective-permute-start | bytes 296 | tf_op jit(solution)/shard_map/ppermute | solution.py:78
  112.9 1.9 %collective-permute-done.20 = f32[3,8]{1,0:T(4,128)S(1)} collective-permute-done((f32[3,8]{1,0:T(4,128)S(1)}, f32[3,8]{1,0:T(4,128)S(1)}, u32[]{:S(2)}, u32[]{:S(2)}) %collective-permute-start.20) | collective-permute-done | bytes 128 | tf_op jit(solution)/shard_map/ppermute | solution.py:78
  (92 shorter events, 26.5 us)
Async XLA Ops:
  0.6 59.5 %copy-start = (bf16[2560,80]{0,1:T(8,128)(2,1)S(1)}, bf16[2560,80]{0,1:T(8,128)(2,1)}, u32[]{:S(2)}) copy-start(bf16[2560,80]{0,1:T(8,128)(2,1)} %param.27) | copy-start | bytes 1228804
  0.6 16.0 %collective-permute-start.1 = (bf16[1,512,512]{2,1,0:T(8,128)(2,1)}, bf16[1,512,512]{2,1,0:T(8,128)(2,1)S(1)}, u32[]{:S(2)}, u32[]{:S(2)}) collective-permute-start(bf16[1,512,512]{2,1,0:T(8,128)(2,1)} %refs_10_.1), channel_id=1, source_target_pairs={{0,2},{1,3},{2,0},{3,1},{4,6},{5,7},{6,4},{7,5},{8,10},{9,11},{10,... | collective-permute-start | bytes 1572872 | tf_op jit(solution)/shard_map/ppermute | solution.py:95
  3.6 17.8 %collective-permute-start = (bf16[1,512,512]{2,1,0:T(8,128)(2,1)}, bf16[1,512,512]{2,1,0:T(8,128)(2,1)S(1)}, u32[]{:S(2)}, u32[]{:S(2)}) collective-permute-start(bf16[1,512,512]{2,1,0:T(8,128)(2,1)} %refs_10_.1), channel_id=1, source_target_pairs={{0,1},{1,0},{2,3},{3,2},{4,5},{5,4},{6,7},{7,6},{8,9},{9,8},{10,11... | collective-permute-start | bytes 1572872 | tf_op jit(solution)/shard_map/ppermute | solution.py:91
  3.7 16.3 %collective-permute-start.4 = (bf16[1,192,512]{2,1,0:T(8,128)(2,1)}, bf16[1,192,512]{2,1,0:T(8,128)(2,1)S(1)}, u32[]{:S(2)}, u32[]{:S(2)}) collective-permute-start(bf16[1,192,512]{2,1,0:T(8,128)(2,1)} %refs_18_.1), channel_id=1, source_target_pairs={{0,2},{1,3},{2,0},{3,1},{4,6},{5,7},{6,4},{7,5},{8,10},{9,11},{10,... | collective-permute-start | bytes 589832 | tf_op jit(solution)/shard_map/ppermute | solution.py:95
  3.8 16.8 %collective-permute-start.3 = (bf16[1,192,512]{2,1,0:T(8,128)(2,1)}, bf16[1,192,512]{2,1,0:T(8,128)(2,1)S(1)}, u32[]{:S(2)}, u32[]{:S(2)}) collective-permute-start(bf16[1,192,512]{2,1,0:T(8,128)(2,1)} %refs_18_.1), channel_id=1, source_target_pairs={{0,1},{1,0},{2,3},{3,2},{4,5},{5,4},{6,7},{7,6},{8,9},{9,8},{10,11... | collective-permute-start | bytes 589832 | tf_op jit(solution)/shard_map/ppermute | solution.py:91
  16.6 4.8 %collective-permute-start.2 = (bf16[1,512,512]{2,1,0:T(8,128)(2,1)S(1)}, bf16[1,512,512]{2,1,0:T(8,128)(2,1)S(1)}, u32[]{:S(2)}, u32[]{:S(2)}) collective-permute-start(bf16[1,512,512]{2,1,0:T(8,128)(2,1)S(1)} %collective-permute-done.1.refs_15_.refs_16_), channel_id=1, source_target_pairs={{0,1},{1,0},{2,3},{3,2},{4,5},{5,4},{6,7},{7,6},{8,9},{9,8},{10,11... | collective-permute-start | bytes 1572872 | tf_op jit(solution)/shard_map/ppermute | solution.py:105
  20.0 1.4 %collective-permute-start.5 = (bf16[1,192,512]{2,1,0:T(8,128)(2,1)S(1)}, bf16[1,192,512]{2,1,0:T(8,128)(2,1)S(1)}, u32[]{:S(2)}, u32[]{:S(2)}) collective-permute-start(bf16[1,192,512]{2,1,0:T(8,128)(2,1)S(1)} %collective-permute-done.4.refs_23_.refs_24_), channel_id=1, source_target_pairs={{0,1},{1,0},{2,3},{3,2},{4,5},{5,4},{6,7},{7,6},{8,9},{9,8},{10,11... | collective-permute-start | bytes 589832 | tf_op jit(solution)/shard_map/ppermute | solution.py:105
  39.4 1.2 %collective-permute-start.6 = (bf16[1,2560]{1,0:T(2,128)(2,1)S(1)}, bf16[1,2560]{1,0:T(2,128)(2,1)S(1)}, u32[]{:S(2)}, u32[]{:S(2)}) collective-permute-start(bf16[1,2560]{1,0:T(2,128)(2,1)S(1)} %fusion.10), channel_id=1, source_target_pairs={{0,1},{1,0},{2,3},{3,2},{4,5},{5,4},{6,7},{7,6},{8,9},{9,8},{10,11... | collective-permute-start | bytes 15368 | tf_op jit(solution)/shard_map/ppermute | solution.py:25
  41.4 5.6 %collective-permute-start.7 = (bf16[1,2560]{1,0:T(2,128)(2,1)S(1)}, bf16[1,2560]{1,0:T(2,128)(2,1)S(1)}, u32[]{:S(2)}, u32[]{:S(2)}) collective-permute-start(bf16[1,2560]{1,0:T(2,128)(2,1)S(1)} %fusion.44), channel_id=1, source_target_pairs={{0,2},{1,3},{2,0},{3,1},{4,6},{5,7},{6,4},{7,5},{8,10},{9,11},{10,... | collective-permute-start | bytes 15368 | tf_op jit(solution)/shard_map/ppermute | solution.py:25
  47.7 5.2 %collective-permute-start.8 = (bf16[1,2560]{1,0:T(2,128)(2,1)}, bf16[1,2560]{1,0:T(2,128)(2,1)}, u32[]{:S(2)}, u32[]{:S(2)}) collective-permute-start(bf16[1,2560]{1,0:T(2,128)(2,1)} %add.591), channel_id=1, source_target_pairs={{0,4},{4,0},{8,12},{12,8},{16,20},{20,16},{24,28},{28,24},{1,5},{5... | collective-permute-start | bytes 15368 | tf_op jit(solution)/shard_map/ppermute | solution.py:51
  52.8 25.4 %copy-start.12 = (s32[8]{0:T(128)S(1)}, s32[8]{0:T(128)}, u32[]{:S(2)}) copy-start(s32[8]{0:T(128)} %param.31) | copy-start | bytes 100
  52.8 25.4 %copy-start.11 = (bf16[2560]{0:T(1024)(128)(2,1)S(1)}, bf16[2560]{0:T(1024)(128)(2,1)}, u32[]{:S(2)}) copy-start(bf16[2560]{0:T(1024)(128)(2,1)} %param.29) | copy-start | bytes 15364
  53.7 3.7 %collective-permute-start.9 = (bf16[2,2560]{1,0:T(2,128)(2,1)S(1)}, bf16[2,2560]{1,0:T(2,128)(2,1)S(1)}, u32[]{:S(2)}, u32[]{:S(2)}) collective-permute-start(bf16[2,2560]{1,0:T(2,128)(2,1)S(1)} %broadcast_select_fusion.1), channel_id=1, source_target_pairs={{0,8},{4,12},{8,0},{12,4},{16,24},{20,28},{24,16},{28,20},{1,9},{5... | collective-permute-start | bytes 30728 | tf_op jit(solution)/shard_map/ppermute | solution.py:51
  57.4 4.7 %collective-permute-start.10 = (bf16[4,2560]{1,0:T(4,128)(2,1)S(1)}, bf16[4,2560]{1,0:T(4,128)(2,1)S(1)}, u32[]{:S(2)}, u32[]{:S(2)}) collective-permute-start(bf16[4,2560]{1,0:T(4,128)(2,1)S(1)} %maximum_select_fusion.1), channel_id=1, source_target_pairs={{0,16},{4,20},{8,24},{12,28},{16,0},{20,4},{24,8},{28,12},{1,17},{... | collective-permute-start | bytes 61448 | tf_op jit(solution)/shard_map/ppermute | solution.py:274
  63.2 1.2 %collective-permute-start.11 = (bf16[8,80]{1,0:T(8,128)(2,1)S(1)}, bf16[8,80]{1,0:T(8,128)(2,1)S(1)}, u32[]{:S(2)}, u32[]{:S(2)}) collective-permute-start(bf16[8,80]{1,0:T(8,128)(2,1)S(1)} %maximum_select_fusion.7), channel_id=1, source_target_pairs={{0,1},{1,0},{2,3},{3,2},{4,5},{5,4},{6,7},{7,6},{8,9},{9,8},{10,11... | collective-permute-start | bytes 3848 | tf_op jit(solution)/shard_map/ppermute | solution.py:37
  64.5 3.6 %collective-permute-start.12 = (bf16[8,160]{1,0:T(8,128)(2,1)S(1)}, bf16[8,160]{1,0:T(8,128)(2,1)S(1)}, u32[]{:S(2)}, u32[]{:S(2)}) collective-permute-start(bf16[8,160]{1,0:T(8,128)(2,1)S(1)} %maximum_select_fusion.6), channel_id=1, source_target_pairs={{0,2},{1,3},{2,0},{3,1},{4,6},{5,7},{6,4},{7,5},{8,10},{9,11},{10,... | collective-permute-start | bytes 7688 | tf_op jit(solution)/shard_map/ppermute | solution.py:37
  68.2 3.6 %collective-permute-start.13 = (bf16[8,320]{1,0:T(8,128)(2,1)S(1)}, bf16[8,320]{1,0:T(8,128)(2,1)S(1)}, u32[]{:S(2)}, u32[]{:S(2)}) collective-permute-start(bf16[8,320]{1,0:T(8,128)(2,1)S(1)} %maximum_select_fusion.5), channel_id=1, source_target_pairs={{0,4},{4,0},{8,12},{12,8},{16,20},{20,16},{24,28},{28,24},{1,5},{5... | collective-permute-start | bytes 15368 | tf_op jit(solution)/shard_map/ppermute | solution.py:37
  71.9 3.7 %collective-permute-start.14 = (bf16[8,640]{1,0:T(8,128)(2,1)S(1)}, bf16[8,640]{1,0:T(8,128)(2,1)S(1)}, u32[]{:S(2)}, u32[]{:S(2)}) collective-permute-start(bf16[8,640]{1,0:T(8,128)(2,1)S(1)} %maximum_select_fusion.3), channel_id=1, source_target_pairs={{0,8},{4,12},{8,0},{12,4},{16,24},{20,28},{24,16},{28,20},{1,9},{5... | collective-permute-start | bytes 30728 | tf_op jit(solution)/shard_map/ppermute | solution.py:37
  75.6 4.7 %collective-permute-start.15 = (bf16[8,1280]{1,0:T(8,128)(2,1)S(1)}, bf16[8,1280]{1,0:T(8,128)(2,1)S(1)}, u32[]{:S(2)}, u32[]{:S(2)}) collective-permute-start(bf16[8,1280]{1,0:T(8,128)(2,1)S(1)} %maximum_select_fusion.2), channel_id=1, source_target_pairs={{0,16},{4,20},{8,24},{12,28},{16,0},{20,4},{24,8},{28,12},{1,17},{... | collective-permute-start | bytes 61448 | tf_op jit(solution)/shard_map/ppermute | solution.py:37
  97.9 1.2 %collective-permute-start.16 = (f32[3,8]{1,0:T(4,128)S(1)}, f32[3,8]{1,0:T(4,128)S(1)}, u32[]{:S(2)}, u32[]{:S(2)}) collective-permute-start(f32[3,8]{1,0:T(4,128)S(1)} %pad_maximum_fusion), channel_id=1, source_target_pairs={{0,1},{1,0},{2,3},{3,2},{4,5},{5,4},{6,7},{7,6},{8,9},{9,8},{10,11... | collective-permute-start | bytes 296 | tf_op jit(solution)/shard_map/ppermute | solution.py:78
  99.2 3.7 %collective-permute-start.17 = (f32[3,8]{1,0:T(4,128)S(1)}, f32[3,8]{1,0:T(4,128)S(1)}, u32[]{:S(2)}, u32[]{:S(2)}) collective-permute-start(f32[3,8]{1,0:T(4,128)S(1)} %pad_maximum_fusion.1), channel_id=1, source_target_pairs={{0,2},{1,3},{2,0},{3,1},{4,6},{5,7},{6,4},{7,5},{8,10},{9,11},{10,... | collective-permute-start | bytes 296 | tf_op jit(solution)/shard_map/ppermute | solution.py:78
  102.9 3.7 %collective-permute-start.18 = (f32[3,8]{1,0:T(4,128)S(1)}, f32[3,8]{1,0:T(4,128)S(1)}, u32[]{:S(2)}, u32[]{:S(2)}) collective-permute-start(f32[3,8]{1,0:T(4,128)S(1)} %pad_maximum_fusion.2), channel_id=1, source_target_pairs={{0,4},{4,0},{8,12},{12,8},{16,20},{20,16},{24,28},{28,24},{1,5},{5... | collective-permute-start | bytes 296 | tf_op jit(solution)/shard_map/ppermute | solution.py:78
  106.5 3.7 %collective-permute-start.19 = (f32[3,8]{1,0:T(4,128)S(1)}, f32[3,8]{1,0:T(4,128)S(1)}, u32[]{:S(2)}, u32[]{:S(2)}) collective-permute-start(f32[3,8]{1,0:T(4,128)S(1)} %pad_maximum_fusion.3), channel_id=1, source_target_pairs={{0,8},{4,12},{8,0},{12,4},{16,24},{20,28},{24,16},{28,20},{1,9},{5... | collective-permute-start | bytes 296 | tf_op jit(solution)/shard_map/ppermute | solution.py:78
  110.2 4.5 %collective-permute-start.20 = (f32[3,8]{1,0:T(4,128)S(1)}, f32[3,8]{1,0:T(4,128)S(1)}, u32[]{:S(2)}, u32[]{:S(2)}) collective-permute-start(f32[3,8]{1,0:T(4,128)S(1)} %pad_maximum_fusion.4), channel_id=1, source_target_pairs={{0,16},{4,20},{8,24},{12,28},{16,0},{20,4},{24,8},{28,12},{1,17},{... | collective-permute-start | bytes 296 | tf_op jit(solution)/shard_map/ppermute | solution.py:78
  (10 other events, 44.8 us)
